TPU v7x, 1024 devices: a whole 8x8x8 slice. The times are simulated.
1024 devices in a mesh: leaf: 64 (over x, y), sub: 16 (over z, core).
Axes of the slice: x: 8, y: 8, z: 8, core: 2. Of those that a mesh axis runs over, the one named last changes fastest.
Arguments:
- p_dirs: float32 [16, 2097152], P(None, ('leaf', 'sub')), may hold values from -6 to 6
- resid: float32 [16, 2097152], P(None, ('leaf', 'sub')), may hold values from -6 to 6
- perm: int32 [1024, 2048], P(('leaf', 'sub')), may hold values from 0 to 2047, each once within a row
- col_basis: bfloat16 [32768, 64, 32], P(('leaf', 'sub')), may hold values from -0.75 to 0.75
- row_basis: bfloat16 [32768, 64, 32], P(('leaf', 'sub')), may hold values from -0.25 to 0.25
- near_blocks: bfloat16 [32768, 6, 4096], P(('leaf', 'sub')), may hold values from -0.3125 to 0.3125
- near_scale: float32 [32768, 6], P(('leaf', 'sub')), may hold values from 0.3 to 3
- near_index: int32 [32768, 6], P(('leaf', 'sub')), may hold values from 0 to 96, as said below
- far_blocks: bfloat16 [32768, 6, 1024], P(('leaf', 'sub')), may hold values from -0.4375 to 0.4375
- far_scale: float32 [32768, 6], P(('leaf', 'sub')), may hold values from 0.3 to 3
- far_index: int32 [32768, 6], P(('leaf', 'sub')), may hold values from 0 to 96, as said below
- loc_col: bfloat16 [1024, 62, 32, 32], P(('leaf', 'sub')), may hold values from -0.084852814 to 0.804852814
- loc_row: bfloat16 [1024, 62, 32, 32], P(('leaf', 'sub')), may hold values from -0.11844038584874671 to 1.1284404
- up_col: float32 [2, 32, 32], replicated, may hold values from -0.084852814 to 0.804852814
- up_row: float32 [2, 32, 32], replicated, may hold values from -0.11844038584874671 to 1.1284404
- up_cpl: float32 [2, 32, 32], replicated, may hold values from -1 to 1
Outputs:
- p_image: float32 [16, 2097152], P(None, ('leaf', 'sub'))
- r_image: float32 [16, 2097152], P(None, ('leaf', 'sub'))
Inputs may be any that keep to these rules, and one draw needn't show every extreme that they name: `perm`: each row names every number once. `near_index`: slot 0 of leaf g's list names the leaf itself, 32 + g mod 32. Live slots come first; every list has two or more, and the rest hold 96. `far_index`: live slots come first; every list has two or more, and the rest hold 96.
All inputs are finite; a program needn't handle non-finite values.
Results may differ from a plain program's by a relative error of at most 0.0039.
Values may be sent and summed in bfloat16 or wider, within the bound.
No kernel may reach another device: no remote copies, remote signals or barrier semaphores. Data moves between devices by JAX's collectives and lax.ppermute only.
A program may use at most 128 MiB of HBM per device.

v0:
```python
import jax
import jax.numpy as jnp
from jax import lax
from jax.sharding import PartitionSpec as P

best_precision = lax.Precision.HIGHEST


def from_partner(value, axis, distance):
    mask = 2**distance
    pairs = [(source, source ^ mask) for source in range(lax.axis_size(axis))]
    return lax.ppermute(value, axis, pairs)


def extended(block, sides, width):
    for axis, dim in sides:
        count = lax.axis_size(axis)
        forward = [(i, i + 1) for i in range(count - 1)]
        backward = [(target, source) for source, target in forward]
        low = lax.ppermute(
            lax.slice_in_dim(block, block.shape[dim] - width, None, axis=dim), axis, forward
        )
        high = lax.ppermute(lax.slice_in_dim(block, 0, width, axis=dim), axis, backward)
        block = jnp.concatenate([low, block, high], axis=dim)
    return block


def apply_up(matrix, coeffs):
    return jnp.einsum("...ab,...ac->...bc", matrix, coeffs, precision=best_precision)


def apply_down(matrix, coeffs):
    return jnp.einsum("...ab,...bc->...ac", matrix, coeffs, precision=best_precision)


def shards(
    p_dirs,
    resid,
    perm,
    col_basis,
    row_basis,
    near_blocks,
    near_scale,
    near_index,
    far_blocks,
    far_scale,
    far_index,
    loc_col,
    loc_row,
    up_col,
    up_row,
    up_cpl,
):
    leaves_dev, leaf_size, rank_width = col_basis.shape
    near_square = near_blocks.reshape(leaves_dev, near_blocks.shape[1], leaf_size, leaf_size)
    far_square = far_blocks.reshape(leaves_dev, far_blocks.shape[1], rank_width, rank_width)
    order_row = perm[0]
    col_local = loc_col[0].astype(jnp.float32)
    row_local = loc_row[0].astype(jnp.float32)
    sub_bits = lax.axis_size("sub").bit_length() - 1
    leaf_bits = lax.axis_size("leaf").bit_length() - 1
    sub_pos = lax.axis_index("sub")
    leaf_pos = lax.axis_index("leaf")

    def combine_pair(left_part, right_part):
        return apply_up(up_col[0], left_part) + apply_up(up_col[1], right_part)

    def merge_side(current, sibling, side_bit):
        left_part = jnp.where(side_bit == 1, sibling, current)
        right_part = jnp.where(side_bit == 1, current, sibling)
        return combine_pair(left_part, right_part)

    def leaf_bit_levels(current, records):
        for bit_num in range(leaf_bits):
            sibling = from_partner(current, "leaf", bit_num)
            side_bit = leaf_pos >> bit_num & 1
            records.append((sibling, side_bit))
            if bit_num + 1 < leaf_bits:
                current = merge_side(current, sibling, side_bit)
        return records

    def climb_tree(root_coeff):
        records = []
        current = root_coeff
        for bit_num in range(sub_bits):
            sibling = from_partner(current, "sub", bit_num)
            side_bit = sub_pos >> bit_num & 1
            records.append((sibling, side_bit))
            current = merge_side(current, sibling, side_bit)
        return leaf_bit_levels(current, records)

    def descend_tree(records, columns):
        field_now = jnp.zeros((rank_width, columns), jnp.float32)
        for sibling, side_bit in reversed(records):
            row_pick = lax.dynamic_index_in_dim(up_row, side_bit, 0, keepdims=False)
            cpl_pick = lax.dynamic_index_in_dim(up_cpl, side_bit, 0, keepdims=False)
            field_now = apply_down(row_pick, field_now) + apply_down(cpl_pick, sibling)
        return field_now

    def apply_image(vectors):
        columns = vectors.shape[0]
        ordered = jnp.take(vectors, order_row, axis=1).astype(jnp.bfloat16)
        leaf_blocks = ordered.reshape(columns, leaves_dev, leaf_size)
        x_window = extended(leaf_blocks, (("sub", 1),), leaves_dev)
        leaf_coeff = jnp.einsum(
            "clp,lpk->lkc", leaf_blocks, col_basis, preferred_element_type=jnp.float32
        )
        leaf_round = leaf_coeff.astype(jnp.bfloat16)
        coeff_window = extended(leaf_round, (("sub", 0),), leaves_dev)
        current = leaf_coeff
        offsets = []
        start_at = 0
        while current.shape[0] > 1:
            node_count = current.shape[0]
            moved_up = apply_up(col_local[start_at : start_at + node_count], current)
            paired = moved_up.reshape(node_count // 2, 2, rank_width, columns)
            current = paired[:, 0] + paired[:, 1]
            offsets.append(start_at)
            start_at = start_at + node_count
        records = climb_tree(current[0])
        local_field = descend_tree(records, columns)[None]
        for start_at in reversed(offsets):
            node_count = local_field.shape[0] * 2
            local_field = apply_down(
                row_local[start_at : start_at + node_count], jnp.repeat(local_field, 2, axis=0)
            )
        width_all = 3 * leaves_dev
        far_live = far_index < width_all
        far_safe = jnp.minimum(far_index, width_all - 1)
        picked = coeff_window[far_safe]
        far_terms = jnp.einsum(
            "lkab,lkbc->lkac", far_square, picked, preferred_element_type=jnp.float32
        )
        far_weight = jnp.where(far_live, far_scale, jnp.zeros_like(far_scale))
        leaf_field = local_field + jnp.einsum(
            "lkac,lk->lac", far_terms, far_weight, precision=best_precision
        )
        field_round = leaf_field.astype(jnp.bfloat16)
        far_out = jnp.einsum(
            "lpk,lkc->clp", row_basis, field_round, preferred_element_type=jnp.float32
        )
        near_live = near_index < width_all
        near_safe = jnp.minimum(near_index, width_all - 1)
        near_pick = x_window[:, near_safe]
        near_terms = jnp.einsum(
            "lkpq,clkq->clkp", near_square, near_pick, preferred_element_type=jnp.float32
        )
        near_weight = jnp.where(near_live, near_scale, jnp.zeros_like(near_scale))
        near_sum = jnp.einsum("clkp,lk->clp", near_terms, near_weight, precision=best_precision)
        image = (far_out + near_sum).reshape(columns, leaves_dev * leaf_size)
        return jnp.zeros_like(image).at[:, order_row].set(image)

    return (apply_image(p_dirs), apply_image(resid))


def solution(mesh):
    return jax.shard_map(
        shards,
        mesh=mesh,
        in_specs=(
            P(None, ("leaf", "sub")),
            P(None, ("leaf", "sub")),
            P(("leaf", "sub"), None),
            P(("leaf", "sub"), None, None),
            P(("leaf", "sub"), None, None),
            P(("leaf", "sub"), None, None),
            P(("leaf", "sub"), None),
            P(("leaf", "sub"), None),
            P(("leaf", "sub"), None, None),
            P(("leaf", "sub"), None),
            P(("leaf", "sub"), None),
            P(("leaf", "sub"), None, None, None),
            P(("leaf", "sub"), None, None, None),
            P(),
            P(),
            P(),
        ),
        out_specs=(P(None, ("leaf", "sub")), P(None, ("leaf", "sub"))),
        check_vma=False,
    )
```

profile of v0, /device:TPU:14, one launch (start us, length us, event | category | flops | bytes accessed | tf_op | source)
XLA Modules:
  0.0 261.4 jit_solution(8603584989882755216)
XLA Ops:
  4.5 6.2 %gather_fusion.4 = bf16[2048,16]{1,0:T(8,128)(2,1)S(1)} fusion(bf16[16,2048]{0,1:T(8,128)(2,1)S(1)} %copy.206, s32[2048]{0:T(1024)S(1)} %fusion.290), kind=kCustom, calls=%fused_computation.clone | custom fusion | bytes 139264 | tf_op jit(solution)/shard_map/jit(_take)/gather | solution.py:102
  10.7 6.2 %gather_fusion.5 = bf16[2048,16]{1,0:T(8,128)(2,1)S(1)} fusion(bf16[16,2048]{0,1:T(8,128)(2,1)S(1)} %copy.235, s32[2048]{0:T(1024)S(1)} %fusion.290), kind=kCustom, calls=%fused_computation.1.clone | custom fusion | bytes 139264 | tf_op jit(solution)/shard_map/jit(_take)/gather | solution.py:102
  19.6 3.7 %collective-permute-start.24 = (bf16[32,32,16]{1,2,0:T(8,128)(2,1)}, bf16[32,32,16]{1,2,0:T(8,128)(2,1)}, u32[]{:S(2)}, u32[]{:S(2)}) collective-permute-start(bf16[32,32,16]{1,2,0:T(8,128)(2,1)} %convert_bitcast_fusion), channel_id=1, source_target_pairs={{0,1},{1,2},{2,3},{3,4},{4,5},{5,6},{6,7},{7,8},{8,9},{9,10},{10,1... | collective-permute-start | bytes 98312 | tf_op jit(solution)/shard_map/ppermute | solution.py:20
  25.6 5.5 %collective-permute-start.10 = (bf16[32,32,16]{1,2,0:T(8,128)(2,1)}, bf16[32,32,16]{1,2,0:T(8,128)(2,1)}, u32[]{:S(2)}, u32[]{:S(2)}) collective-permute-start(bf16[32,32,16]{1,2,0:T(8,128)(2,1)} %convert_bitcast_fusion.1), channel_id=1, source_target_pairs={{0,1},{1,2},{2,3},{3,4},{4,5},{5,6},{6,7},{7,8},{8,9},{9,10},{10,1... | collective-permute-start | bytes 98312 | tf_op jit(solution)/shard_map/ppermute | solution.py:20
  34.2 3.0 %collective-permute-start = (f32[32,16]{0,1:T(8,128)S(1)}, f32[32,16]{0,1:T(8,128)}, u32[]{:S(2)}, u32[]{:S(2)}) collective-permute-start(f32[32,16]{0,1:T(8,128)S(1)} %fusion.250), channel_id=1, source_target_pairs={{0,1},{1,0},{2,3},{3,2},{4,5},{5,4},{6,7},{7,6},{8,9},{9,8},{10,11... | collective-permute-start | bytes 6152 | tf_op jit(solution)/shard_map/ppermute | solution.py:12
  50.7 4.3 %reshape.161 = bf16[32,6,64,64]{3,2,0,1:T(8,128)(2,1)S(1)} reshape(bf16[32,6,4096]{2,0,1:T(8,128)(2,1)} %param.23) | data formatting | bytes 3145728 | tf_op jit(solution)/shard_map/reshape | solution.py:55
  58.4 5.2 %collective-permute-start.1 = (f32[32,16]{0,1:T(8,128)S(1)}, f32[32,16]{0,1:T(8,128)S(1)}, u32[]{:S(2)}, u32[]{:S(2)}) collective-permute-start(f32[32,16]{0,1:T(8,128)S(1)} %fusion.41), channel_id=1, source_target_pairs={{0,2},{1,3},{2,0},{3,1},{4,6},{5,7},{6,4},{7,5},{8,10},{9,11},{10,... | collective-permute-start | bytes 6152 | tf_op jit(solution)/shard_map/ppermute | solution.py:12
  65.2 3.9 %collective-permute-start.15 = (f32[32,16]{0,1:T(8,128)S(1)}, f32[32,16]{0,1:T(8,128)S(1)}, u32[]{:S(2)}, u32[]{:S(2)}) collective-permute-start(f32[32,16]{0,1:T(8,128)S(1)} %fusion.32), channel_id=1, source_target_pairs={{0,2},{1,3},{2,0},{3,1},{4,6},{5,7},{6,4},{7,5},{8,10},{9,11},{10,... | collective-permute-start | bytes 6152 | tf_op jit(solution)/shard_map/ppermute | solution.py:12
  70.7 10.3 %collective-permute-start.2 = (f32[32,16]{0,1:T(8,128)S(1)}, f32[32,16]{0,1:T(8,128)S(1)}, u32[]{:S(2)}, u32[]{:S(2)}) collective-permute-start(f32[32,16]{0,1:T(8,128)S(1)} %fusion.40), channel_id=1, source_target_pairs={{0,4},{1,5},{2,6},{3,7},{4,0},{5,1},{6,2},{7,3},{8,12},{9,13},{10,... | collective-permute-start | bytes 6152 | tf_op jit(solution)/shard_map/ppermute | solution.py:12
  82.7 4.8 %collective-permute-start.16 = (f32[32,16]{0,1:T(8,128)S(1)}, f32[32,16]{0,1:T(8,128)S(1)}, u32[]{:S(2)}, u32[]{:S(2)}) collective-permute-start(f32[32,16]{0,1:T(8,128)S(1)} %fusion.31), channel_id=1, source_target_pairs={{0,4},{1,5},{2,6},{3,7},{4,0},{5,1},{6,2},{7,3},{8,12},{9,13},{10,... | collective-permute-start | bytes 6152 | tf_op jit(solution)/shard_map/ppermute | solution.py:12
  89.1 8.2 %collective-permute-start.3 = (f32[32,16]{0,1:T(8,128)S(1)}, f32[32,16]{0,1:T(8,128)S(1)}, u32[]{:S(2)}, u32[]{:S(2)}) collective-permute-start(f32[32,16]{0,1:T(8,128)S(1)} %fusion.39), channel_id=1, source_target_pairs={{0,8},{1,9},{2,10},{3,11},{4,12},{5,13},{6,14},{7,15},{8,0},{9,1},... | collective-permute-start | bytes 6152 | tf_op jit(solution)/shard_map/ppermute | solution.py:12
  98.9 7.9 %collective-permute-start.17 = (f32[32,16]{0,1:T(8,128)S(1)}, f32[32,16]{0,1:T(8,128)S(1)}, u32[]{:S(2)}, u32[]{:S(2)}) collective-permute-start(f32[32,16]{0,1:T(8,128)S(1)} %fusion.30), channel_id=1, source_target_pairs={{0,8},{1,9},{2,10},{3,11},{4,12},{5,13},{6,14},{7,15},{8,0},{9,1},... | collective-permute-start | bytes 6152 | tf_op jit(solution)/shard_map/ppermute | solution.py:12
  108.4 3.6 %collective-permute-start.4 = (f32[32,16]{0,1:T(8,128)S(1)}, f32[32,16]{0,1:T(8,128)S(1)}, u32[]{:S(2)}, u32[]{:S(2)}) collective-permute-start(f32[32,16]{0,1:T(8,128)S(1)} %fusion.38), channel_id=1, source_target_pairs={{0,16},{16,0},{32,48},{48,32},{64,80},{80,64},{96,112},{112,96},{1... | collective-permute-start | bytes 6152 | tf_op jit(solution)/shard_map/ppermute | solution.py:12
  113.9 3.6 %collective-permute-start.18 = (f32[32,16]{0,1:T(8,128)S(1)}, f32[32,16]{0,1:T(8,128)S(1)}, u32[]{:S(2)}, u32[]{:S(2)}) collective-permute-start(f32[32,16]{0,1:T(8,128)S(1)} %fusion.29), channel_id=1, source_target_pairs={{0,16},{16,0},{32,48},{48,32},{64,80},{80,64},{96,112},{112,96},{1... | collective-permute-start | bytes 6152 | tf_op jit(solution)/shard_map/ppermute | solution.py:12
  119.5 4.7 %collective-permute-start.5 = (f32[32,16]{0,1:T(8,128)S(1)}, f32[32,16]{0,1:T(8,128)S(1)}, u32[]{:S(2)}, u32[]{:S(2)}) collective-permute-start(f32[32,16]{0,1:T(8,128)S(1)} %fusion.37), channel_id=1, source_target_pairs={{0,32},{16,48},{32,0},{48,16},{64,96},{80,112},{96,64},{112,80},{1... | collective-permute-start | bytes 6152 | tf_op jit(solution)/shard_map/ppermute | solution.py:12
  125.9 4.7 %collective-permute-start.19 = (f32[32,16]{0,1:T(8,128)S(1)}, f32[32,16]{0,1:T(8,128)S(1)}, u32[]{:S(2)}, u32[]{:S(2)}) collective-permute-start(f32[32,16]{0,1:T(8,128)S(1)} %fusion.28), channel_id=1, source_target_pairs={{0,32},{16,48},{32,0},{48,16},{64,96},{80,112},{96,64},{112,80},{1... | collective-permute-start | bytes 6152 | tf_op jit(solution)/shard_map/ppermute | solution.py:12
  132.3 8.2 %collective-permute-start.6 = (f32[32,16]{0,1:T(8,128)S(1)}, f32[32,16]{0,1:T(8,128)S(1)}, u32[]{:S(2)}, u32[]{:S(2)}) collective-permute-start(f32[32,16]{0,1:T(8,128)S(1)} %fusion.36), channel_id=1, source_target_pairs={{0,64},{16,80},{32,96},{48,112},{64,0},{80,16},{96,32},{112,48},{1... | collective-permute-start | bytes 6152 | tf_op jit(solution)/shard_map/ppermute | solution.py:12
  142.1 7.8 %collective-permute-start.20 = (f32[32,16]{0,1:T(8,128)S(1)}, f32[32,16]{0,1:T(8,128)S(1)}, u32[]{:S(2)}, u32[]{:S(2)}) collective-permute-start(f32[32,16]{0,1:T(8,128)S(1)} %fusion.27), channel_id=1, source_target_pairs={{0,64},{16,80},{32,96},{48,112},{64,0},{80,16},{96,32},{112,48},{1... | collective-permute-start | bytes 6152 | tf_op jit(solution)/shard_map/ppermute | solution.py:12
  151.6 3.3 %collective-permute-start.7 = (f32[32,16]{0,1:T(8,128)S(1)}, f32[32,16]{0,1:T(8,128)S(1)}, u32[]{:S(2)}, u32[]{:S(2)}) collective-permute-start(f32[32,16]{0,1:T(8,128)S(1)} %fusion.35), channel_id=1, source_target_pairs={{0,128},{16,144},{32,160},{48,176},{64,192},{80,208},{96,224},{112... | collective-permute-start | bytes 6152 | tf_op jit(solution)/shard_map/ppermute | solution.py:12
  157.1 3.3 %collective-permute-start.21 = (f32[32,16]{0,1:T(8,128)S(1)}, f32[32,16]{0,1:T(8,128)S(1)}, u32[]{:S(2)}, u32[]{:S(2)}) collective-permute-start(f32[32,16]{0,1:T(8,128)S(1)} %fusion.26), channel_id=1, source_target_pairs={{0,128},{16,144},{32,160},{48,176},{64,192},{80,208},{96,224},{112... | collective-permute-start | bytes 6152 | tf_op jit(solution)/shard_map/ppermute | solution.py:12
  162.6 4.2 %collective-permute-start.8 = (f32[32,16]{0,1:T(8,128)S(1)}, f32[32,16]{0,1:T(8,128)S(1)}, u32[]{:S(2)}, u32[]{:S(2)}) collective-permute-start(f32[32,16]{0,1:T(8,128)S(1)} %fusion.34), channel_id=1, source_target_pairs={{0,256},{16,272},{32,288},{48,304},{64,320},{80,336},{96,352},{112... | collective-permute-start | bytes 6152 | tf_op jit(solution)/shard_map/ppermute | solution.py:12
  169.1 4.3 %collective-permute-start.22 = (f32[32,16]{0,1:T(8,128)S(1)}, f32[32,16]{0,1:T(8,128)S(1)}, u32[]{:S(2)}, u32[]{:S(2)}) collective-permute-start(f32[32,16]{0,1:T(8,128)S(1)} %fusion.25), channel_id=1, source_target_pairs={{0,256},{16,272},{32,288},{48,304},{64,320},{80,336},{96,352},{112... | collective-permute-start | bytes 6152 | tf_op jit(solution)/shard_map/ppermute | solution.py:12
  175.5 5.1 %collective-permute-start.9 = (f32[32,16]{0,1:T(8,128)S(1)}, f32[32,16]{0,1:T(8,128)S(1)}, u32[]{:S(2)}, u32[]{:S(2)}) collective-permute-start(f32[32,16]{0,1:T(8,128)S(1)} %fusion.33), channel_id=1, source_target_pairs={{0,512},{16,528},{32,544},{48,560},{64,576},{80,592},{96,608},{112... | collective-permute-start | bytes 6152 | tf_op jit(solution)/shard_map/ppermute | solution.py:12
  180.9 4.1 %collective-permute-done.9 = f32[32,16]{0,1:T(8,128)S(1)} collective-permute-done((f32[32,16]{0,1:T(8,128)S(1)}, f32[32,16]{0,1:T(8,128)S(1)}, u32[]{:S(2)}, u32[]{:S(2)}) %collective-permute-start.9) | collective-permute-done | bytes 2080 | tf_op jit(solution)/shard_map/ppermute | solution.py:12
  185.0 5.1 %collective-permute-start.23 = (f32[32,16]{0,1:T(8,128)S(1)}, f32[32,16]{0,1:T(8,128)S(1)}, u32[]{:S(2)}, u32[]{:S(2)}) collective-permute-start(f32[32,16]{0,1:T(8,128)S(1)} %fusion.24), channel_id=1, source_target_pairs={{0,512},{16,528},{32,544},{48,560},{64,576},{80,592},{96,608},{112... | collective-permute-start | bytes 6152 | tf_op jit(solution)/shard_map/ppermute | solution.py:12
  190.4 4.0 %collective-permute-done.23 = f32[32,16]{0,1:T(8,128)S(1)} collective-permute-done((f32[32,16]{0,1:T(8,128)S(1)}, f32[32,16]{0,1:T(8,128)S(1)}, u32[]{:S(2)}, u32[]{:S(2)}) %collective-permute-start.23) | collective-permute-done | bytes 2080 | tf_op jit(solution)/shard_map/ppermute | solution.py:12
  204.6 3.7 %collective-permute-start.26 = (bf16[16,32,64]{2,0,1:T(8,128)(2,1)}, bf16[16,32,64]{2,0,1:T(8,128)(2,1)}, u32[]{:S(2)}, u32[]{:S(2)}) collective-permute-start(bf16[16,32,64]{2,0,1:T(8,128)(2,1)} %copy.246), channel_id=1, source_target_pairs={{0,1},{1,2},{2,3},{3,4},{4,5},{5,6},{6,7},{7,8},{8,9},{9,10},{10,1... | collective-permute-start | bytes 196616 | tf_op jit(solution)/shard_map/ppermute | solution.py:20
  214.1 3.8 %collective-permute-start.12 = (bf16[16,32,64]{2,0,1:T(8,128)(2,1)}, bf16[16,32,64]{2,0,1:T(8,128)(2,1)}, u32[]{:S(2)}, u32[]{:S(2)}) collective-permute-start(bf16[16,32,64]{2,0,1:T(8,128)(2,1)} %copy.228), channel_id=1, source_target_pairs={{0,1},{1,2},{2,3},{3,4},{4,5},{5,6},{6,7},{7,8},{8,9},{9,10},{10,1... | collective-permute-start | bytes 196616 | tf_op jit(solution)/shard_map/ppermute | solution.py:20
  222.4 2.7 %fusion.8 = f32[32,32,16]{1,2,0:T(8,128)S(1)} fusion(bf16[32,6,32,16]{2,3,1,0:T(8,128)(2,1)} %bitcast.575, bf16[32,6,32,32]{3,2,0,1:T(8,128)(2,1)} %reshape.160, f32[32,6]{1,0:T(8,128)} %copy.295), kind=kOutput, calls=%fused_computation.17 | convolution fusion | flops 6471680 | bytes 656128 | tf_op jit(solution)/shard_map/lkab,lkbc->lkac/dot_general | solution.py:131
  236.9 2.9 %fusion.13 = f32[16,32,6,64]{3,0,2,1:T(8,128)S(1)} fusion(bf16[16,32,6,64]{3,0,2,1:T(8,128)(2,1)} %bitcast.573, bf16[32,6,64,64]{3,2,0,1:T(8,128)(2,1)S(1)} %reshape.161), kind=kOutput, calls=%fused_computation.21 | convolution fusion | flops 25165824 | bytes 2752512 | tf_op jit(solution)/shard_map/lkpq,clkq->clkp/dot_general | solution.py:145
  247.2 6.0 %scatter_custom_fusion = f32[16,2048]{0,1:T(8,128)S(1)} fusion(s32[2048]{0:T(1024)} %bitcast.598, f32[2048,16]{1,0:T(8,128)S(1)} %copy.234, f32[]{:T(128)} %constant.112.clone.1), kind=kCustom, calls=%fused_computation.104 | custom fusion | bytes 131584 | tf_op jit(solution)/shard_map/scatter | solution.py:151
  254.4 6.0 %scatter_custom_fusion.1 = f32[16,2048]{0,1:T(8,128)S(1)} fusion(s32[2048]{0:T(1024)} %bitcast.599, f32[2048,16]{1,0:T(8,128)S(1)} %copy.251, f32[]{:T(128)} %constant.112.clone.1), kind=kCustom, calls=%fused_computation.102 | custom fusion | bytes 131584 | tf_op jit(solution)/shard_map/scatter | solution.py:151
  (250 shorter events, 99.7 us)
Async XLA Ops:
  0.6 245.3 %copy-start = (bf16[32,64,32]{1,2,0:T(8,128)(2,1)S(1)}, bf16[32,64,32]{1,2,0:T(8,128)(2,1)}, u32[]{:S(2)}) copy-start(bf16[32,64,32]{1,2,0:T(8,128)(2,1)} %param.22) | copy-start | bytes 393220
  18.3 195.8 %collective-permute-start.25 = (bf16[32,32,16]{1,2,0:T(8,128)(2,1)}, bf16[32,32,16]{1,2,0:T(8,128)(2,1)}, u32[]{:S(2)}, u32[]{:S(2)}) collective-permute-start(bf16[32,32,16]{1,2,0:T(8,128)(2,1)} %convert_bitcast_fusion), channel_id=1, source_target_pairs={{1,0},{2,1},{3,2},{4,3},{5,4},{6,5},{7,6},{8,7},{9,8},{10,9},{11,1... | collective-permute-start | bytes 98312 | tf_op jit(solution)/shard_map/ppermute | solution.py:23
  19.6 198.3 %collective-permute-start.24 = (bf16[32,32,16]{1,2,0:T(8,128)(2,1)}, bf16[32,32,16]{1,2,0:T(8,128)(2,1)}, u32[]{:S(2)}, u32[]{:S(2)}) collective-permute-start(bf16[32,32,16]{1,2,0:T(8,128)(2,1)} %convert_bitcast_fusion), channel_id=1, source_target_pairs={{0,1},{1,2},{2,3},{3,4},{4,5},{5,6},{6,7},{7,8},{8,9},{9,10},{10,1... | collective-permute-start | bytes 98312 | tf_op jit(solution)/shard_map/ppermute | solution.py:20
  24.3 180.3 %collective-permute-start.11 = (bf16[32,32,16]{1,2,0:T(8,128)(2,1)}, bf16[32,32,16]{1,2,0:T(8,128)(2,1)}, u32[]{:S(2)}, u32[]{:S(2)}) collective-permute-start(bf16[32,32,16]{1,2,0:T(8,128)(2,1)} %convert_bitcast_fusion.1), channel_id=1, source_target_pairs={{1,0},{2,1},{3,2},{4,3},{5,4},{6,5},{7,6},{8,7},{9,8},{10,9},{11,1... | collective-permute-start | bytes 98312 | tf_op jit(solution)/shard_map/ppermute | solution.py:23
  25.6 182.7 %collective-permute-start.10 = (bf16[32,32,16]{1,2,0:T(8,128)(2,1)}, bf16[32,32,16]{1,2,0:T(8,128)(2,1)}, u32[]{:S(2)}, u32[]{:S(2)}) collective-permute-start(bf16[32,32,16]{1,2,0:T(8,128)(2,1)} %convert_bitcast_fusion.1), channel_id=1, source_target_pairs={{0,1},{1,2},{2,3},{3,4},{4,5},{5,6},{6,7},{7,8},{8,9},{9,10},{10,1... | collective-permute-start | bytes 98312 | tf_op jit(solution)/shard_map/ppermute | solution.py:20
  34.2 20.9 %collective-permute-start = (f32[32,16]{0,1:T(8,128)S(1)}, f32[32,16]{0,1:T(8,128)}, u32[]{:S(2)}, u32[]{:S(2)}) collective-permute-start(f32[32,16]{0,1:T(8,128)S(1)} %fusion.250), channel_id=1, source_target_pairs={{0,1},{1,0},{2,3},{3,2},{4,5},{5,4},{6,7},{7,6},{8,9},{9,8},{10,11... | collective-permute-start | bytes 6152 | tf_op jit(solution)/shard_map/ppermute | solution.py:12
  55.1 135.0 %copy-start.5 = (f32[2,32,32]{2,1,0:T(8,128)S(1)}, f32[2,32,32]{2,1,0:T(8,128)}, u32[]{:S(2)}) copy-start(f32[2,32,32]{2,1,0:T(8,128)} %param.33) | copy-start | bytes 24580
  55.1 135.0 %copy-start.19 = (f32[32,16]{0,1:T(8,128)S(1)}, f32[32,16]{0,1:T(8,128)}, u32[]{:S(2)}) copy-start(f32[32,16]{0,1:T(8,128)} %fusion.172) | copy-start | bytes 6148
  55.1 146.9 %copy-start.17 = (bf16[1,2,32,32]{3,2,1,0:T(8,128)(2,1)S(1)}, bf16[1,2,32,32]{3,2,1,0:T(8,128)(2,1)}, u32[]{:S(2)}) copy-start(bf16[1,2,32,32]{3,2,1,0:T(8,128)(2,1)} %copy.282) | copy-start | bytes 12292
  55.1 3.3 %collective-permute-start.14 = (f32[32,16]{0,1:T(8,128)}, f32[32,16]{0,1:T(8,128)S(1)}, u32[]{:S(2)}, u32[]{:S(2)}) collective-permute-start(f32[32,16]{0,1:T(8,128)} %fusion.249), channel_id=1, source_target_pairs={{0,1},{1,0},{2,3},{3,2},{4,5},{5,4},{6,7},{7,6},{8,9},{9,8},{10,11... | collective-permute-start | bytes 6152 | tf_op jit(solution)/shard_map/ppermute | solution.py:12
  58.4 6.8 %collective-permute-start.1 = (f32[32,16]{0,1:T(8,128)S(1)}, f32[32,16]{0,1:T(8,128)S(1)}, u32[]{:S(2)}, u32[]{:S(2)}) collective-permute-start(f32[32,16]{0,1:T(8,128)S(1)} %fusion.41), channel_id=1, source_target_pairs={{0,2},{1,3},{2,0},{3,1},{4,6},{5,7},{6,4},{7,5},{8,10},{9,11},{10,... | collective-permute-start | bytes 6152 | tf_op jit(solution)/shard_map/ppermute | solution.py:12
  65.2 5.5 %collective-permute-start.15 = (f32[32,16]{0,1:T(8,128)S(1)}, f32[32,16]{0,1:T(8,128)S(1)}, u32[]{:S(2)}, u32[]{:S(2)}) collective-permute-start(f32[32,16]{0,1:T(8,128)S(1)} %fusion.32), channel_id=1, source_target_pairs={{0,2},{1,3},{2,0},{3,1},{4,6},{5,7},{6,4},{7,5},{8,10},{9,11},{10,... | collective-permute-start | bytes 6152 | tf_op jit(solution)/shard_map/ppermute | solution.py:12
  70.7 11.9 %collective-permute-start.2 = (f32[32,16]{0,1:T(8,128)S(1)}, f32[32,16]{0,1:T(8,128)S(1)}, u32[]{:S(2)}, u32[]{:S(2)}) collective-permute-start(f32[32,16]{0,1:T(8,128)S(1)} %fusion.40), channel_id=1, source_target_pairs={{0,4},{1,5},{2,6},{3,7},{4,0},{5,1},{6,2},{7,3},{8,12},{9,13},{10,... | collective-permute-start | bytes 6152 | tf_op jit(solution)/shard_map/ppermute | solution.py:12
  82.7 6.4 %collective-permute-start.16 = (f32[32,16]{0,1:T(8,128)S(1)}, f32[32,16]{0,1:T(8,128)S(1)}, u32[]{:S(2)}, u32[]{:S(2)}) collective-permute-start(f32[32,16]{0,1:T(8,128)S(1)} %fusion.31), channel_id=1, source_target_pairs={{0,4},{1,5},{2,6},{3,7},{4,0},{5,1},{6,2},{7,3},{8,12},{9,13},{10,... | collective-permute-start | bytes 6152 | tf_op jit(solution)/shard_map/ppermute | solution.py:12
  89.1 9.8 %collective-permute-start.3 = (f32[32,16]{0,1:T(8,128)S(1)}, f32[32,16]{0,1:T(8,128)S(1)}, u32[]{:S(2)}, u32[]{:S(2)}) collective-permute-start(f32[32,16]{0,1:T(8,128)S(1)} %fusion.39), channel_id=1, source_target_pairs={{0,8},{1,9},{2,10},{3,11},{4,12},{5,13},{6,14},{7,15},{8,0},{9,1},... | collective-permute-start | bytes 6152 | tf_op jit(solution)/shard_map/ppermute | solution.py:12
  98.9 9.5 %collective-permute-start.17 = (f32[32,16]{0,1:T(8,128)S(1)}, f32[32,16]{0,1:T(8,128)S(1)}, u32[]{:S(2)}, u32[]{:S(2)}) collective-permute-start(f32[32,16]{0,1:T(8,128)S(1)} %fusion.30), channel_id=1, source_target_pairs={{0,8},{1,9},{2,10},{3,11},{4,12},{5,13},{6,14},{7,15},{8,0},{9,1},... | collective-permute-start | bytes 6152 | tf_op jit(solution)/shard_map/ppermute | solution.py:12
  108.4 5.5 %collective-permute-start.4 = (f32[32,16]{0,1:T(8,128)S(1)}, f32[32,16]{0,1:T(8,128)S(1)}, u32[]{:S(2)}, u32[]{:S(2)}) collective-permute-start(f32[32,16]{0,1:T(8,128)S(1)} %fusion.38), channel_id=1, source_target_pairs={{0,16},{16,0},{32,48},{48,32},{64,80},{80,64},{96,112},{112,96},{1... | collective-permute-start | bytes 6152 | tf_op jit(solution)/shard_map/ppermute | solution.py:12
  113.9 5.5 %collective-permute-start.18 = (f32[32,16]{0,1:T(8,128)S(1)}, f32[32,16]{0,1:T(8,128)S(1)}, u32[]{:S(2)}, u32[]{:S(2)}) collective-permute-start(f32[32,16]{0,1:T(8,128)S(1)} %fusion.29), channel_id=1, source_target_pairs={{0,16},{16,0},{32,48},{48,32},{64,80},{80,64},{96,112},{112,96},{1... | collective-permute-start | bytes 6152 | tf_op jit(solution)/shard_map/ppermute | solution.py:12
  119.5 6.4 %collective-permute-start.5 = (f32[32,16]{0,1:T(8,128)S(1)}, f32[32,16]{0,1:T(8,128)S(1)}, u32[]{:S(2)}, u32[]{:S(2)}) collective-permute-start(f32[32,16]{0,1:T(8,128)S(1)} %fusion.37), channel_id=1, source_target_pairs={{0,32},{16,48},{32,0},{48,16},{64,96},{80,112},{96,64},{112,80},{1... | collective-permute-start | bytes 6152 | tf_op jit(solution)/shard_map/ppermute | solution.py:12
  125.9 6.4 %collective-permute-start.19 = (f32[32,16]{0,1:T(8,128)S(1)}, f32[32,16]{0,1:T(8,128)S(1)}, u32[]{:S(2)}, u32[]{:S(2)}) collective-permute-start(f32[32,16]{0,1:T(8,128)S(1)} %fusion.28), channel_id=1, source_target_pairs={{0,32},{16,48},{32,0},{48,16},{64,96},{80,112},{96,64},{112,80},{1... | collective-permute-start | bytes 6152 | tf_op jit(solution)/shard_map/ppermute | solution.py:12
  132.3 9.8 %collective-permute-start.6 = (f32[32,16]{0,1:T(8,128)S(1)}, f32[32,16]{0,1:T(8,128)S(1)}, u32[]{:S(2)}, u32[]{:S(2)}) collective-permute-start(f32[32,16]{0,1:T(8,128)S(1)} %fusion.36), channel_id=1, source_target_pairs={{0,64},{16,80},{32,96},{48,112},{64,0},{80,16},{96,32},{112,48},{1... | collective-permute-start | bytes 6152 | tf_op jit(solution)/shard_map/ppermute | solution.py:12
  142.1 9.4 %collective-permute-start.20 = (f32[32,16]{0,1:T(8,128)S(1)}, f32[32,16]{0,1:T(8,128)S(1)}, u32[]{:S(2)}, u32[]{:S(2)}) collective-permute-start(f32[32,16]{0,1:T(8,128)S(1)} %fusion.27), channel_id=1, source_target_pairs={{0,64},{16,80},{32,96},{48,112},{64,0},{80,16},{96,32},{112,48},{1... | collective-permute-start | bytes 6152 | tf_op jit(solution)/shard_map/ppermute | solution.py:12
  151.6 5.5 %collective-permute-start.7 = (f32[32,16]{0,1:T(8,128)S(1)}, f32[32,16]{0,1:T(8,128)S(1)}, u32[]{:S(2)}, u32[]{:S(2)}) collective-permute-start(f32[32,16]{0,1:T(8,128)S(1)} %fusion.35), channel_id=1, source_target_pairs={{0,128},{16,144},{32,160},{48,176},{64,192},{80,208},{96,224},{112... | collective-permute-start | bytes 6152 | tf_op jit(solution)/shard_map/ppermute | solution.py:12
  157.1 5.5 %collective-permute-start.21 = (f32[32,16]{0,1:T(8,128)S(1)}, f32[32,16]{0,1:T(8,128)S(1)}, u32[]{:S(2)}, u32[]{:S(2)}) collective-permute-start(f32[32,16]{0,1:T(8,128)S(1)} %fusion.26), channel_id=1, source_target_pairs={{0,128},{16,144},{32,160},{48,176},{64,192},{80,208},{96,224},{112... | collective-permute-start | bytes 6152 | tf_op jit(solution)/shard_map/ppermute | solution.py:12
  162.6 6.4 %collective-permute-start.8 = (f32[32,16]{0,1:T(8,128)S(1)}, f32[32,16]{0,1:T(8,128)S(1)}, u32[]{:S(2)}, u32[]{:S(2)}) collective-permute-start(f32[32,16]{0,1:T(8,128)S(1)} %fusion.34), channel_id=1, source_target_pairs={{0,256},{16,272},{32,288},{48,304},{64,320},{80,336},{96,352},{112... | collective-permute-start | bytes 6152 | tf_op jit(solution)/shard_map/ppermute | solution.py:12
  169.1 6.4 %collective-permute-start.22 = (f32[32,16]{0,1:T(8,128)S(1)}, f32[32,16]{0,1:T(8,128)S(1)}, u32[]{:S(2)}, u32[]{:S(2)}) collective-permute-start(f32[32,16]{0,1:T(8,128)S(1)} %fusion.25), channel_id=1, source_target_pairs={{0,256},{16,272},{32,288},{48,304},{64,320},{80,336},{96,352},{112... | collective-permute-start | bytes 6152 | tf_op jit(solution)/shard_map/ppermute | solution.py:12
  175.5 9.4 %collective-permute-start.9 = (f32[32,16]{0,1:T(8,128)S(1)}, f32[32,16]{0,1:T(8,128)S(1)}, u32[]{:S(2)}, u32[]{:S(2)}) collective-permute-start(f32[32,16]{0,1:T(8,128)S(1)} %fusion.33), channel_id=1, source_target_pairs={{0,512},{16,528},{32,544},{48,560},{64,576},{80,592},{96,608},{112... | collective-permute-start | bytes 6152 | tf_op jit(solution)/shard_map/ppermute | solution.py:12
  185.0 9.4 %collective-permute-start.23 = (f32[32,16]{0,1:T(8,128)S(1)}, f32[32,16]{0,1:T(8,128)S(1)}, u32[]{:S(2)}, u32[]{:S(2)}) collective-permute-start(f32[32,16]{0,1:T(8,128)S(1)} %fusion.24), channel_id=1, source_target_pairs={{0,512},{16,528},{32,544},{48,560},{64,576},{80,592},{96,608},{112... | collective-permute-start | bytes 6152 | tf_op jit(solution)/shard_map/ppermute | solution.py:12
  194.4 38.0 %collective-permute-start.27 = (bf16[16,32,64]{2,0,1:T(8,128)(2,1)}, bf16[16,32,64]{2,0,1:T(8,128)(2,1)}, u32[]{:S(2)}, u32[]{:S(2)}) collective-permute-start(bf16[16,32,64]{2,0,1:T(8,128)(2,1)} %copy.246), channel_id=1, source_target_pairs={{1,0},{2,1},{3,2},{4,3},{5,4},{6,5},{7,6},{8,7},{9,8},{10,9},{11,1... | collective-permute-start | bytes 196616 | tf_op jit(solution)/shard_map/ppermute | solution.py:23
  204.6 27.8 %collective-permute-start.26 = (bf16[16,32,64]{2,0,1:T(8,128)(2,1)}, bf16[16,32,64]{2,0,1:T(8,128)(2,1)}, u32[]{:S(2)}, u32[]{:S(2)}) collective-permute-start(bf16[16,32,64]{2,0,1:T(8,128)(2,1)} %copy.246), channel_id=1, source_target_pairs={{0,1},{1,2},{2,3},{3,4},{4,5},{5,6},{6,7},{7,8},{8,9},{9,10},{10,1... | collective-permute-start | bytes 196616 | tf_op jit(solution)/shard_map/ppermute | solution.py:20
  208.3 19.6 %collective-permute-start.13 = (bf16[16,32,64]{2,0,1:T(8,128)(2,1)}, bf16[16,32,64]{2,0,1:T(8,128)(2,1)}, u32[]{:S(2)}, u32[]{:S(2)}) collective-permute-start(bf16[16,32,64]{2,0,1:T(8,128)(2,1)} %copy.228), channel_id=1, source_target_pairs={{1,0},{2,1},{3,2},{4,3},{5,4},{6,5},{7,6},{8,7},{9,8},{10,9},{11,1... | collective-permute-start | bytes 196616 | tf_op jit(solution)/shard_map/ppermute | solution.py:23
  214.1 13.8 %collective-permute-start.12 = (bf16[16,32,64]{2,0,1:T(8,128)(2,1)}, bf16[16,32,64]{2,0,1:T(8,128)(2,1)}, u32[]{:S(2)}, u32[]{:S(2)}) collective-permute-start(bf16[16,32,64]{2,0,1:T(8,128)(2,1)} %copy.228), channel_id=1, source_target_pairs={{0,1},{1,2},{2,3},{3,4},{4,5},{5,6},{6,7},{7,8},{8,9},{9,10},{10,1... | collective-permute-start | bytes 196616 | tf_op jit(solution)/shard_map/ppermute | solution.py:20
  (21 other events, 277.0 us)
where the time goes:
time: 266 us; the launch traced here: 261 us
  starting transfers between devices  125 us (47%)
  local copies, waits for them, and re-layouts  57.2 us (22%)
  matrix products  33.1 us (12%)
  waiting for transfers between devices  32.5 us (12%)
  other arithmetic  12 us (5%)
    ppermute x20, starting transfers between devices, from_partner(): return lax.ppermute(value, axis, pairs)  103 us
    ppermute x20, waiting for transfers between devices, from_partner(): return lax.ppermute(value, axis, pairs)  32.5 us
    ppermute x4, starting transfers between devices, extended(): lax.ppermute(lax.slice_in_dim(block, block.shape[dim] - width, None, axis...  16.6 us
    gather x2, local copies, waits for them, and re-layouts, apply_image(): ordered = jnp.take(vectors, order_row, axis=1).astype(jnp.bfloat16)  12.4 us
    scatter x2, local copies, waits for them, and re-layouts, apply_image(): return jnp.zeros_like(image).at[:, order_row].set(image)  11.9 us
    dot_general x49, matrix products, apply_down(): jnp.einsum('...ab,...bc->...ac', matrix, coeffs, precision=best_precision)  11.3 us
    unnamed x65, local copies, waits for them, and re-layouts  10.6 us
    dot_general x46, matrix products, apply_up(): jnp.einsum('...ab,...ac->...bc', matrix, coeffs, precision=best_precision)  8.17 us
  transfers between devices with their start and end apart: 28, of which 19 were waited for; matrix products, arithmetic and copies ran while one was open for 21% of the time, Pallas kernels for 0%

commit v1 on v0

--- a/solution.py
+++ b/solution.py
@@ -6,23 +6,13 @@
 best_precision = lax.Precision.HIGHEST
 
 
-def from_partner(value, axis, distance):
-    mask = 2**distance
-    pairs = [(source, source ^ mask) for source in range(lax.axis_size(axis))]
-    return lax.ppermute(value, axis, pairs)
-
-
-def extended(block, sides, width):
-    for axis, dim in sides:
-        count = lax.axis_size(axis)
-        forward = [(i, i + 1) for i in range(count - 1)]
-        backward = [(target, source) for source, target in forward]
-        low = lax.ppermute(
-            lax.slice_in_dim(block, block.shape[dim] - width, None, axis=dim), axis, forward
-        )
-        high = lax.ppermute(lax.slice_in_dim(block, 0, width, axis=dim), axis, backward)
-        block = jnp.concatenate([low, block, high], axis=dim)
-    return block
+def extended(block, axis, dim):
+    count = lax.axis_size(axis)
+    forward = [(i, i + 1) for i in range(count - 1)]
+    backward = [(target, source) for source, target in forward]
+    low = lax.ppermute(block, axis, forward)
+    high = lax.ppermute(block, axis, backward)
+    return jnp.concatenate([low, block, high], axis=dim)
 
 
 def apply_up(matrix, coeffs):
@@ -62,32 +52,26 @@
     sub_pos = lax.axis_index("sub")
     leaf_pos = lax.axis_index("leaf")
 
-    def combine_pair(left_part, right_part):
-        return apply_up(up_col[0], left_part) + apply_up(up_col[1], right_part)
+    def combine_level(nodes):
+        pairs = nodes.reshape(nodes.shape[0] // 2, 2, *nodes.shape[1:])
+        return apply_up(up_col[0], pairs[:, 0]) + apply_up(up_col[1], pairs[:, 1])
 
-    def merge_side(current, sibling, side_bit):
-        left_part = jnp.where(side_bit == 1, sibling, current)
-        right_part = jnp.where(side_bit == 1, current, sibling)
-        return combine_pair(left_part, right_part)
-
-    def leaf_bit_levels(current, records):
-        for bit_num in range(leaf_bits):
-            sibling = from_partner(current, "leaf", bit_num)
-            side_bit = leaf_pos >> bit_num & 1
-            records.append((sibling, side_bit))
-            if bit_num + 1 < leaf_bits:
-                current = merge_side(current, sibling, side_bit)
-        return records
+    def group_levels(nodes, pos, bits, records, last):
+        for bit_num in range(bits):
+            here = pos >> bit_num
+            sibling = lax.dynamic_index_in_dim(nodes, here ^ 1, 0, keepdims=False)
+            records.append((sibling, here & 1))
+            if not (last and bit_num + 1 == bits):
+                nodes = combine_level(nodes)
+        return nodes
 
     def climb_tree(root_coeff):
         records = []
-        current = root_coeff
-        for bit_num in range(sub_bits):
-            sibling = from_partner(current, "sub", bit_num)
-            side_bit = sub_pos >> bit_num & 1
-            records.append((sibling, side_bit))
-            current = merge_side(current, sibling, side_bit)
-        return leaf_bit_levels(current, records)
+        sub_nodes = lax.all_gather(root_coeff, "sub")
+        group_root = group_levels(sub_nodes, sub_pos, sub_bits, records, False)[0]
+        leaf_nodes = lax.all_gather(group_root, "leaf")
+        group_levels(leaf_nodes, leaf_pos, leaf_bits, records, True)
+        return records
 
     def descend_tree(records, columns):
         field_now = jnp.zeros((rank_width, columns), jnp.float32)
@@ -101,12 +85,12 @@
         columns = vectors.shape[0]
         ordered = jnp.take(vectors, order_row, axis=1).astype(jnp.bfloat16)
         leaf_blocks = ordered.reshape(columns, leaves_dev, leaf_size)
-        x_window = extended(leaf_blocks, (("sub", 1),), leaves_dev)
+        x_window = extended(leaf_blocks, "sub", 1)
         leaf_coeff = jnp.einsum(
             "clp,lpk->lkc", leaf_blocks, col_basis, preferred_element_type=jnp.float32
         )
         leaf_round = leaf_coeff.astype(jnp.bfloat16)
-        coeff_window = extended(leaf_round, (("sub", 0),), leaves_dev)
+        coeff_window = extended(leaf_round, "sub", 0)
         current = leaf_coeff
         offsets = []
         start_at = 0
@@ -150,7 +134,9 @@
         image = (far_out + near_sum).reshape(columns, leaves_dev * leaf_size)
         return jnp.zeros_like(image).at[:, order_row].set(image)
 
-    return (apply_image(p_dirs), apply_image(resid))
+    rhs = p_dirs.shape[0]
+    both = apply_image(jnp.concatenate([p_dirs, resid], axis=0))
+    return (both[:rhs], both[rhs:])
 
 
 def solution(mesh):

time: 266 us -> 181 us (0.68)
  starting transfers between devices: 125 us -> 11.1 us
  blocking collectives: 0 us -> 81.4 us
  waiting for transfers between devices: 32.5 us -> 0.01 us
  local copies, waits for them, and re-layouts: 57.2 us -> 43.7 us
  other arithmetic: 12 us -> 8.32 us
    ppermute x28 -> x4, starting transfers between devices: 125 us -> 11.1 us  [the longest x2 8.58 us: extended(): low = lax.ppermute(block, axis, forward)]
    all_gather x0 -> x2, blocking collectives: none -> 81.4 us  [the longest x1 51.2 us: climb_tree(): leaf_nodes = lax.all_gather(group_root, 'leaf')]
    ppermute x28 -> x4, waiting for transfers between devices: 32.5 us -> 0.01 us  [the longest x2 0.01 us: extended(): low = lax.ppermute(block, axis, forward)]
    scatter x2 -> x1, local copies, waits for them, and re-layouts: 11.9 us -> 5.97 us  [apply_image(): return jnp.zeros_like(image).at[:, order_row].set(image)]
    gather x2, local copies, waits for them, and re-layouts: 12.4 us -> 6.41 us  [apply_image(): ordered = jnp.take(vectors, order_row, axis=1).astype(jnp.bfloat16)]
    concatenate x4 -> x3, other arithmetic: 7.47 us -> 5.31 us  [the longest x2 4.33 us: extended(): return jnp.concatenate([low, block, high], axis=dim)]
    dot_general x49 -> x25, matrix products: 11.3 us -> 11.7 us  [apply_down(): jnp.einsum('...ab,...bc->...ac', matrix, coeffs, precision=best_precision)]
    unnamed x65 -> x64, local copies, waits for them, and re-layouts: 10.6 us -> 10.2 us
  transfers between devices with their start and end apart: 28 -> 4, of which waited for: 19 -> 0; matrix products, arithmetic and copies ran while one was open for 21% -> 27% of each run, Pallas kernels for 0% -> 0%
where the time goes in v1:
time: 181 us; the launch traced here: 178 us
  blocking collectives  81.4 us (45%)
  local copies, waits for them, and re-layouts  43.7 us (24%)
  matrix products  32.5 us (18%)
  starting transfers between devices  11.1 us (6%)
  other arithmetic  8.32 us (5%)
    all_gather x1, blocking collectives, climb_tree(): leaf_nodes = lax.all_gather(group_root, 'leaf')  51.2 us
    all_gather x1, blocking collectives, climb_tree(): sub_nodes = lax.all_gather(root_coeff, 'sub')  30.2 us
    dot_general x25, matrix products, apply_down(): jnp.einsum('...ab,...bc->...ac', matrix, coeffs, precision=best_precision)  11.7 us
    unnamed x64, local copies, waits for them, and re-layouts  10.2 us
    ppermute x2, starting transfers between devices, extended(): low = lax.ppermute(block, axis, forward)  8.58 us
    dot_general x23, matrix products, apply_up(): jnp.einsum('...ab,...ac->...bc', matrix, coeffs, precision=best_precision)  7.97 us
    gather x2, local copies, waits for them, and re-layouts, apply_image(): ordered = jnp.take(vectors, order_row, axis=1).astype(jnp.bfloat16)  6.41 us
    scatter x1, local copies, waits for them, and re-layouts, apply_image(): return jnp.zeros_like(image).at[:, order_row].set(image)  5.97 us
  transfers between devices with their start and end apart: 4, of which 0 were waited for; matrix products, arithmetic and copies ran while one was open for 27% of the time, Pallas kernels for 0%

profile of v1, /device:TPU:14, one launch (start us, length us, event | category | flops | bytes accessed | tf_op | source)
XLA Modules:
  0.0 178.4 jit_solution(4713910785882863651)
XLA Ops:
  2.0 1.0 pad_maximum_fusion.2
  3.3 6.2 %gather_fusion = bf16[2048,32]{1,0:T(8,128)(2,1)S(1)} fusion(bf16[32,2048]{0,1:T(8,128)(2,1)S(1)} %copy.199, s32[2048]{0:T(1024)S(1)} %broadcast_clamp_fusion), kind=kCustom, calls=%fused_computation | custom fusion | bytes 270336 | tf_op jit(solution)/shard_map/jit(_take)/gather | solution.py:86
  11.8 1.2 fusion.182
  13.7 2.4 %collective-permute-start = (bf16[32,32,32]{1,2,0:T(8,128)(2,1)}, bf16[32,32,32]{1,2,0:T(8,128)(2,1)}, u32[]{:S(2)}, u32[]{:S(2)}) collective-permute-start(bf16[32,32,32]{1,2,0:T(8,128)(2,1)} %convert_bitcast_fusion), channel_id=1, source_target_pairs={{0,1},{1,2},{2,3},{3,4},{4,5},{5,6},{6,7},{7,8},{8,9},{9,10},{10,1... | collective-permute-start | bytes 196616 | tf_op jit(solution)/shard_map/ppermute | solution.py:13
  16.2 1.3 collective-permute-start.1
  17.5 6.1 %collective-permute-start.2 = (bf16[32,32,64]{2,0,1:T(8,128)(2,1)}, bf16[32,32,64]{2,0,1:T(8,128)(2,1)}, u32[]{:S(2)}, u32[]{:S(2)}) collective-permute-start(bf16[32,32,64]{2,0,1:T(8,128)(2,1)} %select_convert_fusion), channel_id=1, source_target_pairs={{0,1},{1,2},{2,3},{3,4},{4,5},{5,6},{6,7},{7,8},{8,9},{9,10},{10,1... | collective-permute-start | bytes 393224 | tf_op jit(solution)/shard_map/ppermute | solution.py:13
  23.6 1.3 collective-permute-start.3
  28.2 30.2 %all-gather = f32[16,1,32,32]{3,2,1,0:T(8,128)S(1)} all-gather(f32[1,1,32,32]{3,2,1,0:T(8,128)S(1)} %copy.214), channel_id=2, replica_groups=mesh['leaf'=64,'sub'=16] {'sub'}, dimensions={0}, use_global_device_ids=true | all-gather | bytes 69632 | tf_op jit(solution)/shard_map/all_gather | solution.py:70
  60.4 51.2 %all_gather.7 = f32[64,32,32]{2,1,0:T(8,128)S(1)} all-gather(f32[1,32,32]{2,1,0:T(8,128)S(1)} %copy.221), channel_id=1, replica_groups=mesh['leaf'=64,'sub'=16] {'leaf'}, dimensions={0}, use_global_device_ids=true | all-gather | bytes 266240 | tf_op jit(solution)/shard_map/all_gather | solution.py:72
  111.5 1.0 fusion.13
  112.5 1.0 convolution_add_fusion.1
  122.5 0.9 convolution_add_fusion.10
  125.4 1.8 %copy.285 = bf16[1,2,32,32]{3,2,1,0:T(8,128)(2,1)} copy(bf16[1,2,32,32]{1,3,2,0:T(8,128)(2,1)} %slice.212) | data formatting | bytes 8192
  127.2 0.9 copy.286
  129.4 2.4 %reshape.178 = bf16[32,6,32,32]{3,2,0,1:T(8,128)(2,1)} reshape(bf16[32,6,1024]{2,0,1:T(8,128)(2,1)S(1)} %copy-done.11) | data formatting | bytes 786432 | tf_op jit(solution)/shard_map/reshape | solution.py:46
  132.5 1.1 copy.289
  134.4 4.3 %reshape.179 = bf16[32,6,64,64]{3,2,0,1:T(8,128)(2,1)S(1)} reshape(bf16[32,6,4096]{2,0,1:T(8,128)(2,1)} %param.21) | data formatting | bytes 3145728 | tf_op jit(solution)/shard_map/reshape | solution.py:45
  140.3 0.9 convolution_bitcast_fusion.3
  141.3 1.1 convolution_bitcast_fusion.2
  142.4 1.0 convolution_bitcast_fusion.1
  143.5 2.2 %pad_maximum_fusion = bf16[96,32,32]{1,2,0:T(8,128)(2,1)} fusion(bf16[32,32,32]{1,2,0:T(8,128)(2,1)} %collective-permute-done.1, bf16[32,32,32]{1,2,0:T(8,128)(2,1)} %convert_bitcast_fusion, bf16[32,32,32]{1,2,0:T(8,128)(2,1)} %collective-permute-done), kind=kLoop, calls=%fused_computation.41 | loop fusion | flops 196608 | bytes 393216 | tf_op jit(solution)/shard_map/concatenate | solution.py:15
  145.6 2.3 %copy.239 = bf16[96,32,32]{2,1,0:T(8,128)(2,1)} copy(bf16[96,32,32]{1,2,0:T(8,128)(2,1)} %pad_maximum_fusion) | data formatting | bytes 393216 | tf_op jit(solution)/shard_map/concatenate | solution.py:15
  147.9 3.1 %gather_fusion.1 = bf16[192,32,32]{2,1,0:T(8,128)(2,1)} fusion(bf16[96,32,32]{2,1,0:T(8,128)(2,1)} %copy.239, s32[1024]{0:T(1024)S(1)} %pad_clamp_fusion.1), kind=kCustom, calls=%fused_computation.1 | custom fusion | bytes 787200 | tf_op jit(solution)/shard_map/gather | solution.py:114
  151.1 3.0 %fusion.2 = f32[32,32,32]{1,2,0:T(8,128)S(1)} fusion(bf16[32,6,32,32]{3,2,1,0:T(8,128)(2,1)} %bitcast.440, f32[32,6]{1,0:T(8,128)S(1)} %copy-done.19, bf16[32,6,32,32]{3,2,0,1:T(8,128)(2,1)} %reshape.178), kind=kOutput, calls=%fused_computation.7 | convolution fusion | flops 12943360 | bytes 918272 | tf_op jit(solution)/shard_map/lkab,lkbc->lkac/dot_general | solution.py:115
  154.2 1.2 fusion.11
  155.4 2.2 %pad_maximum_fusion.1 = bf16[32,96,64]{2,0,1:T(8,128)(2,1)} fusion(bf16[32,32,64]{2,0,1:T(8,128)(2,1)} %collective-permute-done.3, bf16[32,32,64]{2,0,1:T(8,128)(2,1)} %select_convert_fusion, bf16[32,32,64]{2,0,1:T(8,128)(2,1)} %collective-permute-done.2), kind=kLoop, calls=%fused_computation.42 | loop fusion | flops 393216 | bytes 786432 | tf_op jit(solution)/shard_map/concatenate | solution.py:15
  157.6 3.1 %gather_fusion.2 = bf16[192,32,64]{2,1,0:T(8,128)(2,1)} fusion(bf16[32,96,64]{2,0,1:T(8,128)(2,1)} %pad_maximum_fusion.1, s32[1024]{0:T(1024)S(1)} %pad_clamp_fusion), kind=kCustom, calls=%fused_computation.2 | custom fusion | bytes 1573632 | tf_op jit(solution)/shard_map/gather | solution.py:128
  160.7 3.1 %fusion.5 = f32[32,32,6,64]{3,0,2,1:T(8,128)S(1)} fusion(bf16[32,32,6,64]{3,0,2,1:T(8,128)(2,1)} %bitcast.431, bf16[32,6,64,64]{3,2,0,1:T(8,128)(2,1)S(1)} %reshape.179), kind=kOutput, calls=%fused_computation.10 | convolution fusion | flops 50331648 | bytes 3932160 | tf_op jit(solution)/shard_map/lkpq,clkq->clkp/dot_general | solution.py:129
  163.9 5.2 %fusion = f32[32,1,32,64]{3,1,2,0:T(1,128)S(1)} fusion(f32[32,6,1,1]{1,2,3,0:T(1,128)S(1)} %copy-done.16, f32[32,32,6,64]{3,0,2,1:T(8,128)S(1)} %fusion.5), kind=kOutput, calls=%fused_computation.4 | convolution fusion | flops 4718592 | bytes 1835776 | tf_op jit(solution)/shard_map/clkp,lk->clp/dot_general | solution.py:133
  170.2 6.0 %scatter_custom_fusion = f32[32,2048]{0,1:T(8,128)S(1)} fusion(s32[2048]{0:T(1024)} %bitcast.465, f32[2048,32]{1,0:T(8,128)S(1)} %copy.245, f32[]{:T(128)} %constant.104.clone.1), kind=kCustom, calls=%fused_computation.47 | custom fusion | bytes 262656 | tf_op jit(solution)/shard_map/scatter | solution.py:135
  176.5 1.0 copy.246
  177.5 1.0 copy.247
  (144 shorter events, 26.2 us)
Async XLA Ops:
  0.6 168.5 %copy-start = (bf16[32,64,32]{1,2,0:T(8,128)(2,1)S(1)}, bf16[32,64,32]{1,2,0:T(8,128)(2,1)}, u32[]{:S(2)}) copy-start(bf16[32,64,32]{1,2,0:T(8,128)(2,1)} %param.20) | copy-start | bytes 393220
  0.6 9.6 %copy-start.17 = (s32[1,2048]{1,0:T(1,128)S(1)}, s32[1,2048]{1,0:T(1,128)}, u32[]{:S(2)}) copy-start(s32[1,2048]{1,0:T(1,128)} %param.18) | copy-start | bytes 24580
  1.4 0.6 copy-start.18
  3.0 8.8 %copy-start.14 = (bf16[32,64,32]{1,2,0:T(8,128)(2,1)S(1)}, bf16[32,64,32]{1,2,0:T(8,128)(2,1)}, u32[]{:S(2)}) copy-start(bf16[32,64,32]{1,2,0:T(8,128)(2,1)} %param.19) | copy-start | bytes 393220
  9.5 15.4 %copy-start.1 = (bf16[1,62,32,32]{1,3,2,0:T(8,128)(2,1)S(1)}, bf16[1,62,32,32]{1,3,2,0:T(8,128)(2,1)}, u32[]{:S(2)}) copy-start(bf16[1,62,32,32]{1,3,2,0:T(8,128)(2,1)} %param.27) | copy-start | bytes 380932
  13.7 129.7 %collective-permute-start = (bf16[32,32,32]{1,2,0:T(8,128)(2,1)}, bf16[32,32,32]{1,2,0:T(8,128)(2,1)}, u32[]{:S(2)}, u32[]{:S(2)}) collective-permute-start(bf16[32,32,32]{1,2,0:T(8,128)(2,1)} %convert_bitcast_fusion), channel_id=1, source_target_pairs={{0,1},{1,2},{2,3},{3,4},{4,5},{5,6},{6,7},{7,8},{8,9},{9,10},{10,1... | collective-permute-start | bytes 196616 | tf_op jit(solution)/shard_map/ppermute | solution.py:13
  16.2 127.3 %collective-permute-start.1 = (bf16[32,32,32]{1,2,0:T(8,128)(2,1)}, bf16[32,32,32]{1,2,0:T(8,128)(2,1)}, u32[]{:S(2)}, u32[]{:S(2)}) collective-permute-start(bf16[32,32,32]{1,2,0:T(8,128)(2,1)} %convert_bitcast_fusion), channel_id=1, source_target_pairs={{1,0},{2,1},{3,2},{4,3},{5,4},{6,5},{7,6},{8,7},{9,8},{10,9},{11,1... | collective-permute-start | bytes 196616 | tf_op jit(solution)/shard_map/ppermute | solution.py:14
  17.5 137.9 %collective-permute-start.2 = (bf16[32,32,64]{2,0,1:T(8,128)(2,1)}, bf16[32,32,64]{2,0,1:T(8,128)(2,1)}, u32[]{:S(2)}, u32[]{:S(2)}) collective-permute-start(bf16[32,32,64]{2,0,1:T(8,128)(2,1)} %select_convert_fusion), channel_id=1, source_target_pairs={{0,1},{1,2},{2,3},{3,4},{4,5},{5,6},{6,7},{7,8},{8,9},{9,10},{10,1... | collective-permute-start | bytes 393224 | tf_op jit(solution)/shard_map/ppermute | solution.py:13
  23.6 131.8 %collective-permute-start.3 = (bf16[32,32,64]{2,0,1:T(8,128)(2,1)}, bf16[32,32,64]{2,0,1:T(8,128)(2,1)}, u32[]{:S(2)}, u32[]{:S(2)}) collective-permute-start(bf16[32,32,64]{2,0,1:T(8,128)(2,1)} %select_convert_fusion), channel_id=1, source_target_pairs={{1,0},{2,1},{3,2},{4,3},{5,4},{6,5},{7,6},{8,7},{9,8},{10,9},{11,1... | collective-permute-start | bytes 393224 | tf_op jit(solution)/shard_map/ppermute | solution.py:14
  26.3 32.1 %copy-start.3 = (f32[2,32,32]{2,1,0:T(8,128)S(1)}, f32[2,32,32]{2,1,0:T(8,128)}, u32[]{:S(2)}) copy-start(f32[2,32,32]{2,1,0:T(8,128)} %param.29) | copy-start | bytes 24580
  59.2 52.3 %copy-start.9 = (f32[8,32,32]{2,1,0:T(8,128)}, f32[8,32,32]{2,1,0:T(8,128)S(1)}, u32[]{:S(2)}) copy-start(f32[8,32,32]{2,1,0:T(8,128)S(1)} %convolution_add_fusion.4) | copy-start | bytes 98308
  59.6 51.9 %copy-start.12 = (f32[4,32,32]{2,1,0:T(8,128)}, f32[4,32,32]{2,1,0:T(8,128)S(1)}, u32[]{:S(2)}) copy-start(f32[4,32,32]{2,1,0:T(8,128)S(1)} %convolution_add_fusion.6) | copy-start | bytes 49156
  113.5 3.2 %copy-start.2 = (bf16[1,62,32,32]{1,3,2,0:T(8,128)(2,1)S(1)}, bf16[1,62,32,32]{1,3,2,0:T(8,128)(2,1)}, u32[]{:S(2)}) copy-start(bf16[1,62,32,32]{1,3,2,0:T(8,128)(2,1)} %param.28) | copy-start | bytes 380932
  114.5 3.5 %copy-start.7 = (f32[2,32,32]{2,1,0:T(8,128)S(1)}, f32[2,32,32]{2,1,0:T(8,128)}, u32[]{:S(2)}) copy-start(f32[2,32,32]{2,1,0:T(8,128)} %param.30) | copy-start | bytes 24580
  114.5 3.6 %copy-start.8 = (f32[2,32,32]{2,1,0:T(8,128)S(1)}, f32[2,32,32]{2,1,0:T(8,128)}, u32[]{:S(2)}) copy-start(f32[2,32,32]{2,1,0:T(8,128)} %param.31) | copy-start | bytes 24580
  114.8 2.8 %copy-start.10 = (f32[8,32,32]{2,1,0:T(8,128)}, f32[8,32,32]{2,1,0:T(8,128)S(1)}, u32[]{:S(2)}) copy-start(f32[8,32,32]{2,1,0:T(8,128)S(1)} %convolution_add_fusion.3) | copy-start | bytes 98308
  115.2 2.4 %copy-start.13 = (f32[4,32,32]{2,1,0:T(8,128)}, f32[4,32,32]{2,1,0:T(8,128)S(1)}, u32[]{:S(2)}) copy-start(f32[4,32,32]{2,1,0:T(8,128)S(1)} %convolution_add_fusion.5) | copy-start | bytes 49156
  116.7 1.4 copy-start.15
  119.0 10.1 %copy-start.20 = (s32[32,6]{0,1:T(8,128)S(1)}, s32[32,6]{0,1:T(8,128)}, u32[]{:S(2)}) copy-start(s32[32,6]{0,1:T(8,128)} %param.26) | copy-start | bytes 2308
  119.1 10.1 %copy-start.21 = (s32[32,6]{0,1:T(8,128)S(1)}, s32[32,6]{0,1:T(8,128)}, u32[]{:S(2)}) copy-start(s32[32,6]{0,1:T(8,128)} %param.23) | copy-start | bytes 2308
  121.7 7.7 %copy-start.11 = (bf16[32,6,1024]{2,0,1:T(8,128)(2,1)S(1)}, bf16[32,6,1024]{2,0,1:T(8,128)(2,1)}, u32[]{:S(2)}) copy-start(bf16[32,6,1024]{2,0,1:T(8,128)(2,1)} %param.24) | copy-start | bytes 1179652
  127.2 4.6 %copy-start.22 = (f32[32,6]{0,1:T(8,128)S(1)}, f32[32,6]{0,1:T(8,128)}, u32[]{:S(2)}) copy-start(f32[32,6]{0,1:T(8,128)} %param.25) | copy-start | bytes 2308
  134.4 4.3 %copy-start.23 = (f32[32,6]{0,1:T(8,128)S(1)}, f32[32,6]{0,1:T(8,128)}, u32[]{:S(2)}) copy-start(f32[32,6]{0,1:T(8,128)} %param.22) | copy-start | bytes 2308
  138.7 4.7 %copy-start.24 = (s32[192]{0:T(256)S(1)}, s32[192]{0:T(256)}, u32[]{:S(2)}) copy-start(s32[192]{0:T(256)} %reshape.199) | copy-start | bytes 2308
  147.9 3.1 %copy-start.19 = (f32[32,6]{1,0:T(8,128)S(1)}, f32[32,6]{1,0:T(8,128)}, u32[]{:S(2)}) copy-start(f32[32,6]{1,0:T(8,128)} %copy.290) | copy-start | bytes 2308
  151.0 3.0 %copy-start.4 = (f32[16,32,32]{1,2,0:T(8,128)S(1)}, f32[16,32,32]{1,2,0:T(8,128)}, u32[]{:S(2)}) copy-start(f32[16,32,32]{1,2,0:T(8,128)} %convolution_bitcast_fusion.1) | copy-start | bytes 196612
  151.0 3.1 %copy-start.5 = (bf16[1,32,32,32]{3,2,1,0:T(8,128)(2,1)S(1)}, bf16[1,32,32,32]{3,2,1,0:T(8,128)(2,1)}, u32[]{:S(2)}) copy-start(bf16[1,32,32,32]{3,2,1,0:T(8,128)(2,1)} %copy.289) | copy-start | bytes 196612
  160.7 3.2 %copy-start.16 = (f32[32,6,1,1]{1,2,3,0:T(1,128)S(1)}, f32[32,6,1,1]{1,2,3,0:T(1,128)}, u32[]{:S(2)}) copy-start(f32[32,6,1,1]{1,2,3,0:T(1,128)} %copy.253) | copy-start | bytes 2308
  163.9 5.3 %copy-start.6 = (bf16[32,32,32]{1,2,0:T(8,128)(2,1)S(1)}, bf16[32,32,32]{1,2,0:T(8,128)(2,1)}, u32[]{:S(2)}) copy-start(bf16[32,32,32]{1,2,0:T(8,128)(2,1)} %fusion.11) | copy-start | bytes 196612

commit v2 on v1

--- a/solution.py
+++ b/solution.py
@@ -4,10 +4,15 @@
 from jax.sharding import PartitionSpec as P
 
 best_precision = lax.Precision.HIGHEST
+LEAF_AXES = ("lx", "ly")
+SUB_AXES = ("lz", "lc")
+CLIMB_AXES = ("lc", "lz", "ly", "lx")
 
 
 def extended(block, axis, dim):
-    count = lax.axis_size(axis)
+    count = 1
+    for name in axis:
+        count = count * lax.axis_size(name)
     forward = [(i, i + 1) for i in range(count - 1)]
     backward = [(target, source) for source, target in forward]
     low = lax.ppermute(block, axis, forward)
@@ -47,10 +52,6 @@
     order_row = perm[0]
     col_local = loc_col[0].astype(jnp.float32)
     row_local = loc_row[0].astype(jnp.float32)
-    sub_bits = lax.axis_size("sub").bit_length() - 1
-    leaf_bits = lax.axis_size("leaf").bit_length() - 1
-    sub_pos = lax.axis_index("sub")
-    leaf_pos = lax.axis_index("leaf")
 
     def combine_level(nodes):
         pairs = nodes.reshape(nodes.shape[0] // 2, 2, *nodes.shape[1:])
@@ -67,10 +68,12 @@
 
     def climb_tree(root_coeff):
         records = []
-        sub_nodes = lax.all_gather(root_coeff, "sub")
-        group_root = group_levels(sub_nodes, sub_pos, sub_bits, records, False)[0]
-        leaf_nodes = lax.all_gather(group_root, "leaf")
-        group_levels(leaf_nodes, leaf_pos, leaf_bits, records, True)
+        node = root_coeff
+        for step, name in enumerate(CLIMB_AXES):
+            bits = lax.axis_size(name).bit_length() - 1
+            gathered = lax.all_gather(node, name)
+            last = step + 1 == len(CLIMB_AXES)
+            node = group_levels(gathered, lax.axis_index(name), bits, records, last)[0]
         return records
 
     def descend_tree(records, columns):
@@ -85,12 +88,12 @@
         columns = vectors.shape[0]
         ordered = jnp.take(vectors, order_row, axis=1).astype(jnp.bfloat16)
         leaf_blocks = ordered.reshape(columns, leaves_dev, leaf_size)
-        x_window = extended(leaf_blocks, "sub", 1)
+        x_window = extended(leaf_blocks, SUB_AXES, 1)
         leaf_coeff = jnp.einsum(
             "clp,lpk->lkc", leaf_blocks, col_basis, preferred_element_type=jnp.float32
         )
         leaf_round = leaf_coeff.astype(jnp.bfloat16)
-        coeff_window = extended(leaf_round, "sub", 0)
+        coeff_window = extended(leaf_round, SUB_AXES, 0)
         current = leaf_coeff
         offsets = []
         start_at = 0
@@ -139,28 +142,39 @@
     return (both[:rhs], both[rhs:])
 
 
+def split_mesh(mesh):
+    grid = mesh.devices
+    n_leaf, n_sub = grid.shape
+    n_x = len({dev.coords[0] for dev in grid[:, 0]})
+    n_z = len({dev.coords[2] for dev in grid[0, :]})
+    cube = grid.reshape(n_x, n_leaf // n_x, n_z, n_sub // n_z)
+    return jax.sharding.Mesh(cube, LEAF_AXES + SUB_AXES)
+
+
 def solution(mesh):
+    flat = LEAF_AXES + SUB_AXES
+    rows = P(flat, None)
     return jax.shard_map(
         shards,
-        mesh=mesh,
+        mesh=split_mesh(mesh),
         in_specs=(
-            P(None, ("leaf", "sub")),
-            P(None, ("leaf", "sub")),
-            P(("leaf", "sub"), None),
-            P(("leaf", "sub"), None, None),
-            P(("leaf", "sub"), None, None),
-            P(("leaf", "sub"), None, None),
-            P(("leaf", "sub"), None),
-            P(("leaf", "sub"), None),
-            P(("leaf", "sub"), None, None),
-            P(("leaf", "sub"), None),
-            P(("leaf", "sub"), None),
-            P(("leaf", "sub"), None, None, None),
-            P(("leaf", "sub"), None, None, None),
+            P(None, flat),
+            P(None, flat),
+            rows,
+            P(flat, None, None),
+            P(flat, None, None),
+            P(flat, None, None),
+            rows,
+            rows,
+            P(flat, None, None),
+            rows,
+            rows,
+            P(flat, None, None, None),
+            P(flat, None, None, None),
             P(),
             P(),
             P(),
         ),
-        out_specs=(P(None, ("leaf", "sub")), P(None, ("leaf", "sub"))),
+        out_specs=(P(None, flat), P(None, flat)),
         check_vma=False,
     )

time: 181 us -> 181 us (level)
  blocking collectives: 81.4 us -> 90.1 us
  matrix products: 32.5 us -> 25.7 us
  local copies, waits for them, and re-layouts: 43.7 us -> 41.5 us
    all_gather x2 -> x4, blocking collectives: 81.4 us -> 90.1 us  [climb_tree(): gathered = lax.all_gather(node, name)]
    dot_general x25, matrix products: 11.7 us -> 8.12 us  [apply_down(): jnp.einsum('...ab,...bc->...ac', matrix, coeffs, precision=best_precision)]
    dot_general x23, matrix products: 7.97 us -> 4.77 us  [apply_up(): jnp.einsum('...ab,...ac->...bc', matrix, coeffs, precision=best_precision)]
    unnamed x64 -> x50, local copies, waits for them, and re-layouts: 10.2 us -> 8.65 us
  transfers between devices with their start and end apart: 4 -> 4, of which waited for: 0 -> 0; matrix products, arithmetic and copies ran while one was open for 27% -> 23% of each run, Pallas kernels for 0% -> 0%
where the time goes in v2:
time: 181 us; the launch traced here: 179 us
  blocking collectives  90.1 us (50%)
  local copies, waits for them, and re-layouts  41.5 us (23%)
  matrix products  25.7 us (14%)
  starting transfers between devices  11.1 us (6%)
  other arithmetic  9.05 us (5%)
    all_gather x4, blocking collectives, climb_tree(): gathered = lax.all_gather(node, name)  90.1 us
    unnamed x50, local copies, waits for them, and re-layouts  8.65 us
    ppermute x2, starting transfers between devices, extended(): low = lax.ppermute(block, axis, forward)  8.56 us
    dot_general x25, matrix products, apply_down(): jnp.einsum('...ab,...bc->...ac', matrix, coeffs, precision=best_precision)  8.12 us
    gather x2, local copies, waits for them, and re-layouts, apply_image(): ordered = jnp.take(vectors, order_row, axis=1).astype(jnp.bfloat16)  6.41 us
    scatter x1, local copies, waits for them, and re-layouts, apply_image(): return jnp.zeros_like(image).at[:, order_row].set(image)  5.85 us
    dot_general x1, matrix products, apply_image(): jnp.einsum('clkp,lk->clp', near_terms, near_weight, precision=best_precis...  5.23 us
    dot_general x23, matrix products, apply_up(): jnp.einsum('...ab,...ac->...bc', matrix, coeffs, precision=best_precision)  4.77 us
  transfers between devices with their start and end apart: 4, of which 0 were waited for; matrix products, arithmetic and copies ran while one was open for 23% of the time, Pallas kernels for 0%

profile of v2, /device:TPU:14, one launch (start us, length us, event | category | flops | bytes accessed | tf_op | source)
XLA Modules:
  0.0 179.0 jit_solution(3428896063394493203)
XLA Ops:
  1.4 1.0 pad_maximum_fusion.2
  2.7 6.2 %gather_fusion = bf16[2048,32]{1,0:T(8,128)(2,1)S(1)} fusion(bf16[32,2048]{0,1:T(8,128)(2,1)S(1)} %copy.185, s32[2048]{0:T(1024)S(1)} %broadcast_clamp_fusion), kind=kCustom, calls=%fused_computation | custom fusion | bytes 270336 | tf_op jit(solution)/shard_map/jit(_take)/gather | solution.py:89
  11.2 1.2 fusion.184
  13.2 2.5 %collective-permute-start = (bf16[32,32,32]{1,2,0:T(8,128)(2,1)}, bf16[32,32,32]{1,2,0:T(8,128)(2,1)}, u32[]{:S(2)}, u32[]{:S(2)}) collective-permute-start(bf16[32,32,32]{1,2,0:T(8,128)(2,1)} %convert_bitcast_fusion), channel_id=1, source_target_pairs={{0,1},{1,2},{2,3},{3,4},{4,5},{5,6},{6,7},{7,8},{8,9},{9,10},{10,1... | collective-permute-start | bytes 196616 | tf_op jit(solution)/shard_map/ppermute | solution.py:18
  15.6 1.3 collective-permute-start.1
  16.9 6.1 %collective-permute-start.2 = (bf16[32,32,64]{2,0,1:T(8,128)(2,1)}, bf16[32,32,64]{2,0,1:T(8,128)(2,1)}, u32[]{:S(2)}, u32[]{:S(2)}) collective-permute-start(bf16[32,32,64]{2,0,1:T(8,128)(2,1)} %select_convert_fusion), channel_id=1, source_target_pairs={{0,1},{1,2},{2,3},{3,4},{4,5},{5,6},{6,7},{7,8},{8,9},{9,10},{10,1... | collective-permute-start | bytes 393224 | tf_op jit(solution)/shard_map/ppermute | solution.py:18
  23.0 1.3 collective-permute-start.3
  27.6 3.2 %all-gather = f32[2,1,32,32]{3,2,1,0:T(8,128)S(1)} all-gather(f32[1,1,32,32]{3,2,1,0:T(8,128)S(1)} %copy.200), channel_id=2, replica_groups=mesh['lx'=8,'ly'=8,'lz'=8,'lc'=2] {'lc'}, dimensions={0}, use_global_device_ids=true | all-gather | bytes 12288 | tf_op jit(solution)/shard_map/all_gather | solution.py:74
  31.3 35.5 %all_gather.13 = f32[8,32,32]{2,1,0:T(8,128)S(1)} all-gather(f32[1,32,32]{2,1,0:T(8,128)S(1)} %copy.201), channel_id=1, replica_groups=mesh['lx'=8,'ly'=8,'lz'=8,'lc'=2] {'lz'}, dimensions={0}, use_global_device_ids=true | all-gather | bytes 36864 | tf_op jit(solution)/shard_map/all_gather | solution.py:74
  68.1 26.9 %all_gather.14 = f32[8,32,32]{2,1,0:T(8,128)S(1)} all-gather(f32[1,32,32]{2,1,0:T(8,128)S(1)} %copy.206), channel_id=1, replica_groups=mesh['lx'=8,'ly'=8,'lz'=8,'lc'=2] {'ly'}, dimensions={0}, use_global_device_ids=true | all-gather | bytes 36864 | tf_op jit(solution)/shard_map/all_gather | solution.py:74
  96.3 24.6 %all_gather.15 = f32[8,32,32]{2,1,0:T(8,128)S(1)} all-gather(f32[1,32,32]{2,1,0:T(8,128)S(1)} %copy.211), channel_id=1, replica_groups=mesh['lx'=8,'ly'=8,'lz'=8,'lc'=2] {'lx'}, dimensions={0}, use_global_device_ids=true | all-gather | bytes 36864 | tf_op jit(solution)/shard_map/all_gather | solution.py:74
  126.2 0.9 copy.265
  127.1 0.9 copy.266
  129.3 2.4 %reshape.204 = bf16[32,6,32,32]{3,2,0,1:T(8,128)(2,1)} reshape(bf16[32,6,1024]{2,0,1:T(8,128)(2,1)S(1)} %copy-done.9) | data formatting | bytes 786432 | tf_op jit(solution)/shard_map/reshape | solution.py:51
  132.4 1.1 copy.269
  134.3 4.3 %reshape.205 = bf16[32,6,64,64]{3,2,0,1:T(8,128)(2,1)S(1)} reshape(bf16[32,6,4096]{2,0,1:T(8,128)(2,1)} %param.21) | data formatting | bytes 3145728 | tf_op jit(solution)/shard_map/reshape | solution.py:50
  140.0 0.9 convolution_bitcast_fusion.4
  140.9 0.9 convolution_bitcast_fusion.3
  141.9 1.1 convolution_bitcast_fusion.2
  143.0 1.1 convolution_bitcast_fusion.1
  144.1 2.2 %pad_maximum_fusion = bf16[96,32,32]{1,2,0:T(8,128)(2,1)} fusion(bf16[32,32,32]{1,2,0:T(8,128)(2,1)} %collective-permute-done.1, bf16[32,32,32]{1,2,0:T(8,128)(2,1)} %convert_bitcast_fusion, bf16[32,32,32]{1,2,0:T(8,128)(2,1)} %collective-permute-done), kind=kLoop, calls=%fused_computation.43 | loop fusion | flops 196608 | bytes 393216 | tf_op jit(solution)/shard_map/concatenate | solution.py:20
  146.2 2.3 %copy.223 = bf16[96,32,32]{2,1,0:T(8,128)(2,1)} copy(bf16[96,32,32]{1,2,0:T(8,128)(2,1)} %pad_maximum_fusion) | data formatting | bytes 393216 | tf_op jit(solution)/shard_map/concatenate | solution.py:20
  148.6 3.1 %gather_fusion.1 = bf16[192,32,32]{2,1,0:T(8,128)(2,1)} fusion(bf16[96,32,32]{2,1,0:T(8,128)(2,1)} %copy.223, s32[1024]{0:T(1024)S(1)} %pad_clamp_fusion.1), kind=kCustom, calls=%fused_computation.1 | custom fusion | bytes 787200 | tf_op jit(solution)/shard_map/gather | solution.py:117
  151.7 3.0 %fusion.2 = f32[32,32,32]{1,2,0:T(8,128)S(1)} fusion(bf16[32,6,32,32]{3,2,1,0:T(8,128)(2,1)} %bitcast.426, f32[32,6]{1,0:T(8,128)S(1)} %copy-done.13, bf16[32,6,32,32]{3,2,0,1:T(8,128)(2,1)} %reshape.204), kind=kOutput, calls=%fused_computation.7 | convolution fusion | flops 12943360 | bytes 918272 | tf_op jit(solution)/shard_map/lkab,lkbc->lkac/dot_general | solution.py:118
  154.8 1.2 fusion.11
  156.1 2.2 %pad_maximum_fusion.1 = bf16[32,96,64]{2,0,1:T(8,128)(2,1)} fusion(bf16[32,32,64]{2,0,1:T(8,128)(2,1)} %collective-permute-done.3, bf16[32,32,64]{2,0,1:T(8,128)(2,1)} %select_convert_fusion, bf16[32,32,64]{2,0,1:T(8,128)(2,1)} %collective-permute-done.2), kind=kLoop, calls=%fused_computation.44 | loop fusion | flops 393216 | bytes 786432 | tf_op jit(solution)/shard_map/concatenate | solution.py:20
  158.3 3.2 %gather_fusion.2 = bf16[192,32,64]{2,1,0:T(8,128)(2,1)} fusion(bf16[32,96,64]{2,0,1:T(8,128)(2,1)} %pad_maximum_fusion.1, s32[1024]{0:T(1024)S(1)} %pad_clamp_fusion), kind=kCustom, calls=%fused_computation.2 | custom fusion | bytes 1573632 | tf_op jit(solution)/shard_map/gather | solution.py:131
  161.4 3.1 %fusion.5 = f32[32,32,6,64]{3,0,2,1:T(8,128)S(1)} fusion(bf16[32,32,6,64]{3,0,2,1:T(8,128)(2,1)} %bitcast.421, bf16[32,6,64,64]{3,2,0,1:T(8,128)(2,1)S(1)} %reshape.205), kind=kOutput, calls=%fused_computation.10 | convolution fusion | flops 50331648 | bytes 3932160 | tf_op jit(solution)/shard_map/lkpq,clkq->clkp/dot_general | solution.py:132
  164.6 5.2 %fusion = f32[32,1,32,64]{3,1,2,0:T(1,128)S(1)} fusion(f32[32,6,1,1]{1,2,3,0:T(1,128)S(1)} %copy-done.11, f32[32,32,6,64]{3,0,2,1:T(8,128)S(1)} %fusion.5), kind=kOutput, calls=%fused_computation.4 | convolution fusion | flops 4718592 | bytes 1835776 | tf_op jit(solution)/shard_map/clkp,lk->clp/dot_general | solution.py:136
  170.9 5.8 %scatter_custom_fusion = f32[32,2048]{0,1:T(8,128)S(1)} fusion(s32[2048]{0:T(1024)S(1)} %bitcast.455, f32[2048,32]{1,0:T(8,128)S(1)} %copy.229, f32[]{:T(128)} %constant.101.clone.1), kind=kCustom, calls=%fused_computation.46 | custom fusion | bytes 262148 | tf_op jit(solution)/shard_map/scatter | solution.py:138
  177.1 1.0 copy.230
  178.0 1.0 copy.231
  (134 shorter events, 21.0 us)
Async XLA Ops:
  0.6 169.2 %copy-start = (bf16[32,64,32]{1,2,0:T(8,128)(2,1)S(1)}, bf16[32,64,32]{1,2,0:T(8,128)(2,1)}, u32[]{:S(2)}) copy-start(bf16[32,64,32]{1,2,0:T(8,128)(2,1)} %param.20) | copy-start | bytes 393220
  0.6 9.0 %copy-start.12 = (s32[1,2048]{1,0:T(1,128)S(1)}, s32[1,2048]{1,0:T(1,128)}, u32[]{:S(2)}) copy-start(s32[1,2048]{1,0:T(1,128)} %param.18) | copy-start | bytes 24580
  2.4 8.8 %copy-start.10 = (bf16[32,64,32]{1,2,0:T(8,128)(2,1)S(1)}, bf16[32,64,32]{1,2,0:T(8,128)(2,1)}, u32[]{:S(2)}) copy-start(bf16[32,64,32]{1,2,0:T(8,128)(2,1)} %param.19) | copy-start | bytes 393220
  8.9 15.4 %copy-start.1 = (bf16[1,62,32,32]{1,3,2,0:T(8,128)(2,1)S(1)}, bf16[1,62,32,32]{1,3,2,0:T(8,128)(2,1)}, u32[]{:S(2)}) copy-start(bf16[1,62,32,32]{1,3,2,0:T(8,128)(2,1)} %param.27) | copy-start | bytes 380932
  13.2 130.9 %collective-permute-start = (bf16[32,32,32]{1,2,0:T(8,128)(2,1)}, bf16[32,32,32]{1,2,0:T(8,128)(2,1)}, u32[]{:S(2)}, u32[]{:S(2)}) collective-permute-start(bf16[32,32,32]{1,2,0:T(8,128)(2,1)} %convert_bitcast_fusion), channel_id=1, source_target_pairs={{0,1},{1,2},{2,3},{3,4},{4,5},{5,6},{6,7},{7,8},{8,9},{9,10},{10,1... | collective-permute-start | bytes 196616 | tf_op jit(solution)/shard_map/ppermute | solution.py:18
  15.6 128.4 %collective-permute-start.1 = (bf16[32,32,32]{1,2,0:T(8,128)(2,1)}, bf16[32,32,32]{1,2,0:T(8,128)(2,1)}, u32[]{:S(2)}, u32[]{:S(2)}) collective-permute-start(bf16[32,32,32]{1,2,0:T(8,128)(2,1)} %convert_bitcast_fusion), channel_id=1, source_target_pairs={{1,0},{2,1},{3,2},{4,3},{5,4},{6,5},{7,6},{8,7},{9,8},{10,9},{11,1... | collective-permute-start | bytes 196616 | tf_op jit(solution)/shard_map/ppermute | solution.py:19
  16.9 139.2 %collective-permute-start.2 = (bf16[32,32,64]{2,0,1:T(8,128)(2,1)}, bf16[32,32,64]{2,0,1:T(8,128)(2,1)}, u32[]{:S(2)}, u32[]{:S(2)}) collective-permute-start(bf16[32,32,64]{2,0,1:T(8,128)(2,1)} %select_convert_fusion), channel_id=1, source_target_pairs={{0,1},{1,2},{2,3},{3,4},{4,5},{5,6},{6,7},{7,8},{8,9},{9,10},{10,1... | collective-permute-start | bytes 393224 | tf_op jit(solution)/shard_map/ppermute | solution.py:18
  23.0 133.1 %collective-permute-start.3 = (bf16[32,32,64]{2,0,1:T(8,128)(2,1)}, bf16[32,32,64]{2,0,1:T(8,128)(2,1)}, u32[]{:S(2)}, u32[]{:S(2)}) collective-permute-start(bf16[32,32,64]{2,0,1:T(8,128)(2,1)} %select_convert_fusion), channel_id=1, source_target_pairs={{1,0},{2,1},{3,2},{4,3},{5,4},{6,5},{7,6},{8,7},{9,8},{10,9},{11,1... | collective-permute-start | bytes 393224 | tf_op jit(solution)/shard_map/ppermute | solution.py:19
  25.7 5.1 %copy-start.3 = (f32[2,32,32]{2,1,0:T(8,128)S(1)}, f32[2,32,32]{2,1,0:T(8,128)}, u32[]{:S(2)}) copy-start(f32[2,32,32]{2,1,0:T(8,128)} %param.29) | copy-start | bytes 24580
  27.2 94.6 %copy-start.2 = (bf16[1,62,32,32]{1,3,2,0:T(8,128)(2,1)S(1)}, bf16[1,62,32,32]{1,3,2,0:T(8,128)(2,1)}, u32[]{:S(2)}) copy-start(bf16[1,62,32,32]{1,3,2,0:T(8,128)(2,1)} %param.28) | copy-start | bytes 380932
  95.7 26.7 %copy-start.7 = (f32[2,32,32]{2,1,0:T(8,128)S(1)}, f32[2,32,32]{2,1,0:T(8,128)}, u32[]{:S(2)}) copy-start(f32[2,32,32]{2,1,0:T(8,128)} %param.30) | copy-start | bytes 24580
  95.9 26.7 %copy-start.8 = (f32[2,32,32]{2,1,0:T(8,128)S(1)}, f32[2,32,32]{2,1,0:T(8,128)}, u32[]{:S(2)}) copy-start(f32[2,32,32]{2,1,0:T(8,128)} %param.31) | copy-start | bytes 24580
  122.3 6.8 %copy-start.14 = (s32[32,6]{0,1:T(8,128)S(1)}, s32[32,6]{0,1:T(8,128)}, u32[]{:S(2)}) copy-start(s32[32,6]{0,1:T(8,128)} %param.26) | copy-start | bytes 2308
  122.3 6.8 %copy-start.15 = (s32[32,6]{0,1:T(8,128)S(1)}, s32[32,6]{0,1:T(8,128)}, u32[]{:S(2)}) copy-start(s32[32,6]{0,1:T(8,128)} %param.23) | copy-start | bytes 2308
  122.3 7.0 %copy-start.9 = (bf16[32,6,1024]{2,0,1:T(8,128)(2,1)S(1)}, bf16[32,6,1024]{2,0,1:T(8,128)(2,1)}, u32[]{:S(2)}) copy-start(bf16[32,6,1024]{2,0,1:T(8,128)(2,1)} %param.24) | copy-start | bytes 1179652
  127.1 4.6 %copy-start.16 = (f32[32,6]{0,1:T(8,128)S(1)}, f32[32,6]{0,1:T(8,128)}, u32[]{:S(2)}) copy-start(f32[32,6]{0,1:T(8,128)} %param.25) | copy-start | bytes 2308
  140.0 4.0 %copy-start.17 = (s32[192]{0:T(256)S(1)}, s32[192]{0:T(256)}, u32[]{:S(2)}) copy-start(s32[192]{0:T(256)} %reshape.225) | copy-start | bytes 2308
  148.6 3.1 %copy-start.13 = (f32[32,6]{1,0:T(8,128)S(1)}, f32[32,6]{1,0:T(8,128)}, u32[]{:S(2)}) copy-start(f32[32,6]{1,0:T(8,128)} %copy.270) | copy-start | bytes 2308
  151.7 3.0 %copy-start.4 = (f32[16,32,32]{1,2,0:T(8,128)S(1)}, f32[16,32,32]{1,2,0:T(8,128)}, u32[]{:S(2)}) copy-start(f32[16,32,32]{1,2,0:T(8,128)} %convolution_bitcast_fusion.1) | copy-start | bytes 196612
  151.7 3.1 %copy-start.5 = (bf16[1,32,32,32]{3,2,1,0:T(8,128)(2,1)S(1)}, bf16[1,32,32,32]{3,2,1,0:T(8,128)(2,1)}, u32[]{:S(2)}) copy-start(bf16[1,32,32,32]{3,2,1,0:T(8,128)(2,1)} %copy.269) | copy-start | bytes 196612
  161.4 3.2 %copy-start.11 = (f32[32,6,1,1]{1,2,3,0:T(1,128)S(1)}, f32[32,6,1,1]{1,2,3,0:T(1,128)}, u32[]{:S(2)}) copy-start(f32[32,6,1,1]{1,2,3,0:T(1,128)} %copy.237) | copy-start | bytes 2308
  164.6 5.3 %copy-start.6 = (bf16[32,32,32]{1,2,0:T(8,128)(2,1)S(1)}, bf16[32,32,32]{1,2,0:T(8,128)(2,1)}, u32[]{:S(2)}) copy-start(bf16[32,32,32]{1,2,0:T(8,128)(2,1)} %fusion.11) | copy-start | bytes 196612

commit v3 on v2

--- a/solution.py
+++ b/solution.py
@@ -6,7 +6,7 @@
 best_precision = lax.Precision.HIGHEST
 LEAF_AXES = ("lx", "ly")
 SUB_AXES = ("lz", "lc")
-CLIMB_AXES = ("lc", "lz", "ly", "lx")
+CLIMB_AXES = (SUB_AXES, LEAF_AXES)
 
 
 def extended(block, axis, dim):
@@ -69,11 +69,17 @@
     def climb_tree(root_coeff):
         records = []
         node = root_coeff
-        for step, name in enumerate(CLIMB_AXES):
-            bits = lax.axis_size(name).bit_length() - 1
-            gathered = lax.all_gather(node, name)
+        for step, names in enumerate(CLIMB_AXES):
+            count = 1
+            pos = 0
+            for name in names:
+                count = count * lax.axis_size(name)
+                pos = pos * lax.axis_size(name) + lax.axis_index(name)
+            bits = count.bit_length() - 1
+            slots = jnp.zeros((count,) + node.shape, node.dtype)
+            gathered = lax.psum(lax.dynamic_update_index_in_dim(slots, node, pos, 0), names)
             last = step + 1 == len(CLIMB_AXES)
-            node = group_levels(gathered, lax.axis_index(name), bits, records, last)[0]
+            node = group_levels(gathered, pos, bits, records, last)[0]
         return records
 
     def descend_tree(records, columns):

time: 181 us -> 377 us (2.08)
  waiting for transfers between devices: 0.01 us -> 263 us
  blocking collectives: 90.1 us -> 0 us
  between operations: 1.46 us -> 15 us
  matrix products: 25.7 us -> 32.1 us
  local copies, waits for them, and re-layouts: 41.5 us -> 46.1 us
    psum x0 -> x2, waiting for transfers between devices: none -> 263 us  [climb_tree(): lax.psum(lax.dynamic_update_index_in_dim(slots, node, pos, 0), names)]
    all_gather x4 -> x0, blocking collectives: 90.1 us -> none  [climb_tree(): gathered = lax.all_gather(node, name)]
    dot_general x23, matrix products: 4.77 us -> 11.3 us  [apply_up(): jnp.einsum('...ab,...ac->...bc', matrix, coeffs, precision=best_precision)]
    unnamed x50 -> x64, local copies, waits for them, and re-layouts: 8.65 us -> 10.9 us
  transfers between devices with their start and end apart: 4 -> 6, of which waited for: 0 -> 2; matrix products, arithmetic and copies ran while one was open for 23% -> 14% of each run, Pallas kernels for 0% -> 0%
where the time goes in v3:
time: 377 us; the launch traced here: 376 us
  waiting for transfers between devices  263 us (70%)
  local copies, waits for them, and re-layouts  46.1 us (12%)
  matrix products  32.1 us (9%)
  between operations  15 us (4%)
  starting transfers between devices  11.4 us (3%)
  other arithmetic  8.3 us (2%)
    psum x2, waiting for transfers between devices, climb_tree(): lax.psum(lax.dynamic_update_index_in_dim(slots, node, pos, 0), names)  263 us
    dot_general x23, matrix products, apply_up(): jnp.einsum('...ab,...ac->...bc', matrix, coeffs, precision=best_precision)  11.3 us
    unnamed x64, local copies, waits for them, and re-layouts  10.9 us
    ppermute x2, starting transfers between devices, extended(): low = lax.ppermute(block, axis, forward)  8.55 us
  transfers between devices with their start and end apart: 6, of which 2 were waited for; matrix products, arithmetic and copies ran while one was open for 14% of the time, Pallas kernels for 0%

profile of v3, /device:TPU:14, one launch (start us, length us, event | category | flops | bytes accessed | tf_op | source)
XLA Modules:
  0.0 375.5 jit_solution(14808207148871422927)
XLA Ops:
  8.0 1.0 pad_maximum_fusion.2
  9.3 6.2 %gather_fusion = bf16[2048,32]{1,0:T(8,128)(2,1)S(1)} fusion(bf16[32,2048]{0,1:T(8,128)(2,1)S(1)} %copy.201, s32[2048]{0:T(1024)S(1)} %broadcast_clamp_fusion), kind=kCustom, calls=%fused_computation | custom fusion | bytes 270336 | tf_op jit(solution)/shard_map/jit(_take)/gather | solution.py:95
  17.8 1.2 fusion.183
  19.7 2.4 collective-permute-start
  22.1 1.3 collective-permute-start.1
  23.4 6.1 %collective-permute-start.2 = (bf16[32,32,64]{2,0,1:T(8,128)(2,1)}, bf16[32,32,64]{2,0,1:T(8,128)(2,1)}, u32[]{:S(2)}, u32[]{:S(2)}) collective-permute-start(bf16[32,32,64]{2,0,1:T(8,128)(2,1)} %select_convert_fusion), channel_id=1, source_target_pairs={{0,1},{1,2},{2,3},{3,4},{4,5},{5,6},{6,7},{7,8},{8,9},{9,10},{10,1... | collective-permute-start | bytes 393224 | tf_op jit(solution)/shard_map/ppermute | solution.py:18
  29.5 1.3 collective-permute-start.3
  38.0 0.9 copy.288
  39.7 0.9 copy.290
  40.6 2.4 reshape.179
  43.6 1.1 copy.291
  44.8 4.3 %reshape.180 = bf16[32,6,64,64]{3,2,0,1:T(8,128)(2,1)S(1)} reshape(bf16[32,6,4096]{2,0,1:T(8,128)(2,1)} %param.21) | data formatting | bytes 3145728 | tf_op jit(solution)/shard_map/reshape | solution.py:50
  49.8 118.5 %all-reduce.3.cloned.1.call-done = f32[16,32,32]{2,1,0:T(8,128)} async-done(((f32[16,32,32]{2,1,0:T(8,128)}), f32[16,32,32]{2,1,0:T(8,128)}) %all-reduce.3.cloned.1.call-update) | async-done | bytes 65552 | tf_op jit(solution)/shard_map/psum | solution.py:80
  168.2 1.3 fusion.25
  169.5 1.3 convolution_add_fusion.4
  173.4 1.4 copy.223
  174.7 1.1 broadcast_in_dim.49
  175.9 1.3 constant_dynamic-update-slice_fusion
  177.2 2.2 pad_maximum_fusion
  179.4 2.3 copy.241
  181.7 3.1 gather_fusion.1
  184.8 3.8 %fusion.2 = f32[32,32,32]{1,2,0:T(8,128)} fusion(bf16[32,6,32,32]{3,2,1,0:T(8,128)(2,1)} %bitcast.440, f32[32,6]{1,0:T(8,128)} %copy.292, bf16[32,6,32,32]{3,2,0,1:T(8,128)(2,1)} %reshape.179), kind=kOutput, calls=%fused_computation.7 | convolution fusion | flops 12943360 | bytes 918272 | tf_op jit(solution)/shard_map/lkab,lkbc->lkac/dot_general | solution.py:124
  188.6 2.2 pad_maximum_fusion.1
  190.7 3.1 gather_fusion.2
  193.9 3.1 fusion.5
  197.0 5.4 %fusion = f32[32,1,32,64]{3,1,2,0:T(1,128)S(1)} fusion(f32[32,6,1,1]{1,2,3,0:T(1,128)S(1)} %copy-done.17, f32[32,32,6,64]{3,0,2,1:T(8,128)S(1)} %fusion.5), kind=kOutput, calls=%fused_computation.4 | convolution fusion | flops 4718592 | bytes 1835776 | tf_op jit(solution)/shard_map/clkp,lk->clp/dot_general | solution.py:142
  202.5 144.1 %all-reduce.5.cloned.1.call-done = f32[64,32,32]{2,1,0:T(8,128)} async-done(((f32[64,32,32]{2,1,0:T(8,128)}), f32[64,32,32]{2,1,0:T(8,128)}) %all-reduce.5.cloned.1.call-update) | async-done | bytes 262160 | tf_op jit(solution)/shard_map/psum | solution.py:80
  346.6 2.0 fusion.13
  348.6 2.0 convolution_add_fusion.1
  360.6 5.8 %scatter_custom_fusion = f32[32,2048]{0,1:T(8,128)S(1)} fusion(s32[2048]{0:T(1024)S(1)} %bitcast.467, f32[2048,32]{1,0:T(8,128)S(1)} %copy.247, f32[]{:T(128)} %constant.121.clone.1), kind=kCustom, calls=%fused_computation.47 | custom fusion | bytes 262148 | tf_op jit(solution)/shard_map/scatter | solution.py:144
  366.7 1.0 copy.248
  367.7 1.0 copy.249
  (152 shorter events, 25.4 us)
Async XLA Ops:
  7.2 352.3 %copy-start = (bf16[32,64,32]{1,2,0:T(8,128)(2,1)S(1)}, bf16[32,64,32]{1,2,0:T(8,128)(2,1)}, u32[]{:S(2)}) copy-start(bf16[32,64,32]{1,2,0:T(8,128)(2,1)} %param.20) | copy-start | bytes 393220
  7.2 9.0 %copy-start.20 = (s32[1,2048]{1,0:T(1,128)S(1)}, s32[1,2048]{1,0:T(1,128)}, u32[]{:S(2)}) copy-start(s32[1,2048]{1,0:T(1,128)} %param.18) | copy-start | bytes 24580
  7.2 161.0 %all-reduce.3.cloned.1.call-start = ((), (), s32[]{:S(2)}) async-start(), calls=%async_computation | async-start | bytes 524288 | tf_op jit(solution)/shard_map/psum | solution.py:80
  9.0 8.8 %copy-start.13 = (bf16[32,64,32]{1,2,0:T(8,128)(2,1)S(1)}, bf16[32,64,32]{1,2,0:T(8,128)(2,1)}, u32[]{:S(2)}) copy-start(bf16[32,64,32]{1,2,0:T(8,128)(2,1)} %param.19) | copy-start | bytes 393220
  15.5 15.4 %copy-start.1 = (bf16[1,62,32,32]{1,3,2,0:T(8,128)(2,1)S(1)}, bf16[1,62,32,32]{1,3,2,0:T(8,128)(2,1)}, u32[]{:S(2)}) copy-start(bf16[1,62,32,32]{1,3,2,0:T(8,128)(2,1)} %param.27) | copy-start | bytes 380932
  19.7 157.5 %collective-permute-start = (bf16[32,32,32]{1,2,0:T(8,128)(2,1)}, bf16[32,32,32]{1,2,0:T(8,128)(2,1)}, u32[]{:S(2)}, u32[]{:S(2)}) collective-permute-start(bf16[32,32,32]{1,2,0:T(8,128)(2,1)} %convert_bitcast_fusion), channel_id=1, source_target_pairs={{0,1},{1,2},{2,3},{3,4},{4,5},{5,6},{6,7},{7,8},{8,9},{9,10},{10,1... | collective-permute-start | bytes 196616 | tf_op jit(solution)/shard_map/ppermute | solution.py:18
  22.1 155.1 %collective-permute-start.1 = (bf16[32,32,32]{1,2,0:T(8,128)(2,1)}, bf16[32,32,32]{1,2,0:T(8,128)(2,1)}, u32[]{:S(2)}, u32[]{:S(2)}) collective-permute-start(bf16[32,32,32]{1,2,0:T(8,128)(2,1)} %convert_bitcast_fusion), channel_id=1, source_target_pairs={{1,0},{2,1},{3,2},{4,3},{5,4},{6,5},{7,6},{8,7},{9,8},{10,9},{11,1... | collective-permute-start | bytes 196616 | tf_op jit(solution)/shard_map/ppermute | solution.py:19
  23.4 165.1 %collective-permute-start.2 = (bf16[32,32,64]{2,0,1:T(8,128)(2,1)}, bf16[32,32,64]{2,0,1:T(8,128)(2,1)}, u32[]{:S(2)}, u32[]{:S(2)}) collective-permute-start(bf16[32,32,64]{2,0,1:T(8,128)(2,1)} %select_convert_fusion), channel_id=1, source_target_pairs={{0,1},{1,2},{2,3},{3,4},{4,5},{5,6},{6,7},{7,8},{8,9},{9,10},{10,1... | collective-permute-start | bytes 393224 | tf_op jit(solution)/shard_map/ppermute | solution.py:18
  29.5 159.0 %collective-permute-start.3 = (bf16[32,32,64]{2,0,1:T(8,128)(2,1)}, bf16[32,32,64]{2,0,1:T(8,128)(2,1)}, u32[]{:S(2)}, u32[]{:S(2)}) collective-permute-start(bf16[32,32,64]{2,0,1:T(8,128)(2,1)} %select_convert_fusion), channel_id=1, source_target_pairs={{1,0},{2,1},{3,2},{4,3},{5,4},{6,5},{7,6},{8,7},{9,8},{10,9},{11,1... | collective-permute-start | bytes 393224 | tf_op jit(solution)/shard_map/ppermute | solution.py:19
  32.3 3.0 copy-start.21
  32.3 3.0 copy-start.22
  32.3 3.2 copy-start.23
  32.3 3.4 copy-start.24
  32.3 3.4 copy-start.6
  32.6 3.9 %copy-start.2 = (bf16[1,62,32,32]{1,3,2,0:T(8,128)(2,1)S(1)}, bf16[1,62,32,32]{1,3,2,0:T(8,128)(2,1)}, u32[]{:S(2)}) copy-start(bf16[1,62,32,32]{1,3,2,0:T(8,128)(2,1)} %param.28) | copy-start | bytes 380932
  34.3 0.7 copy-start.4
  35.0 311.6 %all-reduce.5.cloned.1.call-start = ((), (), s32[]{:S(2)}) async-start(), calls=%async_computation.1 | async-start | bytes 2097152 | tf_op jit(solution)/shard_map/psum | solution.py:80
  36.5 4.1 %copy-start.11 = (bf16[32,6,1024]{2,0,1:T(8,128)(2,1)S(1)}, bf16[32,6,1024]{2,0,1:T(8,128)(2,1)}, u32[]{:S(2)}) copy-start(bf16[32,6,1024]{2,0,1:T(8,128)(2,1)} %param.24) | copy-start | bytes 1179652
  44.8 123.5 %copy-start.3 = (f32[2,32,32]{2,1,0:T(8,128)S(1)}, f32[2,32,32]{2,1,0:T(8,128)}, u32[]{:S(2)}) copy-start(f32[2,32,32]{2,1,0:T(8,128)} %param.29) | copy-start | bytes 24580
  170.8 0.7 copy-start.8
  172.0 0.6 copy-start.14
  193.9 3.2 copy-start.17
  350.7 2.0 copy-start.7
  350.7 2.0 copy-start.19
  350.7 4.6 %copy-start.15 = (f32[2,32,32]{2,1,0:T(8,128)S(1)}, f32[2,32,32]{2,1,0:T(8,128)}, u32[]{:S(2)}) copy-start(f32[2,32,32]{2,1,0:T(8,128)} %copy-done.14) | copy-start | bytes 24580
  351.1 6.8 %copy-start.18 = (bf16[1,2,32,32]{3,2,1,0:T(8,128)(2,1)S(1)}, bf16[1,2,32,32]{3,2,1,0:T(8,128)(2,1)}, u32[]{:S(2)}) copy-start(bf16[1,2,32,32]{3,2,1,0:T(8,128)(2,1)} %copy.287) | copy-start | bytes 12292
  351.1 7.0 %copy-start.16 = (bf16[1,4,32,32]{3,2,1,0:T(8,128)(2,1)S(1)}, bf16[1,4,32,32]{3,2,1,0:T(8,128)(2,1)}, u32[]{:S(2)}) copy-start(bf16[1,4,32,32]{3,2,1,0:T(8,128)(2,1)} %copy.288) | copy-start | bytes 24580
  351.5 6.8 %copy-start.12 = (bf16[1,8,32,32]{3,2,1,0:T(8,128)(2,1)S(1)}, bf16[1,8,32,32]{3,2,1,0:T(8,128)(2,1)}, u32[]{:S(2)}) copy-start(bf16[1,8,32,32]{3,2,1,0:T(8,128)(2,1)} %copy.289) | copy-start | bytes 49156
  351.7 6.8 %copy-start.10 = (bf16[1,16,32,32]{3,2,1,0:T(8,128)(2,1)S(1)}, bf16[1,16,32,32]{3,2,1,0:T(8,128)(2,1)}, u32[]{:S(2)}) copy-start(bf16[1,16,32,32]{3,2,1,0:T(8,128)(2,1)} %copy.290) | copy-start | bytes 98308
  355.3 3.6 copy-start.5
  355.3 3.6 copy-start.9
Sparse Core Ops, SparseCore 0:
  35.1 133.0 all-reduce.2
  177.3 169.2 all-reduce.4

commit v4 on v2

--- a/solution.py
+++ b/solution.py
@@ -7,6 +7,12 @@
 LEAF_AXES = ("lx", "ly")
 SUB_AXES = ("lz", "lc")
 CLIMB_AXES = ("lc", "lz", "ly", "lx")
+
+
+def from_partner(value, axis, distance):
+    mask = 2**distance
+    pairs = [(source, source ^ mask) for source in range(lax.axis_size(axis))]
+    return lax.ppermute(value, axis, pairs)
 
 
 def extended(block, axis, dim):
@@ -53,36 +59,34 @@
     col_local = loc_col[0].astype(jnp.float32)
     row_local = loc_row[0].astype(jnp.float32)
 
-    def combine_level(nodes):
-        pairs = nodes.reshape(nodes.shape[0] // 2, 2, *nodes.shape[1:])
-        return apply_up(up_col[0], pairs[:, 0]) + apply_up(up_col[1], pairs[:, 1])
-
-    def group_levels(nodes, pos, bits, records, last):
-        for bit_num in range(bits):
-            here = pos >> bit_num
-            sibling = lax.dynamic_index_in_dim(nodes, here ^ 1, 0, keepdims=False)
-            records.append((sibling, here & 1))
-            if not (last and bit_num + 1 == bits):
-                nodes = combine_level(nodes)
-        return nodes
-
-    def climb_tree(root_coeff):
-        records = []
-        node = root_coeff
+    def side_pick(table, side_bit):
+        return lax.dynamic_index_in_dim(table, side_bit, 0, keepdims=False)
+
+    def climb_tree(root_coeff, tied):
+        current = root_coeff
+        field_sum = None
+        path_rows = None
+        level = 0
         for step, name in enumerate(CLIMB_AXES):
             bits = lax.axis_size(name).bit_length() - 1
-            gathered = lax.all_gather(node, name)
-            last = step + 1 == len(CLIMB_AXES)
-            node = group_levels(gathered, lax.axis_index(name), bits, records, last)[0]
-        return records
-
-    def descend_tree(records, columns):
-        field_now = jnp.zeros((rank_width, columns), jnp.float32)
-        for sibling, side_bit in reversed(records):
-            row_pick = lax.dynamic_index_in_dim(up_row, side_bit, 0, keepdims=False)
-            cpl_pick = lax.dynamic_index_in_dim(up_cpl, side_bit, 0, keepdims=False)
-            field_now = apply_down(row_pick, field_now) + apply_down(cpl_pick, sibling)
-        return field_now
+            for bit_num in range(bits):
+                sibling = from_partner(current, name, bit_num)
+                side_bit = lax.axis_index(name) >> bit_num & 1
+                term = apply_down(side_pick(up_cpl, side_bit), sibling)
+                if path_rows is None:
+                    field_sum = term
+                    path_rows = side_pick(up_row, side_bit)
+                else:
+                    field_sum = field_sum + apply_down(path_rows, term)
+                    path_rows = apply_down(path_rows, side_pick(up_row, side_bit))
+                if step + 1 < len(CLIMB_AXES) or bit_num + 1 < bits:
+                    left_part = jnp.where(side_bit == 1, sibling, current)
+                    right_part = jnp.where(side_bit == 1, current, sibling)
+                    current = apply_up(up_col[0], left_part) + apply_up(up_col[1], right_part)
+                    if level < len(tied):
+                        current, tied[level] = lax.optimization_barrier((current, tied[level]()))
+                level += 1
+        return field_sum
 
     def apply_image(vectors):
         columns = vectors.shape[0]
@@ -104,36 +108,58 @@
             current = paired[:, 0] + paired[:, 1]
             offsets.append(start_at)
             start_at = start_at + node_count
-        records = climb_tree(current[0])
-        local_field = descend_tree(records, columns)[None]
-        for start_at in reversed(offsets):
-            node_count = local_field.shape[0] * 2
-            local_field = apply_down(
-                row_local[start_at : start_at + node_count], jnp.repeat(local_field, 2, axis=0)
-            )
         width_all = 3 * leaves_dev
-        far_live = far_index < width_all
-        far_safe = jnp.minimum(far_index, width_all - 1)
-        picked = coeff_window[far_safe]
-        far_terms = jnp.einsum(
-            "lkab,lkbc->lkac", far_square, picked, preferred_element_type=jnp.float32
-        )
-        far_weight = jnp.where(far_live, far_scale, jnp.zeros_like(far_scale))
-        leaf_field = local_field + jnp.einsum(
-            "lkac,lk->lac", far_terms, far_weight, precision=best_precision
-        )
+
+        def leaf_paths():
+            paths = None
+            for start_at in reversed(offsets):
+                node_count = 2 if paths is None else paths.shape[0] * 2
+                rows = row_local[start_at : start_at + node_count]
+                if paths is None:
+                    paths = rows
+                else:
+                    paths = apply_down(rows, jnp.repeat(paths, 2, axis=0))
+            return paths
+
+        def far_part(lo, hi):
+            def run():
+                idx = far_index[lo:hi]
+                far_live = idx < width_all
+                picked = coeff_window[jnp.minimum(idx, width_all - 1)]
+                far_terms = jnp.einsum(
+                    "lkab,lkbc->lkac", far_square[lo:hi], picked, preferred_element_type=jnp.float32
+                )
+                far_weight = jnp.where(far_live, far_scale[lo:hi], jnp.zeros_like(far_scale[lo:hi]))
+                return jnp.einsum("lkac,lk->lac", far_terms, far_weight, precision=best_precision)
+            return run
+
+        def near_part(lo, hi):
+            def run():
+                idx = near_index[lo:hi]
+                near_live = idx < width_all
+                near_pick = x_window[:, jnp.minimum(idx, width_all - 1)]
+                near_terms = jnp.einsum(
+                    "lkpq,clkq->clkp", near_square[lo:hi], near_pick, preferred_element_type=jnp.float32
+                )
+                near_weight = jnp.where(near_live, near_scale[lo:hi], jnp.zeros_like(near_scale[lo:hi]))
+                return jnp.einsum("clkp,lk->clp", near_terms, near_weight, precision=best_precision)
+            return run
+
+        half = leaves_dev // 2
+        quarter = leaves_dev // 4
+        tied = [leaf_paths, far_part(0, half), far_part(half, leaves_dev)]
+        tied += [near_part(i * quarter, (i + 1) * quarter) for i in range(4)]
+        root_field = climb_tree(current[0], tied)
+        tied = [part() if callable(part) else part for part in tied]
+        paths = tied[0]
+        far_acc = jnp.concatenate(tied[1:3], axis=0)
+        near_sum = jnp.concatenate(tied[3:7], axis=1)
+        local_field = apply_down(paths, jnp.broadcast_to(root_field, (leaves_dev,) + root_field.shape))
+        leaf_field = local_field + far_acc
         field_round = leaf_field.astype(jnp.bfloat16)
         far_out = jnp.einsum(
             "lpk,lkc->clp", row_basis, field_round, preferred_element_type=jnp.float32
         )
-        near_live = near_index < width_all
-        near_safe = jnp.minimum(near_index, width_all - 1)
-        near_pick = x_window[:, near_safe]
-        near_terms = jnp.einsum(
-            "lkpq,clkq->clkp", near_square, near_pick, preferred_element_type=jnp.float32
-        )
-        near_weight = jnp.where(near_live, near_scale, jnp.zeros_like(near_scale))
-        near_sum = jnp.einsum("clkp,lk->clp", near_terms, near_weight, precision=best_precision)
         image = (far_out + near_sum).reshape(columns, leaves_dev * leaf_size)
         return jnp.zeros_like(image).at[:, order_row].set(image)
 

time: 181 us -> 182 us (level)
  blocking collectives: 90.1 us -> 0 us
  starting transfers between devices: 11.1 us -> 65.8 us
  matrix products: 25.7 us -> 38.7 us
  waiting for transfers between devices: 0.01 us -> 12.7 us
  local copies, waits for them, and re-layouts: 41.5 us -> 48.5 us
  other arithmetic: 9.05 us -> 13 us
    all_gather x4 -> x0, blocking collectives: 90.1 us -> none  [climb_tree(): gathered = lax.all_gather(node, name)]
    ppermute x0 -> x10, starting transfers between devices: none -> 54.1 us  [from_partner(): return lax.ppermute(value, axis, pairs)]
    ppermute x0 -> x10, waiting for transfers between devices: none -> 12.7 us  [from_partner(): return lax.ppermute(value, axis, pairs)]
    slice x4 -> x12, local copies, waits for them, and re-layouts: 0.55 us -> 12 us  [the longest x5 6.05 us: run(): near_square[lo:hi]]
    reshape x2 -> x0, local copies, waits for them, and re-layouts: 6.7 us -> none  [the longest x1 4.31 us: shards(): near_blocks.reshape(leaves_dev, near_blocks.shape[1], leaf_size, leaf_size)]
    dot_general x25 -> x32, matrix products: 8.12 us -> 13.3 us  [apply_down(): jnp.einsum('...ab,...bc->...ac', matrix, coeffs, precision=best_precision)]
    dot_general x23, matrix products: 4.77 us -> 9.34 us  [apply_up(): jnp.einsum('...ab,...ac->...bc', matrix, coeffs, precision=best_precision)]
    gather x2 -> x6, other arithmetic: 0.01 us -> 3.59 us  [the longest x4 2.39 us: run(): near_pick = x_window[:, jnp.minimum(idx, width_all - 1)]]
  transfers between devices with their start and end apart: 4 -> 14, of which waited for: 0 -> 6; matrix products, arithmetic and copies ran while one was open for 23% -> 37% of each run, Pallas kernels for 0% -> 0%
where the time goes in v4:
time: 182 us; the launch traced here: 180 us
  starting transfers between devices  65.8 us (36%)
  local copies, waits for them, and re-layouts  48.5 us (27%)
  matrix products  38.7 us (21%)
  other arithmetic  13 us (7%)
  waiting for transfers between devices  12.7 us (7%)
    ppermute x10, starting transfers between devices, from_partner(): return lax.ppermute(value, axis, pairs)  54.1 us
    dot_general x32, matrix products, apply_down(): jnp.einsum('...ab,...bc->...ac', matrix, coeffs, precision=best_precision)  13.3 us
    ppermute x10, waiting for transfers between devices, from_partner(): return lax.ppermute(value, axis, pairs)  12.7 us
    dot_general x23, matrix products, apply_up(): jnp.einsum('...ab,...ac->...bc', matrix, coeffs, precision=best_precision)  9.34 us
    ppermute x2, starting transfers between devices, extended(): low = lax.ppermute(block, axis, forward)  9.19 us
    unnamed x106, local copies, waits for them, and re-layouts  8.01 us
    gather x2, local copies, waits for them, and re-layouts, apply_image(): ordered = jnp.take(vectors, order_row, axis=1).astype(jnp.bfloat16)  6.41 us
    dot_general x4, matrix products, run(): jnp.einsum('clkp,lk->clp', near_terms, near_weight, precision=best_precis...  6.29 us
  transfers between devices with their start and end apart: 14, of which 6 were waited for; matrix products, arithmetic and copies ran while one was open for 37% of the time, Pallas kernels for 0%

profile of v4, /device:TPU:14, one launch (start us, length us, event | category | flops | bytes accessed | tf_op | source)
XLA Modules:
  0.0 180.4 jit_solution(8369172806310946912)
XLA Ops:
  2.7 6.2 %gather_fusion = bf16[2048,32]{1,0:T(8,128)(2,1)S(1)} fusion(bf16[32,2048]{0,1:T(8,128)(2,1)S(1)} %copy.170, s32[2048]{0:T(1024)S(1)} %broadcast_clamp_fusion), kind=kCustom, calls=%fused_computation | custom fusion | bytes 270336 | tf_op jit(solution)/shard_map/jit(_take)/gather | solution.py:93
  14.5 3.7 %collective-permute-start.2 = (bf16[32,32,32]{1,2,0:T(8,128)(2,1)}, bf16[32,32,32]{1,2,0:T(8,128)(2,1)}, u32[]{:S(2)}, u32[]{:S(2)}) collective-permute-start(bf16[32,32,32]{1,2,0:T(8,128)(2,1)} %convert_bitcast_fusion), channel_id=1, source_target_pairs={{0,1},{1,2},{2,3},{3,4},{4,5},{5,6},{6,7},{7,8},{8,9},{9,10},{10,1... | collective-permute-start | bytes 196616 | tf_op jit(solution)/shard_map/ppermute | solution.py:24
  19.5 5.5 %collective-permute-start.6 = (bf16[32,32,64]{2,0,1:T(8,128)(2,1)}, bf16[32,32,64]{2,0,1:T(8,128)(2,1)}, u32[]{:S(2)}, u32[]{:S(2)}) collective-permute-start(bf16[32,32,64]{2,0,1:T(8,128)(2,1)} %select_convert_fusion), channel_id=1, source_target_pairs={{0,1},{1,2},{2,3},{3,4},{4,5},{5,6},{6,7},{7,8},{8,9},{9,10},{10,1... | collective-permute-start | bytes 393224 | tf_op jit(solution)/shard_map/ppermute | solution.py:24
  28.8 2.9 %collective-permute-start = (f32[32,32]{0,1:T(8,128)}, f32[32,32]{0,1:T(8,128)}, u32[]{:S(2)}, u32[]{:S(2)}) collective-permute-start(f32[32,32]{0,1:T(8,128)} %fusion.56), channel_id=1, source_target_pairs={{0,1},{1,0},{2,3},{3,2},{4,5},{5,4},{6,7},{7,6},{8,9},{9,8},{10,11... | collective-permute-start | bytes 12296 | tf_op jit(solution)/shard_map/ppermute | solution.py:15
  37.3 1.8 %fusion.218 = (bf16[16,6,1024]{2,0,1:T(8,128)(2,1)}, bf16[16,6,1024]{2,0,1:T(8,128)(2,1)}) fusion(bf16[32,6,1024]{2,0,1:T(8,128)(2,1)} %param.24), kind=kLoop, calls=%fused_computation.288 | loop fusion | bytes 786432 | tf_op jit(solution)/shard_map/slice | solution.py:130
  52.2 5.4 %collective-permute-start.1 = (f32[32,32]{0,1:T(8,128)S(1)}, f32[32,32]{0,1:T(8,128)S(1)}, u32[]{:S(2)}, u32[]{:S(2)}) collective-permute-start(f32[32,32]{0,1:T(8,128)S(1)} %fusion.13), channel_id=1, source_target_pairs={{0,2},{2,0},{4,6},{6,4},{8,10},{10,8},{12,14},{14,12},{1,3},{3,1},... | collective-permute-start | bytes 12296 | tf_op jit(solution)/shard_map/ppermute | solution.py:15
  58.9 1.4 slice.228
  61.0 1.4 slice.232
  63.1 1.7 slice.237
  65.5 1.7 slice.241
  74.6 2.5 %fusion.1 = f32[16,32,32]{1,2,0:T(8,128)} fusion(bf16[16,6,32,32]{3,2,1,0:T(8,128)(2,1)S(1)} %bitcast.380, f32[16,6]{1,0:T(8,128)} %copy.257, bf16[16,6,32,32]{3,2,0,1:T(8,128)(2,1)} %slice.228), kind=kOutput, calls=%fused_computation.11 | convolution fusion | flops 6471680 | bytes 459136 | tf_op jit(solution)/shard_map/lkab,lkbc->lkac/dot_general | solution.py:129
  77.1 1.8 copy.219
  78.9 10.3 %collective-permute-start.4 = (f32[32,32]{0,1:T(8,128)}, f32[32,32]{0,1:T(8,128)}, u32[]{:S(2)}, u32[]{:S(2)}) collective-permute-start(f32[32,32]{0,1:T(8,128)} %fusion.11), channel_id=1, source_target_pairs={{0,4},{2,6},{4,0},{6,2},{8,12},{10,14},{12,8},{14,10},{1,5},{3,7},... | collective-permute-start | bytes 12296 | tf_op jit(solution)/shard_map/ppermute | solution.py:15
  90.1 1.8 fusion
  95.5 6.7 %collective-permute-start.5 = (f32[32,32]{0,1:T(8,128)S(1)}, f32[32,32]{0,1:T(8,128)S(1)}, u32[]{:S(2)}, u32[]{:S(2)}) collective-permute-start(f32[32,32]{0,1:T(8,128)S(1)} %fusion.10), channel_id=1, source_target_pairs={{0,8},{2,10},{4,12},{6,14},{8,0},{10,2},{12,4},{14,6},{1,9},{3,11}... | collective-permute-start | bytes 12296 | tf_op jit(solution)/shard_map/ppermute | solution.py:15
  103.2 1.9 %collective-permute-done.5 = f32[32,32]{0,1:T(8,128)S(1)} collective-permute-done((f32[32,32]{0,1:T(8,128)S(1)}, f32[32,32]{0,1:T(8,128)S(1)}, u32[]{:S(2)}, u32[]{:S(2)}) %collective-permute-start.5) | collective-permute-done | bytes 4128 | tf_op jit(solution)/shard_map/ppermute | solution.py:15
  106.1 1.5 convolution_add_fusion.13
  108.9 1.5 gather_fusion.3
  110.4 1.5 convolution_bitcast_fusion.3
  111.9 2.1 %fusion.20 = f32[8,1,32,64]{3,1,2,0:T(1,128)} fusion(f32[8,6,1,1]{1,2,3,0:T(1,128)S(1)} %copy-done.37, f32[32,8,6,64]{3,0,2,1:T(8,128)S(1)} %convolution_bitcast_fusion.3), kind=kOutput, calls=%fused_computation.57 | convolution fusion | flops 1179648 | bytes 458944 | tf_op jit(solution)/shard_map/clkp,lk->clp/dot_general | solution.py:145
  114.0 3.9 %collective-permute-start.8 = (f32[32,32]{0,1:T(8,128)}, f32[32,32]{0,1:T(8,128)}, u32[]{:S(2)}, u32[]{:S(2)}) collective-permute-start(f32[32,32]{0,1:T(8,128)} %fusion.9), channel_id=1, source_target_pairs={{0,16},{16,0},{32,48},{48,32},{64,80},{80,64},{96,112},{112,96},{1... | collective-permute-start | bytes 12296 | tf_op jit(solution)/shard_map/ppermute | solution.py:15
  122.0 1.6 convolution_bitcast_fusion.2
  130.8 4.7 %collective-permute-start.9 = (f32[32,32]{0,1:T(8,128)S(1)}, f32[32,32]{0,1:T(8,128)S(1)}, u32[]{:S(2)}, u32[]{:S(2)}) collective-permute-start(f32[32,32]{0,1:T(8,128)S(1)} %fusion.8), channel_id=1, source_target_pairs={{0,32},{16,48},{32,0},{48,16},{64,96},{80,112},{96,64},{112,80},{1... | collective-permute-start | bytes 12296 | tf_op jit(solution)/shard_map/ppermute | solution.py:15
  137.6 7.3 %collective-permute-start.10 = (f32[32,32]{0,1:T(8,128)S(1)}, f32[32,32]{0,1:T(8,128)S(1)}, u32[]{:S(2)}, u32[]{:S(2)}) collective-permute-start(f32[32,32]{0,1:T(8,128)S(1)} %fusion.7), channel_id=1, source_target_pairs={{0,64},{16,80},{32,96},{48,112},{64,0},{80,16},{96,32},{112,48},{1... | collective-permute-start | bytes 12296 | tf_op jit(solution)/shard_map/ppermute | solution.py:15
  145.2 1.9 %collective-permute-done.10 = f32[32,32]{0,1:T(8,128)S(1)} collective-permute-done((f32[32,32]{0,1:T(8,128)S(1)}, f32[32,32]{0,1:T(8,128)S(1)}, u32[]{:S(2)}, u32[]{:S(2)}) %collective-permute-start.10) | collective-permute-done | bytes 4128 | tf_op jit(solution)/shard_map/ppermute | solution.py:15
  147.4 3.3 %collective-permute-start.11 = (f32[32,32]{0,1:T(8,128)S(1)}, f32[32,32]{0,1:T(8,128)S(1)}, u32[]{:S(2)}, u32[]{:S(2)}) collective-permute-start(f32[32,32]{0,1:T(8,128)S(1)} %fusion.6), channel_id=1, source_target_pairs={{0,128},{128,0},{256,384},{384,256},{512,640},{640,512},{768,896},... | collective-permute-start | bytes 12296 | tf_op jit(solution)/shard_map/ppermute | solution.py:15
  151.1 2.0 %collective-permute-done.11 = f32[32,32]{0,1:T(8,128)S(1)} collective-permute-done((f32[32,32]{0,1:T(8,128)S(1)}, f32[32,32]{0,1:T(8,128)S(1)}, u32[]{:S(2)}, u32[]{:S(2)}) %collective-permute-start.11) | collective-permute-done | bytes 4128 | tf_op jit(solution)/shard_map/ppermute | solution.py:15
  153.3 4.2 %collective-permute-start.12 = (f32[32,32]{0,1:T(8,128)S(1)}, f32[32,32]{0,1:T(8,128)S(1)}, u32[]{:S(2)}, u32[]{:S(2)}) collective-permute-start(f32[32,32]{0,1:T(8,128)S(1)} %fusion.5), channel_id=1, source_target_pairs={{0,256},{128,384},{256,0},{384,128},{512,768},{640,896},{768,512},... | collective-permute-start | bytes 12296 | tf_op jit(solution)/shard_map/ppermute | solution.py:15
  157.9 2.0 %collective-permute-done.12 = f32[32,32]{0,1:T(8,128)S(1)} collective-permute-done((f32[32,32]{0,1:T(8,128)S(1)}, f32[32,32]{0,1:T(8,128)S(1)}, u32[]{:S(2)}, u32[]{:S(2)}) %collective-permute-start.12) | collective-permute-done | bytes 4128 | tf_op jit(solution)/shard_map/ppermute | solution.py:15
  160.2 5.2 %collective-permute-start.13 = (f32[32,32]{0,1:T(8,128)S(1)}, f32[32,32]{0,1:T(8,128)S(1)}, u32[]{:S(2)}, u32[]{:S(2)}) collective-permute-start(f32[32,32]{0,1:T(8,128)S(1)} %fusion.4), channel_id=1, source_target_pairs={{0,512},{128,640},{256,768},{384,896},{512,0},{640,128},{768,256},... | collective-permute-start | bytes 12296 | tf_op jit(solution)/shard_map/ppermute | solution.py:15
  165.7 4.0 %collective-permute-done.13 = f32[32,32]{0,1:T(8,128)S(1)} collective-permute-done((f32[32,32]{0,1:T(8,128)S(1)}, f32[32,32]{0,1:T(8,128)S(1)}, u32[]{:S(2)}, u32[]{:S(2)}) %collective-permute-start.13) | collective-permute-done | bytes 4128 | tf_op jit(solution)/shard_map/ppermute | solution.py:15
  172.2 6.0 %scatter_custom_fusion = f32[32,2048]{0,1:T(8,128)S(1)} fusion(s32[2048]{0:T(1024)} %bitcast.391, f32[2048,32]{1,0:T(8,128)S(1)} %copy.210, f32[]{:T(128)} %constant.78.clone.1), kind=kCustom, calls=%fused_computation.68 | custom fusion | bytes 262656 | tf_op jit(solution)/shard_map/scatter | solution.py:164
  (244 shorter events, 69.1 us)
Async XLA Ops:
  0.6 170.4 %copy-start = (bf16[32,64,32]{1,2,0:T(8,128)(2,1)S(1)}, bf16[32,64,32]{1,2,0:T(8,128)(2,1)}, u32[]{:S(2)}) copy-start(bf16[32,64,32]{1,2,0:T(8,128)(2,1)} %param.20) | copy-start | bytes 393220
  8.9 16.1 %copy-start.1 = (bf16[1,62,32,32]{1,3,2,0:T(8,128)(2,1)S(1)}, bf16[1,62,32,32]{1,3,2,0:T(8,128)(2,1)}, u32[]{:S(2)}) copy-start(bf16[1,62,32,32]{1,3,2,0:T(8,128)(2,1)} %param.27) | copy-start | bytes 380932
  13.2 58.9 %collective-permute-start.3 = (bf16[32,32,32]{1,2,0:T(8,128)(2,1)}, bf16[32,32,32]{1,2,0:T(8,128)(2,1)}, u32[]{:S(2)}, u32[]{:S(2)}) collective-permute-start(bf16[32,32,32]{1,2,0:T(8,128)(2,1)} %convert_bitcast_fusion), channel_id=1, source_target_pairs={{1,0},{2,1},{3,2},{4,3},{5,4},{6,5},{7,6},{8,7},{9,8},{10,9},{11,1... | collective-permute-start | bytes 196616 | tf_op jit(solution)/shard_map/ppermute | solution.py:25
  14.5 57.6 %collective-permute-start.2 = (bf16[32,32,32]{1,2,0:T(8,128)(2,1)}, bf16[32,32,32]{1,2,0:T(8,128)(2,1)}, u32[]{:S(2)}, u32[]{:S(2)}) collective-permute-start(bf16[32,32,32]{1,2,0:T(8,128)(2,1)} %convert_bitcast_fusion), channel_id=1, source_target_pairs={{0,1},{1,2},{2,3},{3,4},{4,5},{5,6},{6,7},{7,8},{8,9},{9,10},{10,1... | collective-permute-start | bytes 196616 | tf_op jit(solution)/shard_map/ppermute | solution.py:24
  18.2 89.4 %collective-permute-start.7 = (bf16[32,32,64]{2,0,1:T(8,128)(2,1)}, bf16[32,32,64]{2,0,1:T(8,128)(2,1)}, u32[]{:S(2)}, u32[]{:S(2)}) collective-permute-start(bf16[32,32,64]{2,0,1:T(8,128)(2,1)} %select_convert_fusion), channel_id=1, source_target_pairs={{1,0},{2,1},{3,2},{4,3},{5,4},{6,5},{7,6},{8,7},{9,8},{10,9},{11,1... | collective-permute-start | bytes 393224 | tf_op jit(solution)/shard_map/ppermute | solution.py:25
  19.5 88.1 %collective-permute-start.6 = (bf16[32,32,64]{2,0,1:T(8,128)(2,1)}, bf16[32,32,64]{2,0,1:T(8,128)(2,1)}, u32[]{:S(2)}, u32[]{:S(2)}) collective-permute-start(bf16[32,32,64]{2,0,1:T(8,128)(2,1)} %select_convert_fusion), channel_id=1, source_target_pairs={{0,1},{1,2},{2,3},{3,4},{4,5},{5,6},{6,7},{7,8},{8,9},{9,10},{10,1... | collective-permute-start | bytes 393224 | tf_op jit(solution)/shard_map/ppermute | solution.py:24
  28.8 21.6 %collective-permute-start = (f32[32,32]{0,1:T(8,128)}, f32[32,32]{0,1:T(8,128)}, u32[]{:S(2)}, u32[]{:S(2)}) collective-permute-start(f32[32,32]{0,1:T(8,128)} %fusion.56), channel_id=1, source_target_pairs={{0,1},{1,0},{2,3},{3,2},{4,5},{5,4},{6,7},{7,6},{8,9},{9,8},{10,11... | collective-permute-start | bytes 12296 | tf_op jit(solution)/shard_map/ppermute | solution.py:15
  32.5 9.5 %copy-start.9 = (bf16[32,6,4096]{2,0,1:T(8,128)(2,1)S(1)}, bf16[32,6,4096]{2,0,1:T(8,128)(2,1)}, u32[]{:S(2)}) copy-start(bf16[32,6,4096]{2,0,1:T(8,128)(2,1)} %param.21) | copy-start | bytes 4718596
  46.0 12.2 %copy-start.44 = (f32[16,6]{0,1:T(8,128)S(1)}, f32[16,6]{0,1:T(8,128)}, u32[]{:S(2)}) copy-start(f32[16,6]{0,1:T(8,128)} %get-tuple-element.53) | copy-start | bytes 1156
  46.0 12.9 %copy-start.16 = (bf16[16,6,1024]{2,0,1:T(8,128)(2,1)S(1)}, bf16[16,6,1024]{2,0,1:T(8,128)(2,1)}, u32[]{:S(2)}) copy-start(bf16[16,6,1024]{2,0,1:T(8,128)(2,1)} %get-tuple-element.47) | copy-start | bytes 589828
  46.4 13.9 %copy-start.43 = (f32[16,6]{0,1:T(8,128)S(1)}, f32[16,6]{0,1:T(8,128)}, u32[]{:S(2)}) copy-start(f32[16,6]{0,1:T(8,128)} %get-tuple-element.52) | copy-start | bytes 1156
  46.4 14.6 %copy-start.15 = (bf16[16,6,1024]{2,0,1:T(8,128)(2,1)S(1)}, bf16[16,6,1024]{2,0,1:T(8,128)(2,1)}, u32[]{:S(2)}) copy-start(bf16[16,6,1024]{2,0,1:T(8,128)(2,1)} %get-tuple-element.46) | copy-start | bytes 589828
  47.8 14.7 %copy-start.42 = (f32[8,6,1,1]{0,1,2,3:T(8,128)S(1)}, f32[8,6,1,1]{0,1,2,3:T(8,128)}, u32[]{:S(2)}) copy-start(f32[8,6,1,1]{0,1,2,3:T(8,128)} %get-tuple-element.50) | copy-start | bytes 580
  47.8 15.4 %copy-start.10 = (bf16[8,6,4096]{2,0,1:T(8,128)(2,1)S(1)}, bf16[8,6,4096]{2,0,1:T(8,128)(2,1)}, u32[]{:S(2)}) copy-start(bf16[8,6,4096]{2,0,1:T(8,128)(2,1)} %get-tuple-element.42) | copy-start | bytes 1179652
  48.1 16.8 %copy-start.22 = (f32[32,32]{1,0:T(8,128)}, f32[32,32]{1,0:T(8,128)S(1)}, u32[]{:S(2)}) copy-start(f32[32,32]{1,0:T(8,128)S(1)} %fusion.83) | copy-start | bytes 12292
  52.2 18.1 %collective-permute-start.1 = (f32[32,32]{0,1:T(8,128)S(1)}, f32[32,32]{0,1:T(8,128)S(1)}, u32[]{:S(2)}, u32[]{:S(2)}) collective-permute-start(f32[32,32]{0,1:T(8,128)S(1)} %fusion.13), channel_id=1, source_target_pairs={{0,2},{2,0},{4,6},{6,4},{8,10},{10,8},{12,14},{14,12},{1,3},{3,1},... | collective-permute-start | bytes 12296 | tf_op jit(solution)/shard_map/ppermute | solution.py:15
  78.9 13.8 %collective-permute-start.4 = (f32[32,32]{0,1:T(8,128)}, f32[32,32]{0,1:T(8,128)}, u32[]{:S(2)}, u32[]{:S(2)}) collective-permute-start(f32[32,32]{0,1:T(8,128)} %fusion.11), channel_id=1, source_target_pairs={{0,4},{2,6},{4,0},{6,2},{8,12},{10,14},{12,8},{14,10},{1,5},{3,7},... | collective-permute-start | bytes 12296 | tf_op jit(solution)/shard_map/ppermute | solution.py:15
  93.6 16.8 %copy-start.4 = (bf16[8,6,64,64]{3,2,0,1:T(8,128)(2,1)S(1)}, bf16[8,6,64,64]{3,2,0,1:T(8,128)(2,1)}, u32[]{:S(2)}) copy-start(bf16[8,6,64,64]{3,2,0,1:T(8,128)(2,1)} %slice.237) | copy-start | bytes 1179652
  95.5 9.6 %collective-permute-start.5 = (f32[32,32]{0,1:T(8,128)S(1)}, f32[32,32]{0,1:T(8,128)S(1)}, u32[]{:S(2)}, u32[]{:S(2)}) collective-permute-start(f32[32,32]{0,1:T(8,128)S(1)} %fusion.10), channel_id=1, source_target_pairs={{0,8},{2,10},{4,12},{6,14},{8,0},{10,2},{12,4},{14,6},{1,9},{3,11}... | collective-permute-start | bytes 12296 | tf_op jit(solution)/shard_map/ppermute | solution.py:15
  114.0 15.0 %collective-permute-start.8 = (f32[32,32]{0,1:T(8,128)}, f32[32,32]{0,1:T(8,128)}, u32[]{:S(2)}, u32[]{:S(2)}) collective-permute-start(f32[32,32]{0,1:T(8,128)} %fusion.9), channel_id=1, source_target_pairs={{0,16},{16,0},{32,48},{48,32},{64,80},{80,64},{96,112},{112,96},{1... | collective-permute-start | bytes 12296 | tf_op jit(solution)/shard_map/ppermute | solution.py:15
  127.0 9.4 %copy-start.21 = (f32[32,32]{1,0:T(8,128)S(1)}, f32[32,32]{1,0:T(8,128)}, u32[]{:S(2)}) copy-start(f32[32,32]{1,0:T(8,128)} %copy-done.20) | copy-start | bytes 12292
  127.0 9.4 %copy-start.28 = (f32[32,32]{1,0:T(8,128)S(1)}, f32[32,32]{1,0:T(8,128)}, u32[]{:S(2)}) copy-start(f32[32,32]{1,0:T(8,128)} %convolution_add_fusion.13) | copy-start | bytes 12292
  127.5 42.3 %copy-start.27 = (f32[32,32]{1,0:T(8,128)S(1)}, f32[32,32]{1,0:T(8,128)}, u32[]{:S(2)}) copy-start(f32[32,32]{1,0:T(8,128)} %fusion.59) | copy-start | bytes 12292
  127.5 42.5 %copy-start.8 = (f32[32,32,32]{1,2,0:T(8,128)S(1)}, f32[32,32,32]{1,2,0:T(8,128)}, u32[]{:S(2)}) copy-start(f32[32,32,32]{1,2,0:T(8,128)} %convolution_bitcast_fusion.5) | copy-start | bytes 393220
  127.5 42.5 %copy-start.11 = (f32[16,32,32]{2,1,0:T(8,128)S(1)}, f32[16,32,32]{2,1,0:T(8,128)}, u32[]{:S(2)}) copy-start(f32[16,32,32]{2,1,0:T(8,128)} %copy.219) | copy-start | bytes 196612
  127.6 42.5 %copy-start.12 = (f32[16,32,32]{2,1,0:T(8,128)S(1)}, f32[16,32,32]{2,1,0:T(8,128)}, u32[]{:S(2)}) copy-start(f32[16,32,32]{2,1,0:T(8,128)} %copy.225) | copy-start | bytes 196612
  129.0 42.1 %copy-start.17 = (f32[8,1,32,64]{3,1,2,0:T(1,128)S(1)}, f32[8,1,32,64]{3,1,2,0:T(1,128)}, u32[]{:S(2)}) copy-start(f32[8,1,32,64]{3,1,2,0:T(1,128)} %fusion.20) | copy-start | bytes 196612
  130.8 6.5 %collective-permute-start.9 = (f32[32,32]{0,1:T(8,128)S(1)}, f32[32,32]{0,1:T(8,128)S(1)}, u32[]{:S(2)}, u32[]{:S(2)}) collective-permute-start(f32[32,32]{0,1:T(8,128)S(1)} %fusion.8), channel_id=1, source_target_pairs={{0,32},{16,48},{32,0},{48,16},{64,96},{80,112},{96,64},{112,80},{1... | collective-permute-start | bytes 12296 | tf_op jit(solution)/shard_map/ppermute | solution.py:15
  137.6 9.5 %collective-permute-start.10 = (f32[32,32]{0,1:T(8,128)S(1)}, f32[32,32]{0,1:T(8,128)S(1)}, u32[]{:S(2)}, u32[]{:S(2)}) collective-permute-start(f32[32,32]{0,1:T(8,128)S(1)} %fusion.7), channel_id=1, source_target_pairs={{0,64},{16,80},{32,96},{48,112},{64,0},{80,16},{96,32},{112,48},{1... | collective-permute-start | bytes 12296 | tf_op jit(solution)/shard_map/ppermute | solution.py:15
  147.4 5.6 %collective-permute-start.11 = (f32[32,32]{0,1:T(8,128)S(1)}, f32[32,32]{0,1:T(8,128)S(1)}, u32[]{:S(2)}, u32[]{:S(2)}) collective-permute-start(f32[32,32]{0,1:T(8,128)S(1)} %fusion.6), channel_id=1, source_target_pairs={{0,128},{128,0},{256,384},{384,256},{512,640},{640,512},{768,896},... | collective-permute-start | bytes 12296 | tf_op jit(solution)/shard_map/ppermute | solution.py:15
  153.3 6.5 %collective-permute-start.12 = (f32[32,32]{0,1:T(8,128)S(1)}, f32[32,32]{0,1:T(8,128)S(1)}, u32[]{:S(2)}, u32[]{:S(2)}) collective-permute-start(f32[32,32]{0,1:T(8,128)S(1)} %fusion.5), channel_id=1, source_target_pairs={{0,256},{128,384},{256,0},{384,128},{512,768},{640,896},{768,512},... | collective-permute-start | bytes 12296 | tf_op jit(solution)/shard_map/ppermute | solution.py:15
  160.2 9.6 %collective-permute-start.13 = (f32[32,32]{0,1:T(8,128)S(1)}, f32[32,32]{0,1:T(8,128)S(1)}, u32[]{:S(2)}, u32[]{:S(2)}) collective-permute-start(f32[32,32]{0,1:T(8,128)S(1)} %fusion.4), channel_id=1, source_target_pairs={{0,512},{128,640},{256,768},{384,896},{512,0},{640,128},{768,256},... | collective-permute-start | bytes 12296 | tf_op jit(solution)/shard_map/ppermute | solution.py:15
  (28 other events, 134.3 us)

commit v5 on v2

--- a/solution.py
+++ b/solution.py
@@ -7,6 +7,12 @@
 LEAF_AXES = ("lx", "ly")
 SUB_AXES = ("lz", "lc")
 CLIMB_AXES = ("lc", "lz", "ly", "lx")
+
+
+def from_partner(value, axis, distance):
+    mask = 2**distance
+    pairs = [(source, source ^ mask) for source in range(lax.axis_size(axis))]
+    return lax.ppermute(value, axis, pairs)
 
 
 def extended(block, axis, dim):
@@ -53,36 +59,44 @@
     col_local = loc_col[0].astype(jnp.float32)
     row_local = loc_row[0].astype(jnp.float32)
 
-    def combine_level(nodes):
-        pairs = nodes.reshape(nodes.shape[0] // 2, 2, *nodes.shape[1:])
-        return apply_up(up_col[0], pairs[:, 0]) + apply_up(up_col[1], pairs[:, 1])
+    def climb_sides():
+        sides = []
+        for name in CLIMB_AXES:
+            for bit_num in range(lax.axis_size(name).bit_length() - 1):
+                sides.append((name, bit_num, lax.axis_index(name) >> bit_num & 1))
+        return sides
 
-    def group_levels(nodes, pos, bits, records, last):
-        for bit_num in range(bits):
-            here = pos >> bit_num
-            sibling = lax.dynamic_index_in_dim(nodes, here ^ 1, 0, keepdims=False)
-            records.append((sibling, here & 1))
-            if not (last and bit_num + 1 == bits):
-                nodes = combine_level(nodes)
-        return nodes
+    def pick(table, side_col):
+        return jnp.where(side_col[:, None, None] == 1, table[1][None], table[0][None])
+
+    def field_weights(side_col):
+        level_count = side_col.shape[0]
+        row_sel = pick(up_row, side_col)
+        eye = jnp.broadcast_to(jnp.eye(rank_width, dtype=jnp.float32), row_sel.shape)
+        prefix = row_sel
+        shift = 1
+        while shift < level_count:
+            earlier = jnp.concatenate([eye[:shift], prefix[:-shift]], axis=0)
+            prefix = apply_down(earlier, prefix)
+            shift *= 2
+        before = jnp.concatenate([eye[:1], prefix[:-1]], axis=0)
+        weights = apply_down(before, pick(up_cpl, side_col))
+        return weights.transpose(1, 0, 2).reshape(rank_width, level_count * rank_width)
 
     def climb_tree(root_coeff):
-        records = []
-        node = root_coeff
-        for step, name in enumerate(CLIMB_AXES):
-            bits = lax.axis_size(name).bit_length() - 1
-            gathered = lax.all_gather(node, name)
-            last = step + 1 == len(CLIMB_AXES)
-            node = group_levels(gathered, lax.axis_index(name), bits, records, last)[0]
-        return records
-
-    def descend_tree(records, columns):
-        field_now = jnp.zeros((rank_width, columns), jnp.float32)
-        for sibling, side_bit in reversed(records):
-            row_pick = lax.dynamic_index_in_dim(up_row, side_bit, 0, keepdims=False)
-            cpl_pick = lax.dynamic_index_in_dim(up_cpl, side_bit, 0, keepdims=False)
-            field_now = apply_down(row_pick, field_now) + apply_down(cpl_pick, sibling)
-        return field_now
+        sides = climb_sides()
+        side_col = jnp.stack([side for _, _, side in sides])
+        own_first = jnp.concatenate([pick(up_col, side_col), pick(up_col, 1 - side_col)], axis=1)
+        current = root_coeff
+        siblings = []
+        for level, (name, bit_num, _) in enumerate(sides):
+            sibling = from_partner(current, name, bit_num)
+            siblings.append(sibling)
+            if level + 1 < len(sides):
+                stacked = jnp.concatenate([current, sibling], axis=0)
+                current = apply_up(own_first[level], stacked)
+        stacked = jnp.concatenate(siblings, axis=0)
+        return apply_down(field_weights(side_col), stacked)
 
     def apply_image(vectors):
         columns = vectors.shape[0]
@@ -104,17 +118,16 @@
             current = paired[:, 0] + paired[:, 1]
             offsets.append(start_at)
             start_at = start_at + node_count
-        records = climb_tree(current[0])
-        local_field = descend_tree(records, columns)[None]
+        width_all = 3 * leaves_dev
+        paths = None
         for start_at in reversed(offsets):
-            node_count = local_field.shape[0] * 2
-            local_field = apply_down(
-                row_local[start_at : start_at + node_count], jnp.repeat(local_field, 2, axis=0)
-            )
-        width_all = 3 * leaves_dev
+            node_count = 2 if paths is None else paths.shape[0] * 2
+            rows = row_local[start_at : start_at + node_count]
+            paths = rows if paths is None else apply_down(rows, jnp.repeat(paths, 2, axis=0))
+        root_field = climb_tree(current[0])
+        local_field = apply_down(paths, jnp.broadcast_to(root_field, (leaves_dev,) + root_field.shape))
         far_live = far_index < width_all
-        far_safe = jnp.minimum(far_index, width_all - 1)
-        picked = coeff_window[far_safe]
+        picked = coeff_window[jnp.minimum(far_index, width_all - 1)]
         far_terms = jnp.einsum(
             "lkab,lkbc->lkac", far_square, picked, preferred_element_type=jnp.float32
         )
@@ -127,8 +140,7 @@
             "lpk,lkc->clp", row_basis, field_round, preferred_element_type=jnp.float32
         )
         near_live = near_index < width_all
-        near_safe = jnp.minimum(near_index, width_all - 1)
-        near_pick = x_window[:, near_safe]
+        near_pick = x_window[:, jnp.minimum(near_index, width_all - 1)]
         near_terms = jnp.einsum(
             "lkpq,clkq->clkp", near_square, near_pick, preferred_element_type=jnp.float32
         )

time: 181 us -> 159 us (0.88)
  blocking collectives: 90.1 us -> 0 us
  starting transfers between devices: 11.1 us -> 68.2 us
  waiting for transfers between devices: 0.01 us -> 14 us
  matrix products: 25.7 us -> 22.9 us
    all_gather x4 -> x0, blocking collectives: 90.1 us -> none  [climb_tree(): gathered = lax.all_gather(node, name)]
    ppermute x0 -> x10, starting transfers between devices: none -> 57.1 us  [from_partner(): return lax.ppermute(value, axis, pairs)]
    ppermute x0 -> x10, waiting for transfers between devices: none -> 14 us  [from_partner(): return lax.ppermute(value, axis, pairs)]
    unnamed x50 -> x63, local copies, waits for them, and re-layouts: 8.65 us -> 5.9 us
    dot_general x0 -> x1, local copies, waits for them, and re-layouts: none -> 2.04 us  [apply_image(): jnp.einsum('lkac,lk->lac', far_terms, far_weight, precision=best_precision)]
    dot_general x25 -> x10, matrix products: 8.12 us -> 6.1 us  [apply_down(): jnp.einsum('...ab,...bc->...ac', matrix, coeffs, precision=best_precision)]
    dot_general x23 -> x14, matrix products: 4.77 us -> 2.96 us  [apply_up(): jnp.einsum('...ab,...ac->...bc', matrix, coeffs, precision=best_precision)]
  transfers between devices with their start and end apart: 4 -> 14, of which waited for: 0 -> 8; matrix products, arithmetic and copies ran while one was open for 23% -> 23% of each run, Pallas kernels for 0% -> 0%
where the time goes in v5:
time: 159 us; the launch traced here: 156 us
  starting transfers between devices  68.2 us (43%)
  local copies, waits for them, and re-layouts  40.1 us (25%)
  matrix products  22.9 us (14%)
  waiting for transfers between devices  14 us (9%)
  other arithmetic  8.64 us (5%)
  between operations  1.62 us (1%)
    ppermute x10, starting transfers between devices, from_partner(): return lax.ppermute(value, axis, pairs)  57.1 us
    ppermute x10, waiting for transfers between devices, from_partner(): return lax.ppermute(value, axis, pairs)  14 us
    ppermute x2, starting transfers between devices, extended(): low = lax.ppermute(block, axis, forward)  8.57 us
    gather x2, local copies, waits for them, and re-layouts, apply_image(): ordered = jnp.take(vectors, order_row, axis=1).astype(jnp.bfloat16)  6.41 us
    dot_general x10, matrix products, apply_down(): jnp.einsum('...ab,...bc->...ac', matrix, coeffs, precision=best_precision)  6.1 us
    unnamed x63, local copies, waits for them, and re-layouts  5.9 us
    scatter x1, local copies, waits for them, and re-layouts, apply_image(): return jnp.zeros_like(image).at[:, order_row].set(image)  5.85 us
    dot_general x1, matrix products, apply_image(): jnp.einsum('clkp,lk->clp', near_terms, near_weight, precision=best_precis...  5.22 us
  transfers between devices with their start and end apart: 14, of which 8 were waited for; matrix products, arithmetic and copies ran while one was open for 23% of the time, Pallas kernels for 0%

profile of v5, /device:TPU:14, one launch (start us, length us, event | category | flops | bytes accessed | tf_op | source)
XLA Modules:
  0.0 155.6 jit_solution(13435399400318243952)
XLA Ops:
  2.7 6.2 %gather_fusion = bf16[2048,32]{1,0:T(8,128)(2,1)S(1)} fusion(bf16[32,2048]{0,1:T(8,128)(2,1)S(1)} %copy.153, s32[2048]{0:T(1024)S(1)} %broadcast_clamp_fusion), kind=kCustom, calls=%fused_computation | custom fusion | bytes 270336 | tf_op jit(solution)/shard_map/jit(_take)/gather | solution.py:103
  13.2 2.4 %collective-permute-start.10 = (bf16[32,32,32]{1,2,0:T(8,128)(2,1)}, bf16[32,32,32]{1,2,0:T(8,128)(2,1)}, u32[]{:S(2)}, u32[]{:S(2)}) collective-permute-start(bf16[32,32,32]{1,2,0:T(8,128)(2,1)} %convert_bitcast_fusion), channel_id=1, source_target_pairs={{0,1},{1,2},{2,3},{3,4},{4,5},{5,6},{6,7},{7,8},{8,9},{9,10},{10,1... | collective-permute-start | bytes 196616 | tf_op jit(solution)/shard_map/ppermute | solution.py:24
  16.9 6.1 %collective-permute-start.12 = (bf16[32,32,64]{2,0,1:T(8,128)(2,1)}, bf16[32,32,64]{2,0,1:T(8,128)(2,1)}, u32[]{:S(2)}, u32[]{:S(2)}) collective-permute-start(bf16[32,32,64]{2,0,1:T(8,128)(2,1)} %select_convert_fusion), channel_id=1, source_target_pairs={{0,1},{1,2},{2,3},{3,4},{4,5},{5,6},{6,7},{7,8},{8,9},{9,10},{10,1... | collective-permute-start | bytes 393224 | tf_op jit(solution)/shard_map/ppermute | solution.py:24
  27.6 3.6 %collective-permute-start = (f32[32,32]{0,1:T(8,128)S(1)}, f32[32,32]{0,1:T(8,128)S(1)}, u32[]{:S(2)}, u32[]{:S(2)}) collective-permute-start(f32[32,32]{0,1:T(8,128)S(1)} %fusion.87), channel_id=1, source_target_pairs={{0,1},{1,0},{2,3},{3,2},{4,5},{5,4},{6,7},{7,6},{8,9},{9,8},{10,11... | collective-permute-start | bytes 12296 | tf_op jit(solution)/shard_map/ppermute | solution.py:15
  37.2 5.2 %collective-permute-start.1 = (f32[32,32]{0,1:T(8,128)S(1)}, f32[32,32]{0,1:T(8,128)S(1)}, u32[]{:S(2)}, u32[]{:S(2)}) collective-permute-start(f32[32,32]{0,1:T(8,128)S(1)} %fusion.78), channel_id=1, source_target_pairs={{0,2},{2,0},{4,6},{6,4},{8,10},{10,8},{12,14},{14,12},{1,3},{3,1},... | collective-permute-start | bytes 12296 | tf_op jit(solution)/shard_map/ppermute | solution.py:15
  44.3 10.3 %collective-permute-start.2 = (f32[32,32]{0,1:T(8,128)S(1)}, f32[32,32]{0,1:T(8,128)S(1)}, u32[]{:S(2)}, u32[]{:S(2)}) collective-permute-start(f32[32,32]{0,1:T(8,128)S(1)} %fusion.75), channel_id=1, source_target_pairs={{0,4},{2,6},{4,0},{6,2},{8,12},{10,14},{12,8},{14,10},{1,5},{3,7},... | collective-permute-start | bytes 12296 | tf_op jit(solution)/shard_map/ppermute | solution.py:15
  54.7 1.7 %collective-permute-done.2 = f32[32,32]{0,1:T(8,128)S(1)} collective-permute-done((f32[32,32]{0,1:T(8,128)S(1)}, f32[32,32]{0,1:T(8,128)S(1)}, u32[]{:S(2)}, u32[]{:S(2)}) %collective-permute-start.2) | collective-permute-done | bytes 4128 | tf_op jit(solution)/shard_map/ppermute | solution.py:15
  56.6 8.5 %collective-permute-start.3 = (f32[32,32]{0,1:T(8,128)S(1)}, f32[32,32]{0,1:T(8,128)S(1)}, u32[]{:S(2)}, u32[]{:S(2)}) collective-permute-start(f32[32,32]{0,1:T(8,128)S(1)} %fusion.72), channel_id=1, source_target_pairs={{0,8},{2,10},{4,12},{6,14},{8,0},{10,2},{12,4},{14,6},{1,9},{3,11}... | collective-permute-start | bytes 12296 | tf_op jit(solution)/shard_map/ppermute | solution.py:15
  67.0 3.6 %collective-permute-start.4 = (f32[32,32]{0,1:T(8,128)S(1)}, f32[32,32]{0,1:T(8,128)S(1)}, u32[]{:S(2)}, u32[]{:S(2)}) collective-permute-start(f32[32,32]{0,1:T(8,128)S(1)} %fusion.69), channel_id=1, source_target_pairs={{0,16},{16,0},{32,48},{48,32},{64,80},{80,64},{96,112},{112,96},{1... | collective-permute-start | bytes 12296 | tf_op jit(solution)/shard_map/ppermute | solution.py:15
  70.7 2.0 %collective-permute-done.4 = f32[32,32]{0,1:T(8,128)S(1)} collective-permute-done((f32[32,32]{0,1:T(8,128)S(1)}, f32[32,32]{0,1:T(8,128)S(1)}, u32[]{:S(2)}, u32[]{:S(2)}) %collective-permute-start.4) | collective-permute-done | bytes 4128 | tf_op jit(solution)/shard_map/ppermute | solution.py:15
  72.9 4.7 %collective-permute-start.5 = (f32[32,32]{0,1:T(8,128)S(1)}, f32[32,32]{0,1:T(8,128)S(1)}, u32[]{:S(2)}, u32[]{:S(2)}) collective-permute-start(f32[32,32]{0,1:T(8,128)S(1)} %fusion.66), channel_id=1, source_target_pairs={{0,32},{16,48},{32,0},{48,16},{64,96},{80,112},{96,64},{112,80},{1... | collective-permute-start | bytes 12296 | tf_op jit(solution)/shard_map/ppermute | solution.py:15
  77.7 1.8 %collective-permute-done.5 = f32[32,32]{0,1:T(8,128)S(1)} collective-permute-done((f32[32,32]{0,1:T(8,128)S(1)}, f32[32,32]{0,1:T(8,128)S(1)}, u32[]{:S(2)}, u32[]{:S(2)}) %collective-permute-start.5) | collective-permute-done | bytes 4128 | tf_op jit(solution)/shard_map/ppermute | solution.py:15
  79.6 8.2 %collective-permute-start.6 = (f32[32,32]{0,1:T(8,128)S(1)}, f32[32,32]{0,1:T(8,128)S(1)}, u32[]{:S(2)}, u32[]{:S(2)}) collective-permute-start(f32[32,32]{0,1:T(8,128)S(1)} %fusion.63), channel_id=1, source_target_pairs={{0,64},{16,80},{32,96},{48,112},{64,0},{80,16},{96,32},{112,48},{1... | collective-permute-start | bytes 12296 | tf_op jit(solution)/shard_map/ppermute | solution.py:15
  87.8 1.7 %collective-permute-done.6 = f32[32,32]{0,1:T(8,128)S(1)} collective-permute-done((f32[32,32]{0,1:T(8,128)S(1)}, f32[32,32]{0,1:T(8,128)S(1)}, u32[]{:S(2)}, u32[]{:S(2)}) %collective-permute-start.6) | collective-permute-done | bytes 4128 | tf_op jit(solution)/shard_map/ppermute | solution.py:15
  89.8 3.3 %collective-permute-start.7 = (f32[32,32]{0,1:T(8,128)S(1)}, f32[32,32]{0,1:T(8,128)S(1)}, u32[]{:S(2)}, u32[]{:S(2)}) collective-permute-start(f32[32,32]{0,1:T(8,128)S(1)} %fusion.60), channel_id=1, source_target_pairs={{0,128},{128,0},{256,384},{384,256},{512,640},{640,512},{768,896},... | collective-permute-start | bytes 12296 | tf_op jit(solution)/shard_map/ppermute | solution.py:15
  93.3 2.1 %collective-permute-done.7 = f32[32,32]{0,1:T(8,128)S(1)} collective-permute-done((f32[32,32]{0,1:T(8,128)S(1)}, f32[32,32]{0,1:T(8,128)S(1)}, u32[]{:S(2)}, u32[]{:S(2)}) %collective-permute-start.7) | collective-permute-done | bytes 4128 | tf_op jit(solution)/shard_map/ppermute | solution.py:15
  95.6 4.2 %collective-permute-start.8 = (f32[32,32]{0,1:T(8,128)S(1)}, f32[32,32]{0,1:T(8,128)S(1)}, u32[]{:S(2)}, u32[]{:S(2)}) collective-permute-start(f32[32,32]{0,1:T(8,128)S(1)} %fusion.57), channel_id=1, source_target_pairs={{0,256},{128,384},{256,0},{384,128},{512,768},{640,896},{768,512},... | collective-permute-start | bytes 12296 | tf_op jit(solution)/shard_map/ppermute | solution.py:15
  100.0 2.1 %collective-permute-done.8 = f32[32,32]{0,1:T(8,128)S(1)} collective-permute-done((f32[32,32]{0,1:T(8,128)S(1)}, f32[32,32]{0,1:T(8,128)S(1)}, u32[]{:S(2)}, u32[]{:S(2)}) %collective-permute-start.8) | collective-permute-done | bytes 4128 | tf_op jit(solution)/shard_map/ppermute | solution.py:15
  102.3 5.4 %collective-permute-start.9 = (f32[32,32]{0,1:T(8,128)S(1)}, f32[32,32]{0,1:T(8,128)}, u32[]{:S(2)}, u32[]{:S(2)}) collective-permute-start(f32[32,32]{0,1:T(8,128)S(1)} %fusion.54), channel_id=1, source_target_pairs={{0,512},{128,640},{256,768},{384,896},{512,0},{640,128},{768,256},... | collective-permute-start | bytes 12296 | tf_op jit(solution)/shard_map/ppermute | solution.py:15
  108.0 2.4 %reshape.298 = bf16[32,6,32,32]{3,2,0,1:T(8,128)(2,1)} reshape(bf16[32,6,1024]{2,0,1:T(8,128)(2,1)S(1)} %copy-done.6) | data formatting | bytes 786432 | tf_op jit(solution)/shard_map/reshape | solution.py:57
  111.1 4.3 %reshape.299 = bf16[32,6,64,64]{3,2,0,1:T(8,128)(2,1)S(1)} reshape(bf16[32,6,4096]{2,0,1:T(8,128)(2,1)} %param.21) | data formatting | bytes 3145728 | tf_op jit(solution)/shard_map/reshape | solution.py:56
  116.7 2.2 %pad_maximum_fusion = bf16[96,32,32]{1,2,0:T(8,128)(2,1)} fusion(bf16[32,32,32]{1,2,0:T(8,128)(2,1)} %collective-permute-done.11, bf16[32,32,32]{1,2,0:T(8,128)(2,1)} %convert_bitcast_fusion, bf16[32,32,32]{1,2,0:T(8,128)(2,1)} %collective-permute-done.10), kind=kLoop, calls=%fused_computation.20 | loop fusion | flops 196608 | bytes 393216 | tf_op jit(solution)/shard_map/concatenate | solution.py:26
  118.9 2.3 %copy.171 = bf16[96,32,32]{2,1,0:T(8,128)(2,1)} copy(bf16[96,32,32]{1,2,0:T(8,128)(2,1)} %pad_maximum_fusion) | data formatting | bytes 393216 | tf_op jit(solution)/shard_map/concatenate | solution.py:26
  121.2 3.1 %gather_fusion.1 = bf16[192,32,32]{2,1,0:T(8,128)(2,1)} fusion(bf16[96,32,32]{2,1,0:T(8,128)(2,1)} %copy.171, s32[1024]{0:T(1024)S(1)} %pad_clamp_fusion.1), kind=kCustom, calls=%fused_computation.1 | custom fusion | bytes 787200 | tf_op jit(solution)/shard_map/gather | solution.py:130
  124.3 3.8 %fusion.2 = f32[32,32,32]{1,2,0:T(8,128)} fusion(bf16[32,6,32,32]{3,2,1,0:T(8,128)(2,1)} %bitcast.221, f32[32,6]{1,0:T(8,128)S(1)} %copy-done.20, bf16[32,6,32,32]{3,2,0,1:T(8,128)(2,1)} %reshape.298), kind=kOutput, calls=%fused_computation.7 | convolution fusion | flops 12943360 | bytes 918272 | tf_op jit(solution)/shard_map/lkab,lkbc->lkac/dot_general | solution.py:131
  128.1 2.0 %copy.189 = f32[32,32,32]{2,1,0:T(8,128)} copy(f32[32,32,32]{1,2,0:T(8,128)} %fusion.2) | data formatting | bytes 262144 | tf_op jit(solution)/shard_map/lkac,lk->lac/dot_general | solution.py:135
  130.1 2.5 %fusion.10 = bf16[32,32,32]{2,1,0:T(8,128)(2,1)} fusion(f32[32,32,32]{2,1,0:T(8,128)} %copy.189, f32[32,32,32]{1,2,0:T(8,128)} %fusion.19, f32[32,32]{1,0:T(8,128)S(1)} %fusion.134), kind=kOutput, calls=%fused_computation.15 | convolution fusion | flops 12648448 | bytes 331776 | tf_op jit(solution)/shard_map/...ab,...bc->...ac/dot_general | solution.py:34
  132.6 2.2 %pad_maximum_fusion.1 = bf16[32,96,64]{2,0,1:T(8,128)(2,1)} fusion(bf16[32,32,64]{2,0,1:T(8,128)(2,1)} %collective-permute-done.13, bf16[32,32,64]{2,0,1:T(8,128)(2,1)} %select_convert_fusion, bf16[32,32,64]{2,0,1:T(8,128)(2,1)} %collective-permute-done.12), kind=kLoop, calls=%fused_computation.21 | loop fusion | flops 393216 | bytes 786432 | tf_op jit(solution)/shard_map/concatenate | solution.py:26
  134.8 3.2 %gather_fusion.2 = bf16[192,32,64]{2,1,0:T(8,128)(2,1)} fusion(bf16[32,96,64]{2,0,1:T(8,128)(2,1)} %pad_maximum_fusion.1, s32[1024]{0:T(1024)S(1)} %pad_clamp_fusion), kind=kCustom, calls=%fused_computation.2 | custom fusion | bytes 1573632 | tf_op jit(solution)/shard_map/gather | solution.py:143
  138.0 3.1 %fusion.5 = f32[32,32,6,64]{3,0,2,1:T(8,128)S(1)} fusion(bf16[32,32,6,64]{3,0,2,1:T(8,128)(2,1)} %bitcast.216, bf16[32,6,64,64]{3,2,0,1:T(8,128)(2,1)S(1)} %reshape.299), kind=kOutput, calls=%fused_computation.10 | convolution fusion | flops 50331648 | bytes 3932160 | tf_op jit(solution)/shard_map/lkpq,clkq->clkp/dot_general | solution.py:144
  141.1 5.2 %fusion = f32[32,1,32,64]{3,1,2,0:T(1,128)S(1)} fusion(f32[32,6,1,1]{1,2,3,0:T(1,128)S(1)} %copy.191, f32[32,32,6,64]{3,0,2,1:T(8,128)S(1)} %fusion.5), kind=kOutput, calls=%fused_computation.4 | convolution fusion | flops 4718592 | bytes 1835776 | tf_op jit(solution)/shard_map/clkp,lk->clp/dot_general | solution.py:148
  147.5 5.8 %scatter_custom_fusion = f32[32,2048]{0,1:T(8,128)S(1)} fusion(s32[2048]{0:T(1024)S(1)} %bitcast.232, f32[2048,32]{1,0:T(8,128)S(1)} %copy.178, f32[]{:T(128)} %constant.13.clone.1), kind=kCustom, calls=%fused_computation.23 | custom fusion | bytes 262148 | tf_op jit(solution)/shard_map/scatter | solution.py:150
  (156 shorter events, 28.6 us)
Async XLA Ops:
  0.6 145.7 %copy-start = (bf16[32,64,32]{1,2,0:T(8,128)(2,1)S(1)}, bf16[32,64,32]{1,2,0:T(8,128)(2,1)}, u32[]{:S(2)}) copy-start(bf16[32,64,32]{1,2,0:T(8,128)(2,1)} %param.20) | copy-start | bytes 393220
  0.6 9.0 %copy-start.17 = (s32[1,2048]{1,0:T(1,128)S(1)}, s32[1,2048]{1,0:T(1,128)}, u32[]{:S(2)}) copy-start(s32[1,2048]{1,0:T(1,128)} %param.18) | copy-start | bytes 24580
  2.4 8.8 %copy-start.7 = (bf16[32,64,32]{1,2,0:T(8,128)(2,1)S(1)}, bf16[32,64,32]{1,2,0:T(8,128)(2,1)}, u32[]{:S(2)}) copy-start(bf16[32,64,32]{1,2,0:T(8,128)(2,1)} %param.19) | copy-start | bytes 393220
  8.9 15.4 %copy-start.1 = (bf16[1,62,32,32]{1,3,2,0:T(8,128)(2,1)S(1)}, bf16[1,62,32,32]{1,3,2,0:T(8,128)(2,1)}, u32[]{:S(2)}) copy-start(bf16[1,62,32,32]{1,3,2,0:T(8,128)(2,1)} %param.27) | copy-start | bytes 380932
  13.2 103.5 %collective-permute-start.10 = (bf16[32,32,32]{1,2,0:T(8,128)(2,1)}, bf16[32,32,32]{1,2,0:T(8,128)(2,1)}, u32[]{:S(2)}, u32[]{:S(2)}) collective-permute-start(bf16[32,32,32]{1,2,0:T(8,128)(2,1)} %convert_bitcast_fusion), channel_id=1, source_target_pairs={{0,1},{1,2},{2,3},{3,4},{4,5},{5,6},{6,7},{7,8},{8,9},{9,10},{10,1... | collective-permute-start | bytes 196616 | tf_op jit(solution)/shard_map/ppermute | solution.py:24
  15.6 101.1 %collective-permute-start.11 = (bf16[32,32,32]{1,2,0:T(8,128)(2,1)}, bf16[32,32,32]{1,2,0:T(8,128)(2,1)}, u32[]{:S(2)}, u32[]{:S(2)}) collective-permute-start(bf16[32,32,32]{1,2,0:T(8,128)(2,1)} %convert_bitcast_fusion), channel_id=1, source_target_pairs={{1,0},{2,1},{3,2},{4,3},{5,4},{6,5},{7,6},{8,7},{9,8},{10,9},{11,1... | collective-permute-start | bytes 196616 | tf_op jit(solution)/shard_map/ppermute | solution.py:25
  16.9 115.7 %collective-permute-start.12 = (bf16[32,32,64]{2,0,1:T(8,128)(2,1)}, bf16[32,32,64]{2,0,1:T(8,128)(2,1)}, u32[]{:S(2)}, u32[]{:S(2)}) collective-permute-start(bf16[32,32,64]{2,0,1:T(8,128)(2,1)} %select_convert_fusion), channel_id=1, source_target_pairs={{0,1},{1,2},{2,3},{3,4},{4,5},{5,6},{6,7},{7,8},{8,9},{9,10},{10,1... | collective-permute-start | bytes 393224 | tf_op jit(solution)/shard_map/ppermute | solution.py:24
  23.1 109.6 %collective-permute-start.13 = (bf16[32,32,64]{2,0,1:T(8,128)(2,1)}, bf16[32,32,64]{2,0,1:T(8,128)(2,1)}, u32[]{:S(2)}, u32[]{:S(2)}) collective-permute-start(bf16[32,32,64]{2,0,1:T(8,128)(2,1)} %select_convert_fusion), channel_id=1, source_target_pairs={{1,0},{2,1},{3,2},{4,3},{5,4},{6,5},{7,6},{8,7},{9,8},{10,9},{11,1... | collective-permute-start | bytes 393224 | tf_op jit(solution)/shard_map/ppermute | solution.py:25
  27.6 9.4 %collective-permute-start = (f32[32,32]{0,1:T(8,128)S(1)}, f32[32,32]{0,1:T(8,128)S(1)}, u32[]{:S(2)}, u32[]{:S(2)}) collective-permute-start(f32[32,32]{0,1:T(8,128)S(1)} %fusion.87), channel_id=1, source_target_pairs={{0,1},{1,0},{2,3},{3,2},{4,5},{5,4},{6,7},{7,6},{8,9},{9,8},{10,11... | collective-permute-start | bytes 12296 | tf_op jit(solution)/shard_map/ppermute | solution.py:15
  35.2 19.4 %copy-start.16 = (f32[2,32,32]{2,1,0:T(8,128)S(1)}, f32[2,32,32]{2,1,0:T(8,128)}, u32[]{:S(2)}) copy-start(f32[2,32,32]{2,1,0:T(8,128)} %param.31) | copy-start | bytes 24580
  36.6 34.0 %copy-start.21 = (s32[32,6]{0,1:T(8,128)S(1)}, s32[32,6]{0,1:T(8,128)}, u32[]{:S(2)}) copy-start(s32[32,6]{0,1:T(8,128)} %param.26) | copy-start | bytes 2308
  36.6 34.0 %copy-start.23 = (f32[32,6]{0,1:T(8,128)S(1)}, f32[32,6]{0,1:T(8,128)}, u32[]{:S(2)}) copy-start(f32[32,6]{0,1:T(8,128)} %param.25) | copy-start | bytes 2308
  36.9 40.7 %copy-start.22 = (s32[32,6]{0,1:T(8,128)S(1)}, s32[32,6]{0,1:T(8,128)}, u32[]{:S(2)}) copy-start(s32[32,6]{0,1:T(8,128)} %param.23) | copy-start | bytes 2308
  37.0 40.7 %copy-start.24 = (f32[32,6]{0,1:T(8,128)S(1)}, f32[32,6]{0,1:T(8,128)}, u32[]{:S(2)}) copy-start(f32[32,6]{0,1:T(8,128)} %param.22) | copy-start | bytes 2308
  37.2 6.9 %collective-permute-start.1 = (f32[32,32]{0,1:T(8,128)S(1)}, f32[32,32]{0,1:T(8,128)S(1)}, u32[]{:S(2)}, u32[]{:S(2)}) collective-permute-start(f32[32,32]{0,1:T(8,128)S(1)} %fusion.78), channel_id=1, source_target_pairs={{0,2},{2,0},{4,6},{6,4},{8,10},{10,8},{12,14},{14,12},{1,3},{3,1},... | collective-permute-start | bytes 12296 | tf_op jit(solution)/shard_map/ppermute | solution.py:15
  44.1 21.0 %copy-start.8 = (f32[32,32]{0,1:T(8,128)}, f32[32,32]{0,1:T(8,128)S(1)}, u32[]{:S(2)}) copy-start(f32[32,32]{0,1:T(8,128)S(1)} %collective-permute-done.1) | copy-start | bytes 12292
  44.3 12.0 %collective-permute-start.2 = (f32[32,32]{0,1:T(8,128)S(1)}, f32[32,32]{0,1:T(8,128)S(1)}, u32[]{:S(2)}, u32[]{:S(2)}) collective-permute-start(f32[32,32]{0,1:T(8,128)S(1)} %fusion.75), channel_id=1, source_target_pairs={{0,4},{2,6},{4,0},{6,2},{8,12},{10,14},{12,8},{14,10},{1,5},{3,7},... | collective-permute-start | bytes 12296 | tf_op jit(solution)/shard_map/ppermute | solution.py:15
  56.4 8.8 %copy-start.9 = (f32[32,32]{0,1:T(8,128)}, f32[32,32]{0,1:T(8,128)S(1)}, u32[]{:S(2)}) copy-start(f32[32,32]{0,1:T(8,128)S(1)} %collective-permute-done.2) | copy-start | bytes 12292
  56.6 10.3 %collective-permute-start.3 = (f32[32,32]{0,1:T(8,128)S(1)}, f32[32,32]{0,1:T(8,128)S(1)}, u32[]{:S(2)}, u32[]{:S(2)}) collective-permute-start(f32[32,32]{0,1:T(8,128)S(1)} %fusion.72), channel_id=1, source_target_pairs={{0,8},{2,10},{4,12},{6,14},{8,0},{10,2},{12,4},{14,6},{1,9},{3,11}... | collective-permute-start | bytes 12296 | tf_op jit(solution)/shard_map/ppermute | solution.py:15
  65.5 42.5 %copy-start.6 = (bf16[32,6,1024]{2,0,1:T(8,128)(2,1)S(1)}, bf16[32,6,1024]{2,0,1:T(8,128)(2,1)}, u32[]{:S(2)}) copy-start(bf16[32,6,1024]{2,0,1:T(8,128)(2,1)} %param.24) | copy-start | bytes 1179652
  66.8 43.6 %copy-start.10 = (f32[32,32]{0,1:T(8,128)}, f32[32,32]{0,1:T(8,128)S(1)}, u32[]{:S(2)}) copy-start(f32[32,32]{0,1:T(8,128)S(1)} %collective-permute-done.3) | copy-start | bytes 12292
  67.0 5.6 %collective-permute-start.4 = (f32[32,32]{0,1:T(8,128)S(1)}, f32[32,32]{0,1:T(8,128)S(1)}, u32[]{:S(2)}, u32[]{:S(2)}) collective-permute-start(f32[32,32]{0,1:T(8,128)S(1)} %fusion.69), channel_id=1, source_target_pairs={{0,16},{16,0},{32,48},{48,32},{64,80},{80,64},{96,112},{112,96},{1... | collective-permute-start | bytes 12296 | tf_op jit(solution)/shard_map/ppermute | solution.py:15
  72.7 37.7 %copy-start.11 = (f32[32,32]{0,1:T(8,128)}, f32[32,32]{0,1:T(8,128)S(1)}, u32[]{:S(2)}) copy-start(f32[32,32]{0,1:T(8,128)S(1)} %collective-permute-done.4) | copy-start | bytes 12292
  72.9 6.5 %collective-permute-start.5 = (f32[32,32]{0,1:T(8,128)S(1)}, f32[32,32]{0,1:T(8,128)S(1)}, u32[]{:S(2)}, u32[]{:S(2)}) collective-permute-start(f32[32,32]{0,1:T(8,128)S(1)} %fusion.66), channel_id=1, source_target_pairs={{0,32},{16,48},{32,0},{48,16},{64,96},{80,112},{96,64},{112,80},{1... | collective-permute-start | bytes 12296 | tf_op jit(solution)/shard_map/ppermute | solution.py:15
  79.4 31.0 %copy-start.12 = (f32[32,32]{0,1:T(8,128)}, f32[32,32]{0,1:T(8,128)S(1)}, u32[]{:S(2)}) copy-start(f32[32,32]{0,1:T(8,128)S(1)} %collective-permute-done.5) | copy-start | bytes 12292
  79.6 9.9 %collective-permute-start.6 = (f32[32,32]{0,1:T(8,128)S(1)}, f32[32,32]{0,1:T(8,128)S(1)}, u32[]{:S(2)}, u32[]{:S(2)}) collective-permute-start(f32[32,32]{0,1:T(8,128)S(1)} %fusion.63), channel_id=1, source_target_pairs={{0,64},{16,80},{32,96},{48,112},{64,0},{80,16},{96,32},{112,48},{1... | collective-permute-start | bytes 12296 | tf_op jit(solution)/shard_map/ppermute | solution.py:15
  89.5 18.2 %copy-start.13 = (f32[32,32]{0,1:T(8,128)}, f32[32,32]{0,1:T(8,128)S(1)}, u32[]{:S(2)}) copy-start(f32[32,32]{0,1:T(8,128)S(1)} %collective-permute-done.6) | copy-start | bytes 12292
  89.8 5.6 %collective-permute-start.7 = (f32[32,32]{0,1:T(8,128)S(1)}, f32[32,32]{0,1:T(8,128)S(1)}, u32[]{:S(2)}, u32[]{:S(2)}) collective-permute-start(f32[32,32]{0,1:T(8,128)S(1)} %fusion.60), channel_id=1, source_target_pairs={{0,128},{128,0},{256,384},{384,256},{512,640},{640,512},{768,896},... | collective-permute-start | bytes 12296 | tf_op jit(solution)/shard_map/ppermute | solution.py:15
  95.4 12.4 %copy-start.14 = (f32[32,32]{0,1:T(8,128)}, f32[32,32]{0,1:T(8,128)S(1)}, u32[]{:S(2)}) copy-start(f32[32,32]{0,1:T(8,128)S(1)} %collective-permute-done.7) | copy-start | bytes 12292
  95.6 6.5 %collective-permute-start.8 = (f32[32,32]{0,1:T(8,128)S(1)}, f32[32,32]{0,1:T(8,128)S(1)}, u32[]{:S(2)}, u32[]{:S(2)}) collective-permute-start(f32[32,32]{0,1:T(8,128)S(1)} %fusion.57), channel_id=1, source_target_pairs={{0,256},{128,384},{256,0},{384,128},{512,768},{640,896},{768,512},... | collective-permute-start | bytes 12296 | tf_op jit(solution)/shard_map/ppermute | solution.py:15
  102.1 9.0 %copy-start.15 = (f32[32,32]{0,1:T(8,128)}, f32[32,32]{0,1:T(8,128)S(1)}, u32[]{:S(2)}) copy-start(f32[32,32]{0,1:T(8,128)S(1)} %collective-permute-done.8) | copy-start | bytes 12292
  102.3 13.2 %collective-permute-start.9 = (f32[32,32]{0,1:T(8,128)S(1)}, f32[32,32]{0,1:T(8,128)}, u32[]{:S(2)}, u32[]{:S(2)}) collective-permute-start(f32[32,32]{0,1:T(8,128)S(1)} %fusion.54), channel_id=1, source_target_pairs={{0,512},{128,640},{256,768},{384,896},{512,0},{640,128},{768,256},... | collective-permute-start | bytes 12296 | tf_op jit(solution)/shard_map/ppermute | solution.py:15
  (8 other events, 29.2 us)

commit v6 on v5

--- a/solution.py
+++ b/solution.py
@@ -53,8 +53,6 @@
     up_cpl,
 ):
     leaves_dev, leaf_size, rank_width = col_basis.shape
-    near_square = near_blocks.reshape(leaves_dev, near_blocks.shape[1], leaf_size, leaf_size)
-    far_square = far_blocks.reshape(leaves_dev, far_blocks.shape[1], rank_width, rank_width)
     order_row = perm[0]
     col_local = loc_col[0].astype(jnp.float32)
     row_local = loc_row[0].astype(jnp.float32)
@@ -83,7 +81,7 @@
         weights = apply_down(before, pick(up_cpl, side_col))
         return weights.transpose(1, 0, 2).reshape(rank_width, level_count * rank_width)
 
-    def climb_tree(root_coeff):
+    def climb_tree(root_coeff, stages, results):
         sides = climb_sides()
         side_col = jnp.stack([side for _, _, side in sides])
         own_first = jnp.concatenate([pick(up_col, side_col), pick(up_col, 1 - side_col)], axis=1)
@@ -91,6 +89,9 @@
         siblings = []
         for level, (name, bit_num, _) in enumerate(sides):
             sibling = from_partner(current, name, bit_num)
+            if level < len(stages):
+                key, stage = stages[level]
+                sibling, results[key] = lax.optimization_barrier((sibling, stage()))
             siblings.append(sibling)
             if level + 1 < len(sides):
                 stacked = jnp.concatenate([current, sibling], axis=0)
@@ -119,33 +120,71 @@
             offsets.append(start_at)
             start_at = start_at + node_count
         width_all = 3 * leaves_dev
-        paths = None
-        for start_at in reversed(offsets):
-            node_count = 2 if paths is None else paths.shape[0] * 2
-            rows = row_local[start_at : start_at + node_count]
-            paths = rows if paths is None else apply_down(rows, jnp.repeat(paths, 2, axis=0))
-        root_field = climb_tree(current[0])
+        results = {}
+
+        def leaf_paths():
+            paths = None
+            for start_at in reversed(offsets):
+                node_count = 2 if paths is None else paths.shape[0] * 2
+                rows = row_local[start_at : start_at + node_count]
+                paths = rows if paths is None else apply_down(rows, jnp.repeat(paths, 2, axis=0))
+            return paths
+
+        def near_square():
+            return near_blocks.reshape(leaves_dev, near_blocks.shape[1], leaf_size, leaf_size)
+
+        def far_square():
+            return far_blocks.reshape(leaves_dev, far_blocks.shape[1], rank_width, rank_width)
+
+        def far_picked():
+            return coeff_window[jnp.minimum(far_index, width_all - 1)]
+
+        def far_terms():
+            return jnp.einsum(
+                "lkab,lkbc->lkac", results["far_sq"], results["far_pick"],
+                preferred_element_type=jnp.float32,
+            )
+
+        def far_sum():
+            far_weight = jnp.where(far_index < width_all, far_scale, jnp.zeros_like(far_scale))
+            return jnp.einsum("lkac,lk->lac", results["far_terms"], far_weight, precision=best_precision)
+
+        def near_picked():
+            return x_window[:, jnp.minimum(near_index, width_all - 1)]
+
+        def near_terms():
+            return jnp.einsum(
+                "lkpq,clkq->clkp", results["near_sq"], results["near_pick"],
+                preferred_element_type=jnp.float32,
+            )
+
+        def near_total():
+            near_weight = jnp.where(near_index < width_all, near_scale, jnp.zeros_like(near_scale))
+            return jnp.einsum("clkp,lk->clp", results["near_terms"], near_weight, precision=best_precision)
+
+        stages = [
+            ("near_sq", near_square),
+            ("far_sq", far_square),
+            ("far_pick", far_picked),
+            ("far_terms", far_terms),
+            ("far_sum", far_sum),
+            ("near_pick", near_picked),
+            ("near_terms", near_terms),
+            ("near_sum", near_total),
+            ("paths", leaf_paths),
+        ]
+        root_field = climb_tree(current[0], stages, results)
+        for key, stage in stages:
+            if key not in results:
+                results[key] = stage()
+        paths = results["paths"]
+        near_sum = results["near_sum"]
         local_field = apply_down(paths, jnp.broadcast_to(root_field, (leaves_dev,) + root_field.shape))
-        far_live = far_index < width_all
-        picked = coeff_window[jnp.minimum(far_index, width_all - 1)]
-        far_terms = jnp.einsum(
-            "lkab,lkbc->lkac", far_square, picked, preferred_element_type=jnp.float32
-        )
-        far_weight = jnp.where(far_live, far_scale, jnp.zeros_like(far_scale))
-        leaf_field = local_field + jnp.einsum(
-            "lkac,lk->lac", far_terms, far_weight, precision=best_precision
-        )
+        leaf_field = local_field + results["far_sum"]
         field_round = leaf_field.astype(jnp.bfloat16)
         far_out = jnp.einsum(
             "lpk,lkc->clp", row_basis, field_round, preferred_element_type=jnp.float32
         )
-        near_live = near_index < width_all
-        near_pick = x_window[:, jnp.minimum(near_index, width_all - 1)]
-        near_terms = jnp.einsum(
-            "lkpq,clkq->clkp", near_square, near_pick, preferred_element_type=jnp.float32
-        )
-        near_weight = jnp.where(near_live, near_scale, jnp.zeros_like(near_scale))
-        near_sum = jnp.einsum("clkp,lk->clp", near_terms, near_weight, precision=best_precision)
         image = (far_out + near_sum).reshape(columns, leaves_dev * leaf_size)
         return jnp.zeros_like(image).at[:, order_row].set(image)
 

time: 159 us -> 139 us (0.87); the launches traced: 156 us -> 138 us
  local copies, waits for them, and re-layouts: 40.1 us -> 31.6 us
  waiting for transfers between devices: 14 us -> 7.44 us
  matrix products: 22.9 us -> 26.6 us
  other arithmetic: 8.64 us -> 5.35 us
  starting transfers between devices: 68.2 us -> 65.3 us
    ppermute x10, waiting for transfers between devices: 14 us -> 7.43 us  [from_partner(): return lax.ppermute(value, axis, pairs)]
    dot_general x3 -> x4, matrix products: 12.1 us -> 16.9 us  [the longest x1 6.06 us: far_sum(): jnp.einsum('lkac,lk->lac', results['far_terms'], far_weight, precision=be...]
    gather x2, local copies, waits for them, and re-layouts: 6.32 us -> 1.8 us  [the longest x1 0.9 us: far_picked(): return coeff_window[jnp.minimum(far_index, width_all - 1)]]
    ppermute x10, starting transfers between devices: 57.1 us -> 54.2 us  [from_partner(): return lax.ppermute(value, axis, pairs)]
    dot_general x1 -> x0, local copies, waits for them, and re-layouts: 2.04 us -> none  [apply_image(): jnp.einsum('lkac,lk->lac', far_terms, far_weight, precision=best_precision)]
    concatenate x1, local copies, waits for them, and re-layouts: 2.3 us -> 0.36 us  [extended(): return jnp.concatenate([low, block, high], axis=dim)]
    concatenate x2, other arithmetic: 4.34 us -> 2.41 us  [extended(): return jnp.concatenate([low, block, high], axis=dim)]
    unnamed x63 -> x60, local copies, waits for them, and re-layouts: 5.9 us -> 5.79 us
  transfers between devices with their start and end apart: 14 -> 14, of which waited for: 8 -> 2; matrix products, arithmetic and copies ran while one was open for 23% -> 29% of each run, Pallas kernels for 0% -> 0%
where the time goes in v6:
time: 139 us; the launch traced here: 138 us
  starting transfers between devices  65.3 us (47%)
  local copies, waits for them, and re-layouts  31.6 us (23%)
  matrix products  26.6 us (19%)
  waiting for transfers between devices  7.44 us (5%)
  other arithmetic  5.35 us (4%)
  between operations  1.76 us (1%)
    ppermute x10, starting transfers between devices, from_partner(): return lax.ppermute(value, axis, pairs)  54.2 us
    ppermute x2, starting transfers between devices, extended(): low = lax.ppermute(block, axis, forward)  8.56 us
    ppermute x10, waiting for transfers between devices, from_partner(): return lax.ppermute(value, axis, pairs)  7.43 us
    gather x2, local copies, waits for them, and re-layouts, apply_image(): ordered = jnp.take(vectors, order_row, axis=1).astype(jnp.bfloat16)  6.41 us
    dot_general x1, matrix products, far_sum(): jnp.einsum('lkac,lk->lac', results['far_terms'], far_weight, precision=be...  6.06 us
    scatter x1, local copies, waits for them, and re-layouts, apply_image(): return jnp.zeros_like(image).at[:, order_row].set(image)  5.97 us
    unnamed x60, local copies, waits for them, and re-layouts  5.79 us
    dot_general x1, matrix products, near_total(): jnp.einsum('clkp,lk->clp', results['near_terms'], near_weight, precision=...  5.22 us
  transfers between devices with their start and end apart: 14, of which 2 were waited for; matrix products, arithmetic and copies ran while one was open for 29% of the time, Pallas kernels for 0%

profile of v6, /device:TPU:14, one launch (start us, length us, event | category | flops | bytes accessed | tf_op | source)
XLA Modules:
  0.0 138.0 jit_solution(1127907104749667114)
XLA Ops:
  2.0 1.0 pad_maximum_fusion.2
  3.3 6.2 %gather_fusion = bf16[2048,32]{1,0:T(8,128)(2,1)S(1)} fusion(bf16[32,2048]{0,1:T(8,128)(2,1)S(1)} %copy.151, s32[2048]{0:T(1024)S(1)} %broadcast_clamp_fusion), kind=kCustom, calls=%fused_computation | custom fusion | bytes 270336 | tf_op jit(solution)/shard_map/jit(_take)/gather | solution.py:104
  11.4 2.5 %collective-permute-start.3 = (bf16[32,32,32]{1,2,0:T(8,128)(2,1)S(1)}, bf16[32,32,32]{1,2,0:T(8,128)(2,1)}, u32[]{:S(2)}, u32[]{:S(2)}) collective-permute-start(bf16[32,32,32]{1,2,0:T(8,128)(2,1)S(1)} %convert_bitcast_fusion), channel_id=1, source_target_pairs={{0,1},{1,2},{2,3},{3,4},{4,5},{5,6},{6,7},{7,8},{8,9},{9,10},{10,1... | collective-permute-start | bytes 196616 | tf_op jit(solution)/shard_map/ppermute | solution.py:24
  13.9 1.3 collective-permute-start.4
  15.2 6.1 %collective-permute-start.8 = (bf16[32,32,64]{2,0,1:T(8,128)(2,1)S(1)}, bf16[32,32,64]{2,0,1:T(8,128)(2,1)}, u32[]{:S(2)}, u32[]{:S(2)}) collective-permute-start(bf16[32,32,64]{2,0,1:T(8,128)(2,1)S(1)} %select_convert_fusion), channel_id=1, source_target_pairs={{0,1},{1,2},{2,3},{3,4},{4,5},{5,6},{6,7},{7,8},{8,9},{9,10},{10,1... | collective-permute-start | bytes 393224 | tf_op jit(solution)/shard_map/ppermute | solution.py:24
  21.3 1.3 collective-permute-start.9
  25.9 3.6 %collective-permute-start = (f32[32,32]{0,1:T(8,128)S(1)}, f32[32,32]{0,1:T(8,128)S(1)}, u32[]{:S(2)}, u32[]{:S(2)}) collective-permute-start(f32[32,32]{0,1:T(8,128)S(1)} %fusion.87), channel_id=1, source_target_pairs={{0,1},{1,0},{2,3},{3,2},{4,5},{5,4},{6,7},{7,6},{8,9},{9,8},{10,11... | collective-permute-start | bytes 12296 | tf_op jit(solution)/shard_map/ppermute | solution.py:15
  34.1 1.3 convolution_bitcast_fusion.1
  35.5 0.9 fusion.32
  36.4 4.4 %reshape.293 = bf16[32,6,64,64]{3,2,0,1:T(8,128)(2,1)} reshape(bf16[32,6,4096]{2,0,1:T(8,128)(2,1)S(1)} %copy-done.5) | data formatting | bytes 3145728 | tf_op jit(solution)/shard_map/reshape | solution.py:134
  41.2 5.2 %collective-permute-start.1 = (f32[32,32]{0,1:T(8,128)S(1)}, f32[32,32]{0,1:T(8,128)S(1)}, u32[]{:S(2)}, u32[]{:S(2)}) collective-permute-start(f32[32,32]{0,1:T(8,128)S(1)} %fusion.60), channel_id=1, source_target_pairs={{0,2},{2,0},{4,6},{6,4},{8,10},{10,8},{12,14},{14,12},{1,3},{3,1},... | collective-permute-start | bytes 12296 | tf_op jit(solution)/shard_map/ppermute | solution.py:15
  46.5 2.4 %reshape.294 = bf16[32,6,32,32]{3,2,0,1:T(8,128)(2,1)} reshape(bf16[32,6,1024]{2,0,1:T(8,128)(2,1)S(1)} %copy-done.6) | data formatting | bytes 786432 | tf_op jit(solution)/shard_map/reshape | solution.py:137
  49.2 10.3 %collective-permute-start.2 = (f32[32,32]{0,1:T(8,128)S(1)}, f32[32,32]{0,1:T(8,128)}, u32[]{:S(2)}, u32[]{:S(2)}) collective-permute-start(f32[32,32]{0,1:T(8,128)S(1)} %fusion.63), channel_id=1, source_target_pairs={{0,4},{2,6},{4,0},{6,2},{8,12},{10,14},{12,8},{14,10},{1,5},{3,7},... | collective-permute-start | bytes 12296 | tf_op jit(solution)/shard_map/ppermute | solution.py:15
  59.6 1.2 pad_maximum_fusion
  63.0 7.8 %collective-permute-start.5 = (f32[32,32]{0,1:T(8,128)S(1)}, f32[32,32]{0,1:T(8,128)S(1)}, u32[]{:S(2)}, u32[]{:S(2)}) collective-permute-start(f32[32,32]{0,1:T(8,128)S(1)} %fusion.66), channel_id=1, source_target_pairs={{0,8},{2,10},{4,12},{6,14},{8,0},{10,2},{12,4},{14,6},{1,9},{3,11}... | collective-permute-start | bytes 12296 | tf_op jit(solution)/shard_map/ppermute | solution.py:15
  70.8 2.0 %fusion.9 = f32[32,6,32,32]{3,2,1,0:T(8,128)S(1)} fusion(bf16[32,6,32,32]{3,2,1,0:T(8,128)(2,1)S(1)} %bitcast.224, bf16[32,6,32,32]{3,2,0,1:T(8,128)(2,1)} %reshape.294), kind=kOutput, calls=%fused_computation.11 | convolution fusion | flops 12582912 | bytes 1572864 | tf_op jit(solution)/shard_map/lkab,lkbc->lkac/dot_general | solution.py:143
  73.0 3.8 %collective-permute-start.6 = (f32[32,32]{0,1:T(8,128)S(1)}, f32[32,32]{0,1:T(8,128)S(1)}, u32[]{:S(2)}, u32[]{:S(2)}) collective-permute-start(f32[32,32]{0,1:T(8,128)S(1)} %fusion.69), channel_id=1, source_target_pairs={{0,16},{16,0},{32,48},{48,32},{64,80},{80,64},{96,112},{112,96},{1... | collective-permute-start | bytes 12296 | tf_op jit(solution)/shard_map/ppermute | solution.py:15
  76.8 6.1 %fusion.2 = f32[32,1,32,32]{3,1,2,0:T(1,128)} fusion(f32[32,6,1,1]{1,2,3,0:T(1,128)S(1)} %copy.186, f32[32,6,32,32]{3,2,1,0:T(8,128)S(1)} %fusion.9), kind=kOutput, calls=%fused_computation.6 | convolution fusion | flops 2359296 | bytes 918272 | tf_op jit(solution)/shard_map/lkac,lk->lac/dot_general | solution.py:150
  83.0 4.7 %collective-permute-start.7 = (f32[32,32]{0,1:T(8,128)S(1)}, f32[32,32]{0,1:T(8,128)S(1)}, u32[]{:S(2)}, u32[]{:S(2)}) collective-permute-start(f32[32,32]{0,1:T(8,128)S(1)} %fusion.72), channel_id=1, source_target_pairs={{0,32},{16,48},{32,0},{48,16},{64,96},{80,112},{96,64},{112,80},{1... | collective-permute-start | bytes 12296 | tf_op jit(solution)/shard_map/ppermute | solution.py:15
  87.8 1.2 pad_maximum_fusion.1
  90.1 6.9 %collective-permute-start.10 = (f32[32,32]{0,1:T(8,128)S(1)}, f32[32,32]{0,1:T(8,128)S(1)}, u32[]{:S(2)}, u32[]{:S(2)}) collective-permute-start(f32[32,32]{0,1:T(8,128)S(1)} %fusion.75), channel_id=1, source_target_pairs={{0,64},{16,80},{32,96},{48,112},{64,0},{80,16},{96,32},{112,48},{1... | collective-permute-start | bytes 12296 | tf_op jit(solution)/shard_map/ppermute | solution.py:15
  97.1 3.6 %fusion.6 = f32[32,32,6,64]{3,0,2,1:T(8,128)S(1)} fusion(bf16[32,32,6,64]{3,0,2,1:T(8,128)(2,1)S(1)} %bitcast.221, bf16[32,6,64,64]{3,2,0,1:T(8,128)(2,1)} %reshape.293), kind=kOutput, calls=%fused_computation.10 | convolution fusion | flops 50331648 | bytes 3932160 | tf_op jit(solution)/shard_map/lkpq,clkq->clkp/dot_general | solution.py:156
  100.9 3.5 %collective-permute-start.11 = (f32[32,32]{0,1:T(8,128)S(1)}, f32[32,32]{0,1:T(8,128)S(1)}, u32[]{:S(2)}, u32[]{:S(2)}) collective-permute-start(f32[32,32]{0,1:T(8,128)S(1)} %fusion.78), channel_id=1, source_target_pairs={{0,128},{128,0},{256,384},{384,256},{512,640},{640,512},{768,896},... | collective-permute-start | bytes 12296 | tf_op jit(solution)/shard_map/ppermute | solution.py:15
  104.4 5.2 %fusion = f32[32,1,32,64]{3,1,2,0:T(1,128)S(1)} fusion(f32[32,6,1,1]{1,2,3,0:T(1,128)S(1)} %copy.188, f32[32,32,6,64]{3,0,2,1:T(8,128)S(1)} %fusion.6), kind=kOutput, calls=%fused_computation.4 | convolution fusion | flops 4718592 | bytes 1835776 | tf_op jit(solution)/shard_map/clkp,lk->clp/dot_general | solution.py:163
  109.9 4.4 %collective-permute-start.12 = (f32[32,32]{0,1:T(8,128)S(1)}, f32[32,32]{0,1:T(8,128)S(1)}, u32[]{:S(2)}, u32[]{:S(2)}) collective-permute-start(f32[32,32]{0,1:T(8,128)S(1)} %fusion.81), channel_id=1, source_target_pairs={{0,256},{128,384},{256,0},{384,128},{512,768},{640,896},{768,512},... | collective-permute-start | bytes 12296 | tf_op jit(solution)/shard_map/ppermute | solution.py:15
  114.3 2.5 %collective-permute-done.12 = f32[32,32]{0,1:T(8,128)S(1)} collective-permute-done((f32[32,32]{0,1:T(8,128)S(1)}, f32[32,32]{0,1:T(8,128)S(1)}, u32[]{:S(2)}, u32[]{:S(2)}) %collective-permute-start.12) | collective-permute-done | bytes 4128 | tf_op jit(solution)/shard_map/ppermute | solution.py:15
  117.0 4.0 %collective-permute-start.13 = (f32[32,32]{0,1:T(8,128)S(1)}, f32[32,32]{0,1:T(8,128)S(1)}, u32[]{:S(2)}, u32[]{:S(2)}) collective-permute-start(f32[32,32]{0,1:T(8,128)S(1)} %fusion.54), channel_id=1, source_target_pairs={{0,512},{128,640},{256,768},{384,896},{512,0},{640,128},{768,256},... | collective-permute-start | bytes 12296 | tf_op jit(solution)/shard_map/ppermute | solution.py:15
  121.6 5.0 %collective-permute-done.13 = f32[32,32]{0,1:T(8,128)S(1)} collective-permute-done((f32[32,32]{0,1:T(8,128)S(1)}, f32[32,32]{0,1:T(8,128)S(1)}, u32[]{:S(2)}, u32[]{:S(2)}) %collective-permute-start.13) | collective-permute-done | bytes 4128 | tf_op jit(solution)/shard_map/ppermute | solution.py:15
  127.6 1.0 fusion.11
  129.8 6.0 %scatter_custom_fusion = f32[32,2048]{0,1:T(8,128)S(1)} fusion(s32[2048]{0:T(1024)} %bitcast.238, f32[2048,32]{1,0:T(8,128)S(1)} %copy.182, f32[]{:T(128)} %constant.13.clone.1), kind=kCustom, calls=%fused_computation.24 | custom fusion | bytes 262656 | tf_op jit(solution)/shard_map/scatter | solution.py:189
  136.1 1.0 copy.183
  137.1 1.0 copy.184
  (154 shorter events, 19.3 us)
Async XLA Ops:
  0.6 127.9 %copy-start = (bf16[32,64,32]{1,2,0:T(8,128)(2,1)S(1)}, bf16[32,64,32]{1,2,0:T(8,128)(2,1)}, u32[]{:S(2)}) copy-start(bf16[32,64,32]{1,2,0:T(8,128)(2,1)} %param.20) | copy-start | bytes 393220
  0.6 9.6 %copy-start.14 = (s32[1,2048]{1,0:T(1,128)S(1)}, s32[1,2048]{1,0:T(1,128)}, u32[]{:S(2)}) copy-start(s32[1,2048]{1,0:T(1,128)} %param.18) | copy-start | bytes 24580
  3.0 8.1 %copy-start.7 = (bf16[32,64,32]{1,2,0:T(8,128)(2,1)S(1)}, bf16[32,64,32]{1,2,0:T(8,128)(2,1)}, u32[]{:S(2)}) copy-start(bf16[32,64,32]{1,2,0:T(8,128)(2,1)} %param.19) | copy-start | bytes 393220
  9.5 13.1 %copy-start.1 = (bf16[1,62,32,32]{1,3,2,0:T(8,128)(2,1)S(1)}, bf16[1,62,32,32]{1,3,2,0:T(8,128)(2,1)}, u32[]{:S(2)}) copy-start(bf16[1,62,32,32]{1,3,2,0:T(8,128)(2,1)} %param.27) | copy-start | bytes 380932
  11.4 48.1 %collective-permute-start.3 = (bf16[32,32,32]{1,2,0:T(8,128)(2,1)S(1)}, bf16[32,32,32]{1,2,0:T(8,128)(2,1)}, u32[]{:S(2)}, u32[]{:S(2)}) collective-permute-start(bf16[32,32,32]{1,2,0:T(8,128)(2,1)S(1)} %convert_bitcast_fusion), channel_id=1, source_target_pairs={{0,1},{1,2},{2,3},{3,4},{4,5},{5,6},{6,7},{7,8},{8,9},{9,10},{10,1... | collective-permute-start | bytes 196616 | tf_op jit(solution)/shard_map/ppermute | solution.py:24
  13.9 45.7 %collective-permute-start.4 = (bf16[32,32,32]{1,2,0:T(8,128)(2,1)S(1)}, bf16[32,32,32]{1,2,0:T(8,128)(2,1)}, u32[]{:S(2)}, u32[]{:S(2)}) collective-permute-start(bf16[32,32,32]{1,2,0:T(8,128)(2,1)S(1)} %convert_bitcast_fusion), channel_id=1, source_target_pairs={{1,0},{2,1},{3,2},{4,3},{5,4},{6,5},{7,6},{8,7},{9,8},{10,9},{11,1... | collective-permute-start | bytes 196616 | tf_op jit(solution)/shard_map/ppermute | solution.py:25
  15.2 72.6 %collective-permute-start.8 = (bf16[32,32,64]{2,0,1:T(8,128)(2,1)S(1)}, bf16[32,32,64]{2,0,1:T(8,128)(2,1)}, u32[]{:S(2)}, u32[]{:S(2)}) collective-permute-start(bf16[32,32,64]{2,0,1:T(8,128)(2,1)S(1)} %select_convert_fusion), channel_id=1, source_target_pairs={{0,1},{1,2},{2,3},{3,4},{4,5},{5,6},{6,7},{7,8},{8,9},{9,10},{10,1... | collective-permute-start | bytes 393224 | tf_op jit(solution)/shard_map/ppermute | solution.py:24
  21.3 66.5 %collective-permute-start.9 = (bf16[32,32,64]{2,0,1:T(8,128)(2,1)S(1)}, bf16[32,32,64]{2,0,1:T(8,128)(2,1)}, u32[]{:S(2)}, u32[]{:S(2)}) collective-permute-start(bf16[32,32,64]{2,0,1:T(8,128)(2,1)S(1)} %select_convert_fusion), channel_id=1, source_target_pairs={{1,0},{2,1},{3,2},{4,3},{5,4},{6,5},{7,6},{8,7},{9,8},{10,9},{11,1... | collective-permute-start | bytes 393224 | tf_op jit(solution)/shard_map/ppermute | solution.py:25
  24.0 5.5 %copy-start.2 = (bf16[1,62,32,32]{1,3,2,0:T(8,128)(2,1)S(1)}, bf16[1,62,32,32]{1,3,2,0:T(8,128)(2,1)}, u32[]{:S(2)}) copy-start(bf16[1,62,32,32]{1,3,2,0:T(8,128)(2,1)} %param.28) | copy-start | bytes 380932
  25.3 5.2 %copy-start.22 = (f32[32,6]{0,1:T(8,128)S(1)}, f32[32,6]{0,1:T(8,128)}, u32[]{:S(2)}) copy-start(f32[32,6]{0,1:T(8,128)} %param.25) | copy-start | bytes 2308
  25.3 5.2 %copy-start.19 = (s32[32,6]{0,1:T(8,128)S(1)}, s32[32,6]{0,1:T(8,128)}, u32[]{:S(2)}) copy-start(s32[32,6]{0,1:T(8,128)} %param.23) | copy-start | bytes 2308
  25.3 5.2 %copy-start.23 = (f32[32,6]{0,1:T(8,128)S(1)}, f32[32,6]{0,1:T(8,128)}, u32[]{:S(2)}) copy-start(f32[32,6]{0,1:T(8,128)} %param.22) | copy-start | bytes 2308
  25.9 15.1 %collective-permute-start = (f32[32,32]{0,1:T(8,128)S(1)}, f32[32,32]{0,1:T(8,128)S(1)}, u32[]{:S(2)}, u32[]{:S(2)}) collective-permute-start(f32[32,32]{0,1:T(8,128)S(1)} %fusion.87), channel_id=1, source_target_pairs={{0,1},{1,0},{2,3},{3,2},{4,5},{5,4},{6,7},{7,6},{8,9},{9,8},{10,11... | collective-permute-start | bytes 12296 | tf_op jit(solution)/shard_map/ppermute | solution.py:15
  36.4 10.0 %copy-start.6 = (bf16[32,6,1024]{2,0,1:T(8,128)(2,1)S(1)}, bf16[32,6,1024]{2,0,1:T(8,128)(2,1)}, u32[]{:S(2)}) copy-start(bf16[32,6,1024]{2,0,1:T(8,128)(2,1)} %param.24) | copy-start | bytes 1179652
  41.0 5.4 %copy-start.9 = (f32[32,32]{0,1:T(8,128)}, f32[32,32]{0,1:T(8,128)S(1)}, u32[]{:S(2)}) copy-start(f32[32,32]{0,1:T(8,128)S(1)} %collective-permute-done) | copy-start | bytes 12292
  41.2 7.8 %collective-permute-start.1 = (f32[32,32]{0,1:T(8,128)S(1)}, f32[32,32]{0,1:T(8,128)S(1)}, u32[]{:S(2)}, u32[]{:S(2)}) collective-permute-start(f32[32,32]{0,1:T(8,128)S(1)} %fusion.60), channel_id=1, source_target_pairs={{0,2},{2,0},{4,6},{6,4},{8,10},{10,8},{12,14},{14,12},{1,3},{3,1},... | collective-permute-start | bytes 12296 | tf_op jit(solution)/shard_map/ppermute | solution.py:15
  49.0 10.6 %copy-start.11 = (f32[32,32]{0,1:T(8,128)}, f32[32,32]{0,1:T(8,128)S(1)}, u32[]{:S(2)}) copy-start(f32[32,32]{0,1:T(8,128)S(1)} %collective-permute-done.1) | copy-start | bytes 12292
  49.2 12.8 %collective-permute-start.2 = (f32[32,32]{0,1:T(8,128)S(1)}, f32[32,32]{0,1:T(8,128)}, u32[]{:S(2)}, u32[]{:S(2)}) collective-permute-start(f32[32,32]{0,1:T(8,128)S(1)} %fusion.63), channel_id=1, source_target_pairs={{0,4},{2,6},{4,0},{6,2},{8,12},{10,14},{12,8},{14,10},{1,5},{3,7},... | collective-permute-start | bytes 12296 | tf_op jit(solution)/shard_map/ppermute | solution.py:15
  63.0 9.8 %collective-permute-start.5 = (f32[32,32]{0,1:T(8,128)S(1)}, f32[32,32]{0,1:T(8,128)S(1)}, u32[]{:S(2)}, u32[]{:S(2)}) collective-permute-start(f32[32,32]{0,1:T(8,128)S(1)} %fusion.66), channel_id=1, source_target_pairs={{0,8},{2,10},{4,12},{6,14},{8,0},{10,2},{12,4},{14,6},{1,9},{3,11}... | collective-permute-start | bytes 12296 | tf_op jit(solution)/shard_map/ppermute | solution.py:15
  73.0 9.9 %collective-permute-start.6 = (f32[32,32]{0,1:T(8,128)S(1)}, f32[32,32]{0,1:T(8,128)S(1)}, u32[]{:S(2)}, u32[]{:S(2)}) collective-permute-start(f32[32,32]{0,1:T(8,128)S(1)} %fusion.69), channel_id=1, source_target_pairs={{0,16},{16,0},{32,48},{48,32},{64,80},{80,64},{96,112},{112,96},{1... | collective-permute-start | bytes 12296 | tf_op jit(solution)/shard_map/ppermute | solution.py:15
  83.0 6.9 %collective-permute-start.7 = (f32[32,32]{0,1:T(8,128)S(1)}, f32[32,32]{0,1:T(8,128)S(1)}, u32[]{:S(2)}, u32[]{:S(2)}) collective-permute-start(f32[32,32]{0,1:T(8,128)S(1)} %fusion.72), channel_id=1, source_target_pairs={{0,32},{16,48},{32,0},{48,16},{64,96},{80,112},{96,64},{112,80},{1... | collective-permute-start | bytes 12296 | tf_op jit(solution)/shard_map/ppermute | solution.py:15
  90.1 10.6 %collective-permute-start.10 = (f32[32,32]{0,1:T(8,128)S(1)}, f32[32,32]{0,1:T(8,128)S(1)}, u32[]{:S(2)}, u32[]{:S(2)}) collective-permute-start(f32[32,32]{0,1:T(8,128)S(1)} %fusion.75), channel_id=1, source_target_pairs={{0,64},{16,80},{32,96},{48,112},{64,0},{80,16},{96,32},{112,48},{1... | collective-permute-start | bytes 12296 | tf_op jit(solution)/shard_map/ppermute | solution.py:15
  100.9 13.4 %copy-start.13 = (f32[2,32,32]{2,1,0:T(8,128)S(1)}, f32[2,32,32]{2,1,0:T(8,128)}, u32[]{:S(2)}) copy-start(f32[2,32,32]{2,1,0:T(8,128)} %param.31) | copy-start | bytes 24580
  100.9 20.0 %copy-start.8 = (f32[9,32,32]{2,1,0:T(8,128)S(1)}, f32[9,32,32]{2,1,0:T(8,128)}, u32[]{:S(2)}) copy-start(f32[9,32,32]{2,1,0:T(8,128)} %fusion.32) | copy-start | bytes 110596
  100.9 20.0 %copy-start.21 = (pred[10]{0:T(512)(128)(4,1)S(1)}, pred[10]{0:T(512)(128)(4,1)}, u32[]{:S(2)}) copy-start(pred[10]{0:T(512)(128)(4,1)} %copy-done.20) | copy-start | bytes 34
  100.9 8.8 %collective-permute-start.11 = (f32[32,32]{0,1:T(8,128)S(1)}, f32[32,32]{0,1:T(8,128)S(1)}, u32[]{:S(2)}, u32[]{:S(2)}) collective-permute-start(f32[32,32]{0,1:T(8,128)S(1)} %fusion.78), channel_id=1, source_target_pairs={{0,128},{128,0},{256,384},{384,256},{512,640},{640,512},{768,896},... | collective-permute-start | bytes 12296 | tf_op jit(solution)/shard_map/ppermute | solution.py:15
  109.7 16.9 %copy-start.10 = (f32[32,32]{0,1:T(8,128)S(1)}, f32[32,32]{0,1:T(8,128)}, u32[]{:S(2)}) copy-start(f32[32,32]{0,1:T(8,128)} %copy-done.9) | copy-start | bytes 12292
  109.7 16.9 %copy-start.12 = (f32[32,32]{0,1:T(8,128)S(1)}, f32[32,32]{0,1:T(8,128)}, u32[]{:S(2)}) copy-start(f32[32,32]{0,1:T(8,128)} %copy-done.11) | copy-start | bytes 12292
  109.7 17.9 %copy-start.3 = (f32[32,1,32,32]{3,1,2,0:T(1,128)S(1)}, f32[32,1,32,32]{3,1,2,0:T(1,128)}, u32[]{:S(2)}) copy-start(f32[32,1,32,32]{3,1,2,0:T(1,128)} %fusion.2) | copy-start | bytes 393220
  109.7 17.9 %copy-start.4 = (f32[32,32,32]{1,2,0:T(8,128)S(1)}, f32[32,32,32]{1,2,0:T(8,128)}, u32[]{:S(2)}) copy-start(f32[32,32,32]{1,2,0:T(8,128)} %convolution_bitcast_fusion.1) | copy-start | bytes 393220
  109.9 6.8 %collective-permute-start.12 = (f32[32,32]{0,1:T(8,128)S(1)}, f32[32,32]{0,1:T(8,128)S(1)}, u32[]{:S(2)}, u32[]{:S(2)}) collective-permute-start(f32[32,32]{0,1:T(8,128)S(1)} %fusion.81), channel_id=1, source_target_pairs={{0,256},{128,384},{256,0},{384,128},{512,768},{640,896},{768,512},... | collective-permute-start | bytes 12296 | tf_op jit(solution)/shard_map/ppermute | solution.py:15
  117.0 9.5 %collective-permute-start.13 = (f32[32,32]{0,1:T(8,128)S(1)}, f32[32,32]{0,1:T(8,128)S(1)}, u32[]{:S(2)}, u32[]{:S(2)}) collective-permute-start(f32[32,32]{0,1:T(8,128)S(1)} %fusion.54), channel_id=1, source_target_pairs={{0,512},{128,640},{256,768},{384,896},{512,0},{640,128},{768,256},... | collective-permute-start | bytes 12296 | tf_op jit(solution)/shard_map/ppermute | solution.py:15
  (6 other events, 14.3 us)

commit v7 on v6

--- a/solution.py
+++ b/solution.py
@@ -139,37 +139,25 @@
         def far_picked():
             return coeff_window[jnp.minimum(far_index, width_all - 1)]
 
-        def far_terms():
-            return jnp.einsum(
-                "lkab,lkbc->lkac", results["far_sq"], results["far_pick"],
-                preferred_element_type=jnp.float32,
-            )
-
         def far_sum():
             far_weight = jnp.where(far_index < width_all, far_scale, jnp.zeros_like(far_scale))
-            return jnp.einsum("lkac,lk->lac", results["far_terms"], far_weight, precision=best_precision)
+            scaled = results["far_pick"].astype(jnp.float32) * far_weight[:, :, None, None]
+            return jnp.einsum("lkab,lkbc->lac", results["far_sq"], scaled, precision=best_precision)
 
         def near_picked():
             return x_window[:, jnp.minimum(near_index, width_all - 1)]
 
-        def near_terms():
-            return jnp.einsum(
-                "lkpq,clkq->clkp", results["near_sq"], results["near_pick"],
-                preferred_element_type=jnp.float32,
-            )
-
         def near_total():
             near_weight = jnp.where(near_index < width_all, near_scale, jnp.zeros_like(near_scale))
-            return jnp.einsum("clkp,lk->clp", results["near_terms"], near_weight, precision=best_precision)
+            scaled = results["near_pick"].astype(jnp.float32) * near_weight[None, :, :, None]
+            return jnp.einsum("lkpq,clkq->clp", results["near_sq"], scaled, precision=best_precision)
 
         stages = [
             ("near_sq", near_square),
             ("far_sq", far_square),
             ("far_pick", far_picked),
-            ("far_terms", far_terms),
             ("far_sum", far_sum),
             ("near_pick", near_picked),
-            ("near_terms", near_terms),
             ("near_sum", near_total),
             ("paths", leaf_paths),
         ]

time: 139 us -> 137 us (0.986)
  matrix products: 26.6 us -> 17.8 us
  waiting for transfers between devices: 7.44 us -> 10.9 us
  local copies, waits for them, and re-layouts: 31.6 us -> 33.9 us
    dot_general x4 -> x2, matrix products: 16.9 us -> 9.55 us  [the longest x1 4.97 us: far_sum(): jnp.einsum('lkab,lkbc->lac', results['far_sq'], scaled, precision=best_pr...]
    ppermute x10, waiting for transfers between devices: 7.43 us -> 10.8 us  [from_partner(): return lax.ppermute(value, axis, pairs)]
  transfers between devices with their start and end apart: 14 -> 14, of which waited for: 2 -> 4; matrix products, arithmetic and copies ran while one was open for 29% -> 25% of each run, Pallas kernels for 0% -> 0%
where the time goes in v7:
time: 137 us; the launch traced here: 136 us
  starting transfers between devices  65.9 us (48%)
  local copies, waits for them, and re-layouts  33.9 us (25%)
  matrix products  17.8 us (13%)
  waiting for transfers between devices  10.9 us (8%)
  other arithmetic  6.16 us (4%)
  between operations  1.73 us (1%)
    ppermute x10, starting transfers between devices, from_partner(): return lax.ppermute(value, axis, pairs)  54.8 us
    ppermute x10, waiting for transfers between devices, from_partner(): return lax.ppermute(value, axis, pairs)  10.8 us
    ppermute x2, starting transfers between devices, extended(): low = lax.ppermute(block, axis, forward)  8.55 us
    gather x2, local copies, waits for them, and re-layouts, apply_image(): ordered = jnp.take(vectors, order_row, axis=1).astype(jnp.bfloat16)  6.41 us
    scatter x1, local copies, waits for them, and re-layouts, apply_image(): return jnp.zeros_like(image).at[:, order_row].set(image)  5.85 us
    reshape x1, local copies, waits for them, and re-layouts, near_square(): near_blocks.reshape(leaves_dev, near_blocks.shape[1], leaf_size, leaf_size)  5.58 us
    unnamed x60, local copies, waits for them, and re-layouts  5.21 us
    dot_general x1, matrix products, far_sum(): jnp.einsum('lkab,lkbc->lac', results['far_sq'], scaled, precision=best_pr...  4.97 us
  transfers between devices with their start and end apart: 14, of which 4 were waited for; matrix products, arithmetic and copies ran while one was open for 25% of the time, Pallas kernels for 0%

profile of v7, /device:TPU:14, one launch (start us, length us, event | category | flops | bytes accessed | tf_op | source)
XLA Modules:
  0.0 136.3 jit_solution(5815438525838448639)
XLA Ops:
  1.4 1.0 pad_maximum_fusion.2
  2.7 6.2 %gather_fusion = bf16[2048,32]{1,0:T(8,128)(2,1)S(1)} fusion(bf16[32,2048]{0,1:T(8,128)(2,1)S(1)} %copy.159, s32[2048]{0:T(1024)S(1)} %broadcast_clamp_fusion), kind=kCustom, calls=%fused_computation | custom fusion | bytes 270336 | tf_op jit(solution)/shard_map/jit(_take)/gather | solution.py:104
  11.5 2.4 %collective-permute-start.3 = (bf16[32,32,32]{1,2,0:T(8,128)(2,1)}, bf16[32,32,32]{1,2,0:T(8,128)(2,1)}, u32[]{:S(2)}, u32[]{:S(2)}) collective-permute-start(bf16[32,32,32]{1,2,0:T(8,128)(2,1)} %convert_bitcast_fusion), channel_id=1, source_target_pairs={{0,1},{1,2},{2,3},{3,4},{4,5},{5,6},{6,7},{7,8},{8,9},{9,10},{10,1... | collective-permute-start | bytes 196616 | tf_op jit(solution)/shard_map/ppermute | solution.py:24
  14.0 1.3 collective-permute-start.4
  15.3 6.1 %collective-permute-start.7 = (bf16[32,32,64]{2,0,1:T(8,128)(2,1)S(1)}, bf16[32,32,64]{2,0,1:T(8,128)(2,1)}, u32[]{:S(2)}, u32[]{:S(2)}) collective-permute-start(bf16[32,32,64]{2,0,1:T(8,128)(2,1)S(1)} %select_convert_fusion), channel_id=1, source_target_pairs={{0,1},{1,2},{2,3},{3,4},{4,5},{5,6},{6,7},{7,8},{8,9},{9,10},{10,1... | collective-permute-start | bytes 393224 | tf_op jit(solution)/shard_map/ppermute | solution.py:24
  21.4 1.3 collective-permute-start.8
  26.0 3.6 %collective-permute-start = (f32[32,32]{0,1:T(8,128)S(1)}, f32[32,32]{0,1:T(8,128)S(1)}, u32[]{:S(2)}, u32[]{:S(2)}) collective-permute-start(f32[32,32]{0,1:T(8,128)S(1)} %fusion.91), channel_id=1, source_target_pairs={{0,1},{1,0},{2,3},{3,2},{4,5},{5,4},{6,7},{7,6},{8,9},{9,8},{10,11... | collective-permute-start | bytes 12296 | tf_op jit(solution)/shard_map/ppermute | solution.py:15
  34.5 5.6 %reshape.295 = bf16[32,6,64,64]{3,2,0,1:T(8,128)(2,1)} reshape(bf16[32,6,4096]{2,0,1:T(8,128)(2,1)} %param.21) | data formatting | bytes 3145728 | tf_op jit(solution)/shard_map/reshape | solution.py:134
  40.5 5.2 %collective-permute-start.1 = (f32[32,32]{0,1:T(8,128)S(1)}, f32[32,32]{0,1:T(8,128)S(1)}, u32[]{:S(2)}, u32[]{:S(2)}) collective-permute-start(f32[32,32]{0,1:T(8,128)S(1)} %fusion.70), channel_id=1, source_target_pairs={{0,2},{2,0},{4,6},{6,4},{8,10},{10,8},{12,14},{14,12},{1,3},{3,1},... | collective-permute-start | bytes 12296 | tf_op jit(solution)/shard_map/ppermute | solution.py:15
  45.7 2.4 %reshape.296 = bf16[32,6,32,32]{3,2,0,1:T(8,128)(2,1)} reshape(bf16[32,6,1024]{2,0,1:T(8,128)(2,1)S(1)} %copy-done.6) | data formatting | bytes 786432 | tf_op jit(solution)/shard_map/reshape | solution.py:137
  49.0 10.3 %collective-permute-start.2 = (f32[32,32]{0,1:T(8,128)S(1)}, f32[32,32]{0,1:T(8,128)S(1)}, u32[]{:S(2)}, u32[]{:S(2)}) collective-permute-start(f32[32,32]{0,1:T(8,128)S(1)} %fusion.73), channel_id=1, source_target_pairs={{0,4},{2,6},{4,0},{6,2},{8,12},{10,14},{12,8},{14,10},{1,5},{3,7},... | collective-permute-start | bytes 12296 | tf_op jit(solution)/shard_map/ppermute | solution.py:15
  59.4 1.3 pad_maximum_fusion
  61.0 2.1 %gather_fusion.1 = bf16[192,32,32]{2,1,0:T(8,128)(2,1)} fusion(bf16[96,32,32]{2,1,0:T(8,128)(2,1)S(1)} %copy.175, s32[1024]{0:T(1024)S(1)} %pad_clamp_fusion.1), kind=kCustom, calls=%fused_computation.1 | custom fusion | bytes 787200 | tf_op jit(solution)/shard_map/gather | solution.py:140
  63.3 8.0 %collective-permute-start.5 = (f32[32,32]{0,1:T(8,128)S(1)}, f32[32,32]{0,1:T(8,128)S(1)}, u32[]{:S(2)}, u32[]{:S(2)}) collective-permute-start(f32[32,32]{0,1:T(8,128)S(1)} %fusion.76), channel_id=1, source_target_pairs={{0,8},{2,10},{4,12},{6,14},{8,0},{10,2},{12,4},{14,6},{1,9},{3,11}... | collective-permute-start | bytes 12296 | tf_op jit(solution)/shard_map/ppermute | solution.py:15
  71.3 5.0 %fusion.12 = f32[32,32,32]{2,1,0:T(8,128)} fusion(bf16[32,6,32,32]{3,2,0,1:T(8,128)(2,1)} %reshape.296, bf16[32,6,32,32]{3,2,1,0:T(8,128)(2,1)} %bitcast.217, f32[32,6]{1,0:T(8,128)S(1)} %copy.176), kind=kOutput, calls=%fused_computation.16 | convolution fusion | flops 75890688 | bytes 918272 | tf_op jit(solution)/shard_map/lkab,lkbc->lac/dot_general | solution.py:145
  76.5 3.6 %collective-permute-start.6 = (f32[32,32]{0,1:T(8,128)S(1)}, f32[32,32]{0,1:T(8,128)}, u32[]{:S(2)}, u32[]{:S(2)}) collective-permute-start(f32[32,32]{0,1:T(8,128)S(1)} %fusion.79), channel_id=1, source_target_pairs={{0,16},{16,0},{32,48},{48,32},{64,80},{80,64},{96,112},{112,96},{1... | collective-permute-start | bytes 12296 | tf_op jit(solution)/shard_map/ppermute | solution.py:15
  80.1 1.2 pad_maximum_fusion.1
  82.2 0.9 fusion.82
  83.2 4.9 %collective-permute-start.9 = (f32[32,32]{0,1:T(8,128)S(1)}, f32[32,32]{0,1:T(8,128)S(1)}, u32[]{:S(2)}, u32[]{:S(2)}) collective-permute-start(f32[32,32]{0,1:T(8,128)S(1)} %fusion.82), channel_id=1, source_target_pairs={{0,32},{16,48},{32,0},{48,16},{64,96},{80,112},{96,64},{112,80},{1... | collective-permute-start | bytes 12296 | tf_op jit(solution)/shard_map/ppermute | solution.py:15
  88.1 4.6 %fusion.7 = f32[32,32,64]{2,0,1:T(8,128)S(1)} fusion(bf16[32,6,64,64]{3,2,0,1:T(8,128)(2,1)} %reshape.295, bf16[32,32,6,64]{3,0,2,1:T(8,128)(2,1)S(1)} %bitcast.215, f32[32,6]{1,0:T(8,128)} %copy.179), kind=kOutput, calls=%fused_computation.12 | convolution fusion | flops 302776320 | bytes 2622208 | tf_op jit(solution)/shard_map/lkpq,clkq->clp/dot_general | solution.py:153
  92.9 6.4 %collective-permute-start.10 = (f32[32,32]{0,1:T(8,128)S(1)}, f32[32,32]{0,1:T(8,128)S(1)}, u32[]{:S(2)}, u32[]{:S(2)}) collective-permute-start(f32[32,32]{0,1:T(8,128)S(1)} %fusion.85), channel_id=1, source_target_pairs={{0,64},{16,80},{32,96},{48,112},{64,0},{80,16},{96,32},{112,48},{1... | collective-permute-start | bytes 12296 | tf_op jit(solution)/shard_map/ppermute | solution.py:15
  99.7 2.8 %collective-permute-done.10 = f32[32,32]{0,1:T(8,128)S(1)} collective-permute-done((f32[32,32]{0,1:T(8,128)S(1)}, f32[32,32]{0,1:T(8,128)S(1)}, u32[]{:S(2)}, u32[]{:S(2)}) %collective-permute-start.10) | collective-permute-done | bytes 4128 | tf_op jit(solution)/shard_map/ppermute | solution.py:15
  102.7 3.5 %collective-permute-start.11 = (f32[32,32]{0,1:T(8,128)S(1)}, f32[32,32]{0,1:T(8,128)S(1)}, u32[]{:S(2)}, u32[]{:S(2)}) collective-permute-start(f32[32,32]{0,1:T(8,128)S(1)} %fusion.64), channel_id=1, source_target_pairs={{0,128},{128,0},{256,384},{384,256},{512,640},{640,512},{768,896},... | collective-permute-start | bytes 12296 | tf_op jit(solution)/shard_map/ppermute | solution.py:15
  106.4 2.0 %collective-permute-done.11 = f32[32,32]{0,1:T(8,128)S(1)} collective-permute-done((f32[32,32]{0,1:T(8,128)S(1)}, f32[32,32]{0,1:T(8,128)S(1)}, u32[]{:S(2)}, u32[]{:S(2)}) %collective-permute-start.11) | collective-permute-done | bytes 4128 | tf_op jit(solution)/shard_map/ppermute | solution.py:15
  108.6 4.2 %collective-permute-start.12 = (f32[32,32]{0,1:T(8,128)S(1)}, f32[32,32]{0,1:T(8,128)S(1)}, u32[]{:S(2)}, u32[]{:S(2)}) collective-permute-start(f32[32,32]{0,1:T(8,128)S(1)} %fusion.61), channel_id=1, source_target_pairs={{0,256},{128,384},{256,0},{384,128},{512,768},{640,896},{768,512},... | collective-permute-start | bytes 12296 | tf_op jit(solution)/shard_map/ppermute | solution.py:15
  112.9 2.3 %collective-permute-done.12 = f32[32,32]{0,1:T(8,128)S(1)} collective-permute-done((f32[32,32]{0,1:T(8,128)S(1)}, f32[32,32]{0,1:T(8,128)S(1)}, u32[]{:S(2)}, u32[]{:S(2)}) %collective-permute-start.12) | collective-permute-done | bytes 4128 | tf_op jit(solution)/shard_map/ppermute | solution.py:15
  115.4 5.2 %collective-permute-start.13 = (f32[32,32]{0,1:T(8,128)S(1)}, f32[32,32]{0,1:T(8,128)S(1)}, u32[]{:S(2)}, u32[]{:S(2)}) collective-permute-start(f32[32,32]{0,1:T(8,128)S(1)} %fusion.58), channel_id=1, source_target_pairs={{0,512},{128,640},{256,768},{384,896},{512,0},{640,128},{768,256},... | collective-permute-start | bytes 12296 | tf_op jit(solution)/shard_map/ppermute | solution.py:15
  121.2 3.8 %collective-permute-done.13 = f32[32,32]{0,1:T(8,128)S(1)} collective-permute-done((f32[32,32]{0,1:T(8,128)S(1)}, f32[32,32]{0,1:T(8,128)S(1)}, u32[]{:S(2)}, u32[]{:S(2)}) %collective-permute-start.13) | collective-permute-done | bytes 4128 | tf_op jit(solution)/shard_map/ppermute | solution.py:15
  126.0 1.0 fusion.15
  128.2 5.8 %scatter_custom_fusion = f32[32,2048]{0,1:T(8,128)S(1)} fusion(s32[2048]{0:T(1024)S(1)} %bitcast.228, f32[2048,32]{1,0:T(8,128)S(1)} %copy.192, f32[]{:T(128)} %constant.13.clone.1), kind=kCustom, calls=%fused_computation.25 | custom fusion | bytes 262148 | tf_op jit(solution)/shard_map/scatter | solution.py:177
  134.4 1.0 copy.193
  135.4 1.0 copy.194
  (153 shorter events, 19.0 us)
Async XLA Ops:
  0.6 126.4 %copy-start = (bf16[32,64,32]{1,2,0:T(8,128)(2,1)S(1)}, bf16[32,64,32]{1,2,0:T(8,128)(2,1)}, u32[]{:S(2)}) copy-start(bf16[32,64,32]{1,2,0:T(8,128)(2,1)} %param.20) | copy-start | bytes 393220
  0.6 9.0 %copy-start.17 = (s32[1,2048]{1,0:T(1,128)S(1)}, s32[1,2048]{1,0:T(1,128)}, u32[]{:S(2)}) copy-start(s32[1,2048]{1,0:T(1,128)} %param.18) | copy-start | bytes 24580
  2.4 8.1 %copy-start.7 = (bf16[32,64,32]{1,2,0:T(8,128)(2,1)S(1)}, bf16[32,64,32]{1,2,0:T(8,128)(2,1)}, u32[]{:S(2)}) copy-start(bf16[32,64,32]{1,2,0:T(8,128)(2,1)} %param.19) | copy-start | bytes 393220
  8.9 13.8 %copy-start.1 = (bf16[1,62,32,32]{1,3,2,0:T(8,128)(2,1)S(1)}, bf16[1,62,32,32]{1,3,2,0:T(8,128)(2,1)}, u32[]{:S(2)}) copy-start(bf16[1,62,32,32]{1,3,2,0:T(8,128)(2,1)} %param.27) | copy-start | bytes 380932
  11.5 47.8 %collective-permute-start.3 = (bf16[32,32,32]{1,2,0:T(8,128)(2,1)}, bf16[32,32,32]{1,2,0:T(8,128)(2,1)}, u32[]{:S(2)}, u32[]{:S(2)}) collective-permute-start(bf16[32,32,32]{1,2,0:T(8,128)(2,1)} %convert_bitcast_fusion), channel_id=1, source_target_pairs={{0,1},{1,2},{2,3},{3,4},{4,5},{5,6},{6,7},{7,8},{8,9},{9,10},{10,1... | collective-permute-start | bytes 196616 | tf_op jit(solution)/shard_map/ppermute | solution.py:24
  14.0 45.4 %collective-permute-start.4 = (bf16[32,32,32]{1,2,0:T(8,128)(2,1)}, bf16[32,32,32]{1,2,0:T(8,128)(2,1)}, u32[]{:S(2)}, u32[]{:S(2)}) collective-permute-start(bf16[32,32,32]{1,2,0:T(8,128)(2,1)} %convert_bitcast_fusion), channel_id=1, source_target_pairs={{1,0},{2,1},{3,2},{4,3},{5,4},{6,5},{7,6},{8,7},{9,8},{10,9},{11,1... | collective-permute-start | bytes 196616 | tf_op jit(solution)/shard_map/ppermute | solution.py:25
  15.3 64.8 %collective-permute-start.7 = (bf16[32,32,64]{2,0,1:T(8,128)(2,1)S(1)}, bf16[32,32,64]{2,0,1:T(8,128)(2,1)}, u32[]{:S(2)}, u32[]{:S(2)}) collective-permute-start(bf16[32,32,64]{2,0,1:T(8,128)(2,1)S(1)} %select_convert_fusion), channel_id=1, source_target_pairs={{0,1},{1,2},{2,3},{3,4},{4,5},{5,6},{6,7},{7,8},{8,9},{9,10},{10,1... | collective-permute-start | bytes 393224 | tf_op jit(solution)/shard_map/ppermute | solution.py:24
  21.4 58.7 %collective-permute-start.8 = (bf16[32,32,64]{2,0,1:T(8,128)(2,1)S(1)}, bf16[32,32,64]{2,0,1:T(8,128)(2,1)}, u32[]{:S(2)}, u32[]{:S(2)}) collective-permute-start(bf16[32,32,64]{2,0,1:T(8,128)(2,1)S(1)} %select_convert_fusion), channel_id=1, source_target_pairs={{1,0},{2,1},{3,2},{4,3},{5,4},{6,5},{7,6},{8,7},{9,8},{10,9},{11,1... | collective-permute-start | bytes 393224 | tf_op jit(solution)/shard_map/ppermute | solution.py:25
  24.1 5.5 %copy-start.2 = (bf16[1,62,32,32]{1,3,2,0:T(8,128)(2,1)S(1)}, bf16[1,62,32,32]{1,3,2,0:T(8,128)(2,1)}, u32[]{:S(2)}) copy-start(bf16[1,62,32,32]{1,3,2,0:T(8,128)(2,1)} %param.28) | copy-start | bytes 380932
  26.0 14.2 %collective-permute-start = (f32[32,32]{0,1:T(8,128)S(1)}, f32[32,32]{0,1:T(8,128)S(1)}, u32[]{:S(2)}, u32[]{:S(2)}) collective-permute-start(f32[32,32]{0,1:T(8,128)S(1)} %fusion.91), channel_id=1, source_target_pairs={{0,1},{1,0},{2,3},{3,2},{4,5},{5,4},{6,7},{7,6},{8,9},{9,8},{10,11... | collective-permute-start | bytes 12296 | tf_op jit(solution)/shard_map/ppermute | solution.py:15
  34.4 14.4 %copy-start.3 = (f32[10,32,32]{2,1,0:T(8,128)}, f32[10,32,32]{2,1,0:T(8,128)S(1)}, u32[]{:S(2)}) copy-start(f32[10,32,32]{2,1,0:T(8,128)S(1)} %fusion.28) | copy-start | bytes 122884
  34.4 11.2 %copy-start.6 = (bf16[32,6,1024]{2,0,1:T(8,128)(2,1)S(1)}, bf16[32,6,1024]{2,0,1:T(8,128)(2,1)}, u32[]{:S(2)}) copy-start(bf16[32,6,1024]{2,0,1:T(8,128)(2,1)} %param.24) | copy-start | bytes 1179652
  40.5 8.4 %collective-permute-start.1 = (f32[32,32]{0,1:T(8,128)S(1)}, f32[32,32]{0,1:T(8,128)S(1)}, u32[]{:S(2)}, u32[]{:S(2)}) collective-permute-start(f32[32,32]{0,1:T(8,128)S(1)} %fusion.70), channel_id=1, source_target_pairs={{0,2},{2,0},{4,6},{6,4},{8,10},{10,8},{12,14},{14,12},{1,3},{3,1},... | collective-permute-start | bytes 12296 | tf_op jit(solution)/shard_map/ppermute | solution.py:15
  48.8 12.2 %copy-start.8 = (f32[32,32]{0,1:T(8,128)}, f32[32,32]{0,1:T(8,128)S(1)}, u32[]{:S(2)}) copy-start(f32[32,32]{0,1:T(8,128)S(1)} %collective-permute-done.1) | copy-start | bytes 12292
  49.0 14.1 %collective-permute-start.2 = (f32[32,32]{0,1:T(8,128)S(1)}, f32[32,32]{0,1:T(8,128)S(1)}, u32[]{:S(2)}, u32[]{:S(2)}) collective-permute-start(f32[32,32]{0,1:T(8,128)S(1)} %fusion.73), channel_id=1, source_target_pairs={{0,4},{2,6},{4,0},{6,2},{8,12},{10,14},{12,8},{14,10},{1,5},{3,7},... | collective-permute-start | bytes 12296 | tf_op jit(solution)/shard_map/ppermute | solution.py:15
  63.1 13.2 %copy-start.10 = (f32[32,32]{0,1:T(8,128)}, f32[32,32]{0,1:T(8,128)S(1)}, u32[]{:S(2)}) copy-start(f32[32,32]{0,1:T(8,128)S(1)} %collective-permute-done.2) | copy-start | bytes 12292
  63.3 13.0 %collective-permute-start.5 = (f32[32,32]{0,1:T(8,128)S(1)}, f32[32,32]{0,1:T(8,128)S(1)}, u32[]{:S(2)}, u32[]{:S(2)}) collective-permute-start(f32[32,32]{0,1:T(8,128)S(1)} %fusion.76), channel_id=1, source_target_pairs={{0,8},{2,10},{4,12},{6,14},{8,0},{10,2},{12,4},{14,6},{1,9},{3,11}... | collective-permute-start | bytes 12296 | tf_op jit(solution)/shard_map/ppermute | solution.py:15
  76.5 5.8 %collective-permute-start.6 = (f32[32,32]{0,1:T(8,128)S(1)}, f32[32,32]{0,1:T(8,128)}, u32[]{:S(2)}, u32[]{:S(2)}) collective-permute-start(f32[32,32]{0,1:T(8,128)S(1)} %fusion.79), channel_id=1, source_target_pairs={{0,16},{16,0},{32,48},{48,32},{64,80},{80,64},{96,112},{112,96},{1... | collective-permute-start | bytes 12296 | tf_op jit(solution)/shard_map/ppermute | solution.py:15
  83.2 16.1 %copy-start.4 = (f32[10,32,32]{2,1,0:T(8,128)S(1)}, f32[10,32,32]{2,1,0:T(8,128)}, u32[]{:S(2)}) copy-start(f32[10,32,32]{2,1,0:T(8,128)} %copy-done.3) | copy-start | bytes 122884
  83.2 16.1 %slice-start = ((f32[10,32,32]{2,1,0:T(8,128)}), f32[6,32,32]{2,1,0:T(8,128)S(1)}, s32[]{:S(2)}) async-start(f32[10,32,32]{2,1,0:T(8,128)} %copy-done.3), calls=%async_computation | async-start | bytes 196608 | tf_op jit(solution)/shard_map/slice | solution.py:77
  83.2 9.5 %collective-permute-start.9 = (f32[32,32]{0,1:T(8,128)S(1)}, f32[32,32]{0,1:T(8,128)S(1)}, u32[]{:S(2)}, u32[]{:S(2)}) collective-permute-start(f32[32,32]{0,1:T(8,128)S(1)} %fusion.82), channel_id=1, source_target_pairs={{0,32},{16,48},{32,0},{48,16},{64,96},{80,112},{96,64},{112,80},{1... | collective-permute-start | bytes 12296 | tf_op jit(solution)/shard_map/ppermute | solution.py:15
  92.7 20.2 %copy-start.16 = (f32[2,32,32]{2,1,0:T(8,128)S(1)}, f32[2,32,32]{2,1,0:T(8,128)}, u32[]{:S(2)}) copy-start(f32[2,32,32]{2,1,0:T(8,128)} %param.31) | copy-start | bytes 24580
  92.7 6.6 %copy-start.14 = (f32[32,32]{0,1:T(8,128)}, f32[32,32]{0,1:T(8,128)S(1)}, u32[]{:S(2)}) copy-start(f32[32,32]{0,1:T(8,128)S(1)} %collective-permute-done.9) | copy-start | bytes 12292
  92.9 9.5 %collective-permute-start.10 = (f32[32,32]{0,1:T(8,128)S(1)}, f32[32,32]{0,1:T(8,128)S(1)}, u32[]{:S(2)}, u32[]{:S(2)}) collective-permute-start(f32[32,32]{0,1:T(8,128)S(1)} %fusion.85), channel_id=1, source_target_pairs={{0,64},{16,80},{32,96},{48,112},{64,0},{80,16},{96,32},{112,48},{1... | collective-permute-start | bytes 12296 | tf_op jit(solution)/shard_map/ppermute | solution.py:15
  99.6 25.3 %copy-start.9 = (f32[32,32]{0,1:T(8,128)S(1)}, f32[32,32]{0,1:T(8,128)}, u32[]{:S(2)}) copy-start(f32[32,32]{0,1:T(8,128)} %copy-done.8) | copy-start | bytes 12292
  99.6 25.3 %copy-start.11 = (f32[32,32]{0,1:T(8,128)S(1)}, f32[32,32]{0,1:T(8,128)}, u32[]{:S(2)}) copy-start(f32[32,32]{0,1:T(8,128)} %copy-done.10) | copy-start | bytes 12292
  99.6 25.3 %copy-start.13 = (f32[32,32]{0,1:T(8,128)S(1)}, f32[32,32]{0,1:T(8,128)}, u32[]{:S(2)}) copy-start(f32[32,32]{0,1:T(8,128)} %copy-done.12) | copy-start | bytes 12292
  99.6 25.3 %copy-start.15 = (f32[32,32]{0,1:T(8,128)S(1)}, f32[32,32]{0,1:T(8,128)}, u32[]{:S(2)}) copy-start(f32[32,32]{0,1:T(8,128)} %copy-done.14) | copy-start | bytes 12292
  102.7 23.3 %copy-start.5 = (f32[32,32,32]{2,1,0:T(8,128)S(1)}, f32[32,32,32]{2,1,0:T(8,128)}, u32[]{:S(2)}) copy-start(f32[32,32,32]{2,1,0:T(8,128)} %fusion.12) | copy-start | bytes 393220
  102.7 5.8 %collective-permute-start.11 = (f32[32,32]{0,1:T(8,128)S(1)}, f32[32,32]{0,1:T(8,128)S(1)}, u32[]{:S(2)}, u32[]{:S(2)}) collective-permute-start(f32[32,32]{0,1:T(8,128)S(1)} %fusion.64), channel_id=1, source_target_pairs={{0,128},{128,0},{256,384},{384,256},{512,640},{640,512},{768,896},... | collective-permute-start | bytes 12296 | tf_op jit(solution)/shard_map/ppermute | solution.py:15
  108.6 6.5 %collective-permute-start.12 = (f32[32,32]{0,1:T(8,128)S(1)}, f32[32,32]{0,1:T(8,128)S(1)}, u32[]{:S(2)}, u32[]{:S(2)}) collective-permute-start(f32[32,32]{0,1:T(8,128)S(1)} %fusion.61), channel_id=1, source_target_pairs={{0,256},{128,384},{256,0},{384,128},{512,768},{640,896},{768,512},... | collective-permute-start | bytes 12296 | tf_op jit(solution)/shard_map/ppermute | solution.py:15
  115.4 9.6 %collective-permute-start.13 = (f32[32,32]{0,1:T(8,128)S(1)}, f32[32,32]{0,1:T(8,128)S(1)}, u32[]{:S(2)}, u32[]{:S(2)}) collective-permute-start(f32[32,32]{0,1:T(8,128)S(1)} %fusion.58), channel_id=1, source_target_pairs={{0,512},{128,640},{256,768},{384,896},{512,0},{640,128},{768,256},... | collective-permute-start | bytes 12296 | tf_op jit(solution)/shard_map/ppermute | solution.py:15
  (7 other events, 28.7 us)

commit v8 on v7

--- a/solution.py
+++ b/solution.py
@@ -103,12 +103,10 @@
         columns = vectors.shape[0]
         ordered = jnp.take(vectors, order_row, axis=1).astype(jnp.bfloat16)
         leaf_blocks = ordered.reshape(columns, leaves_dev, leaf_size)
-        x_window = extended(leaf_blocks, SUB_AXES, 1)
         leaf_coeff = jnp.einsum(
             "clp,lpk->lkc", leaf_blocks, col_basis, preferred_element_type=jnp.float32
         )
         leaf_round = leaf_coeff.astype(jnp.bfloat16)
-        coeff_window = extended(leaf_round, SUB_AXES, 0)
         current = leaf_coeff
         offsets = []
         start_at = 0
@@ -137,6 +135,7 @@
             return far_blocks.reshape(leaves_dev, far_blocks.shape[1], rank_width, rank_width)
 
         def far_picked():
+            coeff_window = extended(results["win_in"][1], SUB_AXES, 0)
             return coeff_window[jnp.minimum(far_index, width_all - 1)]
 
         def far_sum():
@@ -145,6 +144,7 @@
             return jnp.einsum("lkab,lkbc->lac", results["far_sq"], scaled, precision=best_precision)
 
         def near_picked():
+            x_window = extended(results["win_in"][0], SUB_AXES, 1)
             return x_window[:, jnp.minimum(near_index, width_all - 1)]
 
         def near_total():
@@ -153,6 +153,7 @@
             return jnp.einsum("lkpq,clkq->clp", results["near_sq"], scaled, precision=best_precision)
 
         stages = [
+            ("win_in", lambda: (leaf_blocks, leaf_round)),
             ("near_sq", near_square),
             ("far_sq", far_square),
             ("far_pick", far_picked),

time: 137 us -> 140 us (1.022)
  local copies, waits for them, and re-layouts: 33.9 us -> 37.4 us
  starting transfers between devices: 65.9 us -> 69.2 us
  other arithmetic: 6.16 us -> 3.11 us
  waiting for transfers between devices: 10.9 us -> 8.87 us
    ppermute x10, starting transfers between devices: 54.8 us -> 61.7 us  [from_partner(): return lax.ppermute(value, axis, pairs)]
    ppermute x2, starting transfers between devices: 8.55 us -> 4.9 us  [extended(): low = lax.ppermute(block, axis, forward)]
    slice x4, local copies, waits for them, and re-layouts: 0.55 us -> 3.45 us  [apply_image(): moved_up = apply_up(col_local[start_at:start_at + node_count], current)]
    ppermute x10, waiting for transfers between devices: 10.8 us -> 8.86 us  [from_partner(): return lax.ppermute(value, axis, pairs)]
    unnamed x60 -> x72, local copies, waits for them, and re-layouts: 5.21 us -> 5.24 us
  transfers between devices with their start and end apart: 14 -> 14, of which waited for: 4 -> 4; matrix products, arithmetic and copies ran while one was open for 25% -> 23% of each run, Pallas kernels for 0% -> 0%
where the time goes in v8:
time: 140 us; the launch traced here: 139 us
  starting transfers between devices  69.2 us (49%)
  local copies, waits for them, and re-layouts  37.4 us (27%)
  matrix products  18.5 us (13%)
  waiting for transfers between devices  8.87 us (6%)
  other arithmetic  3.11 us (2%)
  between operations  1.87 us (1%)
    ppermute x10, starting transfers between devices, from_partner(): return lax.ppermute(value, axis, pairs)  61.7 us
    ppermute x10, waiting for transfers between devices, from_partner(): return lax.ppermute(value, axis, pairs)  8.86 us
    gather x2, local copies, waits for them, and re-layouts, apply_image(): ordered = jnp.take(vectors, order_row, axis=1).astype(jnp.bfloat16)  6.41 us
    scatter x1, local copies, waits for them, and re-layouts, apply_image(): return jnp.zeros_like(image).at[:, order_row].set(image)  5.85 us
    reshape x1, local copies, waits for them, and re-layouts, near_square(): near_blocks.reshape(leaves_dev, near_blocks.shape[1], leaf_size, leaf_size)  5.55 us
    unnamed x72, local copies, waits for them, and re-layouts  5.24 us
    dot_general x1, matrix products, far_sum(): jnp.einsum('lkab,lkbc->lac', results['far_sq'], scaled, precision=best_pr...  4.96 us
    ppermute x2, starting transfers between devices, extended(): low = lax.ppermute(block, axis, forward)  4.9 us
  transfers between devices with their start and end apart: 14, of which 4 were waited for; matrix products, arithmetic and copies ran while one was open for 23% of the time, Pallas kernels for 0%

profile of v8, /device:TPU:14, one launch (start us, length us, event | category | flops | bytes accessed | tf_op | source)
XLA Modules:
  0.0 139.0 jit_solution(1723561091017749366)
XLA Ops:
  0.7 1.1 slice.185
  1.8 1.1 slice.189
  2.9 1.1 slice.193
  4.5 6.2 %gather_fusion = bf16[2048,32]{1,0:T(8,128)(2,1)S(1)} fusion(bf16[32,2048]{0,1:T(8,128)(2,1)S(1)} %copy.159, s32[2048]{0:T(1024)S(1)} %broadcast_clamp_fusion), kind=kCustom, calls=%fused_computation | custom fusion | bytes 270336 | tf_op jit(solution)/shard_map/jit(_take)/gather | solution.py:104
  15.3 1.9 %collective-permute-start = (f32[32,32]{0,1:T(8,128)S(1)}, f32[32,32]{0,1:T(8,128)S(1)}, u32[]{:S(2)}, u32[]{:S(2)}) collective-permute-start(f32[32,32]{0,1:T(8,128)S(1)} %fusion.91), channel_id=1, source_target_pairs={{0,1},{1,0},{2,3},{3,2},{4,5},{5,4},{6,7},{7,6},{8,9},{9,8},{10,11... | collective-permute-start | bytes 12296 | tf_op jit(solution)/shard_map/ppermute | solution.py:15
  23.3 5.2 %collective-permute-start.1 = (f32[32,32]{0,1:T(8,128)S(1)}, f32[32,32]{0,1:T(8,128)S(1)}, u32[]{:S(2)}, u32[]{:S(2)}) collective-permute-start(f32[32,32]{0,1:T(8,128)S(1)} %fusion.67), channel_id=1, source_target_pairs={{0,2},{2,0},{4,6},{6,4},{8,10},{10,8},{12,14},{14,12},{1,3},{3,1},... | collective-permute-start | bytes 12296 | tf_op jit(solution)/shard_map/ppermute | solution.py:15
  28.5 5.6 %reshape.295 = bf16[32,6,64,64]{3,2,0,1:T(8,128)(2,1)} reshape(bf16[32,6,4096]{2,0,1:T(8,128)(2,1)} %param.21) | data formatting | bytes 3145728 | tf_op jit(solution)/shard_map/reshape | solution.py:132
  34.5 7.9 %collective-permute-start.2 = (f32[32,32]{0,1:T(8,128)S(1)}, f32[32,32]{0,1:T(8,128)S(1)}, u32[]{:S(2)}, u32[]{:S(2)}) collective-permute-start(f32[32,32]{0,1:T(8,128)S(1)} %fusion.70), channel_id=1, source_target_pairs={{0,4},{2,6},{4,0},{6,2},{8,12},{10,14},{12,8},{14,10},{1,5},{3,7},... | collective-permute-start | bytes 12296 | tf_op jit(solution)/shard_map/ppermute | solution.py:15
  42.4 2.4 %reshape.296 = bf16[32,6,32,32]{3,2,0,1:T(8,128)(2,1)} reshape(bf16[32,6,1024]{2,0,1:T(8,128)(2,1)S(1)} %copy-done.5) | data formatting | bytes 786432 | tf_op jit(solution)/shard_map/reshape | solution.py:135
  46.2 1.9 %collective-permute-start.4 = (bf16[32,32,32]{1,2,0:T(8,128)(2,1)S(1)}, bf16[32,32,32]{1,2,0:T(8,128)(2,1)S(1)}, u32[]{:S(2)}, u32[]{:S(2)}) collective-permute-start(bf16[32,32,32]{1,2,0:T(8,128)(2,1)S(1)} %convert_bitcast_fusion), channel_id=1, source_target_pairs={{0,1},{1,2},{2,3},{3,4},{4,5},{5,6},{6,7},{7,8},{8,9},{9,10},{10,1... | collective-permute-start | bytes 196616 | tf_op jit(solution)/shard_map/ppermute | solution.py:24
  48.1 1.3 collective-permute-start.5
  49.4 3.0 %collective-permute-start.8 = (bf16[32,32,64]{2,0,1:T(8,128)(2,1)S(1)}, bf16[32,32,64]{2,0,1:T(8,128)(2,1)S(1)}, u32[]{:S(2)}, u32[]{:S(2)}) collective-permute-start(bf16[32,32,64]{2,0,1:T(8,128)(2,1)S(1)} %select_convert_fusion), channel_id=1, source_target_pairs={{0,1},{1,2},{2,3},{3,4},{4,5},{5,6},{6,7},{7,8},{8,9},{9,10},{10,1... | collective-permute-start | bytes 393224 | tf_op jit(solution)/shard_map/ppermute | solution.py:24
  52.4 1.3 collective-permute-start.9
  54.0 17.9 %collective-permute-start.3 = (f32[32,32]{0,1:T(8,128)S(1)}, f32[32,32]{0,1:T(8,128)}, u32[]{:S(2)}, u32[]{:S(2)}) collective-permute-start(f32[32,32]{0,1:T(8,128)S(1)} %fusion.73), channel_id=1, source_target_pairs={{0,8},{2,10},{4,12},{6,14},{8,0},{10,2},{12,4},{14,6},{1,9},{3,11}... | collective-permute-start | bytes 12296 | tf_op jit(solution)/shard_map/ppermute | solution.py:15
  71.9 1.1 pad_maximum_fusion
  73.4 2.0 %gather_fusion.1 = bf16[192,32,32]{2,1,0:T(8,128)(2,1)} fusion(bf16[96,32,32]{2,1,0:T(8,128)(2,1)S(1)} %copy.175, s32[1024]{0:T(1024)S(1)} %pad_clamp_fusion.1), kind=kCustom, calls=%fused_computation.1 | custom fusion | bytes 787200 | tf_op jit(solution)/shard_map/gather | solution.py:139
  75.5 0.9 fusion.76
  76.4 3.8 %collective-permute-start.6 = (f32[32,32]{0,1:T(8,128)S(1)}, f32[32,32]{0,1:T(8,128)S(1)}, u32[]{:S(2)}, u32[]{:S(2)}) collective-permute-start(f32[32,32]{0,1:T(8,128)S(1)} %fusion.76), channel_id=1, source_target_pairs={{0,16},{16,0},{32,48},{48,32},{64,80},{80,64},{96,112},{112,96},{1... | collective-permute-start | bytes 12296 | tf_op jit(solution)/shard_map/ppermute | solution.py:15
  80.2 5.0 %fusion.12 = f32[32,32,32]{2,1,0:T(8,128)} fusion(bf16[32,6,32,32]{3,2,0,1:T(8,128)(2,1)} %reshape.296, bf16[32,6,32,32]{3,2,1,0:T(8,128)(2,1)} %bitcast.217, f32[32,6]{1,0:T(8,128)S(1)} %copy-done.23), kind=kOutput, calls=%fused_computation.16 | convolution fusion | flops 75890688 | bytes 918272 | tf_op jit(solution)/shard_map/lkab,lkbc->lac/dot_general | solution.py:144
  85.4 4.7 %collective-permute-start.7 = (f32[32,32]{0,1:T(8,128)S(1)}, f32[32,32]{0,1:T(8,128)}, u32[]{:S(2)}, u32[]{:S(2)}) collective-permute-start(f32[32,32]{0,1:T(8,128)S(1)} %fusion.79), channel_id=1, source_target_pairs={{0,32},{16,48},{32,0},{48,16},{64,96},{80,112},{96,64},{112,80},{1... | collective-permute-start | bytes 12296 | tf_op jit(solution)/shard_map/ppermute | solution.py:15
  93.0 7.4 %collective-permute-start.10 = (f32[32,32]{0,1:T(8,128)S(1)}, f32[32,32]{0,1:T(8,128)S(1)}, u32[]{:S(2)}, u32[]{:S(2)}) collective-permute-start(f32[32,32]{0,1:T(8,128)S(1)} %fusion.82), channel_id=1, source_target_pairs={{0,64},{16,80},{32,96},{48,112},{64,0},{80,16},{96,32},{112,48},{1... | collective-permute-start | bytes 12296 | tf_op jit(solution)/shard_map/ppermute | solution.py:15
  100.4 4.6 %fusion.7 = f32[32,32,64]{2,0,1:T(8,128)S(1)} fusion(bf16[32,6,64,64]{3,2,0,1:T(8,128)(2,1)} %reshape.295, bf16[32,32,6,64]{3,0,2,1:T(8,128)(2,1)S(1)} %bitcast.215, f32[32,6]{1,0:T(8,128)} %copy.179), kind=kOutput, calls=%fused_computation.12 | convolution fusion | flops 302776320 | bytes 2622208 | tf_op jit(solution)/shard_map/lkpq,clkq->clp/dot_general | solution.py:153
  105.3 3.5 %collective-permute-start.11 = (f32[32,32]{0,1:T(8,128)S(1)}, f32[32,32]{0,1:T(8,128)S(1)}, u32[]{:S(2)}, u32[]{:S(2)}) collective-permute-start(f32[32,32]{0,1:T(8,128)S(1)} %fusion.85), channel_id=1, source_target_pairs={{0,128},{128,0},{256,384},{384,256},{512,640},{640,512},{768,896},... | collective-permute-start | bytes 12296 | tf_op jit(solution)/shard_map/ppermute | solution.py:15
  109.1 2.0 %collective-permute-done.11 = f32[32,32]{0,1:T(8,128)S(1)} collective-permute-done((f32[32,32]{0,1:T(8,128)S(1)}, f32[32,32]{0,1:T(8,128)S(1)}, u32[]{:S(2)}, u32[]{:S(2)}) %collective-permute-start.11) | collective-permute-done | bytes 4128 | tf_op jit(solution)/shard_map/ppermute | solution.py:15
  111.2 4.2 %collective-permute-start.12 = (f32[32,32]{0,1:T(8,128)S(1)}, f32[32,32]{0,1:T(8,128)S(1)}, u32[]{:S(2)}, u32[]{:S(2)}) collective-permute-start(f32[32,32]{0,1:T(8,128)S(1)} %fusion.61), channel_id=1, source_target_pairs={{0,256},{128,384},{256,0},{384,128},{512,768},{640,896},{768,512},... | collective-permute-start | bytes 12296 | tf_op jit(solution)/shard_map/ppermute | solution.py:15
  115.5 2.3 %collective-permute-done.12 = f32[32,32]{0,1:T(8,128)S(1)} collective-permute-done((f32[32,32]{0,1:T(8,128)S(1)}, f32[32,32]{0,1:T(8,128)S(1)}, u32[]{:S(2)}, u32[]{:S(2)}) %collective-permute-start.12) | collective-permute-done | bytes 4128 | tf_op jit(solution)/shard_map/ppermute | solution.py:15
  118.0 5.2 %collective-permute-start.13 = (f32[32,32]{0,1:T(8,128)S(1)}, f32[32,32]{0,1:T(8,128)S(1)}, u32[]{:S(2)}, u32[]{:S(2)}) collective-permute-start(f32[32,32]{0,1:T(8,128)S(1)} %fusion.58), channel_id=1, source_target_pairs={{0,512},{128,640},{256,768},{384,896},{512,0},{640,128},{768,256},... | collective-permute-start | bytes 12296 | tf_op jit(solution)/shard_map/ppermute | solution.py:15
  123.8 3.7 %collective-permute-done.13 = f32[32,32]{0,1:T(8,128)S(1)} collective-permute-done((f32[32,32]{0,1:T(8,128)S(1)}, f32[32,32]{0,1:T(8,128)S(1)}, u32[]{:S(2)}, u32[]{:S(2)}) %collective-permute-start.13) | collective-permute-done | bytes 4128 | tf_op jit(solution)/shard_map/ppermute | solution.py:15
  128.6 1.0 fusion.15
  130.8 5.8 %scatter_custom_fusion = f32[32,2048]{0,1:T(8,128)S(1)} fusion(s32[2048]{0:T(1024)S(1)} %bitcast.228, f32[2048,32]{1,0:T(8,128)S(1)} %copy.192, f32[]{:T(128)} %constant.13.clone.1), kind=kCustom, calls=%fused_computation.25 | custom fusion | bytes 262148 | tf_op jit(solution)/shard_map/scatter | solution.py:178
  137.0 1.0 copy.193
  138.0 1.0 copy.194
  (165 shorter events, 20.0 us)
Async XLA Ops:
  0.6 129.0 %copy-start = (bf16[32,64,32]{1,2,0:T(8,128)(2,1)S(1)}, bf16[32,64,32]{1,2,0:T(8,128)(2,1)}, u32[]{:S(2)}) copy-start(bf16[32,64,32]{1,2,0:T(8,128)(2,1)} %param.20) | copy-start | bytes 393220
  15.3 7.8 %collective-permute-start = (f32[32,32]{0,1:T(8,128)S(1)}, f32[32,32]{0,1:T(8,128)S(1)}, u32[]{:S(2)}, u32[]{:S(2)}) collective-permute-start(f32[32,32]{0,1:T(8,128)S(1)} %fusion.91), channel_id=1, source_target_pairs={{0,1},{1,0},{2,3},{3,2},{4,5},{5,4},{6,7},{7,6},{8,9},{9,8},{10,11... | collective-permute-start | bytes 12296 | tf_op jit(solution)/shard_map/ppermute | solution.py:15
  17.3 30.8 %copy-start.3 = (bf16[32,32,32]{1,2,0:T(8,128)(2,1)}, bf16[32,32,32]{1,2,0:T(8,128)(2,1)S(1)}, u32[]{:S(2)}) copy-start(bf16[32,32,32]{1,2,0:T(8,128)(2,1)S(1)} %convert_bitcast_fusion) | copy-start | bytes 196612
  22.9 23.3 %copy-start.7 = (f32[10,32,32]{2,1,0:T(8,128)}, f32[10,32,32]{2,1,0:T(8,128)S(1)}, u32[]{:S(2)}) copy-start(f32[10,32,32]{2,1,0:T(8,128)S(1)} %fusion.32) | copy-start | bytes 122884
  23.3 11.0 %collective-permute-start.1 = (f32[32,32]{0,1:T(8,128)S(1)}, f32[32,32]{0,1:T(8,128)S(1)}, u32[]{:S(2)}, u32[]{:S(2)}) collective-permute-start(f32[32,32]{0,1:T(8,128)S(1)} %fusion.67), channel_id=1, source_target_pairs={{0,2},{2,0},{4,6},{6,4},{8,10},{10,8},{12,14},{14,12},{1,3},{3,1},... | collective-permute-start | bytes 12296 | tf_op jit(solution)/shard_map/ppermute | solution.py:15
  28.5 13.9 %copy-start.5 = (bf16[32,6,1024]{2,0,1:T(8,128)(2,1)S(1)}, bf16[32,6,1024]{2,0,1:T(8,128)(2,1)}, u32[]{:S(2)}) copy-start(bf16[32,6,1024]{2,0,1:T(8,128)(2,1)} %param.24) | copy-start | bytes 1179652
  34.1 10.7 %copy-start.22 = (f32[32,6]{0,1:T(8,128)S(1)}, f32[32,6]{0,1:T(8,128)}, u32[]{:S(2)}) copy-start(f32[32,6]{0,1:T(8,128)} %compare_select_fusion.5) | copy-start | bytes 2308
  34.3 19.4 %copy-start.11 = (f32[32,32]{0,1:T(8,128)}, f32[32,32]{0,1:T(8,128)S(1)}, u32[]{:S(2)}) copy-start(f32[32,32]{0,1:T(8,128)S(1)} %collective-permute-done.1) | copy-start | bytes 12292
  34.5 19.2 %collective-permute-start.2 = (f32[32,32]{0,1:T(8,128)S(1)}, f32[32,32]{0,1:T(8,128)S(1)}, u32[]{:S(2)}, u32[]{:S(2)}) collective-permute-start(f32[32,32]{0,1:T(8,128)S(1)} %fusion.70), channel_id=1, source_target_pairs={{0,4},{2,6},{4,0},{6,2},{8,12},{10,14},{12,8},{14,10},{1,5},{3,7},... | collective-permute-start | bytes 12296 | tf_op jit(solution)/shard_map/ppermute | solution.py:15
  46.2 25.7 %collective-permute-start.4 = (bf16[32,32,32]{1,2,0:T(8,128)(2,1)S(1)}, bf16[32,32,32]{1,2,0:T(8,128)(2,1)S(1)}, u32[]{:S(2)}, u32[]{:S(2)}) collective-permute-start(bf16[32,32,32]{1,2,0:T(8,128)(2,1)S(1)} %convert_bitcast_fusion), channel_id=1, source_target_pairs={{0,1},{1,2},{2,3},{3,4},{4,5},{5,6},{6,7},{7,8},{8,9},{9,10},{10,1... | collective-permute-start | bytes 196616 | tf_op jit(solution)/shard_map/ppermute | solution.py:24
  48.1 23.9 %collective-permute-start.5 = (bf16[32,32,32]{1,2,0:T(8,128)(2,1)S(1)}, bf16[32,32,32]{1,2,0:T(8,128)(2,1)S(1)}, u32[]{:S(2)}, u32[]{:S(2)}) collective-permute-start(bf16[32,32,32]{1,2,0:T(8,128)(2,1)S(1)} %convert_bitcast_fusion), channel_id=1, source_target_pairs={{1,0},{2,1},{3,2},{4,3},{5,4},{6,5},{7,6},{8,7},{9,8},{10,9},{11,1... | collective-permute-start | bytes 196616 | tf_op jit(solution)/shard_map/ppermute | solution.py:25
  49.4 40.7 %collective-permute-start.8 = (bf16[32,32,64]{2,0,1:T(8,128)(2,1)S(1)}, bf16[32,32,64]{2,0,1:T(8,128)(2,1)S(1)}, u32[]{:S(2)}, u32[]{:S(2)}) collective-permute-start(bf16[32,32,64]{2,0,1:T(8,128)(2,1)S(1)} %select_convert_fusion), channel_id=1, source_target_pairs={{0,1},{1,2},{2,3},{3,4},{4,5},{5,6},{6,7},{7,8},{8,9},{9,10},{10,1... | collective-permute-start | bytes 393224 | tf_op jit(solution)/shard_map/ppermute | solution.py:24
  52.4 37.7 %collective-permute-start.9 = (bf16[32,32,64]{2,0,1:T(8,128)(2,1)S(1)}, bf16[32,32,64]{2,0,1:T(8,128)(2,1)S(1)}, u32[]{:S(2)}, u32[]{:S(2)}) collective-permute-start(bf16[32,32,64]{2,0,1:T(8,128)(2,1)S(1)} %select_convert_fusion), channel_id=1, source_target_pairs={{1,0},{2,1},{3,2},{4,3},{5,4},{6,5},{7,6},{8,7},{9,8},{10,9},{11,1... | collective-permute-start | bytes 393224 | tf_op jit(solution)/shard_map/ppermute | solution.py:25
  53.7 18.2 %copy-start.13 = (f32[32,32]{0,1:T(8,128)}, f32[32,32]{0,1:T(8,128)S(1)}, u32[]{:S(2)}) copy-start(f32[32,32]{0,1:T(8,128)S(1)} %collective-permute-done.2) | copy-start | bytes 12292
  54.0 21.5 %collective-permute-start.3 = (f32[32,32]{0,1:T(8,128)S(1)}, f32[32,32]{0,1:T(8,128)}, u32[]{:S(2)}, u32[]{:S(2)}) collective-permute-start(f32[32,32]{0,1:T(8,128)S(1)} %fusion.73), channel_id=1, source_target_pairs={{0,8},{2,10},{4,12},{6,14},{8,0},{10,2},{12,4},{14,6},{1,9},{3,11}... | collective-permute-start | bytes 12296 | tf_op jit(solution)/shard_map/ppermute | solution.py:15
  73.4 6.8 %copy-start.23 = (f32[32,6]{1,0:T(8,128)S(1)}, f32[32,6]{1,0:T(8,128)}, u32[]{:S(2)}) copy-start(f32[32,6]{1,0:T(8,128)} %copy.176) | copy-start | bytes 2308
  76.4 8.7 %collective-permute-start.6 = (f32[32,32]{0,1:T(8,128)S(1)}, f32[32,32]{0,1:T(8,128)S(1)}, u32[]{:S(2)}, u32[]{:S(2)}) collective-permute-start(f32[32,32]{0,1:T(8,128)S(1)} %fusion.76), channel_id=1, source_target_pairs={{0,16},{16,0},{32,48},{48,32},{64,80},{80,64},{96,112},{112,96},{1... | collective-permute-start | bytes 12296 | tf_op jit(solution)/shard_map/ppermute | solution.py:15
  85.2 5.0 %copy-start.15 = (f32[32,32]{0,1:T(8,128)}, f32[32,32]{0,1:T(8,128)S(1)}, u32[]{:S(2)}) copy-start(f32[32,32]{0,1:T(8,128)S(1)} %collective-permute-done.6) | copy-start | bytes 12292
  85.4 6.6 %collective-permute-start.7 = (f32[32,32]{0,1:T(8,128)S(1)}, f32[32,32]{0,1:T(8,128)}, u32[]{:S(2)}, u32[]{:S(2)}) collective-permute-start(f32[32,32]{0,1:T(8,128)S(1)} %fusion.79), channel_id=1, source_target_pairs={{0,32},{16,48},{32,0},{48,16},{64,96},{80,112},{96,64},{112,80},{1... | collective-permute-start | bytes 12296 | tf_op jit(solution)/shard_map/ppermute | solution.py:15
  92.9 15.8 %copy-start.8 = (f32[10,32,32]{2,1,0:T(8,128)S(1)}, f32[10,32,32]{2,1,0:T(8,128)}, u32[]{:S(2)}) copy-start(f32[10,32,32]{2,1,0:T(8,128)} %copy-done.7) | copy-start | bytes 122884
  92.9 15.8 %slice-start = ((f32[10,32,32]{2,1,0:T(8,128)}), f32[2,32,32]{2,1,0:T(8,128)S(1)}, s32[]{:S(2)}) async-start(f32[10,32,32]{2,1,0:T(8,128)} %copy-done.7), calls=%async_computation | async-start | bytes 65536 | tf_op jit(solution)/shard_map/slice | solution.py:77
  93.0 22.5 %copy-start.18 = (f32[2,32,32]{2,1,0:T(8,128)S(1)}, f32[2,32,32]{2,1,0:T(8,128)}, u32[]{:S(2)}) copy-start(f32[2,32,32]{2,1,0:T(8,128)} %param.31) | copy-start | bytes 24580
  93.0 12.1 %collective-permute-start.10 = (f32[32,32]{0,1:T(8,128)S(1)}, f32[32,32]{0,1:T(8,128)S(1)}, u32[]{:S(2)}, u32[]{:S(2)}) collective-permute-start(f32[32,32]{0,1:T(8,128)S(1)} %fusion.82), channel_id=1, source_target_pairs={{0,64},{16,80},{32,96},{48,112},{64,0},{80,16},{96,32},{112,48},{1... | collective-permute-start | bytes 12296 | tf_op jit(solution)/shard_map/ppermute | solution.py:15
  105.0 18.2 %copy-start.27 = (pred[10]{0:T(512)(128)(4,1)S(1)}, pred[10]{0:T(512)(128)(4,1)}, u32[]{:S(2)}) copy-start(pred[10]{0:T(512)(128)(4,1)} %copy-done.26) | copy-start | bytes 34
  105.0 22.6 %copy-start.12 = (f32[32,32]{0,1:T(8,128)S(1)}, f32[32,32]{0,1:T(8,128)}, u32[]{:S(2)}) copy-start(f32[32,32]{0,1:T(8,128)} %copy-done.11) | copy-start | bytes 12292
  105.0 22.5 %copy-start.14 = (f32[32,32]{0,1:T(8,128)S(1)}, f32[32,32]{0,1:T(8,128)}, u32[]{:S(2)}) copy-start(f32[32,32]{0,1:T(8,128)} %copy-done.13) | copy-start | bytes 12292
  105.0 22.5 %copy-start.16 = (f32[32,32]{0,1:T(8,128)S(1)}, f32[32,32]{0,1:T(8,128)}, u32[]{:S(2)}) copy-start(f32[32,32]{0,1:T(8,128)} %copy-done.15) | copy-start | bytes 12292
  105.0 18.1 %copy-start.17 = (f32[32,32]{0,1:T(8,128)}, f32[32,32]{0,1:T(8,128)S(1)}, u32[]{:S(2)}) copy-start(f32[32,32]{0,1:T(8,128)S(1)} %collective-permute-done.10) | copy-start | bytes 12292
  105.3 23.4 %copy-start.4 = (f32[32,32,32]{2,1,0:T(8,128)S(1)}, f32[32,32,32]{2,1,0:T(8,128)}, u32[]{:S(2)}) copy-start(f32[32,32,32]{2,1,0:T(8,128)} %fusion.12) | copy-start | bytes 393220
  105.3 5.8 %collective-permute-start.11 = (f32[32,32]{0,1:T(8,128)S(1)}, f32[32,32]{0,1:T(8,128)S(1)}, u32[]{:S(2)}, u32[]{:S(2)}) collective-permute-start(f32[32,32]{0,1:T(8,128)S(1)} %fusion.85), channel_id=1, source_target_pairs={{0,128},{128,0},{256,384},{384,256},{512,640},{640,512},{768,896},... | collective-permute-start | bytes 12296 | tf_op jit(solution)/shard_map/ppermute | solution.py:15
  111.2 6.6 %collective-permute-start.12 = (f32[32,32]{0,1:T(8,128)S(1)}, f32[32,32]{0,1:T(8,128)S(1)}, u32[]{:S(2)}, u32[]{:S(2)}) collective-permute-start(f32[32,32]{0,1:T(8,128)S(1)} %fusion.61), channel_id=1, source_target_pairs={{0,256},{128,384},{256,0},{384,128},{512,768},{640,896},{768,512},... | collective-permute-start | bytes 12296 | tf_op jit(solution)/shard_map/ppermute | solution.py:15
  118.0 9.5 %collective-permute-start.13 = (f32[32,32]{0,1:T(8,128)S(1)}, f32[32,32]{0,1:T(8,128)S(1)}, u32[]{:S(2)}, u32[]{:S(2)}) collective-permute-start(f32[32,32]{0,1:T(8,128)S(1)} %fusion.58), channel_id=1, source_target_pairs={{0,512},{128,640},{256,768},{384,896},{512,0},{640,128},{768,256},... | collective-permute-start | bytes 12296 | tf_op jit(solution)/shard_map/ppermute | solution.py:15
  (13 other events, 33.1 us)

commit v9 on v8

--- a/solution.py
+++ b/solution.py
@@ -153,14 +153,15 @@
             return jnp.einsum("lkpq,clkq->clp", results["near_sq"], scaled, precision=best_precision)
 
         stages = [
-            ("win_in", lambda: (leaf_blocks, leaf_round)),
             ("near_sq", near_square),
             ("far_sq", far_square),
+            ("paths", leaf_paths),
+            ("win_in", lambda: (leaf_blocks, leaf_round)),
+            ("spare", lambda: jnp.zeros((), jnp.float32)),
             ("far_pick", far_picked),
             ("far_sum", far_sum),
             ("near_pick", near_picked),
             ("near_sum", near_total),
-            ("paths", leaf_paths),
         ]
         root_field = climb_tree(current[0], stages, results)
         for key, stage in stages:

time: 140 us -> 135 us (0.964)
  starting transfers between devices: 69.2 us -> 62.8 us
    ppermute x10, starting transfers between devices: 61.7 us -> 52.9 us  [from_partner(): return lax.ppermute(value, axis, pairs)]
    ppermute x2, starting transfers between devices: 4.9 us -> 7.26 us  [extended(): low = lax.ppermute(block, axis, forward)]
    unnamed x72 -> x66, local copies, waits for them, and re-layouts: 5.24 us -> 5.22 us
where the time goes in v9:
time: 135 us; the launch traced here: 133 us
  starting transfers between devices  62.8 us (47%)
  local copies, waits for them, and re-layouts  37.5 us (28%)
  matrix products  19.9 us (15%)
  waiting for transfers between devices  9.01 us (7%)
  other arithmetic  2.52 us (2%)
  between operations  1.77 us (1%)
    ppermute x10, starting transfers between devices, from_partner(): return lax.ppermute(value, axis, pairs)  52.9 us
    ppermute x10, waiting for transfers between devices, from_partner(): return lax.ppermute(value, axis, pairs)  9 us
    ppermute x2, starting transfers between devices, extended(): low = lax.ppermute(block, axis, forward)  7.26 us
    gather x2, local copies, waits for them, and re-layouts, apply_image(): ordered = jnp.take(vectors, order_row, axis=1).astype(jnp.bfloat16)  6.41 us
    scatter x1, local copies, waits for them, and re-layouts, apply_image(): return jnp.zeros_like(image).at[:, order_row].set(image)  5.85 us
    reshape x1, local copies, waits for them, and re-layouts, near_square(): near_blocks.reshape(leaves_dev, near_blocks.shape[1], leaf_size, leaf_size)  5.56 us
    unnamed x66, local copies, waits for them, and re-layouts  5.22 us
    dot_general x14, matrix products, apply_up(): jnp.einsum('...ab,...ac->...bc', matrix, coeffs, precision=best_precision)  5.1 us
  transfers between devices with their start and end apart: 14, of which 4 were waited for; matrix products, arithmetic and copies ran while one was open for 23% of the time, Pallas kernels for 0%

profile of v9, /device:TPU:14, one launch (start us, length us, event | category | flops | bytes accessed | tf_op | source)
XLA Modules:
  0.0 133.4 jit_solution(17956330699458382319)
XLA Ops:
  0.7 1.1 slice.180
  1.8 1.1 slice.184
  2.9 1.1 slice.188
  4.5 6.2 %gather_fusion = bf16[2048,32]{1,0:T(8,128)(2,1)S(1)} fusion(bf16[32,2048]{0,1:T(8,128)(2,1)S(1)} %copy.159, s32[2048]{0:T(1024)S(1)} %broadcast_clamp_fusion), kind=kCustom, calls=%fused_computation | custom fusion | bytes 270336 | tf_op jit(solution)/shard_map/jit(_take)/gather | solution.py:104
  15.3 1.9 %collective-permute-start = (f32[32,32]{0,1:T(8,128)S(1)}, f32[32,32]{0,1:T(8,128)}, u32[]{:S(2)}, u32[]{:S(2)}) collective-permute-start(f32[32,32]{0,1:T(8,128)S(1)} %fusion.91), channel_id=1, source_target_pairs={{0,1},{1,0},{2,3},{3,2},{4,5},{5,4},{6,7},{7,6},{8,9},{9,8},{10,11... | collective-permute-start | bytes 12296 | tf_op jit(solution)/shard_map/ppermute | solution.py:15
  23.2 5.6 %reshape.295 = bf16[32,6,64,64]{3,2,0,1:T(8,128)(2,1)} reshape(bf16[32,6,4096]{2,0,1:T(8,128)(2,1)} %param.21) | data formatting | bytes 3145728 | tf_op jit(solution)/shard_map/reshape | solution.py:132
  29.7 5.2 %collective-permute-start.1 = (f32[32,32]{0,1:T(8,128)S(1)}, f32[32,32]{0,1:T(8,128)S(1)}, u32[]{:S(2)}, u32[]{:S(2)}) collective-permute-start(f32[32,32]{0,1:T(8,128)S(1)} %fusion.82), channel_id=1, source_target_pairs={{0,2},{2,0},{4,6},{6,4},{8,10},{10,8},{12,14},{14,12},{1,3},{3,1},... | collective-permute-start | bytes 12296 | tf_op jit(solution)/shard_map/ppermute | solution.py:15
  34.9 2.4 %reshape.296 = bf16[32,6,32,32]{3,2,0,1:T(8,128)(2,1)} reshape(bf16[32,6,1024]{2,0,1:T(8,128)(2,1)S(1)} %copy-done.4) | data formatting | bytes 786432 | tf_op jit(solution)/shard_map/reshape | solution.py:135
  37.5 7.9 %collective-permute-start.2 = (f32[32,32]{0,1:T(8,128)S(1)}, f32[32,32]{0,1:T(8,128)S(1)}, u32[]{:S(2)}, u32[]{:S(2)}) collective-permute-start(f32[32,32]{0,1:T(8,128)S(1)} %fusion.85), channel_id=1, source_target_pairs={{0,4},{2,6},{4,0},{6,2},{8,12},{10,14},{12,8},{14,10},{1,5},{3,7},... | collective-permute-start | bytes 12296 | tf_op jit(solution)/shard_map/ppermute | solution.py:15
  45.6 1.5 %collective-permute-done.2 = f32[32,32]{0,1:T(8,128)S(1)} collective-permute-done((f32[32,32]{0,1:T(8,128)S(1)}, f32[32,32]{0,1:T(8,128)S(1)}, u32[]{:S(2)}, u32[]{:S(2)}) %collective-permute-start.2) | collective-permute-done | bytes 4128 | tf_op jit(solution)/shard_map/ppermute | solution.py:15
  47.3 11.9 %collective-permute-start.3 = (f32[32,32]{0,1:T(8,128)S(1)}, f32[32,32]{0,1:T(8,128)S(1)}, u32[]{:S(2)}, u32[]{:S(2)}) collective-permute-start(f32[32,32]{0,1:T(8,128)S(1)} %fusion.76), channel_id=1, source_target_pairs={{0,8},{2,10},{4,12},{6,14},{8,0},{10,2},{12,4},{14,6},{1,9},{3,11}... | collective-permute-start | bytes 12296 | tf_op jit(solution)/shard_map/ppermute | solution.py:15
  59.4 1.5 %collective-permute-done.3 = f32[32,32]{0,1:T(8,128)S(1)} collective-permute-done((f32[32,32]{0,1:T(8,128)S(1)}, f32[32,32]{0,1:T(8,128)S(1)}, u32[]{:S(2)}, u32[]{:S(2)}) %collective-permute-start.3) | collective-permute-done | bytes 4128 | tf_op jit(solution)/shard_map/ppermute | solution.py:15
  61.1 3.6 %collective-permute-start.4 = (f32[32,32]{0,1:T(8,128)S(1)}, f32[32,32]{0,1:T(8,128)S(1)}, u32[]{:S(2)}, u32[]{:S(2)}) collective-permute-start(f32[32,32]{0,1:T(8,128)S(1)} %fusion.73), channel_id=1, source_target_pairs={{0,16},{16,0},{32,48},{48,32},{64,80},{80,64},{96,112},{112,96},{1... | collective-permute-start | bytes 12296 | tf_op jit(solution)/shard_map/ppermute | solution.py:15
  66.1 1.3 collective-permute-start.7
  67.4 3.0 %collective-permute-start.6 = (bf16[32,32,32]{1,2,0:T(8,128)(2,1)S(1)}, bf16[32,32,32]{1,2,0:T(8,128)(2,1)S(1)}, u32[]{:S(2)}, u32[]{:S(2)}) collective-permute-start(bf16[32,32,32]{1,2,0:T(8,128)(2,1)S(1)} %convert_bitcast_fusion), channel_id=1, source_target_pairs={{0,1},{1,2},{2,3},{3,4},{4,5},{5,6},{6,7},{7,8},{8,9},{9,10},{10,1... | collective-permute-start | bytes 196616 | tf_op jit(solution)/shard_map/ppermute | solution.py:24
  70.5 1.3 collective-permute-start.11
  71.8 4.2 %collective-permute-start.10 = (bf16[32,32,64]{2,0,1:T(8,128)(2,1)S(1)}, bf16[32,32,64]{2,0,1:T(8,128)(2,1)}, u32[]{:S(2)}, u32[]{:S(2)}) collective-permute-start(bf16[32,32,64]{2,0,1:T(8,128)(2,1)S(1)} %select_convert_fusion), channel_id=1, source_target_pairs={{0,1},{1,2},{2,3},{3,4},{4,5},{5,6},{6,7},{7,8},{8,9},{9,10},{10,1... | collective-permute-start | bytes 393224 | tf_op jit(solution)/shard_map/ppermute | solution.py:24
  76.2 4.7 %collective-permute-start.5 = (f32[32,32]{0,1:T(8,128)S(1)}, f32[32,32]{0,1:T(8,128)}, u32[]{:S(2)}, u32[]{:S(2)}) collective-permute-start(f32[32,32]{0,1:T(8,128)S(1)} %fusion.70), channel_id=1, source_target_pairs={{0,32},{16,48},{32,0},{48,16},{64,96},{80,112},{96,64},{112,80},{1... | collective-permute-start | bytes 12296 | tf_op jit(solution)/shard_map/ppermute | solution.py:15
  81.5 2.1 %gather_fusion.1 = bf16[192,32,32]{2,1,0:T(8,128)(2,1)} fusion(bf16[96,32,32]{2,1,0:T(8,128)(2,1)S(1)} %copy.182, s32[1024]{0:T(1024)S(1)} %pad_clamp_fusion.1), kind=kCustom, calls=%fused_computation.1 | custom fusion | bytes 787200 | tf_op jit(solution)/shard_map/gather | solution.py:139
  84.5 6.8 %collective-permute-start.8 = (f32[32,32]{0,1:T(8,128)S(1)}, f32[32,32]{0,1:T(8,128)S(1)}, u32[]{:S(2)}, u32[]{:S(2)}) collective-permute-start(f32[32,32]{0,1:T(8,128)S(1)} %fusion.67), channel_id=1, source_target_pairs={{0,64},{16,80},{32,96},{48,112},{64,0},{80,16},{96,32},{112,48},{1... | collective-permute-start | bytes 12296 | tf_op jit(solution)/shard_map/ppermute | solution.py:15
  91.3 5.0 %fusion.12 = f32[32,32,32]{2,1,0:T(8,128)} fusion(bf16[32,6,32,32]{3,2,0,1:T(8,128)(2,1)} %reshape.296, bf16[32,6,32,32]{3,2,1,0:T(8,128)(2,1)} %bitcast.217, f32[32,6]{1,0:T(8,128)S(1)} %copy-done.20), kind=kOutput, calls=%fused_computation.16 | convolution fusion | flops 75890688 | bytes 918272 | tf_op jit(solution)/shard_map/lkab,lkbc->lac/dot_general | solution.py:144
  96.5 3.3 %collective-permute-start.9 = (f32[32,32]{0,1:T(8,128)S(1)}, f32[32,32]{0,1:T(8,128)}, u32[]{:S(2)}, u32[]{:S(2)}) collective-permute-start(f32[32,32]{0,1:T(8,128)S(1)} %fusion.64), channel_id=1, source_target_pairs={{0,128},{128,0},{256,384},{384,256},{512,640},{640,512},{768,896},... | collective-permute-start | bytes 12296 | tf_op jit(solution)/shard_map/ppermute | solution.py:15
  99.9 1.1 pad_maximum_fusion.1
  103.2 4.3 %collective-permute-start.12 = (f32[32,32]{0,1:T(8,128)S(1)}, f32[32,32]{0,1:T(8,128)S(1)}, u32[]{:S(2)}, u32[]{:S(2)}) collective-permute-start(f32[32,32]{0,1:T(8,128)S(1)} %fusion.61), channel_id=1, source_target_pairs={{0,256},{128,384},{256,0},{384,128},{512,768},{640,896},{768,512},... | collective-permute-start | bytes 12296 | tf_op jit(solution)/shard_map/ppermute | solution.py:15
  107.6 4.6 %fusion.7 = f32[32,32,64]{2,0,1:T(8,128)S(1)} fusion(bf16[32,6,64,64]{3,2,0,1:T(8,128)(2,1)} %reshape.295, bf16[32,32,6,64]{3,0,2,1:T(8,128)(2,1)S(1)} %bitcast.215, f32[32,6]{1,0:T(8,128)} %copy.186), kind=kOutput, calls=%fused_computation.12 | convolution fusion | flops 302776320 | bytes 2622208 | tf_op jit(solution)/shard_map/lkpq,clkq->clp/dot_general | solution.py:153
  112.4 3.3 %collective-permute-start.13 = (f32[32,32]{0,1:T(8,128)S(1)}, f32[32,32]{0,1:T(8,128)S(1)}, u32[]{:S(2)}, u32[]{:S(2)}) collective-permute-start(f32[32,32]{0,1:T(8,128)S(1)} %fusion.58), channel_id=1, source_target_pairs={{0,512},{128,640},{256,768},{384,896},{512,0},{640,128},{768,256},... | collective-permute-start | bytes 12296 | tf_op jit(solution)/shard_map/ppermute | solution.py:15
  116.3 5.7 %collective-permute-done.13 = f32[32,32]{0,1:T(8,128)S(1)} collective-permute-done((f32[32,32]{0,1:T(8,128)S(1)}, f32[32,32]{0,1:T(8,128)S(1)}, u32[]{:S(2)}, u32[]{:S(2)}) %collective-permute-start.13) | collective-permute-done | bytes 4128 | tf_op jit(solution)/shard_map/ppermute | solution.py:15
  121.9 0.9 concatenate.83
  123.1 1.0 fusion.15
  125.3 5.8 %scatter_custom_fusion = f32[32,2048]{0,1:T(8,128)S(1)} fusion(s32[2048]{0:T(1024)S(1)} %bitcast.228, f32[2048,32]{1,0:T(8,128)S(1)} %copy.192, f32[]{:T(128)} %constant.13.clone.1), kind=kCustom, calls=%fused_computation.25 | custom fusion | bytes 262148 | tf_op jit(solution)/shard_map/scatter | solution.py:179
  131.5 1.0 copy.193
  132.5 1.0 copy.194
  (158 shorter events, 20.4 us)
Async XLA Ops:
  0.6 123.5 %copy-start = (bf16[32,64,32]{1,2,0:T(8,128)(2,1)S(1)}, bf16[32,64,32]{1,2,0:T(8,128)(2,1)}, u32[]{:S(2)}) copy-start(bf16[32,64,32]{1,2,0:T(8,128)(2,1)} %param.20) | copy-start | bytes 393220
  0.6 3.4 %copy-start.1 = (bf16[1,62,32,32]{1,3,2,0:T(8,128)(2,1)S(1)}, bf16[1,62,32,32]{1,3,2,0:T(8,128)(2,1)}, u32[]{:S(2)}) copy-start(bf16[1,62,32,32]{1,3,2,0:T(8,128)(2,1)} %param.27) | copy-start | bytes 380932
  0.7 3.5 %copy-start.17 = (s32[1,2048]{1,0:T(1,128)S(1)}, s32[1,2048]{1,0:T(1,128)}, u32[]{:S(2)}) copy-start(s32[1,2048]{1,0:T(1,128)} %param.18) | copy-start | bytes 24580
  0.7 3.5 %copy-start.7 = (f32[16,2048]{1,0:T(8,128)S(1)}, f32[16,2048]{1,0:T(8,128)}, u32[]{:S(2)}) copy-start(f32[16,2048]{1,0:T(8,128)} %param.17) | copy-start | bytes 393220
  0.7 3.5 %copy-start.8 = (f32[16,2048]{1,0:T(8,128)S(1)}, f32[16,2048]{1,0:T(8,128)}, u32[]{:S(2)}) copy-start(f32[16,2048]{1,0:T(8,128)} %param.16) | copy-start | bytes 393220
  14.1 3.1 %copy-start.2 = (bf16[1,62,32,32]{1,3,2,0:T(8,128)(2,1)S(1)}, bf16[1,62,32,32]{1,3,2,0:T(8,128)(2,1)}, u32[]{:S(2)}) copy-start(bf16[1,62,32,32]{1,3,2,0:T(8,128)(2,1)} %param.28) | copy-start | bytes 380932
  15.3 13.5 %collective-permute-start = (f32[32,32]{0,1:T(8,128)S(1)}, f32[32,32]{0,1:T(8,128)}, u32[]{:S(2)}, u32[]{:S(2)}) collective-permute-start(f32[32,32]{0,1:T(8,128)S(1)} %fusion.91), channel_id=1, source_target_pairs={{0,1},{1,0},{2,3},{3,2},{4,5},{5,4},{6,7},{7,6},{8,9},{9,8},{10,11... | collective-permute-start | bytes 12296 | tf_op jit(solution)/shard_map/ppermute | solution.py:15
  23.2 11.7 %copy-start.4 = (bf16[32,6,1024]{2,0,1:T(8,128)(2,1)S(1)}, bf16[32,6,1024]{2,0,1:T(8,128)(2,1)}, u32[]{:S(2)}) copy-start(bf16[32,6,1024]{2,0,1:T(8,128)(2,1)} %param.24) | copy-start | bytes 1179652
  29.7 7.6 %collective-permute-start.1 = (f32[32,32]{0,1:T(8,128)S(1)}, f32[32,32]{0,1:T(8,128)S(1)}, u32[]{:S(2)}, u32[]{:S(2)}) collective-permute-start(f32[32,32]{0,1:T(8,128)S(1)} %fusion.82), channel_id=1, source_target_pairs={{0,2},{2,0},{4,6},{6,4},{8,10},{10,8},{12,14},{14,12},{1,3},{3,1},... | collective-permute-start | bytes 12296 | tf_op jit(solution)/shard_map/ppermute | solution.py:15
  37.3 10.1 %copy-start.9 = (f32[32,32]{0,1:T(8,128)}, f32[32,32]{0,1:T(8,128)S(1)}, u32[]{:S(2)}) copy-start(f32[32,32]{0,1:T(8,128)S(1)} %collective-permute-done.1) | copy-start | bytes 12292
  37.5 9.6 %collective-permute-start.2 = (f32[32,32]{0,1:T(8,128)S(1)}, f32[32,32]{0,1:T(8,128)S(1)}, u32[]{:S(2)}, u32[]{:S(2)}) collective-permute-start(f32[32,32]{0,1:T(8,128)S(1)} %fusion.85), channel_id=1, source_target_pairs={{0,4},{2,6},{4,0},{6,2},{8,12},{10,14},{12,8},{14,10},{1,5},{3,7},... | collective-permute-start | bytes 12296 | tf_op jit(solution)/shard_map/ppermute | solution.py:15
  47.1 20.3 %copy-start.11 = (f32[32,32]{0,1:T(8,128)}, f32[32,32]{0,1:T(8,128)S(1)}, u32[]{:S(2)}) copy-start(f32[32,32]{0,1:T(8,128)S(1)} %collective-permute-done.2) | copy-start | bytes 12292
  47.3 13.6 %collective-permute-start.3 = (f32[32,32]{0,1:T(8,128)S(1)}, f32[32,32]{0,1:T(8,128)S(1)}, u32[]{:S(2)}, u32[]{:S(2)}) collective-permute-start(f32[32,32]{0,1:T(8,128)S(1)} %fusion.76), channel_id=1, source_target_pairs={{0,8},{2,10},{4,12},{6,14},{8,0},{10,2},{12,4},{14,6},{1,9},{3,11}... | collective-permute-start | bytes 12296 | tf_op jit(solution)/shard_map/ppermute | solution.py:15
  60.9 6.5 %copy-start.12 = (f32[32,32]{0,1:T(8,128)}, f32[32,32]{0,1:T(8,128)S(1)}, u32[]{:S(2)}) copy-start(f32[32,32]{0,1:T(8,128)S(1)} %collective-permute-done.3) | copy-start | bytes 12292
  61.1 14.9 %collective-permute-start.4 = (f32[32,32]{0,1:T(8,128)S(1)}, f32[32,32]{0,1:T(8,128)S(1)}, u32[]{:S(2)}, u32[]{:S(2)}) collective-permute-start(f32[32,32]{0,1:T(8,128)S(1)} %fusion.73), channel_id=1, source_target_pairs={{0,16},{16,0},{32,48},{48,32},{64,80},{80,64},{96,112},{112,96},{1... | collective-permute-start | bytes 12296 | tf_op jit(solution)/shard_map/ppermute | solution.py:15
  66.1 14.8 %collective-permute-start.7 = (bf16[32,32,32]{1,2,0:T(8,128)(2,1)S(1)}, bf16[32,32,32]{1,2,0:T(8,128)(2,1)S(1)}, u32[]{:S(2)}, u32[]{:S(2)}) collective-permute-start(bf16[32,32,32]{1,2,0:T(8,128)(2,1)S(1)} %convert_bitcast_fusion), channel_id=1, source_target_pairs={{1,0},{2,1},{3,2},{4,3},{5,4},{6,5},{7,6},{8,7},{9,8},{10,9},{11,1... | collective-permute-start | bytes 196616 | tf_op jit(solution)/shard_map/ppermute | solution.py:25
  67.4 13.5 %collective-permute-start.6 = (bf16[32,32,32]{1,2,0:T(8,128)(2,1)S(1)}, bf16[32,32,32]{1,2,0:T(8,128)(2,1)S(1)}, u32[]{:S(2)}, u32[]{:S(2)}) collective-permute-start(bf16[32,32,32]{1,2,0:T(8,128)(2,1)S(1)} %convert_bitcast_fusion), channel_id=1, source_target_pairs={{0,1},{1,2},{2,3},{3,4},{4,5},{5,6},{6,7},{7,8},{8,9},{9,10},{10,1... | collective-permute-start | bytes 196616 | tf_op jit(solution)/shard_map/ppermute | solution.py:24
  70.5 29.4 %collective-permute-start.11 = (bf16[32,32,64]{2,0,1:T(8,128)(2,1)S(1)}, bf16[32,32,64]{2,0,1:T(8,128)(2,1)S(1)}, u32[]{:S(2)}, u32[]{:S(2)}) collective-permute-start(bf16[32,32,64]{2,0,1:T(8,128)(2,1)S(1)} %select_convert_fusion), channel_id=1, source_target_pairs={{1,0},{2,1},{3,2},{4,3},{5,4},{6,5},{7,6},{8,7},{9,8},{10,9},{11,1... | collective-permute-start | bytes 393224 | tf_op jit(solution)/shard_map/ppermute | solution.py:25
  71.8 28.1 %collective-permute-start.10 = (bf16[32,32,64]{2,0,1:T(8,128)(2,1)S(1)}, bf16[32,32,64]{2,0,1:T(8,128)(2,1)}, u32[]{:S(2)}, u32[]{:S(2)}) collective-permute-start(bf16[32,32,64]{2,0,1:T(8,128)(2,1)S(1)} %select_convert_fusion), channel_id=1, source_target_pairs={{0,1},{1,2},{2,3},{3,4},{4,5},{5,6},{6,7},{7,8},{8,9},{9,10},{10,1... | collective-permute-start | bytes 393224 | tf_op jit(solution)/shard_map/ppermute | solution.py:24
  76.0 5.0 %copy-start.13 = (f32[32,32]{0,1:T(8,128)}, f32[32,32]{0,1:T(8,128)S(1)}, u32[]{:S(2)}) copy-start(f32[32,32]{0,1:T(8,128)S(1)} %collective-permute-done.4) | copy-start | bytes 12292
  76.2 7.4 %collective-permute-start.5 = (f32[32,32]{0,1:T(8,128)S(1)}, f32[32,32]{0,1:T(8,128)}, u32[]{:S(2)}, u32[]{:S(2)}) collective-permute-start(f32[32,32]{0,1:T(8,128)S(1)} %fusion.70), channel_id=1, source_target_pairs={{0,32},{16,48},{32,0},{48,16},{64,96},{80,112},{96,64},{112,80},{1... | collective-permute-start | bytes 12296 | tf_op jit(solution)/shard_map/ppermute | solution.py:15
  81.5 9.8 %copy-start.20 = (f32[32,6]{1,0:T(8,128)S(1)}, f32[32,6]{1,0:T(8,128)}, u32[]{:S(2)}) copy-start(f32[32,6]{1,0:T(8,128)} %copy.183) | copy-start | bytes 2308
  84.5 11.8 %collective-permute-start.8 = (f32[32,32]{0,1:T(8,128)S(1)}, f32[32,32]{0,1:T(8,128)S(1)}, u32[]{:S(2)}, u32[]{:S(2)}) collective-permute-start(f32[32,32]{0,1:T(8,128)S(1)} %fusion.67), channel_id=1, source_target_pairs={{0,64},{16,80},{32,96},{48,112},{64,0},{80,16},{96,32},{112,48},{1... | collective-permute-start | bytes 12296 | tf_op jit(solution)/shard_map/ppermute | solution.py:15
  96.3 3.6 %copy-start.14 = (f32[32,32]{0,1:T(8,128)}, f32[32,32]{0,1:T(8,128)S(1)}, u32[]{:S(2)}) copy-start(f32[32,32]{0,1:T(8,128)S(1)} %collective-permute-done.8) | copy-start | bytes 12292
  96.5 5.7 %collective-permute-start.9 = (f32[32,32]{0,1:T(8,128)S(1)}, f32[32,32]{0,1:T(8,128)}, u32[]{:S(2)}, u32[]{:S(2)}) collective-permute-start(f32[32,32]{0,1:T(8,128)S(1)} %fusion.64), channel_id=1, source_target_pairs={{0,128},{128,0},{256,384},{384,256},{512,640},{640,512},{768,896},... | collective-permute-start | bytes 12296 | tf_op jit(solution)/shard_map/ppermute | solution.py:15
  103.2 12.5 %copy-start.6 = (f32[9,32,32]{2,1,0:T(8,128)S(1)}, f32[9,32,32]{2,1,0:T(8,128)}, u32[]{:S(2)}) copy-start(f32[9,32,32]{2,1,0:T(8,128)} %fusion.36) | copy-start | bytes 110596
  103.2 12.5 %copy-start.24 = (pred[10]{0:T(512)(128)(4,1)S(1)}, pred[10]{0:T(512)(128)(4,1)}, u32[]{:S(2)}) copy-start(pred[10]{0:T(512)(128)(4,1)} %copy-done.23) | copy-start | bytes 34
  103.2 18.7 %copy-start.10 = (f32[32,32]{0,1:T(8,128)S(1)}, f32[32,32]{0,1:T(8,128)}, u32[]{:S(2)}) copy-start(f32[32,32]{0,1:T(8,128)} %copy-done.9) | copy-start | bytes 12292
  103.2 8.9 %collective-permute-start.12 = (f32[32,32]{0,1:T(8,128)S(1)}, f32[32,32]{0,1:T(8,128)S(1)}, u32[]{:S(2)}, u32[]{:S(2)}) collective-permute-start(f32[32,32]{0,1:T(8,128)S(1)} %fusion.61), channel_id=1, source_target_pairs={{0,256},{128,384},{256,0},{384,128},{512,768},{640,896},{768,512},... | collective-permute-start | bytes 12296 | tf_op jit(solution)/shard_map/ppermute | solution.py:15
  112.2 10.9 %copy-start.3 = (f32[32,32,32]{2,1,0:T(8,128)S(1)}, f32[32,32,32]{2,1,0:T(8,128)}, u32[]{:S(2)}) copy-start(f32[32,32,32]{2,1,0:T(8,128)} %fusion.12) | copy-start | bytes 393220
  112.2 3.5 %copy-start.15 = (f32[32,32]{0,1:T(8,128)}, f32[32,32]{0,1:T(8,128)S(1)}, u32[]{:S(2)}) copy-start(f32[32,32]{0,1:T(8,128)S(1)} %collective-permute-done.12) | copy-start | bytes 12292
  112.4 9.5 %collective-permute-start.13 = (f32[32,32]{0,1:T(8,128)S(1)}, f32[32,32]{0,1:T(8,128)S(1)}, u32[]{:S(2)}, u32[]{:S(2)}) collective-permute-start(f32[32,32]{0,1:T(8,128)S(1)} %fusion.58), channel_id=1, source_target_pairs={{0,512},{128,640},{256,768},{384,896},{512,0},{640,128},{768,256},... | collective-permute-start | bytes 12296 | tf_op jit(solution)/shard_map/ppermute | solution.py:15
  (9 other events, 14.9 us)

commit v10 on v9

--- a/solution.py
+++ b/solution.py
@@ -153,11 +153,12 @@
             return jnp.einsum("lkpq,clkq->clp", results["near_sq"], scaled, precision=best_precision)
 
         stages = [
+            ("paths", leaf_paths),
+            ("spare_a", lambda: jnp.zeros((), jnp.float32)),
+            ("far_sq", far_square),
             ("near_sq", near_square),
-            ("far_sq", far_square),
-            ("paths", leaf_paths),
             ("win_in", lambda: (leaf_blocks, leaf_round)),
-            ("spare", lambda: jnp.zeros((), jnp.float32)),
+            ("spare_b", lambda: jnp.zeros((), jnp.float32)),
             ("far_pick", far_picked),
             ("far_sum", far_sum),
             ("near_pick", near_picked),

time: 135 us -> 134 us (level)
  waiting for transfers between devices: 9.01 us -> 5.81 us
    ppermute x10, waiting for transfers between devices: 9 us -> 5.8 us  [from_partner(): return lax.ppermute(value, axis, pairs)]
    unnamed x66 -> x68, local copies, waits for them, and re-layouts: 5.22 us -> 5.5 us
  transfers between devices with their start and end apart: 14 -> 14, of which waited for: 4 -> 5; matrix products, arithmetic and copies ran while one was open for 23% -> 24% of each run, Pallas kernels for 0% -> 0%
where the time goes in v10:
time: 134 us; the launch traced here: 132 us
  starting transfers between devices  64 us (48%)
  local copies, waits for them, and re-layouts  38.3 us (29%)
  matrix products  19.2 us (14%)
  waiting for transfers between devices  5.81 us (4%)
  other arithmetic  2.52 us (2%)
  between operations  1.73 us (1%)
    ppermute x10, starting transfers between devices, from_partner(): return lax.ppermute(value, axis, pairs)  53.6 us
    ppermute x2, starting transfers between devices, extended(): low = lax.ppermute(block, axis, forward)  7.9 us
    gather x2, local copies, waits for them, and re-layouts, apply_image(): ordered = jnp.take(vectors, order_row, axis=1).astype(jnp.bfloat16)  6.41 us
    scatter x1, local copies, waits for them, and re-layouts, apply_image(): return jnp.zeros_like(image).at[:, order_row].set(image)  5.97 us
    ppermute x10, waiting for transfers between devices, from_partner(): return lax.ppermute(value, axis, pairs)  5.8 us
    unnamed x68, local copies, waits for them, and re-layouts  5.5 us
    dot_general x1, matrix products, far_sum(): jnp.einsum('lkab,lkbc->lac', results['far_sq'], scaled, precision=best_pr...  4.96 us
    dot_general x1, matrix products, near_total(): jnp.einsum('lkpq,clkq->clp', results['near_sq'], scaled, precision=best_p...  4.58 us
  transfers between devices with their start and end apart: 14, of which 5 were waited for; matrix products, arithmetic and copies ran while one was open for 24% of the time, Pallas kernels for 0%

profile of v10, /device:TPU:14, one launch (start us, length us, event | category | flops | bytes accessed | tf_op | source)
XLA Modules:
  0.0 131.6 jit_solution(11281722287611042439)
XLA Ops:
  0.7 1.1 slice.176
  1.8 1.1 slice.180
  2.9 1.1 slice.184
  4.8 6.2 %gather_fusion = bf16[2048,32]{1,0:T(8,128)(2,1)S(1)} fusion(bf16[32,2048]{0,1:T(8,128)(2,1)S(1)} %copy.161, s32[2048]{0:T(1024)S(1)} %broadcast_clamp_fusion), kind=kCustom, calls=%fused_computation | custom fusion | bytes 270336 | tf_op jit(solution)/shard_map/jit(_take)/gather | solution.py:104
  15.5 1.9 %collective-permute-start = (f32[32,32]{0,1:T(8,128)S(1)}, f32[32,32]{0,1:T(8,128)S(1)}, u32[]{:S(2)}, u32[]{:S(2)}) collective-permute-start(f32[32,32]{0,1:T(8,128)S(1)} %fusion.91), channel_id=1, source_target_pairs={{0,1},{1,0},{2,3},{3,2},{4,5},{5,4},{6,7},{7,6},{8,9},{9,8},{10,11... | collective-permute-start | bytes 12296 | tf_op jit(solution)/shard_map/ppermute | solution.py:15
  22.8 1.0 convolution_bitcast_fusion.3
  24.1 5.3 %collective-permute-start.1 = (f32[32,32]{0,1:T(8,128)S(1)}, f32[32,32]{0,1:T(8,128)S(1)}, u32[]{:S(2)}, u32[]{:S(2)}) collective-permute-start(f32[32,32]{0,1:T(8,128)S(1)} %fusion.82), channel_id=1, source_target_pairs={{0,2},{2,0},{4,6},{6,4},{8,10},{10,8},{12,14},{14,12},{1,3},{3,1},... | collective-permute-start | bytes 12296 | tf_op jit(solution)/shard_map/ppermute | solution.py:15
  29.4 1.7 %collective-permute-done.1 = f32[32,32]{0,1:T(8,128)S(1)} collective-permute-done((f32[32,32]{0,1:T(8,128)S(1)}, f32[32,32]{0,1:T(8,128)S(1)}, u32[]{:S(2)}, u32[]{:S(2)}) %collective-permute-start.1) | collective-permute-done | bytes 4128 | tf_op jit(solution)/shard_map/ppermute | solution.py:15
  31.3 7.9 %collective-permute-start.2 = (f32[32,32]{0,1:T(8,128)S(1)}, f32[32,32]{0,1:T(8,128)S(1)}, u32[]{:S(2)}, u32[]{:S(2)}) collective-permute-start(f32[32,32]{0,1:T(8,128)S(1)} %fusion.79), channel_id=1, source_target_pairs={{0,4},{2,6},{4,0},{6,2},{8,12},{10,14},{12,8},{14,10},{1,5},{3,7},... | collective-permute-start | bytes 12296 | tf_op jit(solution)/shard_map/ppermute | solution.py:15
  39.2 3.1 %reshape.300 = bf16[32,6,32,32]{3,2,0,1:T(8,128)(2,1)} reshape(bf16[32,6,1024]{2,0,1:T(8,128)(2,1)} %param.24) | data formatting | bytes 786432 | tf_op jit(solution)/shard_map/reshape | solution.py:135
  42.5 11.8 %collective-permute-start.3 = (f32[32,32]{0,1:T(8,128)S(1)}, f32[32,32]{0,1:T(8,128)S(1)}, u32[]{:S(2)}, u32[]{:S(2)}) collective-permute-start(f32[32,32]{0,1:T(8,128)S(1)} %fusion.76), channel_id=1, source_target_pairs={{0,8},{2,10},{4,12},{6,14},{8,0},{10,2},{12,4},{14,6},{1,9},{3,11}... | collective-permute-start | bytes 12296 | tf_op jit(solution)/shard_map/ppermute | solution.py:15
  54.4 4.4 %reshape.301 = bf16[32,6,64,64]{3,2,0,1:T(8,128)(2,1)} reshape(bf16[32,6,4096]{2,0,1:T(8,128)(2,1)S(1)} %copy-done.3) | data formatting | bytes 3145728 | tf_op jit(solution)/shard_map/reshape | solution.py:132
  59.2 3.6 %collective-permute-start.4 = (f32[32,32]{0,1:T(8,128)S(1)}, f32[32,32]{0,1:T(8,128)S(1)}, u32[]{:S(2)}, u32[]{:S(2)}) collective-permute-start(f32[32,32]{0,1:T(8,128)S(1)} %fusion.73), channel_id=1, source_target_pairs={{0,16},{16,0},{32,48},{48,32},{64,80},{80,64},{96,112},{112,96},{1... | collective-permute-start | bytes 12296 | tf_op jit(solution)/shard_map/ppermute | solution.py:15
  63.0 1.8 %collective-permute-done.4 = f32[32,32]{0,1:T(8,128)S(1)} collective-permute-done((f32[32,32]{0,1:T(8,128)S(1)}, f32[32,32]{0,1:T(8,128)S(1)}, u32[]{:S(2)}, u32[]{:S(2)}) %collective-permute-start.4) | collective-permute-done | bytes 4128 | tf_op jit(solution)/shard_map/ppermute | solution.py:15
  65.1 4.7 %collective-permute-start.5 = (f32[32,32]{0,1:T(8,128)S(1)}, f32[32,32]{0,1:T(8,128)S(1)}, u32[]{:S(2)}, u32[]{:S(2)}) collective-permute-start(f32[32,32]{0,1:T(8,128)S(1)} %fusion.70), channel_id=1, source_target_pairs={{0,32},{16,48},{32,0},{48,16},{64,96},{80,112},{96,64},{112,80},{1... | collective-permute-start | bytes 12296 | tf_op jit(solution)/shard_map/ppermute | solution.py:15
  70.5 1.0 copy.182
  72.3 1.3 collective-permute-start.8
  73.6 3.0 %collective-permute-start.7 = (bf16[32,32,32]{1,2,0:T(8,128)(2,1)S(1)}, bf16[32,32,32]{1,2,0:T(8,128)(2,1)S(1)}, u32[]{:S(2)}, u32[]{:S(2)}) collective-permute-start(bf16[32,32,32]{1,2,0:T(8,128)(2,1)S(1)} %convert_bitcast_fusion), channel_id=1, source_target_pairs={{0,1},{1,2},{2,3},{3,4},{4,5},{5,6},{6,7},{7,8},{8,9},{9,10},{10,1... | collective-permute-start | bytes 196616 | tf_op jit(solution)/shard_map/ppermute | solution.py:24
  76.7 1.3 collective-permute-start.12
  78.0 4.9 %collective-permute-start.11 = (bf16[32,32,64]{2,0,1:T(8,128)(2,1)S(1)}, bf16[32,32,64]{2,0,1:T(8,128)(2,1)}, u32[]{:S(2)}, u32[]{:S(2)}) collective-permute-start(bf16[32,32,64]{2,0,1:T(8,128)(2,1)S(1)} %select_convert_fusion), channel_id=1, source_target_pairs={{0,1},{1,2},{2,3},{3,4},{4,5},{5,6},{6,7},{7,8},{8,9},{9,10},{10,1... | collective-permute-start | bytes 393224 | tf_op jit(solution)/shard_map/ppermute | solution.py:24
  83.0 6.4 %collective-permute-start.6 = (f32[32,32]{0,1:T(8,128)S(1)}, f32[32,32]{0,1:T(8,128)}, u32[]{:S(2)}, u32[]{:S(2)}) collective-permute-start(f32[32,32]{0,1:T(8,128)S(1)} %fusion.67), channel_id=1, source_target_pairs={{0,64},{16,80},{32,96},{48,112},{64,0},{80,16},{96,32},{112,48},{1... | collective-permute-start | bytes 12296 | tf_op jit(solution)/shard_map/ppermute | solution.py:15
  90.0 2.0 %gather_fusion.1 = bf16[192,32,32]{2,1,0:T(8,128)(2,1)} fusion(bf16[96,32,32]{2,1,0:T(8,128)(2,1)S(1)} %copy.184, s32[1024]{0:T(1024)S(1)} %pad_clamp_fusion.1), kind=kCustom, calls=%fused_computation.1 | custom fusion | bytes 787200 | tf_op jit(solution)/shard_map/gather | solution.py:139
  93.7 3.5 %collective-permute-start.9 = (f32[32,32]{0,1:T(8,128)S(1)}, f32[32,32]{0,1:T(8,128)S(1)}, u32[]{:S(2)}, u32[]{:S(2)}) collective-permute-start(f32[32,32]{0,1:T(8,128)S(1)} %fusion.64), channel_id=1, source_target_pairs={{0,128},{128,0},{256,384},{384,256},{512,640},{640,512},{768,896},... | collective-permute-start | bytes 12296 | tf_op jit(solution)/shard_map/ppermute | solution.py:15
  97.2 5.0 %fusion.12 = f32[32,32,32]{2,1,0:T(8,128)} fusion(bf16[32,6,32,32]{3,2,0,1:T(8,128)(2,1)} %reshape.300, bf16[32,6,32,32]{3,2,1,0:T(8,128)(2,1)} %bitcast.217, f32[32,6]{1,0:T(8,128)S(1)} %copy-done.23), kind=kOutput, calls=%fused_computation.16 | convolution fusion | flops 75890688 | bytes 918272 | tf_op jit(solution)/shard_map/lkab,lkbc->lac/dot_general | solution.py:144
  102.4 4.2 %collective-permute-start.10 = (f32[32,32]{0,1:T(8,128)S(1)}, f32[32,32]{0,1:T(8,128)}, u32[]{:S(2)}, u32[]{:S(2)}) collective-permute-start(f32[32,32]{0,1:T(8,128)S(1)} %fusion.61), channel_id=1, source_target_pairs={{0,256},{128,384},{256,0},{384,128},{512,768},{640,896},{768,512},... | collective-permute-start | bytes 12296 | tf_op jit(solution)/shard_map/ppermute | solution.py:15
  106.7 1.1 pad_maximum_fusion.1
  110.2 4.1 %collective-permute-start.13 = (f32[32,32]{0,1:T(8,128)S(1)}, f32[32,32]{0,1:T(8,128)}, u32[]{:S(2)}, u32[]{:S(2)}) collective-permute-start(f32[32,32]{0,1:T(8,128)S(1)} %fusion.58), channel_id=1, source_target_pairs={{0,512},{128,640},{256,768},{384,896},{512,0},{640,128},{768,256},... | collective-permute-start | bytes 12296 | tf_op jit(solution)/shard_map/ppermute | solution.py:15
  114.3 4.6 %fusion.7 = f32[32,32,64]{2,0,1:T(8,128)S(1)} fusion(bf16[32,6,64,64]{3,2,0,1:T(8,128)(2,1)} %reshape.301, bf16[32,32,6,64]{3,0,2,1:T(8,128)(2,1)S(1)} %bitcast.215, f32[32,6]{1,0:T(8,128)} %copy.189), kind=kOutput, calls=%fused_computation.12 | convolution fusion | flops 302776320 | bytes 2622208 | tf_op jit(solution)/shard_map/lkpq,clkq->clp/dot_general | solution.py:153
  118.9 1.1 collective-permute-done.13
  121.1 1.0 fusion.15
  123.3 6.0 %scatter_custom_fusion = f32[32,2048]{0,1:T(8,128)S(1)} fusion(s32[2048]{0:T(1024)} %bitcast.228, f32[2048,32]{1,0:T(8,128)S(1)} %copy.194, f32[]{:T(128)} %constant.13.clone.1), kind=kCustom, calls=%fused_computation.25 | custom fusion | bytes 262656 | tf_op jit(solution)/shard_map/scatter | solution.py:180
  129.7 1.0 copy.195
  (160 shorter events, 21.6 us)
Async XLA Ops:
  0.6 121.5 %copy-start = (bf16[32,64,32]{1,2,0:T(8,128)(2,1)S(1)}, bf16[32,64,32]{1,2,0:T(8,128)(2,1)}, u32[]{:S(2)}) copy-start(bf16[32,64,32]{1,2,0:T(8,128)(2,1)} %param.20) | copy-start | bytes 393220
  0.7 3.5 %copy-start.6 = (f32[16,2048]{1,0:T(8,128)S(1)}, f32[16,2048]{1,0:T(8,128)}, u32[]{:S(2)}) copy-start(f32[16,2048]{1,0:T(8,128)} %param.17) | copy-start | bytes 393220
  0.7 3.5 %copy-start.7 = (f32[16,2048]{1,0:T(8,128)S(1)}, f32[16,2048]{1,0:T(8,128)}, u32[]{:S(2)}) copy-start(f32[16,2048]{1,0:T(8,128)} %param.16) | copy-start | bytes 393220
  15.5 8.3 %collective-permute-start = (f32[32,32]{0,1:T(8,128)S(1)}, f32[32,32]{0,1:T(8,128)S(1)}, u32[]{:S(2)}, u32[]{:S(2)}) collective-permute-start(f32[32,32]{0,1:T(8,128)S(1)} %fusion.91), channel_id=1, source_target_pairs={{0,1},{1,0},{2,3},{3,2},{4,5},{5,4},{6,7},{7,6},{8,9},{9,8},{10,11... | collective-permute-start | bytes 12296 | tf_op jit(solution)/shard_map/ppermute | solution.py:15
  21.9 7.4 %copy-start.25 = (s32[32,6]{0,1:T(8,128)S(1)}, s32[32,6]{0,1:T(8,128)}, u32[]{:S(2)}) copy-start(s32[32,6]{0,1:T(8,128)} %param.23) | copy-start | bytes 2308
  21.9 7.4 %copy-start.27 = (f32[32,6]{0,1:T(8,128)S(1)}, f32[32,6]{0,1:T(8,128)}, u32[]{:S(2)}) copy-start(f32[32,6]{0,1:T(8,128)} %param.22) | copy-start | bytes 2308
  23.8 30.6 %copy-start.3 = (bf16[32,6,4096]{2,0,1:T(8,128)(2,1)S(1)}, bf16[32,6,4096]{2,0,1:T(8,128)(2,1)}, u32[]{:S(2)}) copy-start(bf16[32,6,4096]{2,0,1:T(8,128)(2,1)} %param.21) | copy-start | bytes 4718596
  23.8 35.0 %copy-start.8 = (f32[32,32]{0,1:T(8,128)}, f32[32,32]{0,1:T(8,128)S(1)}, u32[]{:S(2)}) copy-start(f32[32,32]{0,1:T(8,128)S(1)} %collective-permute-done) | copy-start | bytes 12292
  24.1 7.0 %collective-permute-start.1 = (f32[32,32]{0,1:T(8,128)S(1)}, f32[32,32]{0,1:T(8,128)S(1)}, u32[]{:S(2)}, u32[]{:S(2)}) collective-permute-start(f32[32,32]{0,1:T(8,128)S(1)} %fusion.82), channel_id=1, source_target_pairs={{0,2},{2,0},{4,6},{6,4},{8,10},{10,8},{12,14},{14,12},{1,3},{3,1},... | collective-permute-start | bytes 12296 | tf_op jit(solution)/shard_map/ppermute | solution.py:15
  31.1 27.7 %copy-start.10 = (f32[32,32]{0,1:T(8,128)}, f32[32,32]{0,1:T(8,128)S(1)}, u32[]{:S(2)}) copy-start(f32[32,32]{0,1:T(8,128)S(1)} %collective-permute-done.1) | copy-start | bytes 12292
  31.3 11.0 %collective-permute-start.2 = (f32[32,32]{0,1:T(8,128)S(1)}, f32[32,32]{0,1:T(8,128)S(1)}, u32[]{:S(2)}, u32[]{:S(2)}) collective-permute-start(f32[32,32]{0,1:T(8,128)S(1)} %fusion.79), channel_id=1, source_target_pairs={{0,4},{2,6},{4,0},{6,2},{8,12},{10,14},{12,8},{14,10},{1,5},{3,7},... | collective-permute-start | bytes 12296 | tf_op jit(solution)/shard_map/ppermute | solution.py:15
  42.3 16.5 %copy-start.12 = (f32[32,32]{0,1:T(8,128)}, f32[32,32]{0,1:T(8,128)S(1)}, u32[]{:S(2)}) copy-start(f32[32,32]{0,1:T(8,128)S(1)} %collective-permute-done.2) | copy-start | bytes 12292
  42.5 16.4 %collective-permute-start.3 = (f32[32,32]{0,1:T(8,128)S(1)}, f32[32,32]{0,1:T(8,128)S(1)}, u32[]{:S(2)}, u32[]{:S(2)}) collective-permute-start(f32[32,32]{0,1:T(8,128)S(1)} %fusion.76), channel_id=1, source_target_pairs={{0,8},{2,10},{4,12},{6,14},{8,0},{10,2},{12,4},{14,6},{1,9},{3,11}... | collective-permute-start | bytes 12296 | tf_op jit(solution)/shard_map/ppermute | solution.py:15
  59.0 10.8 %copy-start.14 = (f32[32,32]{0,1:T(8,128)}, f32[32,32]{0,1:T(8,128)S(1)}, u32[]{:S(2)}) copy-start(f32[32,32]{0,1:T(8,128)S(1)} %collective-permute-done.3) | copy-start | bytes 12292
  59.2 5.6 %collective-permute-start.4 = (f32[32,32]{0,1:T(8,128)S(1)}, f32[32,32]{0,1:T(8,128)S(1)}, u32[]{:S(2)}, u32[]{:S(2)}) collective-permute-start(f32[32,32]{0,1:T(8,128)S(1)} %fusion.73), channel_id=1, source_target_pairs={{0,16},{16,0},{32,48},{48,32},{64,80},{80,64},{96,112},{112,96},{1... | collective-permute-start | bytes 12296 | tf_op jit(solution)/shard_map/ppermute | solution.py:15
  64.9 5.7 %copy-start.15 = (f32[32,32]{0,1:T(8,128)}, f32[32,32]{0,1:T(8,128)S(1)}, u32[]{:S(2)}) copy-start(f32[32,32]{0,1:T(8,128)S(1)} %collective-permute-done.4) | copy-start | bytes 12292
  65.1 17.8 %collective-permute-start.5 = (f32[32,32]{0,1:T(8,128)S(1)}, f32[32,32]{0,1:T(8,128)S(1)}, u32[]{:S(2)}, u32[]{:S(2)}) collective-permute-start(f32[32,32]{0,1:T(8,128)S(1)} %fusion.70), channel_id=1, source_target_pairs={{0,32},{16,48},{32,0},{48,16},{64,96},{80,112},{96,64},{112,80},{1... | collective-permute-start | bytes 12296 | tf_op jit(solution)/shard_map/ppermute | solution.py:15
  72.3 17.1 %collective-permute-start.8 = (bf16[32,32,32]{1,2,0:T(8,128)(2,1)S(1)}, bf16[32,32,32]{1,2,0:T(8,128)(2,1)S(1)}, u32[]{:S(2)}, u32[]{:S(2)}) collective-permute-start(bf16[32,32,32]{1,2,0:T(8,128)(2,1)S(1)} %convert_bitcast_fusion), channel_id=1, source_target_pairs={{1,0},{2,1},{3,2},{4,3},{5,4},{6,5},{7,6},{8,7},{9,8},{10,9},{11,1... | collective-permute-start | bytes 196616 | tf_op jit(solution)/shard_map/ppermute | solution.py:25
  73.6 15.8 %collective-permute-start.7 = (bf16[32,32,32]{1,2,0:T(8,128)(2,1)S(1)}, bf16[32,32,32]{1,2,0:T(8,128)(2,1)S(1)}, u32[]{:S(2)}, u32[]{:S(2)}) collective-permute-start(bf16[32,32,32]{1,2,0:T(8,128)(2,1)S(1)} %convert_bitcast_fusion), channel_id=1, source_target_pairs={{0,1},{1,2},{2,3},{3,4},{4,5},{5,6},{6,7},{7,8},{8,9},{9,10},{10,1... | collective-permute-start | bytes 196616 | tf_op jit(solution)/shard_map/ppermute | solution.py:24
  76.7 30.0 %collective-permute-start.12 = (bf16[32,32,64]{2,0,1:T(8,128)(2,1)S(1)}, bf16[32,32,64]{2,0,1:T(8,128)(2,1)S(1)}, u32[]{:S(2)}, u32[]{:S(2)}) collective-permute-start(bf16[32,32,64]{2,0,1:T(8,128)(2,1)S(1)} %select_convert_fusion), channel_id=1, source_target_pairs={{1,0},{2,1},{3,2},{4,3},{5,4},{6,5},{7,6},{8,7},{9,8},{10,9},{11,1... | collective-permute-start | bytes 393224 | tf_op jit(solution)/shard_map/ppermute | solution.py:25
  78.0 28.7 %collective-permute-start.11 = (bf16[32,32,64]{2,0,1:T(8,128)(2,1)S(1)}, bf16[32,32,64]{2,0,1:T(8,128)(2,1)}, u32[]{:S(2)}, u32[]{:S(2)}) collective-permute-start(bf16[32,32,64]{2,0,1:T(8,128)(2,1)S(1)} %select_convert_fusion), channel_id=1, source_target_pairs={{0,1},{1,2},{2,3},{3,4},{4,5},{5,6},{6,7},{7,8},{8,9},{9,10},{10,1... | collective-permute-start | bytes 393224 | tf_op jit(solution)/shard_map/ppermute | solution.py:24
  82.8 6.6 %copy-start.16 = (f32[32,32]{0,1:T(8,128)}, f32[32,32]{0,1:T(8,128)S(1)}, u32[]{:S(2)}) copy-start(f32[32,32]{0,1:T(8,128)S(1)} %collective-permute-done.5) | copy-start | bytes 12292
  83.0 9.7 %collective-permute-start.6 = (f32[32,32]{0,1:T(8,128)S(1)}, f32[32,32]{0,1:T(8,128)}, u32[]{:S(2)}, u32[]{:S(2)}) collective-permute-start(f32[32,32]{0,1:T(8,128)S(1)} %fusion.67), channel_id=1, source_target_pairs={{0,64},{16,80},{32,96},{48,112},{64,0},{80,16},{96,32},{112,48},{1... | collective-permute-start | bytes 12296 | tf_op jit(solution)/shard_map/ppermute | solution.py:15
  90.0 7.2 %copy-start.23 = (f32[32,6]{1,0:T(8,128)S(1)}, f32[32,6]{1,0:T(8,128)}, u32[]{:S(2)}) copy-start(f32[32,6]{1,0:T(8,128)} %copy.185) | copy-start | bytes 2308
  93.7 8.5 %collective-permute-start.9 = (f32[32,32]{0,1:T(8,128)S(1)}, f32[32,32]{0,1:T(8,128)S(1)}, u32[]{:S(2)}, u32[]{:S(2)}) collective-permute-start(f32[32,32]{0,1:T(8,128)S(1)} %fusion.64), channel_id=1, source_target_pairs={{0,128},{128,0},{256,384},{384,256},{512,640},{640,512},{768,896},... | collective-permute-start | bytes 12296 | tf_op jit(solution)/shard_map/ppermute | solution.py:15
  102.2 4.5 %copy-start.17 = (f32[32,32]{0,1:T(8,128)}, f32[32,32]{0,1:T(8,128)S(1)}, u32[]{:S(2)}) copy-start(f32[32,32]{0,1:T(8,128)S(1)} %collective-permute-done.9) | copy-start | bytes 12292
  102.4 6.8 %collective-permute-start.10 = (f32[32,32]{0,1:T(8,128)S(1)}, f32[32,32]{0,1:T(8,128)}, u32[]{:S(2)}, u32[]{:S(2)}) collective-permute-start(f32[32,32]{0,1:T(8,128)S(1)} %fusion.61), channel_id=1, source_target_pairs={{0,256},{128,384},{256,0},{384,128},{512,768},{640,896},{768,512},... | collective-permute-start | bytes 12296 | tf_op jit(solution)/shard_map/ppermute | solution.py:15
  110.2 9.8 %copy-start.9 = (f32[32,32]{0,1:T(8,128)S(1)}, f32[32,32]{0,1:T(8,128)}, u32[]{:S(2)}) copy-start(f32[32,32]{0,1:T(8,128)} %copy-done.8) | copy-start | bytes 12292
  110.2 9.8 %copy-start.11 = (f32[32,32]{0,1:T(8,128)S(1)}, f32[32,32]{0,1:T(8,128)}, u32[]{:S(2)}) copy-start(f32[32,32]{0,1:T(8,128)} %copy-done.10) | copy-start | bytes 12292
  110.2 9.8 %copy-start.13 = (f32[32,32]{0,1:T(8,128)S(1)}, f32[32,32]{0,1:T(8,128)}, u32[]{:S(2)}) copy-start(f32[32,32]{0,1:T(8,128)} %copy-done.12) | copy-start | bytes 12292
  110.2 10.9 %copy-start.4 = (f32[32,32,32]{2,1,0:T(8,128)S(1)}, f32[32,32,32]{2,1,0:T(8,128)}, u32[]{:S(2)}) copy-start(f32[32,32,32]{2,1,0:T(8,128)} %fusion.12) | copy-start | bytes 393220
  110.2 9.8 %collective-permute-start.13 = (f32[32,32]{0,1:T(8,128)S(1)}, f32[32,32]{0,1:T(8,128)}, u32[]{:S(2)}, u32[]{:S(2)}) collective-permute-start(f32[32,32]{0,1:T(8,128)S(1)} %fusion.58), channel_id=1, source_target_pairs={{0,512},{128,640},{256,768},{384,896},{512,0},{640,128},{768,256},... | collective-permute-start | bytes 12296 | tf_op jit(solution)/shard_map/ppermute | solution.py:15
  (10 other events, 22.2 us)

commit v11 on v10

--- a/solution.py
+++ b/solution.py
@@ -13,6 +13,15 @@
     mask = 2**distance
     pairs = [(source, source ^ mask) for source in range(lax.axis_size(axis))]
     return lax.ppermute(value, axis, pairs)
+
+
+def neighbours(block, axis):
+    count = 1
+    for name in axis:
+        count = count * lax.axis_size(name)
+    forward = [(i, i + 1) for i in range(count - 1)]
+    backward = [(target, source) for source, target in forward]
+    return lax.ppermute(block, axis, forward), lax.ppermute(block, axis, backward)
 
 
 def extended(block, axis, dim):
@@ -134,8 +143,31 @@
         def far_square():
             return far_blocks.reshape(leaves_dev, far_blocks.shape[1], rank_width, rank_width)
 
+        windows = {}
+
+        def window_pair():
+            if not windows:
+                blocks, coeffs = results["win_in"]
+                columns_x, leaf_count, points = blocks.shape
+                coeff_leaves, coeff_rank, coeff_cols = coeffs.shape
+                if coeff_rank == leaf_count and coeff_cols <= points:
+                    padded = jnp.pad(coeffs, ((0, 0), (0, 0), (0, points - coeff_cols)))
+                    packed = jnp.concatenate([blocks, padded], axis=0)
+                    low, high = neighbours(packed, SUB_AXES)
+                    windows["x"] = jnp.concatenate(
+                        [low[:columns_x], blocks, high[:columns_x]], axis=1
+                    )
+                    windows["c"] = jnp.concatenate(
+                        [low[columns_x:, :, :coeff_cols], coeffs, high[columns_x:, :, :coeff_cols]],
+                        axis=0,
+                    )
+                else:
+                    windows["x"] = extended(blocks, SUB_AXES, 1)
+                    windows["c"] = extended(coeffs, SUB_AXES, 0)
+            return windows["x"], windows["c"]
+
         def far_picked():
-            coeff_window = extended(results["win_in"][1], SUB_AXES, 0)
+            coeff_window = window_pair()[1]
             return coeff_window[jnp.minimum(far_index, width_all - 1)]
 
         def far_sum():
@@ -144,7 +176,7 @@
             return jnp.einsum("lkab,lkbc->lac", results["far_sq"], scaled, precision=best_precision)
 
         def near_picked():
-            x_window = extended(results["win_in"][0], SUB_AXES, 1)
+            x_window = window_pair()[0]
             return x_window[:, jnp.minimum(near_index, width_all - 1)]
 
         def near_total():

time: 134 us -> 137 us (1.022)
  local copies, waits for them, and re-layouts: 38.3 us -> 43.1 us
  starting transfers between devices: 64 us -> 60.6 us
  matrix products: 19.2 us -> 21 us
    ppermute x4 -> x2, starting transfers between devices: 10.5 us -> 5.13 us  [the longest x1 3.84 us: neighbours(): lax.ppermute(block, axis, forward)]
    dot_general x14, matrix products: 4.39 us -> 6.51 us  [apply_up(): jnp.einsum('...ab,...ac->...bc', matrix, coeffs, precision=best_precision)]
    slice x0 -> x5, local copies, waits for them, and re-layouts: none -> 1.96 us  [the longest x1 0.97 us: window_pair(): low[:columns_x]]
    ppermute x10, starting transfers between devices: 53.6 us -> 55.4 us  [from_partner(): return lax.ppermute(value, axis, pairs)]
    concatenate x1 -> x3, local copies, waits for them, and re-layouts: 0.36 us -> 2 us  [the longest x1 1.25 us: window_pair(): jnp.concatenate([low[:columns_x], blocks, high[:columns_x]], axis=1)]
    unnamed x68 -> x78, local copies, waits for them, and re-layouts: 5.5 us -> 6.5 us
  transfers between devices with their start and end apart: 14 -> 12, of which waited for: 5 -> 4; matrix products, arithmetic and copies ran while one was open for 24% -> 24% of each run, Pallas kernels for 0% -> 0%
where the time goes in v11:
time: 137 us; the launch traced here: 134 us
  starting transfers between devices  60.6 us (44%)
  local copies, waits for them, and re-layouts  43.1 us (31%)
  matrix products  21 us (15%)
  waiting for transfers between devices  4.76 us (3%)
  other arithmetic  2.9 us (2%)
  between operations  1.85 us (1%)
    ppermute x10, starting transfers between devices, from_partner(): return lax.ppermute(value, axis, pairs)  55.4 us
    gather x2, local copies, waits for them, and re-layouts, apply_image(): ordered = jnp.take(vectors, order_row, axis=1).astype(jnp.bfloat16)  7.29 us
    dot_general x14, matrix products, apply_up(): jnp.einsum('...ab,...ac->...bc', matrix, coeffs, precision=best_precision)  6.51 us
    unnamed x78, local copies, waits for them, and re-layouts  6.5 us
    scatter x1, local copies, waits for them, and re-layouts, apply_image(): return jnp.zeros_like(image).at[:, order_row].set(image)  5.97 us
    ppermute x10, waiting for transfers between devices, from_partner(): return lax.ppermute(value, axis, pairs)  4.75 us
    dot_general x10, matrix products, apply_down(): jnp.einsum('...ab,...bc->...ac', matrix, coeffs, precision=best_precision)  4.62 us
    dot_general x1, matrix products, near_total(): jnp.einsum('lkpq,clkq->clp', results['near_sq'], scaled, precision=best_p...  4.58 us
  transfers between devices with their start and end apart: 12, of which 4 were waited for; matrix products, arithmetic and copies ran while one was open for 24% of the time, Pallas kernels for 0%

profile of v11, /device:TPU:14, one launch (start us, length us, event | category | flops | bytes accessed | tf_op | source)
XLA Modules:
  0.0 134.1 jit_solution(7503426115014630081)
XLA Ops:
  0.7 1.1 slice.196
  1.8 1.1 slice.192
  2.9 1.1 slice.188
  4.0 1.1 slice.200
  8.4 6.2 %gather_fusion = bf16[2048,32]{1,0:T(8,128)(2,1)S(1)} fusion(bf16[32,2048]{0,1:T(8,128)(2,1)S(1)} %copy.194, s32[2048]{0:T(1024)S(1)} %broadcast_clamp_fusion), kind=kCustom, calls=%fused_computation | custom fusion | bytes 270336 | tf_op jit(solution)/shard_map/jit(_take)/gather | solution.py:113
  14.5 1.1 copy.196
  17.7 1.9 %collective-permute-start = (f32[32,32]{0,1:T(8,128)S(1)}, f32[32,32]{0,1:T(8,128)}, u32[]{:S(2)}, u32[]{:S(2)}) collective-permute-start(f32[32,32]{0,1:T(8,128)S(1)} %fusion.93), channel_id=1, source_target_pairs={{0,1},{1,0},{2,3},{3,2},{4,5},{5,4},{6,7},{7,6},{8,9},{9,8},{10,11... | collective-permute-start | bytes 12296 | tf_op jit(solution)/shard_map/ppermute | solution.py:15
  25.0 1.4 %convolution_bitcast_fusion.1 = f32[32,32,32]{1,2,0:T(8,128)} fusion(f32[32,32,32]{1,2,0:T(8,128)S(1)} %bitcast.217, bf16[1,32,32,32]{3,2,1,0:T(8,128)(2,1)S(1)} %copy.262), kind=kOutput, calls=%fused_computation.17 | convolution fusion | flops 12582912 | bytes 327680 | tf_op jit(solution)/shard_map/...ab,...bc->...ac/dot_general | solution.py:43
  27.8 5.2 %collective-permute-start.1 = (f32[32,32]{0,1:T(8,128)S(1)}, f32[32,32]{0,1:T(8,128)S(1)}, u32[]{:S(2)}, u32[]{:S(2)}) collective-permute-start(f32[32,32]{0,1:T(8,128)S(1)} %fusion.84), channel_id=1, source_target_pairs={{0,2},{2,0},{4,6},{6,4},{8,10},{10,8},{12,14},{14,12},{1,3},{3,1},... | collective-permute-start | bytes 12296 | tf_op jit(solution)/shard_map/ppermute | solution.py:15
  33.0 1.7 %collective-permute-done.1 = f32[32,32]{0,1:T(8,128)S(1)} collective-permute-done((f32[32,32]{0,1:T(8,128)S(1)}, f32[32,32]{0,1:T(8,128)S(1)}, u32[]{:S(2)}, u32[]{:S(2)}) %collective-permute-start.1) | collective-permute-done | bytes 4128 | tf_op jit(solution)/shard_map/ppermute | solution.py:15
  35.3 7.9 %collective-permute-start.2 = (f32[32,32]{0,1:T(8,128)S(1)}, f32[32,32]{0,1:T(8,128)S(1)}, u32[]{:S(2)}, u32[]{:S(2)}) collective-permute-start(f32[32,32]{0,1:T(8,128)S(1)} %fusion.81), channel_id=1, source_target_pairs={{0,4},{2,6},{4,0},{6,2},{8,12},{10,14},{12,8},{14,10},{1,5},{3,7},... | collective-permute-start | bytes 12296 | tf_op jit(solution)/shard_map/ppermute | solution.py:15
  43.2 2.4 %reshape.300 = bf16[32,6,32,32]{3,2,0,1:T(8,128)(2,1)} reshape(bf16[32,6,1024]{2,0,1:T(8,128)(2,1)S(1)} %copy-done.7) | data formatting | bytes 786432 | tf_op jit(solution)/shard_map/reshape | solution.py:144
  45.8 11.9 %collective-permute-start.3 = (f32[32,32]{0,1:T(8,128)S(1)}, f32[32,32]{0,1:T(8,128)S(1)}, u32[]{:S(2)}, u32[]{:S(2)}) collective-permute-start(f32[32,32]{0,1:T(8,128)S(1)} %fusion.78), channel_id=1, source_target_pairs={{0,8},{2,10},{4,12},{6,14},{8,0},{10,2},{12,4},{14,6},{1,9},{3,11}... | collective-permute-start | bytes 12296 | tf_op jit(solution)/shard_map/ppermute | solution.py:15
  58.6 4.4 %reshape.301 = bf16[32,6,64,64]{3,2,0,1:T(8,128)(2,1)} reshape(bf16[32,6,4096]{2,0,1:T(8,128)(2,1)S(1)} %copy-done.4) | data formatting | bytes 3145728 | tf_op jit(solution)/shard_map/reshape | solution.py:141
  63.2 3.6 %collective-permute-start.4 = (f32[32,32]{0,1:T(8,128)S(1)}, f32[32,32]{0,1:T(8,128)S(1)}, u32[]{:S(2)}, u32[]{:S(2)}) collective-permute-start(f32[32,32]{0,1:T(8,128)S(1)} %fusion.75), channel_id=1, source_target_pairs={{0,16},{16,0},{32,48},{48,32},{64,80},{80,64},{96,112},{112,96},{1... | collective-permute-start | bytes 12296 | tf_op jit(solution)/shard_map/ppermute | solution.py:15
  67.0 1.8 %collective-permute-done.4 = f32[32,32]{0,1:T(8,128)S(1)} collective-permute-done((f32[32,32]{0,1:T(8,128)S(1)}, f32[32,32]{0,1:T(8,128)S(1)}, u32[]{:S(2)}, u32[]{:S(2)}) %collective-permute-start.4) | collective-permute-done | bytes 4128 | tf_op jit(solution)/shard_map/ppermute | solution.py:15
  69.5 1.3 collective-permute-start.8
  70.8 3.8 %collective-permute-start.7 = (bf16[64,32,64]{2,1,0:T(8,128)(2,1)S(1)}, bf16[64,32,64]{2,1,0:T(8,128)(2,1)}, u32[]{:S(2)}, u32[]{:S(2)}) collective-permute-start(bf16[64,32,64]{2,1,0:T(8,128)(2,1)S(1)} %copy.218), channel_id=1, source_target_pairs={{0,1},{1,2},{2,3},{3,4},{4,5},{5,6},{6,7},{7,8},{8,9},{9,10},{10,1... | collective-permute-start | bytes 786440 | tf_op jit(solution)/shard_map/ppermute | solution.py:24
  74.8 4.7 %collective-permute-start.5 = (f32[32,32]{0,1:T(8,128)S(1)}, f32[32,32]{0,1:T(8,128)S(1)}, u32[]{:S(2)}, u32[]{:S(2)}) collective-permute-start(f32[32,32]{0,1:T(8,128)S(1)} %fusion.72), channel_id=1, source_target_pairs={{0,32},{16,48},{32,0},{48,16},{64,96},{80,112},{96,64},{112,80},{1... | collective-permute-start | bytes 12296 | tf_op jit(solution)/shard_map/ppermute | solution.py:15
  81.6 8.3 %collective-permute-start.6 = (f32[32,32]{0,1:T(8,128)S(1)}, f32[32,32]{0,1:T(8,128)}, u32[]{:S(2)}, u32[]{:S(2)}) collective-permute-start(f32[32,32]{0,1:T(8,128)S(1)} %fusion.69), channel_id=1, source_target_pairs={{0,64},{16,80},{32,96},{48,112},{64,0},{80,16},{96,32},{112,48},{1... | collective-permute-start | bytes 12296 | tf_op jit(solution)/shard_map/ppermute | solution.py:15
  90.2 1.0 slice.265
  92.8 1.5 %fusion.66 = f32[32,32]{0,1:T(8,128)} fusion(f32[10,32,32]{2,1,0:T(8,128)S(1)} %get-tuple-element.57, f32[10,32,32]{2,1,0:T(8,128)S(1)} %get-tuple-element.56, f32[32,32]{0,1:T(8,128)} %collective-permute-done.6, f32[32,32]{0,1:T(8,128)S(1)} %fusion.69), kind=kOutput, calls=%fused_computation.91 | convolution fusion | flops 790528 | bytes 94208 | tf_op jit(solution)/shard_map/...ab,...ac->...bc/dot_general | solution.py:39
  94.3 3.5 %collective-permute-start.9 = (f32[32,32]{0,1:T(8,128)}, f32[32,32]{0,1:T(8,128)}, u32[]{:S(2)}, u32[]{:S(2)}) collective-permute-start(f32[32,32]{0,1:T(8,128)} %fusion.66), channel_id=1, source_target_pairs={{0,128},{128,0},{256,384},{384,256},{512,640},{640,512},{768,896},... | collective-permute-start | bytes 12296 | tf_op jit(solution)/shard_map/ppermute | solution.py:15
  97.8 4.5 %fusion.13 = f32[32,32,32]{2,1,0:T(8,128)} fusion(bf16[32,6,32,32]{3,2,0,1:T(8,128)(2,1)} %reshape.300, bf16[32,6,32,32]{3,2,1,0:T(8,128)(2,1)S(1)} %bitcast.218, f32[32,6]{1,0:T(8,128)} %copy.224), kind=kOutput, calls=%fused_computation.18 | convolution fusion | flops 75890688 | bytes 918272 | tf_op jit(solution)/shard_map/lkab,lkbc->lac/dot_general | solution.py:176
  102.5 1.0 slice.267
  104.8 4.2 %collective-permute-start.10 = (f32[32,32]{0,1:T(8,128)S(1)}, f32[32,32]{0,1:T(8,128)}, u32[]{:S(2)}, u32[]{:S(2)}) collective-permute-start(f32[32,32]{0,1:T(8,128)S(1)} %fusion.63), channel_id=1, source_target_pairs={{0,256},{128,384},{256,0},{384,128},{512,768},{640,896},{768,512},... | collective-permute-start | bytes 12296 | tf_op jit(solution)/shard_map/ppermute | solution.py:15
  109.5 1.3 copy.229
  112.6 4.3 %collective-permute-start.11 = (f32[32,32]{0,1:T(8,128)S(1)}, f32[32,32]{0,1:T(8,128)}, u32[]{:S(2)}, u32[]{:S(2)}) collective-permute-start(f32[32,32]{0,1:T(8,128)S(1)} %fusion.60), channel_id=1, source_target_pairs={{0,512},{128,640},{256,768},{384,896},{512,0},{640,128},{768,256},... | collective-permute-start | bytes 12296 | tf_op jit(solution)/shard_map/ppermute | solution.py:15
  116.9 4.6 %fusion.8 = f32[32,32,64]{2,0,1:T(8,128)S(1)} fusion(bf16[32,6,64,64]{3,2,0,1:T(8,128)(2,1)} %reshape.301, bf16[32,32,6,64]{3,0,2,1:T(8,128)(2,1)S(1)} %bitcast.216, f32[32,6]{1,0:T(8,128)} %copy.231), kind=kOutput, calls=%fused_computation.14 | convolution fusion | flops 302776320 | bytes 2622208 | tf_op jit(solution)/shard_map/lkpq,clkq->clp/dot_general | solution.py:185
  121.5 1.0 collective-permute-done.11
  123.7 1.0 fusion.16
  125.9 6.0 %scatter_custom_fusion = f32[32,2048]{0,1:T(8,128)S(1)} fusion(s32[2048]{0:T(1024)} %bitcast.229, f32[2048,32]{1,0:T(8,128)S(1)} %copy.236, f32[]{:T(128)} %constant.14.clone.1), kind=kCustom, calls=%fused_computation.28 | custom fusion | bytes 262656 | tf_op jit(solution)/shard_map/scatter | solution.py:212
  (176 shorter events, 26.6 us)
Async XLA Ops:
  0.6 124.1 %copy-start = (bf16[32,64,32]{1,2,0:T(8,128)(2,1)S(1)}, bf16[32,64,32]{1,2,0:T(8,128)(2,1)}, u32[]{:S(2)}) copy-start(bf16[32,64,32]{1,2,0:T(8,128)(2,1)} %param.20) | copy-start | bytes 393220
  0.6 5.9 %copy-start.1 = (bf16[1,62,32,32]{1,3,2,0:T(8,128)(2,1)S(1)}, bf16[1,62,32,32]{1,3,2,0:T(8,128)(2,1)}, u32[]{:S(2)}) copy-start(bf16[1,62,32,32]{1,3,2,0:T(8,128)(2,1)} %param.27) | copy-start | bytes 380932
  0.7 4.5 %copy-start.21 = (s32[1,2048]{1,0:T(1,128)S(1)}, s32[1,2048]{1,0:T(1,128)}, u32[]{:S(2)}) copy-start(s32[1,2048]{1,0:T(1,128)} %param.18) | copy-start | bytes 24580
  0.7 7.3 %copy-start.9 = (f32[16,2048]{1,0:T(8,128)S(1)}, f32[16,2048]{1,0:T(8,128)}, u32[]{:S(2)}) copy-start(f32[16,2048]{1,0:T(8,128)} %param.17) | copy-start | bytes 393220
  0.7 7.3 %copy-start.10 = (f32[16,2048]{1,0:T(8,128)S(1)}, f32[16,2048]{1,0:T(8,128)}, u32[]{:S(2)}) copy-start(f32[16,2048]{1,0:T(8,128)} %param.16) | copy-start | bytes 393220
  8.3 7.9 %copy-start.8 = (bf16[32,64,32]{1,2,0:T(8,128)(2,1)S(1)}, bf16[32,64,32]{1,2,0:T(8,128)(2,1)}, u32[]{:S(2)}) copy-start(bf16[32,64,32]{1,2,0:T(8,128)(2,1)} %param.19) | copy-start | bytes 393220
  17.7 9.1 %collective-permute-start = (f32[32,32]{0,1:T(8,128)S(1)}, f32[32,32]{0,1:T(8,128)}, u32[]{:S(2)}, u32[]{:S(2)}) collective-permute-start(f32[32,32]{0,1:T(8,128)S(1)} %fusion.93), channel_id=1, source_target_pairs={{0,1},{1,0},{2,3},{3,2},{4,5},{5,4},{6,7},{7,6},{8,9},{9,8},{10,11... | collective-permute-start | bytes 12296 | tf_op jit(solution)/shard_map/ppermute | solution.py:15
  24.3 8.7 %copy-start.26 = (s32[32,6]{0,1:T(8,128)S(1)}, s32[32,6]{0,1:T(8,128)}, u32[]{:S(2)}) copy-start(s32[32,6]{0,1:T(8,128)} %param.26) | copy-start | bytes 2308
  24.3 8.7 %copy-start.30 = (f32[32,6]{0,1:T(8,128)S(1)}, f32[32,6]{0,1:T(8,128)}, u32[]{:S(2)}) copy-start(f32[32,6]{0,1:T(8,128)} %param.25) | copy-start | bytes 2308
  24.6 18.6 %copy-start.7 = (bf16[32,6,1024]{2,0,1:T(8,128)(2,1)S(1)}, bf16[32,6,1024]{2,0,1:T(8,128)(2,1)}, u32[]{:S(2)}) copy-start(bf16[32,6,1024]{2,0,1:T(8,128)(2,1)} %param.24) | copy-start | bytes 1179652
  26.4 32.2 %copy-start.4 = (bf16[32,6,4096]{2,0,1:T(8,128)(2,1)S(1)}, bf16[32,6,4096]{2,0,1:T(8,128)(2,1)}, u32[]{:S(2)}) copy-start(bf16[32,6,4096]{2,0,1:T(8,128)(2,1)} %param.21) | copy-start | bytes 4718596
  27.8 6.9 %collective-permute-start.1 = (f32[32,32]{0,1:T(8,128)S(1)}, f32[32,32]{0,1:T(8,128)S(1)}, u32[]{:S(2)}, u32[]{:S(2)}) collective-permute-start(f32[32,32]{0,1:T(8,128)S(1)} %fusion.84), channel_id=1, source_target_pairs={{0,2},{2,0},{4,6},{6,4},{8,10},{10,8},{12,14},{14,12},{1,3},{3,1},... | collective-permute-start | bytes 12296 | tf_op jit(solution)/shard_map/ppermute | solution.py:15
  35.3 10.3 %collective-permute-start.2 = (f32[32,32]{0,1:T(8,128)S(1)}, f32[32,32]{0,1:T(8,128)S(1)}, u32[]{:S(2)}, u32[]{:S(2)}) collective-permute-start(f32[32,32]{0,1:T(8,128)S(1)} %fusion.81), channel_id=1, source_target_pairs={{0,4},{2,6},{4,0},{6,2},{8,12},{10,14},{12,8},{14,10},{1,5},{3,7},... | collective-permute-start | bytes 12296 | tf_op jit(solution)/shard_map/ppermute | solution.py:15
  45.6 17.3 %copy-start.14 = (f32[32,32]{0,1:T(8,128)}, f32[32,32]{0,1:T(8,128)S(1)}, u32[]{:S(2)}) copy-start(f32[32,32]{0,1:T(8,128)S(1)} %collective-permute-done.2) | copy-start | bytes 12292
  45.8 17.1 %collective-permute-start.3 = (f32[32,32]{0,1:T(8,128)S(1)}, f32[32,32]{0,1:T(8,128)S(1)}, u32[]{:S(2)}, u32[]{:S(2)}) collective-permute-start(f32[32,32]{0,1:T(8,128)S(1)} %fusion.78), channel_id=1, source_target_pairs={{0,8},{2,10},{4,12},{6,14},{8,0},{10,2},{12,4},{14,6},{1,9},{3,11}... | collective-permute-start | bytes 12296 | tf_op jit(solution)/shard_map/ppermute | solution.py:15
  62.9 11.9 %copy-start.16 = (f32[32,32]{0,1:T(8,128)}, f32[32,32]{0,1:T(8,128)S(1)}, u32[]{:S(2)}) copy-start(f32[32,32]{0,1:T(8,128)S(1)} %collective-permute-done.3) | copy-start | bytes 12292
  63.2 5.6 %collective-permute-start.4 = (f32[32,32]{0,1:T(8,128)S(1)}, f32[32,32]{0,1:T(8,128)S(1)}, u32[]{:S(2)}, u32[]{:S(2)}) collective-permute-start(f32[32,32]{0,1:T(8,128)S(1)} %fusion.75), channel_id=1, source_target_pairs={{0,16},{16,0},{32,48},{48,32},{64,80},{80,64},{96,112},{112,96},{1... | collective-permute-start | bytes 12296 | tf_op jit(solution)/shard_map/ppermute | solution.py:15
  68.8 12.3 %copy-start.18 = (f32[32,32]{0,1:T(8,128)}, f32[32,32]{0,1:T(8,128)S(1)}, u32[]{:S(2)}) copy-start(f32[32,32]{0,1:T(8,128)S(1)} %collective-permute-done.4) | copy-start | bytes 12292
  69.5 20.4 %collective-permute-start.8 = (bf16[64,32,64]{2,1,0:T(8,128)(2,1)S(1)}, bf16[64,32,64]{2,1,0:T(8,128)(2,1)S(1)}, u32[]{:S(2)}, u32[]{:S(2)}) collective-permute-start(bf16[64,32,64]{2,1,0:T(8,128)(2,1)S(1)} %copy.218), channel_id=1, source_target_pairs={{1,0},{2,1},{3,2},{4,3},{5,4},{6,5},{7,6},{8,7},{9,8},{10,9},{11,1... | collective-permute-start | bytes 786440 | tf_op jit(solution)/shard_map/ppermute | solution.py:24
  70.8 19.4 %collective-permute-start.7 = (bf16[64,32,64]{2,1,0:T(8,128)(2,1)S(1)}, bf16[64,32,64]{2,1,0:T(8,128)(2,1)}, u32[]{:S(2)}, u32[]{:S(2)}) collective-permute-start(bf16[64,32,64]{2,1,0:T(8,128)(2,1)S(1)} %copy.218), channel_id=1, source_target_pairs={{0,1},{1,2},{2,3},{3,4},{4,5},{5,6},{6,7},{7,8},{8,9},{9,10},{10,1... | collective-permute-start | bytes 786440 | tf_op jit(solution)/shard_map/ppermute | solution.py:24
  74.8 6.5 %collective-permute-start.5 = (f32[32,32]{0,1:T(8,128)S(1)}, f32[32,32]{0,1:T(8,128)S(1)}, u32[]{:S(2)}, u32[]{:S(2)}) collective-permute-start(f32[32,32]{0,1:T(8,128)S(1)} %fusion.72), channel_id=1, source_target_pairs={{0,32},{16,48},{32,0},{48,16},{64,96},{80,112},{96,64},{112,80},{1... | collective-permute-start | bytes 12296 | tf_op jit(solution)/shard_map/ppermute | solution.py:15
  81.4 8.6 %copy-start.19 = (f32[32,32]{0,1:T(8,128)}, f32[32,32]{0,1:T(8,128)S(1)}, u32[]{:S(2)}) copy-start(f32[32,32]{0,1:T(8,128)S(1)} %collective-permute-done.5) | copy-start | bytes 12292
  81.6 11.2 %collective-permute-start.6 = (f32[32,32]{0,1:T(8,128)S(1)}, f32[32,32]{0,1:T(8,128)}, u32[]{:S(2)}, u32[]{:S(2)}) collective-permute-start(f32[32,32]{0,1:T(8,128)S(1)} %fusion.69), channel_id=1, source_target_pairs={{0,64},{16,80},{32,96},{48,112},{64,0},{80,16},{96,32},{112,48},{1... | collective-permute-start | bytes 12296 | tf_op jit(solution)/shard_map/ppermute | solution.py:15
  94.3 8.0 %slice-start = ((bf16[64,32,64]{2,1,0:T(8,128)(2,1)}), bf16[32,32,64]{2,1,0:T(8,128)(2,1)S(1)}, s32[]{:S(2)}) async-start(bf16[64,32,64]{2,1,0:T(8,128)(2,1)} %copy-done.5), calls=%async_computation | async-start | bytes 524288 | tf_op jit(solution)/shard_map/slice | solution.py:158
  94.3 9.5 %collective-permute-start.9 = (f32[32,32]{0,1:T(8,128)}, f32[32,32]{0,1:T(8,128)}, u32[]{:S(2)}, u32[]{:S(2)}) collective-permute-start(f32[32,32]{0,1:T(8,128)} %fusion.66), channel_id=1, source_target_pairs={{0,128},{128,0},{256,384},{384,256},{512,640},{640,512},{768,896},... | collective-permute-start | bytes 12296 | tf_op jit(solution)/shard_map/ppermute | solution.py:15
  104.8 6.9 %collective-permute-start.10 = (f32[32,32]{0,1:T(8,128)S(1)}, f32[32,32]{0,1:T(8,128)}, u32[]{:S(2)}, u32[]{:S(2)}) collective-permute-start(f32[32,32]{0,1:T(8,128)S(1)} %fusion.63), channel_id=1, source_target_pairs={{0,256},{128,384},{256,0},{384,128},{512,768},{640,896},{768,512},... | collective-permute-start | bytes 12296 | tf_op jit(solution)/shard_map/ppermute | solution.py:15
  112.6 9.9 %copy-start.13 = (f32[32,32]{0,1:T(8,128)S(1)}, f32[32,32]{0,1:T(8,128)}, u32[]{:S(2)}) copy-start(f32[32,32]{0,1:T(8,128)} %copy-done.12) | copy-start | bytes 12292
  112.6 9.9 %copy-start.15 = (f32[32,32]{0,1:T(8,128)S(1)}, f32[32,32]{0,1:T(8,128)}, u32[]{:S(2)}) copy-start(f32[32,32]{0,1:T(8,128)} %copy-done.14) | copy-start | bytes 12292
  112.6 9.9 %copy-start.17 = (f32[32,32]{0,1:T(8,128)S(1)}, f32[32,32]{0,1:T(8,128)}, u32[]{:S(2)}) copy-start(f32[32,32]{0,1:T(8,128)} %copy-done.16) | copy-start | bytes 12292
  112.6 11.0 %copy-start.3 = (f32[32,32,32]{1,2,0:T(8,128)S(1)}, f32[32,32,32]{1,2,0:T(8,128)}, u32[]{:S(2)}) copy-start(f32[32,32,32]{1,2,0:T(8,128)} %convolution_bitcast_fusion.1) | copy-start | bytes 393220
  112.6 11.0 %copy-start.6 = (f32[32,32,32]{2,1,0:T(8,128)S(1)}, f32[32,32,32]{2,1,0:T(8,128)}, u32[]{:S(2)}) copy-start(f32[32,32,32]{2,1,0:T(8,128)} %fusion.13) | copy-start | bytes 393220
  112.6 9.9 %collective-permute-start.11 = (f32[32,32]{0,1:T(8,128)S(1)}, f32[32,32]{0,1:T(8,128)}, u32[]{:S(2)}, u32[]{:S(2)}) collective-permute-start(f32[32,32]{0,1:T(8,128)S(1)} %fusion.60), channel_id=1, source_target_pairs={{0,512},{128,640},{256,768},{384,896},{512,0},{640,128},{768,256},... | collective-permute-start | bytes 12296 | tf_op jit(solution)/shard_map/ppermute | solution.py:15
  (12 other events, 28.5 us)

commit v12 on v10

--- a/solution.py
+++ b/solution.py
@@ -153,8 +153,8 @@
             return jnp.einsum("lkpq,clkq->clp", results["near_sq"], scaled, precision=best_precision)
 
         stages = [
+            ("spare_a", lambda: jnp.zeros((), jnp.float32)),
             ("paths", leaf_paths),
-            ("spare_a", lambda: jnp.zeros((), jnp.float32)),
             ("far_sq", far_square),
             ("near_sq", near_square),
             ("win_in", lambda: (leaf_blocks, leaf_round)),

time: 134 us -> 134 us (level)
  no operation moved by 1% of the time
where the time goes in v12:
time: 134 us; the launch traced here: 132 us
  starting transfers between devices  64.1 us (48%)
  local copies, waits for them, and re-layouts  38.3 us (29%)
  matrix products  19.2 us (14%)
  waiting for transfers between devices  5.79 us (4%)
  other arithmetic  2.52 us (2%)
  between operations  1.73 us (1%)
    ppermute x10, starting transfers between devices, from_partner(): return lax.ppermute(value, axis, pairs)  53.6 us
    ppermute x2, starting transfers between devices, extended(): low = lax.ppermute(block, axis, forward)  7.9 us
    gather x2, local copies, waits for them, and re-layouts, apply_image(): ordered = jnp.take(vectors, order_row, axis=1).astype(jnp.bfloat16)  6.4 us
    scatter x1, local copies, waits for them, and re-layouts, apply_image(): return jnp.zeros_like(image).at[:, order_row].set(image)  5.97 us
    ppermute x10, waiting for transfers between devices, from_partner(): return lax.ppermute(value, axis, pairs)  5.78 us
    unnamed x68, local copies, waits for them, and re-layouts  5.5 us
    dot_general x1, matrix products, far_sum(): jnp.einsum('lkab,lkbc->lac', results['far_sq'], scaled, precision=best_pr...  4.96 us
    dot_general x1, matrix products, near_total(): jnp.einsum('lkpq,clkq->clp', results['near_sq'], scaled, precision=best_p...  4.58 us
  transfers between devices with their start and end apart: 14, of which 5 were waited for; matrix products, arithmetic and copies ran while one was open for 24% of the time, Pallas kernels for 0%

profile of v12, /device:TPU:14, one launch (start us, length us, event | category | flops | bytes accessed | tf_op | source)
XLA Modules:
  0.0 131.6 jit_solution(4284877412954231423)
XLA Ops:
  0.7 1.1 slice.179
  1.8 1.1 slice.183
  2.9 1.1 slice.187
  4.8 6.2 %gather_fusion = bf16[2048,32]{1,0:T(8,128)(2,1)S(1)} fusion(bf16[32,2048]{0,1:T(8,128)(2,1)S(1)} %copy.161, s32[2048]{0:T(1024)S(1)} %broadcast_clamp_fusion), kind=kCustom, calls=%fused_computation | custom fusion | bytes 270336 | tf_op jit(solution)/shard_map/jit(_take)/gather | solution.py:104
  15.5 1.9 %collective-permute-start = (f32[32,32]{0,1:T(8,128)S(1)}, f32[32,32]{0,1:T(8,128)S(1)}, u32[]{:S(2)}, u32[]{:S(2)}) collective-permute-start(f32[32,32]{0,1:T(8,128)S(1)} %fusion.91), channel_id=1, source_target_pairs={{0,1},{1,0},{2,3},{3,2},{4,5},{5,4},{6,7},{7,6},{8,9},{9,8},{10,11... | collective-permute-start | bytes 12296 | tf_op jit(solution)/shard_map/ppermute | solution.py:15
  22.8 1.0 convolution_bitcast_fusion.3
  24.0 5.3 %collective-permute-start.1 = (f32[32,32]{0,1:T(8,128)S(1)}, f32[32,32]{0,1:T(8,128)S(1)}, u32[]{:S(2)}, u32[]{:S(2)}) collective-permute-start(f32[32,32]{0,1:T(8,128)S(1)} %fusion.85), channel_id=1, source_target_pairs={{0,2},{2,0},{4,6},{6,4},{8,10},{10,8},{12,14},{14,12},{1,3},{3,1},... | collective-permute-start | bytes 12296 | tf_op jit(solution)/shard_map/ppermute | solution.py:15
  29.4 1.7 %collective-permute-done.1 = f32[32,32]{0,1:T(8,128)S(1)} collective-permute-done((f32[32,32]{0,1:T(8,128)S(1)}, f32[32,32]{0,1:T(8,128)S(1)}, u32[]{:S(2)}, u32[]{:S(2)}) %collective-permute-start.1) | collective-permute-done | bytes 4128 | tf_op jit(solution)/shard_map/ppermute | solution.py:15
  31.3 7.9 %collective-permute-start.2 = (f32[32,32]{0,1:T(8,128)S(1)}, f32[32,32]{0,1:T(8,128)S(1)}, u32[]{:S(2)}, u32[]{:S(2)}) collective-permute-start(f32[32,32]{0,1:T(8,128)S(1)} %fusion.79), channel_id=1, source_target_pairs={{0,4},{2,6},{4,0},{6,2},{8,12},{10,14},{12,8},{14,10},{1,5},{3,7},... | collective-permute-start | bytes 12296 | tf_op jit(solution)/shard_map/ppermute | solution.py:15
  39.2 3.1 %reshape.300 = bf16[32,6,32,32]{3,2,0,1:T(8,128)(2,1)} reshape(bf16[32,6,1024]{2,0,1:T(8,128)(2,1)} %param.24) | data formatting | bytes 786432 | tf_op jit(solution)/shard_map/reshape | solution.py:135
  42.5 11.9 %collective-permute-start.3 = (f32[32,32]{0,1:T(8,128)S(1)}, f32[32,32]{0,1:T(8,128)S(1)}, u32[]{:S(2)}, u32[]{:S(2)}) collective-permute-start(f32[32,32]{0,1:T(8,128)S(1)} %fusion.76), channel_id=1, source_target_pairs={{0,8},{2,10},{4,12},{6,14},{8,0},{10,2},{12,4},{14,6},{1,9},{3,11}... | collective-permute-start | bytes 12296 | tf_op jit(solution)/shard_map/ppermute | solution.py:15
  54.4 4.4 %reshape.301 = bf16[32,6,64,64]{3,2,0,1:T(8,128)(2,1)} reshape(bf16[32,6,4096]{2,0,1:T(8,128)(2,1)S(1)} %copy-done.3) | data formatting | bytes 3145728 | tf_op jit(solution)/shard_map/reshape | solution.py:132
  59.2 3.6 %collective-permute-start.4 = (f32[32,32]{0,1:T(8,128)S(1)}, f32[32,32]{0,1:T(8,128)S(1)}, u32[]{:S(2)}, u32[]{:S(2)}) collective-permute-start(f32[32,32]{0,1:T(8,128)S(1)} %fusion.73), channel_id=1, source_target_pairs={{0,16},{16,0},{32,48},{48,32},{64,80},{80,64},{96,112},{112,96},{1... | collective-permute-start | bytes 12296 | tf_op jit(solution)/shard_map/ppermute | solution.py:15
  63.0 1.8 %collective-permute-done.4 = f32[32,32]{0,1:T(8,128)S(1)} collective-permute-done((f32[32,32]{0,1:T(8,128)S(1)}, f32[32,32]{0,1:T(8,128)S(1)}, u32[]{:S(2)}, u32[]{:S(2)}) %collective-permute-start.4) | collective-permute-done | bytes 4128 | tf_op jit(solution)/shard_map/ppermute | solution.py:15
  65.1 4.7 %collective-permute-start.5 = (f32[32,32]{0,1:T(8,128)S(1)}, f32[32,32]{0,1:T(8,128)S(1)}, u32[]{:S(2)}, u32[]{:S(2)}) collective-permute-start(f32[32,32]{0,1:T(8,128)S(1)} %fusion.70), channel_id=1, source_target_pairs={{0,32},{16,48},{32,0},{48,16},{64,96},{80,112},{96,64},{112,80},{1... | collective-permute-start | bytes 12296 | tf_op jit(solution)/shard_map/ppermute | solution.py:15
  70.5 1.0 copy.182
  72.3 1.3 collective-permute-start.8
  73.6 3.0 %collective-permute-start.7 = (bf16[32,32,32]{1,2,0:T(8,128)(2,1)S(1)}, bf16[32,32,32]{1,2,0:T(8,128)(2,1)S(1)}, u32[]{:S(2)}, u32[]{:S(2)}) collective-permute-start(bf16[32,32,32]{1,2,0:T(8,128)(2,1)S(1)} %convert_bitcast_fusion), channel_id=1, source_target_pairs={{0,1},{1,2},{2,3},{3,4},{4,5},{5,6},{6,7},{7,8},{8,9},{9,10},{10,1... | collective-permute-start | bytes 196616 | tf_op jit(solution)/shard_map/ppermute | solution.py:24
  76.7 1.3 collective-permute-start.12
  78.0 4.9 %collective-permute-start.11 = (bf16[32,32,64]{2,0,1:T(8,128)(2,1)S(1)}, bf16[32,32,64]{2,0,1:T(8,128)(2,1)}, u32[]{:S(2)}, u32[]{:S(2)}) collective-permute-start(bf16[32,32,64]{2,0,1:T(8,128)(2,1)S(1)} %select_convert_fusion), channel_id=1, source_target_pairs={{0,1},{1,2},{2,3},{3,4},{4,5},{5,6},{6,7},{7,8},{8,9},{9,10},{10,1... | collective-permute-start | bytes 393224 | tf_op jit(solution)/shard_map/ppermute | solution.py:24
  83.0 6.4 %collective-permute-start.6 = (f32[32,32]{0,1:T(8,128)S(1)}, f32[32,32]{0,1:T(8,128)}, u32[]{:S(2)}, u32[]{:S(2)}) collective-permute-start(f32[32,32]{0,1:T(8,128)S(1)} %fusion.67), channel_id=1, source_target_pairs={{0,64},{16,80},{32,96},{48,112},{64,0},{80,16},{96,32},{112,48},{1... | collective-permute-start | bytes 12296 | tf_op jit(solution)/shard_map/ppermute | solution.py:15
  90.0 2.0 %gather_fusion.1 = bf16[192,32,32]{2,1,0:T(8,128)(2,1)} fusion(bf16[96,32,32]{2,1,0:T(8,128)(2,1)S(1)} %copy.184, s32[1024]{0:T(1024)S(1)} %pad_clamp_fusion.1), kind=kCustom, calls=%fused_computation.1 | custom fusion | bytes 787200 | tf_op jit(solution)/shard_map/gather | solution.py:139
  93.7 3.5 %collective-permute-start.9 = (f32[32,32]{0,1:T(8,128)S(1)}, f32[32,32]{0,1:T(8,128)S(1)}, u32[]{:S(2)}, u32[]{:S(2)}) collective-permute-start(f32[32,32]{0,1:T(8,128)S(1)} %fusion.64), channel_id=1, source_target_pairs={{0,128},{128,0},{256,384},{384,256},{512,640},{640,512},{768,896},... | collective-permute-start | bytes 12296 | tf_op jit(solution)/shard_map/ppermute | solution.py:15
  97.2 5.0 %fusion.12 = f32[32,32,32]{2,1,0:T(8,128)} fusion(bf16[32,6,32,32]{3,2,0,1:T(8,128)(2,1)} %reshape.300, bf16[32,6,32,32]{3,2,1,0:T(8,128)(2,1)} %bitcast.217, f32[32,6]{1,0:T(8,128)S(1)} %copy-done.23), kind=kOutput, calls=%fused_computation.16 | convolution fusion | flops 75890688 | bytes 918272 | tf_op jit(solution)/shard_map/lkab,lkbc->lac/dot_general | solution.py:144
  102.4 4.2 %collective-permute-start.10 = (f32[32,32]{0,1:T(8,128)S(1)}, f32[32,32]{0,1:T(8,128)}, u32[]{:S(2)}, u32[]{:S(2)}) collective-permute-start(f32[32,32]{0,1:T(8,128)S(1)} %fusion.61), channel_id=1, source_target_pairs={{0,256},{128,384},{256,0},{384,128},{512,768},{640,896},{768,512},... | collective-permute-start | bytes 12296 | tf_op jit(solution)/shard_map/ppermute | solution.py:15
  106.7 1.1 pad_maximum_fusion.1
  110.2 4.1 %collective-permute-start.13 = (f32[32,32]{0,1:T(8,128)S(1)}, f32[32,32]{0,1:T(8,128)}, u32[]{:S(2)}, u32[]{:S(2)}) collective-permute-start(f32[32,32]{0,1:T(8,128)S(1)} %fusion.58), channel_id=1, source_target_pairs={{0,512},{128,640},{256,768},{384,896},{512,0},{640,128},{768,256},... | collective-permute-start | bytes 12296 | tf_op jit(solution)/shard_map/ppermute | solution.py:15
  114.3 4.6 %fusion.7 = f32[32,32,64]{2,0,1:T(8,128)S(1)} fusion(bf16[32,6,64,64]{3,2,0,1:T(8,128)(2,1)} %reshape.301, bf16[32,32,6,64]{3,0,2,1:T(8,128)(2,1)S(1)} %bitcast.215, f32[32,6]{1,0:T(8,128)} %copy.189), kind=kOutput, calls=%fused_computation.12 | convolution fusion | flops 302776320 | bytes 2622208 | tf_op jit(solution)/shard_map/lkpq,clkq->clp/dot_general | solution.py:153
  118.9 1.1 collective-permute-done.13
  121.1 1.0 fusion.15
  123.3 6.0 %scatter_custom_fusion = f32[32,2048]{0,1:T(8,128)S(1)} fusion(s32[2048]{0:T(1024)} %bitcast.228, f32[2048,32]{1,0:T(8,128)S(1)} %copy.194, f32[]{:T(128)} %constant.13.clone.1), kind=kCustom, calls=%fused_computation.25 | custom fusion | bytes 262656 | tf_op jit(solution)/shard_map/scatter | solution.py:180
  129.7 1.0 copy.195
  (160 shorter events, 21.6 us)
Async XLA Ops:
  0.6 121.5 %copy-start = (bf16[32,64,32]{1,2,0:T(8,128)(2,1)S(1)}, bf16[32,64,32]{1,2,0:T(8,128)(2,1)}, u32[]{:S(2)}) copy-start(bf16[32,64,32]{1,2,0:T(8,128)(2,1)} %param.20) | copy-start | bytes 393220
  0.7 3.5 %copy-start.6 = (f32[16,2048]{1,0:T(8,128)S(1)}, f32[16,2048]{1,0:T(8,128)}, u32[]{:S(2)}) copy-start(f32[16,2048]{1,0:T(8,128)} %param.17) | copy-start | bytes 393220
  0.7 3.5 %copy-start.7 = (f32[16,2048]{1,0:T(8,128)S(1)}, f32[16,2048]{1,0:T(8,128)}, u32[]{:S(2)}) copy-start(f32[16,2048]{1,0:T(8,128)} %param.16) | copy-start | bytes 393220
  15.5 8.3 %collective-permute-start = (f32[32,32]{0,1:T(8,128)S(1)}, f32[32,32]{0,1:T(8,128)S(1)}, u32[]{:S(2)}, u32[]{:S(2)}) collective-permute-start(f32[32,32]{0,1:T(8,128)S(1)} %fusion.91), channel_id=1, source_target_pairs={{0,1},{1,0},{2,3},{3,2},{4,5},{5,4},{6,7},{7,6},{8,9},{9,8},{10,11... | collective-permute-start | bytes 12296 | tf_op jit(solution)/shard_map/ppermute | solution.py:15
  21.9 7.5 %copy-start.25 = (s32[32,6]{0,1:T(8,128)S(1)}, s32[32,6]{0,1:T(8,128)}, u32[]{:S(2)}) copy-start(s32[32,6]{0,1:T(8,128)} %param.23) | copy-start | bytes 2308
  21.9 7.5 %copy-start.27 = (f32[32,6]{0,1:T(8,128)S(1)}, f32[32,6]{0,1:T(8,128)}, u32[]{:S(2)}) copy-start(f32[32,6]{0,1:T(8,128)} %param.22) | copy-start | bytes 2308
  23.8 30.6 %copy-start.3 = (bf16[32,6,4096]{2,0,1:T(8,128)(2,1)S(1)}, bf16[32,6,4096]{2,0,1:T(8,128)(2,1)}, u32[]{:S(2)}) copy-start(bf16[32,6,4096]{2,0,1:T(8,128)(2,1)} %param.21) | copy-start | bytes 4718596
  23.8 35.0 %copy-start.8 = (f32[32,32]{0,1:T(8,128)}, f32[32,32]{0,1:T(8,128)S(1)}, u32[]{:S(2)}) copy-start(f32[32,32]{0,1:T(8,128)S(1)} %collective-permute-done) | copy-start | bytes 12292
  24.0 7.0 %collective-permute-start.1 = (f32[32,32]{0,1:T(8,128)S(1)}, f32[32,32]{0,1:T(8,128)S(1)}, u32[]{:S(2)}, u32[]{:S(2)}) collective-permute-start(f32[32,32]{0,1:T(8,128)S(1)} %fusion.85), channel_id=1, source_target_pairs={{0,2},{2,0},{4,6},{6,4},{8,10},{10,8},{12,14},{14,12},{1,3},{3,1},... | collective-permute-start | bytes 12296 | tf_op jit(solution)/shard_map/ppermute | solution.py:15
  31.1 27.7 %copy-start.10 = (f32[32,32]{0,1:T(8,128)}, f32[32,32]{0,1:T(8,128)S(1)}, u32[]{:S(2)}) copy-start(f32[32,32]{0,1:T(8,128)S(1)} %collective-permute-done.1) | copy-start | bytes 12292
  31.3 11.0 %collective-permute-start.2 = (f32[32,32]{0,1:T(8,128)S(1)}, f32[32,32]{0,1:T(8,128)S(1)}, u32[]{:S(2)}, u32[]{:S(2)}) collective-permute-start(f32[32,32]{0,1:T(8,128)S(1)} %fusion.79), channel_id=1, source_target_pairs={{0,4},{2,6},{4,0},{6,2},{8,12},{10,14},{12,8},{14,10},{1,5},{3,7},... | collective-permute-start | bytes 12296 | tf_op jit(solution)/shard_map/ppermute | solution.py:15
  42.3 16.5 %copy-start.12 = (f32[32,32]{0,1:T(8,128)}, f32[32,32]{0,1:T(8,128)S(1)}, u32[]{:S(2)}) copy-start(f32[32,32]{0,1:T(8,128)S(1)} %collective-permute-done.2) | copy-start | bytes 12292
  42.5 16.5 %collective-permute-start.3 = (f32[32,32]{0,1:T(8,128)S(1)}, f32[32,32]{0,1:T(8,128)S(1)}, u32[]{:S(2)}, u32[]{:S(2)}) collective-permute-start(f32[32,32]{0,1:T(8,128)S(1)} %fusion.76), channel_id=1, source_target_pairs={{0,8},{2,10},{4,12},{6,14},{8,0},{10,2},{12,4},{14,6},{1,9},{3,11}... | collective-permute-start | bytes 12296 | tf_op jit(solution)/shard_map/ppermute | solution.py:15
  59.0 10.8 %copy-start.14 = (f32[32,32]{0,1:T(8,128)}, f32[32,32]{0,1:T(8,128)S(1)}, u32[]{:S(2)}) copy-start(f32[32,32]{0,1:T(8,128)S(1)} %collective-permute-done.3) | copy-start | bytes 12292
  59.2 5.6 %collective-permute-start.4 = (f32[32,32]{0,1:T(8,128)S(1)}, f32[32,32]{0,1:T(8,128)S(1)}, u32[]{:S(2)}, u32[]{:S(2)}) collective-permute-start(f32[32,32]{0,1:T(8,128)S(1)} %fusion.73), channel_id=1, source_target_pairs={{0,16},{16,0},{32,48},{48,32},{64,80},{80,64},{96,112},{112,96},{1... | collective-permute-start | bytes 12296 | tf_op jit(solution)/shard_map/ppermute | solution.py:15
  64.9 5.7 %copy-start.15 = (f32[32,32]{0,1:T(8,128)}, f32[32,32]{0,1:T(8,128)S(1)}, u32[]{:S(2)}) copy-start(f32[32,32]{0,1:T(8,128)S(1)} %collective-permute-done.4) | copy-start | bytes 12292
  65.1 17.8 %collective-permute-start.5 = (f32[32,32]{0,1:T(8,128)S(1)}, f32[32,32]{0,1:T(8,128)S(1)}, u32[]{:S(2)}, u32[]{:S(2)}) collective-permute-start(f32[32,32]{0,1:T(8,128)S(1)} %fusion.70), channel_id=1, source_target_pairs={{0,32},{16,48},{32,0},{48,16},{64,96},{80,112},{96,64},{112,80},{1... | collective-permute-start | bytes 12296 | tf_op jit(solution)/shard_map/ppermute | solution.py:15
  72.3 17.1 %collective-permute-start.8 = (bf16[32,32,32]{1,2,0:T(8,128)(2,1)S(1)}, bf16[32,32,32]{1,2,0:T(8,128)(2,1)S(1)}, u32[]{:S(2)}, u32[]{:S(2)}) collective-permute-start(bf16[32,32,32]{1,2,0:T(8,128)(2,1)S(1)} %convert_bitcast_fusion), channel_id=1, source_target_pairs={{1,0},{2,1},{3,2},{4,3},{5,4},{6,5},{7,6},{8,7},{9,8},{10,9},{11,1... | collective-permute-start | bytes 196616 | tf_op jit(solution)/shard_map/ppermute | solution.py:25
  73.6 15.8 %collective-permute-start.7 = (bf16[32,32,32]{1,2,0:T(8,128)(2,1)S(1)}, bf16[32,32,32]{1,2,0:T(8,128)(2,1)S(1)}, u32[]{:S(2)}, u32[]{:S(2)}) collective-permute-start(bf16[32,32,32]{1,2,0:T(8,128)(2,1)S(1)} %convert_bitcast_fusion), channel_id=1, source_target_pairs={{0,1},{1,2},{2,3},{3,4},{4,5},{5,6},{6,7},{7,8},{8,9},{9,10},{10,1... | collective-permute-start | bytes 196616 | tf_op jit(solution)/shard_map/ppermute | solution.py:24
  76.7 30.0 %collective-permute-start.12 = (bf16[32,32,64]{2,0,1:T(8,128)(2,1)S(1)}, bf16[32,32,64]{2,0,1:T(8,128)(2,1)S(1)}, u32[]{:S(2)}, u32[]{:S(2)}) collective-permute-start(bf16[32,32,64]{2,0,1:T(8,128)(2,1)S(1)} %select_convert_fusion), channel_id=1, source_target_pairs={{1,0},{2,1},{3,2},{4,3},{5,4},{6,5},{7,6},{8,7},{9,8},{10,9},{11,1... | collective-permute-start | bytes 393224 | tf_op jit(solution)/shard_map/ppermute | solution.py:25
  78.0 28.7 %collective-permute-start.11 = (bf16[32,32,64]{2,0,1:T(8,128)(2,1)S(1)}, bf16[32,32,64]{2,0,1:T(8,128)(2,1)}, u32[]{:S(2)}, u32[]{:S(2)}) collective-permute-start(bf16[32,32,64]{2,0,1:T(8,128)(2,1)S(1)} %select_convert_fusion), channel_id=1, source_target_pairs={{0,1},{1,2},{2,3},{3,4},{4,5},{5,6},{6,7},{7,8},{8,9},{9,10},{10,1... | collective-permute-start | bytes 393224 | tf_op jit(solution)/shard_map/ppermute | solution.py:24
  82.8 6.6 %copy-start.16 = (f32[32,32]{0,1:T(8,128)}, f32[32,32]{0,1:T(8,128)S(1)}, u32[]{:S(2)}) copy-start(f32[32,32]{0,1:T(8,128)S(1)} %collective-permute-done.5) | copy-start | bytes 12292
  83.0 9.7 %collective-permute-start.6 = (f32[32,32]{0,1:T(8,128)S(1)}, f32[32,32]{0,1:T(8,128)}, u32[]{:S(2)}, u32[]{:S(2)}) collective-permute-start(f32[32,32]{0,1:T(8,128)S(1)} %fusion.67), channel_id=1, source_target_pairs={{0,64},{16,80},{32,96},{48,112},{64,0},{80,16},{96,32},{112,48},{1... | collective-permute-start | bytes 12296 | tf_op jit(solution)/shard_map/ppermute | solution.py:15
  90.0 7.2 %copy-start.23 = (f32[32,6]{1,0:T(8,128)S(1)}, f32[32,6]{1,0:T(8,128)}, u32[]{:S(2)}) copy-start(f32[32,6]{1,0:T(8,128)} %copy.185) | copy-start | bytes 2308
  93.7 8.5 %collective-permute-start.9 = (f32[32,32]{0,1:T(8,128)S(1)}, f32[32,32]{0,1:T(8,128)S(1)}, u32[]{:S(2)}, u32[]{:S(2)}) collective-permute-start(f32[32,32]{0,1:T(8,128)S(1)} %fusion.64), channel_id=1, source_target_pairs={{0,128},{128,0},{256,384},{384,256},{512,640},{640,512},{768,896},... | collective-permute-start | bytes 12296 | tf_op jit(solution)/shard_map/ppermute | solution.py:15
  102.2 4.5 %copy-start.17 = (f32[32,32]{0,1:T(8,128)}, f32[32,32]{0,1:T(8,128)S(1)}, u32[]{:S(2)}) copy-start(f32[32,32]{0,1:T(8,128)S(1)} %collective-permute-done.9) | copy-start | bytes 12292
  102.4 6.8 %collective-permute-start.10 = (f32[32,32]{0,1:T(8,128)S(1)}, f32[32,32]{0,1:T(8,128)}, u32[]{:S(2)}, u32[]{:S(2)}) collective-permute-start(f32[32,32]{0,1:T(8,128)S(1)} %fusion.61), channel_id=1, source_target_pairs={{0,256},{128,384},{256,0},{384,128},{512,768},{640,896},{768,512},... | collective-permute-start | bytes 12296 | tf_op jit(solution)/shard_map/ppermute | solution.py:15
  110.2 9.8 %copy-start.9 = (f32[32,32]{0,1:T(8,128)S(1)}, f32[32,32]{0,1:T(8,128)}, u32[]{:S(2)}) copy-start(f32[32,32]{0,1:T(8,128)} %copy-done.8) | copy-start | bytes 12292
  110.2 9.8 %copy-start.11 = (f32[32,32]{0,1:T(8,128)S(1)}, f32[32,32]{0,1:T(8,128)}, u32[]{:S(2)}) copy-start(f32[32,32]{0,1:T(8,128)} %copy-done.10) | copy-start | bytes 12292
  110.2 9.8 %copy-start.13 = (f32[32,32]{0,1:T(8,128)S(1)}, f32[32,32]{0,1:T(8,128)}, u32[]{:S(2)}) copy-start(f32[32,32]{0,1:T(8,128)} %copy-done.12) | copy-start | bytes 12292
  110.2 10.9 %copy-start.4 = (f32[32,32,32]{2,1,0:T(8,128)S(1)}, f32[32,32,32]{2,1,0:T(8,128)}, u32[]{:S(2)}) copy-start(f32[32,32,32]{2,1,0:T(8,128)} %fusion.12) | copy-start | bytes 393220
  110.2 9.8 %collective-permute-start.13 = (f32[32,32]{0,1:T(8,128)S(1)}, f32[32,32]{0,1:T(8,128)}, u32[]{:S(2)}, u32[]{:S(2)}) collective-permute-start(f32[32,32]{0,1:T(8,128)S(1)} %fusion.58), channel_id=1, source_target_pairs={{0,512},{128,640},{256,768},{384,896},{512,0},{640,128},{768,256},... | collective-permute-start | bytes 12296 | tf_op jit(solution)/shard_map/ppermute | solution.py:15
  (10 other events, 22.2 us)

commit v13 on v12

--- a/solution.py
+++ b/solution.py
@@ -67,9 +67,9 @@
     def pick(table, side_col):
         return jnp.where(side_col[:, None, None] == 1, table[1][None], table[0][None])
 
-    def field_weights(side_col):
+    def field_weights(side_col, row_table, cpl_table):
         level_count = side_col.shape[0]
-        row_sel = pick(up_row, side_col)
+        row_sel = pick(row_table, side_col)
         eye = jnp.broadcast_to(jnp.eye(rank_width, dtype=jnp.float32), row_sel.shape)
         prefix = row_sel
         shift = 1
@@ -78,7 +78,7 @@
             prefix = apply_down(earlier, prefix)
             shift *= 2
         before = jnp.concatenate([eye[:1], prefix[:-1]], axis=0)
-        weights = apply_down(before, pick(up_cpl, side_col))
+        weights = apply_down(before, pick(cpl_table, side_col))
         return weights.transpose(1, 0, 2).reshape(rank_width, level_count * rank_width)
 
     def climb_tree(root_coeff, stages, results):
@@ -97,7 +97,7 @@
                 stacked = jnp.concatenate([current, sibling], axis=0)
                 current = apply_up(own_first[level], stacked)
         stacked = jnp.concatenate(siblings, axis=0)
-        return apply_down(field_weights(side_col), stacked)
+        return apply_down(results["late"][1], stacked)
 
     def apply_image(vectors):
         columns = vectors.shape[0]
@@ -152,9 +152,10 @@
             scaled = results["near_pick"].astype(jnp.float32) * near_weight[None, :, :, None]
             return jnp.einsum("lkpq,clkq->clp", results["near_sq"], scaled, precision=best_precision)
 
+        side_col = jnp.stack([side for _, _, side in climb_sides()])
         stages = [
-            ("spare_a", lambda: jnp.zeros((), jnp.float32)),
-            ("paths", leaf_paths),
+            ("w_in", lambda: (up_row, up_cpl)),
+            ("late", lambda: (leaf_paths(), field_weights(side_col, *results["w_in"]))),
             ("far_sq", far_square),
             ("near_sq", near_square),
             ("win_in", lambda: (leaf_blocks, leaf_round)),
@@ -168,7 +169,7 @@
         for key, stage in stages:
             if key not in results:
                 results[key] = stage()
-        paths = results["paths"]
+        paths = results["late"][0]
         near_sum = results["near_sum"]
         local_field = apply_down(paths, jnp.broadcast_to(root_field, (leaves_dev,) + root_field.shape))
         leaf_field = local_field + results["far_sum"]

time: 134 us -> 133 us (level)
  other arithmetic: 2.52 us -> 5.1 us
  waiting for transfers between devices: 5.79 us -> 4.14 us
    ppermute x10, waiting for transfers between devices: 5.78 us -> 4.13 us  [from_partner(): return lax.ppermute(value, axis, pairs)]
    unnamed x68 -> x76, local copies, waits for them, and re-layouts: 5.5 us -> 5.53 us
  transfers between devices with their start and end apart: 14 -> 14, of which waited for: 5 -> 4; matrix products, arithmetic and copies ran while one was open for 24% -> 25% of each run, Pallas kernels for 0% -> 0%
where the time goes in v13:
time: 133 us; the launch traced here: 131 us
  starting transfers between devices  63.6 us (48%)
  local copies, waits for them, and re-layouts  37.4 us (28%)
  matrix products  18.5 us (14%)
  other arithmetic  5.1 us (4%)
  waiting for transfers between devices  4.14 us (3%)
  between operations  1.77 us (1%)
    ppermute x10, starting transfers between devices, from_partner(): return lax.ppermute(value, axis, pairs)  53.6 us
    ppermute x2, starting transfers between devices, extended(): low = lax.ppermute(block, axis, forward)  7.49 us
    gather x2, local copies, waits for them, and re-layouts, apply_image(): ordered = jnp.take(vectors, order_row, axis=1).astype(jnp.bfloat16)  6.4 us
    scatter x1, local copies, waits for them, and re-layouts, apply_image(): return jnp.zeros_like(image).at[:, order_row].set(image)  5.97 us
    unnamed x76, local copies, waits for them, and re-layouts  5.53 us
    dot_general x1, matrix products, far_sum(): jnp.einsum('lkab,lkbc->lac', results['far_sq'], scaled, precision=best_pr...  4.96 us
    dot_general x1, matrix products, near_total(): jnp.einsum('lkpq,clkq->clp', results['near_sq'], scaled, precision=best_p...  4.58 us
    dot_general x14, matrix products, apply_up(): jnp.einsum('...ab,...ac->...bc', matrix, coeffs, precision=best_precision)  4.39 us
  transfers between devices with their start and end apart: 14, of which 4 were waited for; matrix products, arithmetic and copies ran while one was open for 25% of the time, Pallas kernels for 0%

profile of v13, /device:TPU:14, one launch (start us, length us, event | category | flops | bytes accessed | tf_op | source)
XLA Modules:
  0.0 130.6 jit_solution(6952470279361540173)
XLA Ops:
  0.7 1.1 slice.179
  1.8 1.1 slice.183
  2.9 1.1 slice.187
  4.8 6.2 %gather_fusion = bf16[2048,32]{1,0:T(8,128)(2,1)S(1)} fusion(bf16[32,2048]{0,1:T(8,128)(2,1)S(1)} %copy.161, s32[2048]{0:T(1024)S(1)} %broadcast_clamp_fusion), kind=kCustom, calls=%fused_computation | custom fusion | bytes 270336 | tf_op jit(solution)/shard_map/jit(_take)/gather | solution.py:104
  15.5 1.9 %collective-permute-start = (f32[32,32]{0,1:T(8,128)S(1)}, f32[32,32]{0,1:T(8,128)S(1)}, u32[]{:S(2)}, u32[]{:S(2)}) collective-permute-start(f32[32,32]{0,1:T(8,128)S(1)} %fusion.91), channel_id=1, source_target_pairs={{0,1},{1,0},{2,3},{3,2},{4,5},{5,4},{6,7},{7,6},{8,9},{9,8},{10,11... | collective-permute-start | bytes 12296 | tf_op jit(solution)/shard_map/ppermute | solution.py:15
  23.6 5.2 %collective-permute-start.1 = (f32[32,32]{0,1:T(8,128)S(1)}, f32[32,32]{0,1:T(8,128)S(1)}, u32[]{:S(2)}, u32[]{:S(2)}) collective-permute-start(f32[32,32]{0,1:T(8,128)S(1)} %fusion.85), channel_id=1, source_target_pairs={{0,2},{2,0},{4,6},{6,4},{8,10},{10,8},{12,14},{14,12},{1,3},{3,1},... | collective-permute-start | bytes 12296 | tf_op jit(solution)/shard_map/ppermute | solution.py:15
  31.0 8.1 %collective-permute-start.2 = (f32[32,32]{0,1:T(8,128)S(1)}, f32[32,32]{0,1:T(8,128)S(1)}, u32[]{:S(2)}, u32[]{:S(2)}) collective-permute-start(f32[32,32]{0,1:T(8,128)S(1)} %fusion.79), channel_id=1, source_target_pairs={{0,4},{2,6},{4,0},{6,2},{8,12},{10,14},{12,8},{14,10},{1,5},{3,7},... | collective-permute-start | bytes 12296 | tf_op jit(solution)/shard_map/ppermute | solution.py:15
  39.7 3.1 %reshape.300 = bf16[32,6,32,32]{3,2,0,1:T(8,128)(2,1)} reshape(bf16[32,6,1024]{2,0,1:T(8,128)(2,1)} %param.24) | data formatting | bytes 786432 | tf_op jit(solution)/shard_map/reshape | solution.py:135
  43.0 11.8 %collective-permute-start.3 = (f32[32,32]{0,1:T(8,128)S(1)}, f32[32,32]{0,1:T(8,128)S(1)}, u32[]{:S(2)}, u32[]{:S(2)}) collective-permute-start(f32[32,32]{0,1:T(8,128)S(1)} %fusion.76), channel_id=1, source_target_pairs={{0,8},{2,10},{4,12},{6,14},{8,0},{10,2},{12,4},{14,6},{1,9},{3,11}... | collective-permute-start | bytes 12296 | tf_op jit(solution)/shard_map/ppermute | solution.py:15
  54.9 4.3 %reshape.301 = bf16[32,6,64,64]{3,2,0,1:T(8,128)(2,1)} reshape(bf16[32,6,4096]{2,0,1:T(8,128)(2,1)S(1)} %copy-done.3) | data formatting | bytes 3145728 | tf_op jit(solution)/shard_map/reshape | solution.py:132
  59.7 3.6 %collective-permute-start.4 = (f32[32,32]{0,1:T(8,128)S(1)}, f32[32,32]{0,1:T(8,128)S(1)}, u32[]{:S(2)}, u32[]{:S(2)}) collective-permute-start(f32[32,32]{0,1:T(8,128)S(1)} %fusion.73), channel_id=1, source_target_pairs={{0,16},{16,0},{32,48},{48,32},{64,80},{80,64},{96,112},{112,96},{1... | collective-permute-start | bytes 12296 | tf_op jit(solution)/shard_map/ppermute | solution.py:15
  63.5 1.8 %collective-permute-done.4 = f32[32,32]{0,1:T(8,128)S(1)} collective-permute-done((f32[32,32]{0,1:T(8,128)S(1)}, f32[32,32]{0,1:T(8,128)S(1)}, u32[]{:S(2)}, u32[]{:S(2)}) %collective-permute-start.4) | collective-permute-done | bytes 4128 | tf_op jit(solution)/shard_map/ppermute | solution.py:15
  65.6 4.7 %collective-permute-start.5 = (f32[32,32]{0,1:T(8,128)S(1)}, f32[32,32]{0,1:T(8,128)S(1)}, u32[]{:S(2)}, u32[]{:S(2)}) collective-permute-start(f32[32,32]{0,1:T(8,128)S(1)} %fusion.70), channel_id=1, source_target_pairs={{0,32},{16,48},{32,0},{48,16},{64,96},{80,112},{96,64},{112,80},{1... | collective-permute-start | bytes 12296 | tf_op jit(solution)/shard_map/ppermute | solution.py:15
  71.7 1.3 collective-permute-start.8
  73.0 3.0 %collective-permute-start.7 = (bf16[32,32,32]{1,2,0:T(8,128)(2,1)S(1)}, bf16[32,32,32]{1,2,0:T(8,128)(2,1)S(1)}, u32[]{:S(2)}, u32[]{:S(2)}) collective-permute-start(bf16[32,32,32]{1,2,0:T(8,128)(2,1)S(1)} %copy-done.4), channel_id=1, source_target_pairs={{0,1},{1,2},{2,3},{3,4},{4,5},{5,6},{6,7},{7,8},{8,9},{9,10},{10,1... | collective-permute-start | bytes 196616 | tf_op jit(solution)/shard_map/ppermute | solution.py:24
  76.1 1.3 collective-permute-start.12
  77.4 4.4 %collective-permute-start.11 = (bf16[32,32,64]{2,0,1:T(8,128)(2,1)S(1)}, bf16[32,32,64]{2,0,1:T(8,128)(2,1)}, u32[]{:S(2)}, u32[]{:S(2)}) collective-permute-start(bf16[32,32,64]{2,0,1:T(8,128)(2,1)S(1)} %select_convert_fusion), channel_id=1, source_target_pairs={{0,1},{1,2},{2,3},{3,4},{4,5},{5,6},{6,7},{7,8},{8,9},{9,10},{10,1... | collective-permute-start | bytes 393224 | tf_op jit(solution)/shard_map/ppermute | solution.py:24
  82.0 6.4 %collective-permute-start.6 = (f32[32,32]{0,1:T(8,128)S(1)}, f32[32,32]{0,1:T(8,128)}, u32[]{:S(2)}, u32[]{:S(2)}) collective-permute-start(f32[32,32]{0,1:T(8,128)S(1)} %fusion.67), channel_id=1, source_target_pairs={{0,64},{16,80},{32,96},{48,112},{64,0},{80,16},{96,32},{112,48},{1... | collective-permute-start | bytes 12296 | tf_op jit(solution)/shard_map/ppermute | solution.py:15
  89.0 2.0 %gather_fusion.1 = bf16[192,32,32]{2,1,0:T(8,128)(2,1)} fusion(bf16[96,32,32]{2,1,0:T(8,128)(2,1)S(1)} %copy.184, s32[1024]{0:T(1024)S(1)} %pad_clamp_fusion.1), kind=kCustom, calls=%fused_computation.1 | custom fusion | bytes 787200 | tf_op jit(solution)/shard_map/gather | solution.py:139
  91.8 0.9 fusion.64
  92.7 3.5 %collective-permute-start.9 = (f32[32,32]{0,1:T(8,128)S(1)}, f32[32,32]{0,1:T(8,128)S(1)}, u32[]{:S(2)}, u32[]{:S(2)}) collective-permute-start(f32[32,32]{0,1:T(8,128)S(1)} %fusion.64), channel_id=1, source_target_pairs={{0,128},{128,0},{256,384},{384,256},{512,640},{640,512},{768,896},... | collective-permute-start | bytes 12296 | tf_op jit(solution)/shard_map/ppermute | solution.py:15
  96.2 5.0 %fusion.12 = f32[32,32,32]{2,1,0:T(8,128)} fusion(bf16[32,6,32,32]{3,2,0,1:T(8,128)(2,1)} %reshape.300, bf16[32,6,32,32]{3,2,1,0:T(8,128)(2,1)} %bitcast.217, f32[32,6]{1,0:T(8,128)S(1)} %copy-done.26), kind=kOutput, calls=%fused_computation.16 | convolution fusion | flops 75890688 | bytes 918272 | tf_op jit(solution)/shard_map/lkab,lkbc->lac/dot_general | solution.py:144
  101.4 4.2 %collective-permute-start.10 = (f32[32,32]{0,1:T(8,128)S(1)}, f32[32,32]{0,1:T(8,128)}, u32[]{:S(2)}, u32[]{:S(2)}) collective-permute-start(f32[32,32]{0,1:T(8,128)S(1)} %fusion.61), channel_id=1, source_target_pairs={{0,256},{128,384},{256,0},{384,128},{512,768},{640,896},{768,512},... | collective-permute-start | bytes 12296 | tf_op jit(solution)/shard_map/ppermute | solution.py:15
  105.7 1.1 pad_maximum_fusion.1
  108.2 0.9 fusion.58
  109.2 4.1 %collective-permute-start.13 = (f32[32,32]{0,1:T(8,128)S(1)}, f32[32,32]{0,1:T(8,128)}, u32[]{:S(2)}, u32[]{:S(2)}) collective-permute-start(f32[32,32]{0,1:T(8,128)S(1)} %fusion.58), channel_id=1, source_target_pairs={{0,512},{128,640},{256,768},{384,896},{512,0},{640,128},{768,256},... | collective-permute-start | bytes 12296 | tf_op jit(solution)/shard_map/ppermute | solution.py:15
  113.3 4.6 %fusion.7 = f32[32,32,64]{2,0,1:T(8,128)S(1)} fusion(bf16[32,6,64,64]{3,2,0,1:T(8,128)(2,1)} %reshape.301, bf16[32,32,6,64]{3,0,2,1:T(8,128)(2,1)S(1)} %bitcast.215, f32[32,6]{1,0:T(8,128)} %copy.189), kind=kOutput, calls=%fused_computation.12 | convolution fusion | flops 302776320 | bytes 2622208 | tf_op jit(solution)/shard_map/lkpq,clkq->clp/dot_general | solution.py:153
  117.9 1.1 collective-permute-done.13
  120.1 1.0 fusion.15
  122.3 6.0 %scatter_custom_fusion = f32[32,2048]{0,1:T(8,128)S(1)} fusion(s32[2048]{0:T(1024)} %bitcast.228, f32[2048,32]{1,0:T(8,128)S(1)} %copy.194, f32[]{:T(128)} %constant.13.clone.1), kind=kCustom, calls=%fused_computation.25 | custom fusion | bytes 262656 | tf_op jit(solution)/shard_map/scatter | solution.py:181
  128.7 1.0 copy.195
  129.6 1.0 copy.196
  (168 shorter events, 21.9 us)
Async XLA Ops:
  0.6 120.5 %copy-start = (bf16[32,64,32]{1,2,0:T(8,128)(2,1)S(1)}, bf16[32,64,32]{1,2,0:T(8,128)(2,1)}, u32[]{:S(2)}) copy-start(bf16[32,64,32]{1,2,0:T(8,128)(2,1)} %param.20) | copy-start | bytes 393220
  15.5 7.6 %collective-permute-start = (f32[32,32]{0,1:T(8,128)S(1)}, f32[32,32]{0,1:T(8,128)S(1)}, u32[]{:S(2)}, u32[]{:S(2)}) collective-permute-start(f32[32,32]{0,1:T(8,128)S(1)} %fusion.91), channel_id=1, source_target_pairs={{0,1},{1,0},{2,3},{3,2},{4,5},{5,4},{6,7},{7,6},{8,9},{9,8},{10,11... | collective-permute-start | bytes 12296 | tf_op jit(solution)/shard_map/ppermute | solution.py:15
  23.2 6.6 %copy-start.9 = (f32[32,32]{0,1:T(8,128)}, f32[32,32]{0,1:T(8,128)S(1)}, u32[]{:S(2)}) copy-start(f32[32,32]{0,1:T(8,128)S(1)} %collective-permute-done) | copy-start | bytes 12292
  23.2 6.6 %copy-start.19 = (f32[2,32,32]{2,1,0:T(8,128)S(1)}, f32[2,32,32]{2,1,0:T(8,128)}, u32[]{:S(2)}) copy-start(f32[2,32,32]{2,1,0:T(8,128)} %param.31) | copy-start | bytes 24580
  23.6 7.2 %collective-permute-start.1 = (f32[32,32]{0,1:T(8,128)S(1)}, f32[32,32]{0,1:T(8,128)S(1)}, u32[]{:S(2)}, u32[]{:S(2)}) collective-permute-start(f32[32,32]{0,1:T(8,128)S(1)} %fusion.85), channel_id=1, source_target_pairs={{0,2},{2,0},{4,6},{6,4},{8,10},{10,8},{12,14},{14,12},{1,3},{3,1},... | collective-permute-start | bytes 12296 | tf_op jit(solution)/shard_map/ppermute | solution.py:15
  30.6 24.3 %copy-start.29 = (s32[32,6]{0,1:T(8,128)S(1)}, s32[32,6]{0,1:T(8,128)}, u32[]{:S(2)}) copy-start(s32[32,6]{0,1:T(8,128)} %param.23) | copy-start | bytes 2308
  30.6 24.3 %copy-start.3 = (bf16[32,6,4096]{2,0,1:T(8,128)(2,1)S(1)}, bf16[32,6,4096]{2,0,1:T(8,128)(2,1)}, u32[]{:S(2)}) copy-start(bf16[32,6,4096]{2,0,1:T(8,128)(2,1)} %param.21) | copy-start | bytes 4718596
  30.7 28.6 %copy-start.11 = (f32[32,32]{0,1:T(8,128)}, f32[32,32]{0,1:T(8,128)S(1)}, u32[]{:S(2)}) copy-start(f32[32,32]{0,1:T(8,128)S(1)} %collective-permute-done.1) | copy-start | bytes 12292
  31.0 11.9 %collective-permute-start.2 = (f32[32,32]{0,1:T(8,128)S(1)}, f32[32,32]{0,1:T(8,128)S(1)}, u32[]{:S(2)}, u32[]{:S(2)}) collective-permute-start(f32[32,32]{0,1:T(8,128)S(1)} %fusion.79), channel_id=1, source_target_pairs={{0,4},{2,6},{4,0},{6,2},{8,12},{10,14},{12,8},{14,10},{1,5},{3,7},... | collective-permute-start | bytes 12296 | tf_op jit(solution)/shard_map/ppermute | solution.py:15
  42.8 16.5 %copy-start.13 = (f32[32,32]{0,1:T(8,128)}, f32[32,32]{0,1:T(8,128)S(1)}, u32[]{:S(2)}) copy-start(f32[32,32]{0,1:T(8,128)S(1)} %collective-permute-done.2) | copy-start | bytes 12292
  43.0 16.5 %collective-permute-start.3 = (f32[32,32]{0,1:T(8,128)S(1)}, f32[32,32]{0,1:T(8,128)S(1)}, u32[]{:S(2)}, u32[]{:S(2)}) collective-permute-start(f32[32,32]{0,1:T(8,128)S(1)} %fusion.76), channel_id=1, source_target_pairs={{0,8},{2,10},{4,12},{6,14},{8,0},{10,2},{12,4},{14,6},{1,9},{3,11}... | collective-permute-start | bytes 12296 | tf_op jit(solution)/shard_map/ppermute | solution.py:15
  54.9 15.4 %copy-start.25 = (f32[32,6]{0,1:T(8,128)S(1)}, f32[32,6]{0,1:T(8,128)}, u32[]{:S(2)}) copy-start(f32[32,6]{0,1:T(8,128)} %compare_select_fusion.5) | copy-start | bytes 2308
  54.9 16.1 %copy-start.24 = (f32[32,6]{0,1:T(8,128)S(1)}, f32[32,6]{0,1:T(8,128)}, u32[]{:S(2)}) copy-start(f32[32,6]{0,1:T(8,128)} %compare_select_fusion.4) | copy-start | bytes 2308
  54.9 16.8 %copy-start.4 = (bf16[32,32,32]{1,2,0:T(8,128)(2,1)S(1)}, bf16[32,32,32]{1,2,0:T(8,128)(2,1)}, u32[]{:S(2)}) copy-start(bf16[32,32,32]{1,2,0:T(8,128)(2,1)} %convert_bitcast_fusion) | copy-start | bytes 196612
  59.5 13.5 %copy-start.15 = (f32[32,32]{0,1:T(8,128)}, f32[32,32]{0,1:T(8,128)S(1)}, u32[]{:S(2)}) copy-start(f32[32,32]{0,1:T(8,128)S(1)} %collective-permute-done.3) | copy-start | bytes 12292
  59.7 5.6 %collective-permute-start.4 = (f32[32,32]{0,1:T(8,128)S(1)}, f32[32,32]{0,1:T(8,128)S(1)}, u32[]{:S(2)}, u32[]{:S(2)}) collective-permute-start(f32[32,32]{0,1:T(8,128)S(1)} %fusion.73), channel_id=1, source_target_pairs={{0,16},{16,0},{32,48},{48,32},{64,80},{80,64},{96,112},{112,96},{1... | collective-permute-start | bytes 12296 | tf_op jit(solution)/shard_map/ppermute | solution.py:15
  65.4 7.7 %copy-start.16 = (f32[32,32]{0,1:T(8,128)}, f32[32,32]{0,1:T(8,128)S(1)}, u32[]{:S(2)}) copy-start(f32[32,32]{0,1:T(8,128)S(1)} %collective-permute-done.4) | copy-start | bytes 12292
  65.6 16.3 %collective-permute-start.5 = (f32[32,32]{0,1:T(8,128)S(1)}, f32[32,32]{0,1:T(8,128)S(1)}, u32[]{:S(2)}, u32[]{:S(2)}) collective-permute-start(f32[32,32]{0,1:T(8,128)S(1)} %fusion.70), channel_id=1, source_target_pairs={{0,32},{16,48},{32,0},{48,16},{64,96},{80,112},{96,64},{112,80},{1... | collective-permute-start | bytes 12296 | tf_op jit(solution)/shard_map/ppermute | solution.py:15
  71.7 16.7 %collective-permute-start.8 = (bf16[32,32,32]{1,2,0:T(8,128)(2,1)S(1)}, bf16[32,32,32]{1,2,0:T(8,128)(2,1)S(1)}, u32[]{:S(2)}, u32[]{:S(2)}) collective-permute-start(bf16[32,32,32]{1,2,0:T(8,128)(2,1)S(1)} %copy-done.4), channel_id=1, source_target_pairs={{1,0},{2,1},{3,2},{4,3},{5,4},{6,5},{7,6},{8,7},{9,8},{10,9},{11,1... | collective-permute-start | bytes 196616 | tf_op jit(solution)/shard_map/ppermute | solution.py:25
  73.0 15.4 %collective-permute-start.7 = (bf16[32,32,32]{1,2,0:T(8,128)(2,1)S(1)}, bf16[32,32,32]{1,2,0:T(8,128)(2,1)S(1)}, u32[]{:S(2)}, u32[]{:S(2)}) collective-permute-start(bf16[32,32,32]{1,2,0:T(8,128)(2,1)S(1)} %copy-done.4), channel_id=1, source_target_pairs={{0,1},{1,2},{2,3},{3,4},{4,5},{5,6},{6,7},{7,8},{8,9},{9,10},{10,1... | collective-permute-start | bytes 196616 | tf_op jit(solution)/shard_map/ppermute | solution.py:24
  76.1 29.6 %collective-permute-start.12 = (bf16[32,32,64]{2,0,1:T(8,128)(2,1)S(1)}, bf16[32,32,64]{2,0,1:T(8,128)(2,1)S(1)}, u32[]{:S(2)}, u32[]{:S(2)}) collective-permute-start(bf16[32,32,64]{2,0,1:T(8,128)(2,1)S(1)} %select_convert_fusion), channel_id=1, source_target_pairs={{1,0},{2,1},{3,2},{4,3},{5,4},{6,5},{7,6},{8,7},{9,8},{10,9},{11,1... | collective-permute-start | bytes 393224 | tf_op jit(solution)/shard_map/ppermute | solution.py:25
  77.4 28.3 %collective-permute-start.11 = (bf16[32,32,64]{2,0,1:T(8,128)(2,1)S(1)}, bf16[32,32,64]{2,0,1:T(8,128)(2,1)}, u32[]{:S(2)}, u32[]{:S(2)}) collective-permute-start(bf16[32,32,64]{2,0,1:T(8,128)(2,1)S(1)} %select_convert_fusion), channel_id=1, source_target_pairs={{0,1},{1,2},{2,3},{3,4},{4,5},{5,6},{6,7},{7,8},{8,9},{9,10},{10,1... | collective-permute-start | bytes 393224 | tf_op jit(solution)/shard_map/ppermute | solution.py:24
  81.8 6.6 %copy-start.17 = (f32[32,32]{0,1:T(8,128)}, f32[32,32]{0,1:T(8,128)S(1)}, u32[]{:S(2)}) copy-start(f32[32,32]{0,1:T(8,128)S(1)} %collective-permute-done.5) | copy-start | bytes 12292
  82.0 9.7 %collective-permute-start.6 = (f32[32,32]{0,1:T(8,128)S(1)}, f32[32,32]{0,1:T(8,128)}, u32[]{:S(2)}, u32[]{:S(2)}) collective-permute-start(f32[32,32]{0,1:T(8,128)S(1)} %fusion.67), channel_id=1, source_target_pairs={{0,64},{16,80},{32,96},{48,112},{64,0},{80,16},{96,32},{112,48},{1... | collective-permute-start | bytes 12296 | tf_op jit(solution)/shard_map/ppermute | solution.py:15
  89.0 7.2 %copy-start.26 = (f32[32,6]{1,0:T(8,128)S(1)}, f32[32,6]{1,0:T(8,128)}, u32[]{:S(2)}) copy-start(f32[32,6]{1,0:T(8,128)} %copy.185) | copy-start | bytes 2308
  92.7 8.5 %collective-permute-start.9 = (f32[32,32]{0,1:T(8,128)S(1)}, f32[32,32]{0,1:T(8,128)S(1)}, u32[]{:S(2)}, u32[]{:S(2)}) collective-permute-start(f32[32,32]{0,1:T(8,128)S(1)} %fusion.64), channel_id=1, source_target_pairs={{0,128},{128,0},{256,384},{384,256},{512,640},{640,512},{768,896},... | collective-permute-start | bytes 12296 | tf_op jit(solution)/shard_map/ppermute | solution.py:15
  101.4 6.8 %collective-permute-start.10 = (f32[32,32]{0,1:T(8,128)S(1)}, f32[32,32]{0,1:T(8,128)}, u32[]{:S(2)}, u32[]{:S(2)}) collective-permute-start(f32[32,32]{0,1:T(8,128)S(1)} %fusion.61), channel_id=1, source_target_pairs={{0,256},{128,384},{256,0},{384,128},{512,768},{640,896},{768,512},... | collective-permute-start | bytes 12296 | tf_op jit(solution)/shard_map/ppermute | solution.py:15
  109.2 9.8 %copy-start.10 = (f32[32,32]{0,1:T(8,128)S(1)}, f32[32,32]{0,1:T(8,128)}, u32[]{:S(2)}) copy-start(f32[32,32]{0,1:T(8,128)} %copy-done.9) | copy-start | bytes 12292
  109.2 9.8 %copy-start.12 = (f32[32,32]{0,1:T(8,128)S(1)}, f32[32,32]{0,1:T(8,128)}, u32[]{:S(2)}) copy-start(f32[32,32]{0,1:T(8,128)} %copy-done.11) | copy-start | bytes 12292
  109.2 9.8 %copy-start.14 = (f32[32,32]{0,1:T(8,128)S(1)}, f32[32,32]{0,1:T(8,128)}, u32[]{:S(2)}) copy-start(f32[32,32]{0,1:T(8,128)} %copy-done.13) | copy-start | bytes 12292
  109.2 10.9 %copy-start.5 = (f32[32,32,32]{2,1,0:T(8,128)S(1)}, f32[32,32,32]{2,1,0:T(8,128)}, u32[]{:S(2)}) copy-start(f32[32,32,32]{2,1,0:T(8,128)} %fusion.12) | copy-start | bytes 393220
  109.2 9.8 %collective-permute-start.13 = (f32[32,32]{0,1:T(8,128)S(1)}, f32[32,32]{0,1:T(8,128)}, u32[]{:S(2)}, u32[]{:S(2)}) collective-permute-start(f32[32,32]{0,1:T(8,128)S(1)} %fusion.58), channel_id=1, source_target_pairs={{0,512},{128,640},{256,768},{384,896},{512,0},{640,128},{768,256},... | collective-permute-start | bytes 12296 | tf_op jit(solution)/shard_map/ppermute | solution.py:15
  (14 other events, 35.0 us)

commit v14 on v13

--- a/solution.py
+++ b/solution.py
@@ -112,7 +112,9 @@
         start_at = 0
         while current.shape[0] > 1:
             node_count = current.shape[0]
-            moved_up = apply_up(col_local[start_at : start_at + node_count], current)
+            total = col_local.shape[0]
+            placed = jnp.pad(current, ((start_at, total - start_at - node_count), (0, 0), (0, 0)))
+            moved_up = apply_up(col_local, placed)[start_at : start_at + node_count]
             paired = moved_up.reshape(node_count // 2, 2, rank_width, columns)
             current = paired[:, 0] + paired[:, 1]
             offsets.append(start_at)

time: 133 us -> 133 us (level)
  local copies, waits for them, and re-layouts: 37.4 us -> 34.1 us
  matrix products: 18.5 us -> 20.8 us
    slice x4, local copies, waits for them, and re-layouts: 3.45 us -> 0.07 us  [apply_image(): moved_up = apply_up(col_local, placed)[start_at:start_at + node_count]]
    squeeze x0 -> x1, local copies, waits for them, and re-layouts: none -> 1.79 us  [shards(): col_local = loc_col[0].astype(jnp.float32)]
    unnamed x76 -> x67, local copies, waits for them, and re-layouts: 5.53 us -> 3.79 us
    dot_general x14, matrix products: 4.39 us -> 5.99 us  [apply_up(): jnp.einsum('...ab,...ac->...bc', matrix, coeffs, precision=best_precision)]
  transfers between devices with their start and end apart: 14 -> 14, of which waited for: 4 -> 4; matrix products, arithmetic and copies ran while one was open for 25% -> 24% of each run, Pallas kernels for 0% -> 0%
where the time goes in v14:
time: 133 us; the launch traced here: 131 us
  starting transfers between devices  63.6 us (48%)
  local copies, waits for them, and re-layouts  34.1 us (26%)
  matrix products  20.8 us (16%)
  other arithmetic  6.12 us (5%)
  waiting for transfers between devices  4.14 us (3%)
  between operations  1.77 us (1%)
    ppermute x10, starting transfers between devices, from_partner(): return lax.ppermute(value, axis, pairs)  53.4 us
    ppermute x2, starting transfers between devices, extended(): low = lax.ppermute(block, axis, forward)  7.44 us
    gather x2, local copies, waits for them, and re-layouts, apply_image(): ordered = jnp.take(vectors, order_row, axis=1).astype(jnp.bfloat16)  6.41 us
    dot_general x14, matrix products, apply_up(): jnp.einsum('...ab,...ac->...bc', matrix, coeffs, precision=best_precision)  5.99 us
    scatter x1, local copies, waits for them, and re-layouts, apply_image(): return jnp.zeros_like(image).at[:, order_row].set(image)  5.97 us
    dot_general x1, matrix products, far_sum(): jnp.einsum('lkab,lkbc->lac', results['far_sq'], scaled, precision=best_pr...  4.95 us
    dot_general x1, matrix products, near_total(): jnp.einsum('lkpq,clkq->clp', results['near_sq'], scaled, precision=best_p...  4.58 us
    reshape x1, local copies, waits for them, and re-layouts, near_square(): near_blocks.reshape(leaves_dev, near_blocks.shape[1], leaf_size, leaf_size)  4.36 us
  transfers between devices with their start and end apart: 14, of which 4 were waited for; matrix products, arithmetic and copies ran while one was open for 24% of the time, Pallas kernels for 0%

profile of v14, /device:TPU:14, one launch (start us, length us, event | category | flops | bytes accessed | tf_op | source)
XLA Modules:
  0.0 130.5 jit_solution(1879258510517349996)
XLA Ops:
  1.4 1.8 %copy.163 = bf16[62,32,32]{2,1,0:T(8,128)(2,1)S(1)} copy(bf16[62,32,32]{0,2,1:T(8,128)(2,1)} %bitcast.262) | data formatting | bytes 253952 | tf_op jit(solution)/shard_map/squeeze | solution.py:57
  3.2 1.0 pad_maximum_fusion.2
  4.5 6.2 %gather_fusion = bf16[2048,32]{1,0:T(8,128)(2,1)S(1)} fusion(bf16[32,2048]{0,1:T(8,128)(2,1)S(1)} %copy.161, s32[2048]{0:T(1024)S(1)} %broadcast_clamp_fusion), kind=kCustom, calls=%fused_computation | custom fusion | bytes 270336 | tf_op jit(solution)/shard_map/jit(_take)/gather | solution.py:104
  12.3 1.0 fusion.128
  16.3 1.9 %collective-permute-start = (f32[32,32]{0,1:T(8,128)S(1)}, f32[32,32]{0,1:T(8,128)S(1)}, u32[]{:S(2)}, u32[]{:S(2)}) collective-permute-start(f32[32,32]{0,1:T(8,128)S(1)} %fusion.83), channel_id=1, source_target_pairs={{0,1},{1,0},{2,3},{3,2},{4,5},{5,4},{6,7},{7,6},{8,9},{9,8},{10,11... | collective-permute-start | bytes 12296 | tf_op jit(solution)/shard_map/ppermute | solution.py:15
  23.6 5.2 %collective-permute-start.1 = (f32[32,32]{0,1:T(8,128)S(1)}, f32[32,32]{0,1:T(8,128)S(1)}, u32[]{:S(2)}, u32[]{:S(2)}) collective-permute-start(f32[32,32]{0,1:T(8,128)S(1)} %fusion.78), channel_id=1, source_target_pairs={{0,2},{2,0},{4,6},{6,4},{8,10},{10,8},{12,14},{14,12},{1,3},{3,1},... | collective-permute-start | bytes 12296 | tf_op jit(solution)/shard_map/ppermute | solution.py:15
  31.0 8.0 %collective-permute-start.2 = (f32[32,32]{0,1:T(8,128)S(1)}, f32[32,32]{0,1:T(8,128)S(1)}, u32[]{:S(2)}, u32[]{:S(2)}) collective-permute-start(f32[32,32]{0,1:T(8,128)S(1)} %fusion.72), channel_id=1, source_target_pairs={{0,4},{2,6},{4,0},{6,2},{8,12},{10,14},{12,8},{14,10},{1,5},{3,7},... | collective-permute-start | bytes 12296 | tf_op jit(solution)/shard_map/ppermute | solution.py:15
  39.7 3.1 %reshape.295 = bf16[32,6,32,32]{3,2,0,1:T(8,128)(2,1)} reshape(bf16[32,6,1024]{2,0,1:T(8,128)(2,1)} %param.24) | data formatting | bytes 786432 | tf_op jit(solution)/shard_map/reshape | solution.py:137
  43.0 11.9 %collective-permute-start.3 = (f32[32,32]{0,1:T(8,128)S(1)}, f32[32,32]{0,1:T(8,128)S(1)}, u32[]{:S(2)}, u32[]{:S(2)}) collective-permute-start(f32[32,32]{0,1:T(8,128)S(1)} %fusion.69), channel_id=1, source_target_pairs={{0,8},{2,10},{4,12},{6,14},{8,0},{10,2},{12,4},{14,6},{1,9},{3,11}... | collective-permute-start | bytes 12296 | tf_op jit(solution)/shard_map/ppermute | solution.py:15
  55.0 4.4 %reshape.296 = bf16[32,6,64,64]{3,2,0,1:T(8,128)(2,1)} reshape(bf16[32,6,4096]{2,0,1:T(8,128)(2,1)S(1)} %copy-done.2) | data formatting | bytes 3145728 | tf_op jit(solution)/shard_map/reshape | solution.py:134
  59.8 3.6 %collective-permute-start.4 = (f32[32,32]{0,1:T(8,128)S(1)}, f32[32,32]{0,1:T(8,128)S(1)}, u32[]{:S(2)}, u32[]{:S(2)}) collective-permute-start(f32[32,32]{0,1:T(8,128)S(1)} %fusion.66), channel_id=1, source_target_pairs={{0,16},{16,0},{32,48},{48,32},{64,80},{80,64},{96,112},{112,96},{1... | collective-permute-start | bytes 12296 | tf_op jit(solution)/shard_map/ppermute | solution.py:15
  63.6 1.8 %collective-permute-done.4 = f32[32,32]{0,1:T(8,128)S(1)} collective-permute-done((f32[32,32]{0,1:T(8,128)S(1)}, f32[32,32]{0,1:T(8,128)S(1)}, u32[]{:S(2)}, u32[]{:S(2)}) %collective-permute-start.4) | collective-permute-done | bytes 4128 | tf_op jit(solution)/shard_map/ppermute | solution.py:15
  65.6 4.7 %collective-permute-start.5 = (f32[32,32]{0,1:T(8,128)S(1)}, f32[32,32]{0,1:T(8,128)S(1)}, u32[]{:S(2)}, u32[]{:S(2)}) collective-permute-start(f32[32,32]{0,1:T(8,128)S(1)} %fusion.63), channel_id=1, source_target_pairs={{0,32},{16,48},{32,0},{48,16},{64,96},{80,112},{96,64},{112,80},{1... | collective-permute-start | bytes 12296 | tf_op jit(solution)/shard_map/ppermute | solution.py:15
  71.7 1.3 collective-permute-start.8
  73.1 3.0 %collective-permute-start.7 = (bf16[32,32,32]{1,2,0:T(8,128)(2,1)S(1)}, bf16[32,32,32]{1,2,0:T(8,128)(2,1)S(1)}, u32[]{:S(2)}, u32[]{:S(2)}) collective-permute-start(bf16[32,32,32]{1,2,0:T(8,128)(2,1)S(1)} %copy-done.3), channel_id=1, source_target_pairs={{0,1},{1,2},{2,3},{3,4},{4,5},{5,6},{6,7},{7,8},{8,9},{9,10},{10,1... | collective-permute-start | bytes 196616 | tf_op jit(solution)/shard_map/ppermute | solution.py:24
  76.1 1.5 %collective-permute-start.12 = (bf16[32,32,64]{2,0,1:T(8,128)(2,1)S(1)}, bf16[32,32,64]{2,0,1:T(8,128)(2,1)S(1)}, u32[]{:S(2)}, u32[]{:S(2)}) collective-permute-start(bf16[32,32,64]{2,0,1:T(8,128)(2,1)S(1)} %select_convert_fusion), channel_id=1, source_target_pairs={{1,0},{2,1},{3,2},{4,3},{5,4},{6,5},{7,6},{8,7},{9,8},{10,9},{11,1... | collective-permute-start | bytes 393224 | tf_op jit(solution)/shard_map/ppermute | solution.py:25
  77.6 4.4 %collective-permute-start.11 = (bf16[32,32,64]{2,0,1:T(8,128)(2,1)S(1)}, bf16[32,32,64]{2,0,1:T(8,128)(2,1)}, u32[]{:S(2)}, u32[]{:S(2)}) collective-permute-start(bf16[32,32,64]{2,0,1:T(8,128)(2,1)S(1)} %select_convert_fusion), channel_id=1, source_target_pairs={{0,1},{1,2},{2,3},{3,4},{4,5},{5,6},{6,7},{7,8},{8,9},{9,10},{10,1... | collective-permute-start | bytes 393224 | tf_op jit(solution)/shard_map/ppermute | solution.py:24
  82.2 6.4 %collective-permute-start.6 = (f32[32,32]{0,1:T(8,128)S(1)}, f32[32,32]{0,1:T(8,128)}, u32[]{:S(2)}, u32[]{:S(2)}) collective-permute-start(f32[32,32]{0,1:T(8,128)S(1)} %fusion.60), channel_id=1, source_target_pairs={{0,64},{16,80},{32,96},{48,112},{64,0},{80,16},{96,32},{112,48},{1... | collective-permute-start | bytes 12296 | tf_op jit(solution)/shard_map/ppermute | solution.py:15
  89.2 2.0 %gather_fusion.1 = bf16[192,32,32]{2,1,0:T(8,128)(2,1)} fusion(bf16[96,32,32]{2,1,0:T(8,128)(2,1)S(1)} %copy.184, s32[1024]{0:T(1024)S(1)} %pad_clamp_fusion.1), kind=kCustom, calls=%fused_computation.1 | custom fusion | bytes 787200 | tf_op jit(solution)/shard_map/gather | solution.py:141
  91.9 0.9 fusion.57
  92.9 3.3 %collective-permute-start.9 = (f32[32,32]{0,1:T(8,128)S(1)}, f32[32,32]{0,1:T(8,128)S(1)}, u32[]{:S(2)}, u32[]{:S(2)}) collective-permute-start(f32[32,32]{0,1:T(8,128)S(1)} %fusion.57), channel_id=1, source_target_pairs={{0,128},{128,0},{256,384},{384,256},{512,640},{640,512},{768,896},... | collective-permute-start | bytes 12296 | tf_op jit(solution)/shard_map/ppermute | solution.py:15
  96.2 4.9 %fusion.12 = f32[32,32,32]{2,1,0:T(8,128)} fusion(bf16[32,6,32,32]{3,2,0,1:T(8,128)(2,1)} %reshape.295, bf16[32,6,32,32]{3,2,1,0:T(8,128)(2,1)} %bitcast.255, f32[32,6]{1,0:T(8,128)S(1)} %copy-done.22), kind=kOutput, calls=%fused_computation.22 | convolution fusion | flops 75890688 | bytes 918272 | tf_op jit(solution)/shard_map/lkab,lkbc->lac/dot_general | solution.py:146
  101.4 4.2 %collective-permute-start.10 = (f32[32,32]{0,1:T(8,128)S(1)}, f32[32,32]{0,1:T(8,128)}, u32[]{:S(2)}, u32[]{:S(2)}) collective-permute-start(f32[32,32]{0,1:T(8,128)S(1)} %fusion.54), channel_id=1, source_target_pairs={{0,256},{128,384},{256,0},{384,128},{512,768},{640,896},{768,512},... | collective-permute-start | bytes 12296 | tf_op jit(solution)/shard_map/ppermute | solution.py:15
  105.6 1.1 pad_maximum_fusion.1
  109.2 4.1 %collective-permute-start.13 = (f32[32,32]{0,1:T(8,128)S(1)}, f32[32,32]{0,1:T(8,128)}, u32[]{:S(2)}, u32[]{:S(2)}) collective-permute-start(f32[32,32]{0,1:T(8,128)S(1)} %fusion.51), channel_id=1, source_target_pairs={{0,512},{128,640},{256,768},{384,896},{512,0},{640,128},{768,256},... | collective-permute-start | bytes 12296 | tf_op jit(solution)/shard_map/ppermute | solution.py:15
  113.3 4.6 %fusion.7 = f32[32,32,64]{2,0,1:T(8,128)S(1)} fusion(bf16[32,6,64,64]{3,2,0,1:T(8,128)(2,1)} %reshape.296, bf16[32,32,6,64]{3,0,2,1:T(8,128)(2,1)S(1)} %bitcast.252, f32[32,6]{1,0:T(8,128)} %copy.189), kind=kOutput, calls=%fused_computation.17 | convolution fusion | flops 302776320 | bytes 2622208 | tf_op jit(solution)/shard_map/lkpq,clkq->clp/dot_general | solution.py:155
  117.9 1.1 collective-permute-done.13
  118.9 0.9 concatenate.83
  120.1 1.0 fusion.15
  122.3 6.0 %scatter_custom_fusion = f32[32,2048]{0,1:T(8,128)S(1)} fusion(s32[2048]{0:T(1024)} %bitcast.266, f32[2048,32]{1,0:T(8,128)S(1)} %copy.194, f32[]{:T(128)} %constant.14.clone.1), kind=kCustom, calls=%fused_computation.30 | custom fusion | bytes 262656 | tf_op jit(solution)/shard_map/scatter | solution.py:183
  128.6 1.0 copy.195
  129.6 1.0 copy.196
  (164 shorter events, 21.5 us)
Async XLA Ops:
  0.6 11.7 %copy-start = (bf16[32,64,32]{1,2,0:T(8,128)(2,1)S(1)}, bf16[32,64,32]{1,2,0:T(8,128)(2,1)}, u32[]{:S(2)}) copy-start(bf16[32,64,32]{1,2,0:T(8,128)(2,1)} %param.19) | copy-start | bytes 393220
  1.4 9.3 %copy-start.17 = (s32[2048,1]{0,1:T(1,128)}, s32[2048,1]{0,1:T(1,128)S(1)}, u32[]{:S(2)}) copy-start(s32[2048,1]{0,1:T(1,128)S(1)} %compare_select_fusion) | copy-start | bytes 24580
  3.2 8.2 %copy-start.16 = (s32[1,2048]{1,0:T(1,128)S(1)}, s32[1,2048]{1,0:T(1,128)}, u32[]{:S(2)}) copy-start(s32[1,2048]{1,0:T(1,128)} %param.18) | copy-start | bytes 24580
  16.3 6.9 %collective-permute-start = (f32[32,32]{0,1:T(8,128)S(1)}, f32[32,32]{0,1:T(8,128)S(1)}, u32[]{:S(2)}, u32[]{:S(2)}) collective-permute-start(f32[32,32]{0,1:T(8,128)S(1)} %fusion.83), channel_id=1, source_target_pairs={{0,1},{1,0},{2,3},{3,2},{4,5},{5,4},{6,7},{7,6},{8,9},{9,8},{10,11... | collective-permute-start | bytes 12296 | tf_op jit(solution)/shard_map/ppermute | solution.py:15
  18.9 9.8 %copy-start.26 = (pred[10]{0:T(512)(128)(4,1)}, pred[10]{0:T(512)(128)(4,1)S(1)}, u32[]{:S(2)}) copy-start(pred[10]{0:T(512)(128)(4,1)S(1)} %get-tuple-element.67) | copy-start | bytes 34
  23.6 7.2 %collective-permute-start.1 = (f32[32,32]{0,1:T(8,128)S(1)}, f32[32,32]{0,1:T(8,128)S(1)}, u32[]{:S(2)}, u32[]{:S(2)}) collective-permute-start(f32[32,32]{0,1:T(8,128)S(1)} %fusion.78), channel_id=1, source_target_pairs={{0,2},{2,0},{4,6},{6,4},{8,10},{10,8},{12,14},{14,12},{1,3},{3,1},... | collective-permute-start | bytes 12296 | tf_op jit(solution)/shard_map/ppermute | solution.py:15
  30.6 24.3 %copy-start.25 = (s32[32,6]{0,1:T(8,128)S(1)}, s32[32,6]{0,1:T(8,128)}, u32[]{:S(2)}) copy-start(s32[32,6]{0,1:T(8,128)} %param.23) | copy-start | bytes 2308
  30.6 24.3 %copy-start.2 = (bf16[32,6,4096]{2,0,1:T(8,128)(2,1)S(1)}, bf16[32,6,4096]{2,0,1:T(8,128)(2,1)}, u32[]{:S(2)}) copy-start(bf16[32,6,4096]{2,0,1:T(8,128)(2,1)} %param.21) | copy-start | bytes 4718596
  30.8 28.6 %copy-start.8 = (f32[32,32]{0,1:T(8,128)}, f32[32,32]{0,1:T(8,128)S(1)}, u32[]{:S(2)}) copy-start(f32[32,32]{0,1:T(8,128)S(1)} %collective-permute-done.1) | copy-start | bytes 12292
  31.0 11.8 %collective-permute-start.2 = (f32[32,32]{0,1:T(8,128)S(1)}, f32[32,32]{0,1:T(8,128)S(1)}, u32[]{:S(2)}, u32[]{:S(2)}) collective-permute-start(f32[32,32]{0,1:T(8,128)S(1)} %fusion.72), channel_id=1, source_target_pairs={{0,4},{2,6},{4,0},{6,2},{8,12},{10,14},{12,8},{14,10},{1,5},{3,7},... | collective-permute-start | bytes 12296 | tf_op jit(solution)/shard_map/ppermute | solution.py:15
  42.8 16.5 %copy-start.10 = (f32[32,32]{0,1:T(8,128)}, f32[32,32]{0,1:T(8,128)S(1)}, u32[]{:S(2)}) copy-start(f32[32,32]{0,1:T(8,128)S(1)} %collective-permute-done.2) | copy-start | bytes 12292
  43.0 16.5 %collective-permute-start.3 = (f32[32,32]{0,1:T(8,128)S(1)}, f32[32,32]{0,1:T(8,128)S(1)}, u32[]{:S(2)}, u32[]{:S(2)}) collective-permute-start(f32[32,32]{0,1:T(8,128)S(1)} %fusion.69), channel_id=1, source_target_pairs={{0,8},{2,10},{4,12},{6,14},{8,0},{10,2},{12,4},{14,6},{1,9},{3,11}... | collective-permute-start | bytes 12296 | tf_op jit(solution)/shard_map/ppermute | solution.py:15
  55.0 15.4 %copy-start.21 = (f32[32,6]{0,1:T(8,128)S(1)}, f32[32,6]{0,1:T(8,128)}, u32[]{:S(2)}) copy-start(f32[32,6]{0,1:T(8,128)} %compare_select_fusion.5) | copy-start | bytes 2308
  55.0 16.1 %copy-start.20 = (f32[32,6]{0,1:T(8,128)S(1)}, f32[32,6]{0,1:T(8,128)}, u32[]{:S(2)}) copy-start(f32[32,6]{0,1:T(8,128)} %compare_select_fusion.4) | copy-start | bytes 2308
  55.0 16.8 %copy-start.3 = (bf16[32,32,32]{1,2,0:T(8,128)(2,1)S(1)}, bf16[32,32,32]{1,2,0:T(8,128)(2,1)}, u32[]{:S(2)}) copy-start(bf16[32,32,32]{1,2,0:T(8,128)(2,1)} %get-tuple-element.34) | copy-start | bytes 196612
  59.6 13.5 %copy-start.11 = (f32[32,32]{0,1:T(8,128)}, f32[32,32]{0,1:T(8,128)S(1)}, u32[]{:S(2)}) copy-start(f32[32,32]{0,1:T(8,128)S(1)} %collective-permute-done.3) | copy-start | bytes 12292
  59.8 5.6 %collective-permute-start.4 = (f32[32,32]{0,1:T(8,128)S(1)}, f32[32,32]{0,1:T(8,128)S(1)}, u32[]{:S(2)}, u32[]{:S(2)}) collective-permute-start(f32[32,32]{0,1:T(8,128)S(1)} %fusion.66), channel_id=1, source_target_pairs={{0,16},{16,0},{32,48},{48,32},{64,80},{80,64},{96,112},{112,96},{1... | collective-permute-start | bytes 12296 | tf_op jit(solution)/shard_map/ppermute | solution.py:15
  65.4 7.6 %copy-start.12 = (f32[32,32]{0,1:T(8,128)}, f32[32,32]{0,1:T(8,128)S(1)}, u32[]{:S(2)}) copy-start(f32[32,32]{0,1:T(8,128)S(1)} %collective-permute-done.4) | copy-start | bytes 12292
  65.6 16.4 %collective-permute-start.5 = (f32[32,32]{0,1:T(8,128)S(1)}, f32[32,32]{0,1:T(8,128)S(1)}, u32[]{:S(2)}, u32[]{:S(2)}) collective-permute-start(f32[32,32]{0,1:T(8,128)S(1)} %fusion.63), channel_id=1, source_target_pairs={{0,32},{16,48},{32,0},{48,16},{64,96},{80,112},{96,64},{112,80},{1... | collective-permute-start | bytes 12296 | tf_op jit(solution)/shard_map/ppermute | solution.py:15
  71.7 16.9 %collective-permute-start.8 = (bf16[32,32,32]{1,2,0:T(8,128)(2,1)S(1)}, bf16[32,32,32]{1,2,0:T(8,128)(2,1)S(1)}, u32[]{:S(2)}, u32[]{:S(2)}) collective-permute-start(bf16[32,32,32]{1,2,0:T(8,128)(2,1)S(1)} %copy-done.3), channel_id=1, source_target_pairs={{1,0},{2,1},{3,2},{4,3},{5,4},{6,5},{7,6},{8,7},{9,8},{10,9},{11,1... | collective-permute-start | bytes 196616 | tf_op jit(solution)/shard_map/ppermute | solution.py:25
  73.1 15.6 %collective-permute-start.7 = (bf16[32,32,32]{1,2,0:T(8,128)(2,1)S(1)}, bf16[32,32,32]{1,2,0:T(8,128)(2,1)S(1)}, u32[]{:S(2)}, u32[]{:S(2)}) collective-permute-start(bf16[32,32,32]{1,2,0:T(8,128)(2,1)S(1)} %copy-done.3), channel_id=1, source_target_pairs={{0,1},{1,2},{2,3},{3,4},{4,5},{5,6},{6,7},{7,8},{8,9},{9,10},{10,1... | collective-permute-start | bytes 196616 | tf_op jit(solution)/shard_map/ppermute | solution.py:24
  76.1 29.5 %collective-permute-start.12 = (bf16[32,32,64]{2,0,1:T(8,128)(2,1)S(1)}, bf16[32,32,64]{2,0,1:T(8,128)(2,1)S(1)}, u32[]{:S(2)}, u32[]{:S(2)}) collective-permute-start(bf16[32,32,64]{2,0,1:T(8,128)(2,1)S(1)} %select_convert_fusion), channel_id=1, source_target_pairs={{1,0},{2,1},{3,2},{4,3},{5,4},{6,5},{7,6},{8,7},{9,8},{10,9},{11,1... | collective-permute-start | bytes 393224 | tf_op jit(solution)/shard_map/ppermute | solution.py:25
  77.6 28.0 %collective-permute-start.11 = (bf16[32,32,64]{2,0,1:T(8,128)(2,1)S(1)}, bf16[32,32,64]{2,0,1:T(8,128)(2,1)}, u32[]{:S(2)}, u32[]{:S(2)}) collective-permute-start(bf16[32,32,64]{2,0,1:T(8,128)(2,1)S(1)} %select_convert_fusion), channel_id=1, source_target_pairs={{0,1},{1,2},{2,3},{3,4},{4,5},{5,6},{6,7},{7,8},{8,9},{9,10},{10,1... | collective-permute-start | bytes 393224 | tf_op jit(solution)/shard_map/ppermute | solution.py:24
  82.0 6.6 %copy-start.13 = (f32[32,32]{0,1:T(8,128)}, f32[32,32]{0,1:T(8,128)S(1)}, u32[]{:S(2)}) copy-start(f32[32,32]{0,1:T(8,128)S(1)} %collective-permute-done.5) | copy-start | bytes 12292
  82.2 9.7 %collective-permute-start.6 = (f32[32,32]{0,1:T(8,128)S(1)}, f32[32,32]{0,1:T(8,128)}, u32[]{:S(2)}, u32[]{:S(2)}) collective-permute-start(f32[32,32]{0,1:T(8,128)S(1)} %fusion.60), channel_id=1, source_target_pairs={{0,64},{16,80},{32,96},{48,112},{64,0},{80,16},{96,32},{112,48},{1... | collective-permute-start | bytes 12296 | tf_op jit(solution)/shard_map/ppermute | solution.py:15
  89.2 7.0 %copy-start.22 = (f32[32,6]{1,0:T(8,128)S(1)}, f32[32,6]{1,0:T(8,128)}, u32[]{:S(2)}) copy-start(f32[32,6]{1,0:T(8,128)} %copy.185) | copy-start | bytes 2308
  92.9 8.3 %collective-permute-start.9 = (f32[32,32]{0,1:T(8,128)S(1)}, f32[32,32]{0,1:T(8,128)S(1)}, u32[]{:S(2)}, u32[]{:S(2)}) collective-permute-start(f32[32,32]{0,1:T(8,128)S(1)} %fusion.57), channel_id=1, source_target_pairs={{0,128},{128,0},{256,384},{384,256},{512,640},{640,512},{768,896},... | collective-permute-start | bytes 12296 | tf_op jit(solution)/shard_map/ppermute | solution.py:15
  101.4 6.8 %collective-permute-start.10 = (f32[32,32]{0,1:T(8,128)S(1)}, f32[32,32]{0,1:T(8,128)}, u32[]{:S(2)}, u32[]{:S(2)}) collective-permute-start(f32[32,32]{0,1:T(8,128)S(1)} %fusion.54), channel_id=1, source_target_pairs={{0,256},{128,384},{256,0},{384,128},{512,768},{640,896},{768,512},... | collective-permute-start | bytes 12296 | tf_op jit(solution)/shard_map/ppermute | solution.py:15
  109.1 9.8 %copy-start.7 = (f32[32,32]{0,1:T(8,128)S(1)}, f32[32,32]{0,1:T(8,128)}, u32[]{:S(2)}) copy-start(f32[32,32]{0,1:T(8,128)} %copy-done.6) | copy-start | bytes 12292
  109.1 9.8 %copy-start.9 = (f32[32,32]{0,1:T(8,128)S(1)}, f32[32,32]{0,1:T(8,128)}, u32[]{:S(2)}) copy-start(f32[32,32]{0,1:T(8,128)} %copy-done.8) | copy-start | bytes 12292
  109.1 10.9 %copy-start.4 = (f32[32,32,32]{2,1,0:T(8,128)S(1)}, f32[32,32,32]{2,1,0:T(8,128)}, u32[]{:S(2)}) copy-start(f32[32,32,32]{2,1,0:T(8,128)} %fusion.12) | copy-start | bytes 393220
  109.2 9.8 %collective-permute-start.13 = (f32[32,32]{0,1:T(8,128)S(1)}, f32[32,32]{0,1:T(8,128)}, u32[]{:S(2)}, u32[]{:S(2)}) collective-permute-start(f32[32,32]{0,1:T(8,128)S(1)} %fusion.51), channel_id=1, source_target_pairs={{0,512},{128,640},{256,768},{384,896},{512,0},{640,128},{768,256},... | collective-permute-start | bytes 12296 | tf_op jit(solution)/shard_map/ppermute | solution.py:15
  (12 other events, 34.2 us)
